TPU v7x, 32 devices: a whole 2x2x4 slice. The times are simulated.
32 devices in a mesh: grp: 4 (over z), band: 8 (over y, x, core).
Axes of the slice: x: 2, y: 2, z: 4, core: 2. Of those that a mesh axis runs over, the one named last changes fastest.
Arguments:
- orbitals: float32 [18432, 512], P('grp', 'band'), may hold values from -6 to 6
- requests: int32 [32, 6], replicated, may hold values from -1 to 11, as said below
- coulomb: float32 [96, 1536, 1536], P(('grp', 'band')), may hold values from -0.001953125 to 0.001953125
Outputs:
- exchange_rows: float32 [18432, 512], P('grp', 'band')
Inputs may be any that keep to these rules, and one draw needn't show every extreme that they name: `requests`: entries 2q and 2q + 1 of row d are the two blocks of slot q of device d, the first not above the second, or both -1 for an empty slot; every pair of the 12 blocks, a block with itself included, stands in exactly one slot.
All inputs are finite; a program needn't handle non-finite values.
Results may differ from a plain program's by a relative error of at most 0.0003.
Values sent between devices are 32-bit elements; how exact they have to be, the bound alone decides.
No kernel may reach another device: no remote copies, remote signals or barrier semaphores. Data moves between devices by JAX's collectives and lax.ppermute only.
A program may use at most 256 MiB of HBM per device.

v0:
```python
import jax
import jax.numpy as jnp
from jax import lax
from jax.sharding import PartitionSpec as P

BLK = 1536


def slot_work(first_block, second_block, coulomb_tile, diagonal):
    density = jnp.dot(
        first_block,
        second_block.T,
        precision=lax.Precision.HIGHEST,
        preferred_element_type=jnp.float32,
    )
    symmetric = jnp.where(diagonal, 0.5 * (coulomb_tile + coulomb_tile.T), coulomb_tile)
    kernel = density * symmetric
    onto_first = jnp.dot(
        kernel, second_block, precision=lax.Precision.HIGHEST, preferred_element_type=jnp.float32
    )
    onto_second = jnp.dot(
        kernel.T, first_block, precision=lax.Precision.HIGHEST, preferred_element_type=jnp.float32
    )
    onto_second = onto_second * jnp.where(diagonal, 0.0, 1.0)
    return jnp.stack([onto_first, onto_second], 0)


def body(orbitals, requests, coulomb):
    group_count = lax.axis_size("grp")
    band_count = lax.axis_size("band")
    devices = group_count * band_count
    orbital_width = orbitals.shape[1] * band_count
    piece_rows = BLK // devices
    point_rows = lax.all_to_all(orbitals, "band", split_axis=0, concat_axis=1, tiled=True)
    block_count = point_rows.shape[0] // piece_rows
    home_blocks = point_rows.reshape(block_count, piece_rows, orbital_width)
    request_count = requests.shape[1]
    wanted = requests.T
    owner_index = lax.axis_index(("grp", "band"))
    own_pairs = lax.dynamic_index_in_dim(requests, owner_index, 0, keepdims=False).reshape(
        request_count // 2, 2
    )
    diagonal = own_pairs[:, 0] == own_pairs[:, 1]
    live_mask = (wanted >= 0).astype(jnp.float32)
    outgoing = jnp.take(home_blocks, jnp.maximum(wanted, 0), axis=0) * live_mask[:, :, None, None]
    arrived = lax.all_to_all(outgoing, ("grp", "band"), split_axis=1, concat_axis=1, tiled=True)
    fetched = arrived.reshape(request_count // 2, 2, BLK, orbital_width)

    def per_slot(slot_item):
        pair_rows, coulomb_tile, diag_flag = slot_item
        return slot_work(pair_rows[0], pair_rows[1], coulomb_tile, diag_flag)

    results = lax.map(per_slot, (fetched, coulomb, diagonal))
    outbound = results.reshape(request_count, devices, piece_rows, orbital_width)
    returned = lax.all_to_all(outbound, ("grp", "band"), split_axis=1, concat_axis=1, tiled=True)
    one_hot = (
        wanted[:, :, None] == jnp.arange(block_count, dtype=jnp.int32)[None, None, :]
    ).astype(jnp.float32)
    summed = jnp.einsum("rdk,rdpx->kpx", one_hot, returned, precision=lax.Precision.HIGHEST)
    home_rows = summed.reshape(block_count * piece_rows, orbital_width)
    return lax.all_to_all(home_rows, "band", split_axis=1, concat_axis=0, tiled=True)


def solution(mesh):
    placed = (P("grp", "band"), P(), P(("grp", "band"), None, None))
    return jax.shard_map(
        body, mesh=mesh, in_specs=placed, out_specs=P("grp", "band"), check_vma=False
    )
```

profile of v0, /device:TPU:2, one launch (start us, length us, event | category | flops | bytes accessed | tf_op | source)
XLA Modules:
  0.0 1197.3 jit_solution(6529304943499796162)
XLA Ops:
  0.0 1.7 all_to_all.32
  1.7 1.3 copy.38
  3.0 4.3 all-to-all-start
  7.3 0.7 broadcast_compare_fusion
  8.0 0.1 copy.41
  8.1 0.7 copy.37
  8.7 0.7 broadcast_maximum_fusion
  9.4 0.1 reshape.40
  9.5 0.6 pad_clamp_fusion
  10.1 13.9 %all-to-all-done = f32[8,576,64]{1,2,0:T(8,128)S(1)} async-done(((f32[8,576,64]{1,2,0:T(8,128)}), f32[8,576,64]{1,2,0:T(8,128)S(1)}, u32[]{:S(2)}, u32[]{:S(2)}) %all-to-all-start) | async-done | bytes 1179680 | tf_op jit(solution)/shard_map/all_to_all | solution.py:34
  24.0 0.0 copy-start.1
  24.0 1.1 copy-done.1
  25.1 2.3 copy.39
  27.4 0.5 reshape.34
  27.9 0.0 copy-start.4
  27.9 8.4 gather_fusion
  36.3 0.0 copy-done.4
  36.3 13.8 %fusion.9 = f32[6,32,48,512]{3,2,0,1:T(8,128)} fusion(f32[6,32,48,512]{3,2,1,0:T(8,128)} %bitcast.78, f32[6,32]{0,1:T(8,128)S(1)} %copy.41, pred[6,32]{0,1:T(8,128)(4,1)S(1)} %copy-done.4), kind=kLoop, calls=%fused_computation.19 | loop fusion | flops 9437184 | bytes 37749696 | tf_op jit(solution)/shard_map/mul | solution.py:45
  50.1 5.3 all-to-all-start.1
  55.4 0.0 copy-done.2
  55.4 0.2 dynamic-slice_reduce_fusion
  55.6 0.1 reshape.36
  55.7 0.2 fusion.16
  55.9 408.5 %all-to-all-done.1 = f32[6,32,48,512]{3,2,0,1:T(8,128)} async-done(((f32[6,32,48,512]{3,2,0,1:T(8,128)}), f32[6,32,48,512]{3,2,0,1:T(8,128)}, u32[]{:S(2)}, u32[]{:S(2)}) %all-to-all-start.1) | async-done | bytes 18874400 | tf_op jit(solution)/shard_map/all_to_all | solution.py:46
  464.4 13.5 %copy.42 = f32[6,32,48,512]{3,2,1,0:T(8,128)} copy(f32[6,32,48,512]{3,2,0,1:T(8,128)} %all-to-all-done.1) | data formatting | bytes 37748736 | tf_op jit(solution)/shard_map/all_to_all | solution.py:46
  477.9 251.0 %while.10 = (s32[]{:T(128)}, f32[3,2,1536,512]{3,2,1,0:T(8,128)}, f32[3,2,1536,512]{3,2,1,0:T(8,128)}, pred[3]{0:T(512)(128)(4,1)S(1)}, f32[3,1536,1536]{2,1,0:T...) while((s32[]{:T(128)}, f32[3,2,1536,512]{3,2,1,0:T(8,128)}, ...), condition=%wide.region_1.2_spmd, body=%wide.region_0.1_spmd.sunk | while | flops 43498340352 | bytes 154144448 | solution.py:53
  477.9 8.1 dynamic-slice_bitcast_fusion.16
  486.0 9.6 copy.57
  495.6 0.6 dynamic_slice.26
  496.2 22.4 %convolution_multiply_fusion.3 = f32[1536,1536]{1,0:T(8,128)S(1)} fusion(f32[1536,1536]{0,1:T(8,128)} %copy.57, pred[]{:T(512)} %bitcast.76, f32[3,2,1536,512]{3,2,1,0:T(8,128)} %get-tuple-element.98, s32[]{:T(128)} %get-tuple-element.86, s32[]{:T(128)S(6)} %add.34, f32[3,1536,1536]{2,1,0:T(8,128)} %get-tuple-element.100), kind=kOutput, calls=%fused_computation.1.clone.1 | convolution fusion | flops 14504951808 | bytes 34605060 | tf_op jit(solution)/shard_map/while/body/eval_jaxpr/dot_general | solution.py:10
  518.6 0.0 copy-start
  518.6 3.6 copy-done
  522.2 17.0 %convolution_bitcast_fusion.2 = f32[1,1536,512]{2,1,0:T(8,128)S(1)} fusion(f32[1536,1536]{1,0:T(8,128)S(1)} %convolution_multiply_fusion.3, f32[3,2,1536,512]{3,2,1,0:T(8,128)} %get-tuple-element.98, s32[]{:T(128)} %get-tuple-element.86, s32[]{:T(128)S(6)} %add.34), kind=kOutput, calls=%fused_computation.10.clone.1 | convolution fusion | flops 14495514624 | bytes 15729156 | tf_op jit(solution)/shard_map/while/body/eval_jaxpr/dot_general | solution.py:18
  539.8 18.4 %fusion.25 = f32[1,1536,512]{2,1,0:T(8,128)S(1)} fusion(f32[1536,1536]{1,0:T(8,128)} %copy-done, f32[3,2,1536,512]{3,2,1,0:T(8,128)} %get-tuple-element.98, s32[]{:T(128)} %get-tuple-element.86, f32[]{:T(128)S(6)} %select_n.37), kind=kOutput, calls=%fused_computation.9.clone.1 | convolution fusion | flops 14496301056 | bytes 15729156 | tf_op jit(solution)/shard_map/while/body/eval_jaxpr/dot_general | solution.py:21
  558.2 3.3 fusion.26
  561.5 8.1 dynamic-slice_bitcast_fusion.16
  569.6 9.6 copy.57
  579.2 0.6 dynamic_slice.26
  579.8 22.4 %convolution_multiply_fusion.3 = f32[1536,1536]{1,0:T(8,128)S(1)} fusion(f32[1536,1536]{0,1:T(8,128)} %copy.57, pred[]{:T(512)} %bitcast.76, f32[3,2,1536,512]{3,2,1,0:T(8,128)} %get-tuple-element.98, s32[]{:T(128)} %get-tuple-element.86, s32[]{:T(128)S(6)} %add.34, f32[3,1536,1536]{2,1,0:T(8,128)} %get-tuple-element.100), kind=kOutput, calls=%fused_computation.1.clone.1 | convolution fusion | flops 14504951808 | bytes 34605060 | tf_op jit(solution)/shard_map/while/body/eval_jaxpr/dot_general | solution.py:10
  602.2 0.0 copy-start
  602.2 3.6 copy-done
  605.8 17.0 %convolution_bitcast_fusion.2 = f32[1,1536,512]{2,1,0:T(8,128)S(1)} fusion(f32[1536,1536]{1,0:T(8,128)S(1)} %convolution_multiply_fusion.3, f32[3,2,1536,512]{3,2,1,0:T(8,128)} %get-tuple-element.98, s32[]{:T(128)} %get-tuple-element.86, s32[]{:T(128)S(6)} %add.34), kind=kOutput, calls=%fused_computation.10.clone.1 | convolution fusion | flops 14495514624 | bytes 15729156 | tf_op jit(solution)/shard_map/while/body/eval_jaxpr/dot_general | solution.py:18
  623.4 18.4 %fusion.25 = f32[1,1536,512]{2,1,0:T(8,128)S(1)} fusion(f32[1536,1536]{1,0:T(8,128)} %copy-done, f32[3,2,1536,512]{3,2,1,0:T(8,128)} %get-tuple-element.98, s32[]{:T(128)} %get-tuple-element.86, f32[]{:T(128)S(6)} %select_n.37), kind=kOutput, calls=%fused_computation.9.clone.1 | convolution fusion | flops 14496301056 | bytes 15729156 | tf_op jit(solution)/shard_map/while/body/eval_jaxpr/dot_general | solution.py:21
  641.8 3.4 fusion.26
  645.2 8.1 dynamic-slice_bitcast_fusion.16
  653.3 9.6 copy.57
  662.9 0.6 dynamic_slice.26
  663.5 22.4 %convolution_multiply_fusion.3 = f32[1536,1536]{1,0:T(8,128)S(1)} fusion(f32[1536,1536]{0,1:T(8,128)} %copy.57, pred[]{:T(512)} %bitcast.76, f32[3,2,1536,512]{3,2,1,0:T(8,128)} %get-tuple-element.98, s32[]{:T(128)} %get-tuple-element.86, s32[]{:T(128)S(6)} %add.34, f32[3,1536,1536]{2,1,0:T(8,128)} %get-tuple-element.100), kind=kOutput, calls=%fused_computation.1.clone.1 | convolution fusion | flops 14504951808 | bytes 34605060 | tf_op jit(solution)/shard_map/while/body/eval_jaxpr/dot_general | solution.py:10
  685.9 0.0 copy-start
  685.9 3.6 copy-done
  689.5 17.0 %convolution_bitcast_fusion.2 = f32[1,1536,512]{2,1,0:T(8,128)S(1)} fusion(f32[1536,1536]{1,0:T(8,128)S(1)} %convolution_multiply_fusion.3, f32[3,2,1536,512]{3,2,1,0:T(8,128)} %get-tuple-element.98, s32[]{:T(128)} %get-tuple-element.86, s32[]{:T(128)S(6)} %add.34), kind=kOutput, calls=%fused_computation.10.clone.1 | convolution fusion | flops 14495514624 | bytes 15729156 | tf_op jit(solution)/shard_map/while/body/eval_jaxpr/dot_general | solution.py:18
  707.1 18.4 %fusion.25 = f32[1,1536,512]{2,1,0:T(8,128)S(1)} fusion(f32[1536,1536]{1,0:T(8,128)} %copy-done, f32[3,2,1536,512]{3,2,1,0:T(8,128)} %get-tuple-element.98, s32[]{:T(128)} %get-tuple-element.86, f32[]{:T(128)S(6)} %select_n.37), kind=kOutput, calls=%fused_computation.9.clone.1 | convolution fusion | flops 14496301056 | bytes 15729156 | tf_op jit(solution)/shard_map/while/body/eval_jaxpr/dot_general | solution.py:21
  725.5 3.4 fusion.26
  728.9 8.2 copy.43
  737.1 0.0 copy-start.3
  737.1 420.8 %all_to_all.45 = f32[6,32,48,512]{3,2,0,1:T(8,128)S(1)} all-to-all(f32[6,32,48,512]{3,2,0,1:T(8,128)S(1)} %copy.43), channel_id=1, replica_groups=mesh['grp'=4,'band'=8] {'grp','band'}, dimensions={1} | all-to-all | bytes 37748736 | tf_op jit(solution)/shard_map/all_to_all | solution.py:55
  1157.9 0.0 copy-done.3
  1157.9 13.5 %fusion.10 = f32[12,48,512]{2,0,1:T(8,128)S(1)} fusion(f32[6,32,48,512]{3,2,0,1:T(8,128)S(1)} %all_to_all.45, s32[6,32]{1,0:T(8,128)S(1)} %bitcast.82), kind=kOutput, calls=%fused_computation.20 | convolution fusion | flops 679479552 | bytes 20054784 | tf_op jit(solution)/shard_map/rdk,rdpx->kpx/dot_general | solution.py:59
  1171.4 0.7 copy.45
  1172.1 0.5 all_to_all.37
  1172.6 2.0 copy.46
  1174.6 20.7 %all_to_all.46 = f32[576,8,64]{0,2,1:T(8,128)S(1)} all-to-all(f32[576,8,64]{0,2,1:T(8,128)} %copy.46), channel_id=1, replica_groups=mesh['grp'=4,'band'=8] {'band'}, dimensions={1} | all-to-all | bytes 2359296 | tf_op jit(solution)/shard_map/all_to_all | solution.py:61
  1195.2 0.8 copy.47
  1196.0 1.3 all_to_all.40
  (2 shorter events, 0.0 us)
Async XLA Ops:
  3.0 21.0 %all-to-all-start = ((f32[8,576,64]{1,2,0:T(8,128)}), f32[8,576,64]{1,2,0:T(8,128)S(1)}, u32[]{:S(2)}, u32[]{:S(2)}) async-start(f32[8,576,64]{1,2,0:T(8,128)} %copy.38), calls=%async_computation | async-start | bytes 2621440 | tf_op jit(solution)/shard_map/all_to_all | solution.py:34
  24.0 1.1 copy-start.1
  27.9 8.4 copy-start.4
  50.1 5.3 copy-start.2
  50.1 414.3 %all-to-all-start.1 = ((f32[6,32,48,512]{3,2,0,1:T(8,128)}), f32[6,32,48,512]{3,2,0,1:T(8,128)}, u32[]{:S(2)}, u32[]{:S(2)}) async-start(f32[6,32,48,512]{3,2,0,1:T(8,128)} %fusion.9), calls=%async_computation.1 | async-start | bytes 37748736 | tf_op jit(solution)/shard_map/all_to_all | solution.py:46
  518.6 3.6 copy-start
  602.2 3.6 copy-start
  685.9 3.6 copy-start
  737.1 420.8 %copy-start.3 = (s32[32,6]{0,1:T(8,128)S(1)}, s32[32,6]{0,1:T(8,128)}, u32[]{:S(2)}) copy-start(s32[32,6]{0,1:T(8,128)} %param.6) | copy-start | bytes 2308
where the time goes:
time: 1200 us
  blocking collectives  441 us (37%)
  waiting for transfers between devices  422 us (35%)
  matrix products  187 us (16%)
  local copies, waits for them, and re-layouts  109 us (9%)
  other arithmetic  26.1 us (2%)
    all_to_all x1, blocking collectives, body(): lax.all_to_all(outbound, ('grp', 'band'), split_axis=1, concat_axis=1, ti...  421 us
    all_to_all x1, waiting for transfers between devices, body(): lax.all_to_all(outgoing, ('grp', 'band'), split_axis=1, concat_axis=1, ti...  409 us
    dot_general x3, matrix products, slot_work(): jnp.dot(first_block, second_block.T, precision=lax.Precision.HIGHEST, pre...  67.3 us
    dot_general x3, matrix products, slot_work(): jnp.dot(kernel.T, first_block, precision=lax.Precision.HIGHEST, preferred...  55.2 us
    squeeze x6, local copies, waits for them, and re-layouts, body(): results = lax.map(per_slot, (fetched, coulomb, diagonal))  53.1 us
    dot_general x3, matrix products, slot_work(): jnp.dot(kernel, second_block, precision=lax.Precision.HIGHEST, preferred_...  51 us
  transfers between devices with their start and end apart: 2, of which 2 were waited for; matrix products, arithmetic and copies ran while one was open for 0% of the time, Pallas kernels for 0%

commit v1 on v0

v1 whole, which is shorter than its diff:
```python
import jax
import jax.numpy as jnp
from jax import lax
from jax.sharding import PartitionSpec as P


def slot_work(first_block, second_block, coulomb_tile, diagonal):
    density = jnp.dot(
        first_block,
        second_block.T,
        precision=lax.Precision.HIGHEST,
        preferred_element_type=jnp.float32,
    )
    symmetric = jnp.where(diagonal, 0.5 * (coulomb_tile + coulomb_tile.T), coulomb_tile)
    kernel = density * symmetric
    onto_first = jnp.dot(
        kernel, second_block, precision=lax.Precision.HIGHEST, preferred_element_type=jnp.float32
    )
    onto_second = jnp.dot(
        kernel.T, first_block, precision=lax.Precision.HIGHEST, preferred_element_type=jnp.float32
    )
    onto_second = onto_second * jnp.where(diagonal, 0.0, 1.0)
    return jnp.stack([onto_first, onto_second], 0)


def body(orbitals, requests, coulomb):
    group_count = lax.axis_size("grp")
    band_count = lax.axis_size("band")
    devices = group_count * band_count
    blk = coulomb.shape[1]
    col_width = orbitals.shape[1]
    orbital_width = col_width * band_count
    piece_rows = blk // devices
    all_points = lax.all_gather(orbitals, "grp", axis=0, tiled=True)
    block_count = all_points.shape[0] // (devices * piece_rows)
    blocks = (
        all_points.reshape(devices, block_count, piece_rows, col_width)
        .transpose(1, 0, 2, 3)
        .reshape(block_count, blk, col_width)
    )
    request_count = requests.shape[1]
    group_index = lax.axis_index("grp")
    band_index = lax.axis_index("band")
    group_requests = lax.dynamic_slice_in_dim(requests, group_index * band_count, band_count, 0)
    live = (group_requests >= 0).astype(jnp.float32)
    outgoing = jnp.take(blocks, jnp.maximum(group_requests, 0), axis=0) * live[:, :, None, None]
    arrived = lax.all_to_all(outgoing, "band", split_axis=0, concat_axis=0, tiled=True)
    fetched = arrived.transpose(1, 2, 0, 3).reshape(request_count // 2, 2, blk, orbital_width)
    own_pairs = lax.dynamic_index_in_dim(group_requests, band_index, 0, keepdims=False).reshape(
        request_count // 2, 2
    )
    diagonal = own_pairs[:, 0] == own_pairs[:, 1]

    def per_slot(slot_item):
        pair_rows, coulomb_tile, diag_flag = slot_item
        return slot_work(pair_rows[0], pair_rows[1], coulomb_tile, diag_flag)

    results = lax.map(per_slot, (fetched, coulomb, diagonal))
    outbound = results.reshape(request_count, blk, band_count, col_width).transpose(2, 0, 1, 3)
    returned = lax.all_to_all(outbound, "band", split_axis=0, concat_axis=0, tiled=True)
    one_hot = (
        group_requests[:, :, None] == jnp.arange(block_count, dtype=jnp.int32)[None, None, :]
    ).astype(jnp.float32)
    summed = jnp.einsum("srk,srpc->kpc", one_hot, returned, precision=lax.Precision.HIGHEST)
    summed = summed.reshape(block_count, group_count, band_count, piece_rows, col_width)
    mine = lax.psum_scatter(summed, "grp", scatter_dimension=1, tiled=True)
    mine = mine.reshape(block_count, band_count, piece_rows, col_width).transpose(1, 0, 2, 3)
    return mine.reshape(band_count * block_count * piece_rows, col_width)


def solution(mesh):
    placed = (P("grp", "band"), P(), P(("grp", "band"), None, None))
    return jax.shard_map(
        body, mesh=mesh, in_specs=placed, out_specs=P("grp", "band"), check_vma=False
    )
```

time: 1200 us -> 1250 us (1.042)
  blocking collectives: 441 us -> 211 us
  waiting for transfers between devices: 422 us -> 530 us
  local copies, waits for them, and re-layouts: 109 us -> 196 us
  matrix products: 187 us -> 233 us
  loops' own time: 1.8 us -> 29 us
  between operations: 0.11 us -> 13.6 us
    all_to_all x2 -> x1, blocking collectives: 441 us -> 211 us  [body(): lax.all_to_all(outbound, 'band', split_axis=0, concat_axis=0, tiled=True)]
    all_to_all x2 -> x1, waiting for transfers between devices: 422 us -> 205 us  [body(): lax.all_to_all(outgoing, 'band', split_axis=0, concat_axis=0, tiled=True)]
    all_gather x0 -> x1, waiting for transfers between devices: none -> 167 us  [body(): all_points = lax.all_gather(orbitals, 'grp', axis=0, tiled=True)]
    reduce_scatter x0 -> x1, waiting for transfers between devices: none -> 159 us  [body(): mine = lax.psum_scatter(summed, 'grp', scatter_dimension=1, tiled=True)]
    dot_general x3, matrix products: 55.2 us -> 98.7 us  [slot_work(): jnp.dot(kernel.T, first_block, precision=lax.Precision.HIGHEST, preferred...]
    transpose x0 -> x4, local copies, waits for them, and re-layouts: none -> 39.1 us  [the longest x1 12.6 us: body(): results.reshape(request_count, blk, band_count, col_width)]
    dynamic_update_slice x0 -> x6, local copies, waits for them, and re-layouts: none -> 37.4 us  [body(): results = lax.map(per_slot, (fetched, coulomb, diagonal))]
    reshape x3 -> x5, local copies, waits for them, and re-layouts: 8.8 us -> 38.1 us  [the longest x2 23.3 us: body(): summed.reshape(block_count, group_count, band_count, piece_rows, col_width)]
  transfers between devices with their start and end apart: 2 -> 3, of which waited for: 2 -> 3; matrix products, arithmetic and copies ran while one was open for 0% -> 0% of each run, Pallas kernels for 0% -> 0%
where the time goes in v1:
time: 1250 us; the launch traced here: 1240 us
  waiting for transfers between devices  530 us (42%)
  matrix products  233 us (19%)
  blocking collectives  211 us (17%)
  local copies, waits for them, and re-layouts  196 us (16%)
  loops' own time  29 us (2%)
  other arithmetic  24 us (2%)
  between operations  13.6 us (1%)
    all_to_all x1, blocking collectives, body(): lax.all_to_all(outbound, 'band', split_axis=0, concat_axis=0, tiled=True)  211 us
    all_to_all x1, waiting for transfers between devices, body(): lax.all_to_all(outgoing, 'band', split_axis=0, concat_axis=0, tiled=True)  205 us
    all_gather x1, waiting for transfers between devices, body(): all_points = lax.all_gather(orbitals, 'grp', axis=0, tiled=True)  167 us
    reduce_scatter x1, waiting for transfers between devices, body(): mine = lax.psum_scatter(summed, 'grp', scatter_dimension=1, tiled=True)  159 us
    dot_general x3, matrix products, slot_work(): jnp.dot(kernel.T, first_block, precision=lax.Precision.HIGHEST, preferred...  98.7 us
    dot_general x3, matrix products, slot_work(): jnp.dot(first_block, second_block.T, precision=lax.Precision.HIGHEST, pre...  68 us
    squeeze x6, local copies, waits for them, and re-layouts, body(): results = lax.map(per_slot, (fetched, coulomb, diagonal))  53.1 us
    dot_general x3, matrix products, slot_work(): jnp.dot(kernel, second_block, precision=lax.Precision.HIGHEST, preferred_...  51.1 us
  transfers between devices with their start and end apart: 3, of which 3 were waited for; matrix products, arithmetic and copies ran while one was open for 0% of the time, Pallas kernels for 0%

profile of v1, /device:TPU:2, one launch (start us, length us, event | category | flops | bytes accessed | tf_op | source)
XLA Modules:
  0.0 1243.5 jit_solution(937388461470944513)
XLA Ops:
  6.5 0.0 all-gather.2.cloned.1.call-start
  6.5 2.9 copy.37
  9.4 0.0 all-gather.2.cloned.1.call-update
  9.4 0.8 broadcast_compare_fusion
  10.2 0.1 copy.39
  10.3 0.1 reshape.47
  10.4 0.1 copy.40
  10.4 0.1 copy.36
  10.6 167.0 %all-gather.2.cloned.1.call-done = f32[18432,64]{1,0:T(8,128)} async-done(((f32[4608,64]{1,0:T(8,128)}), f32[18432,64]{1,0:T(8,128)}) %all-gather.2.cloned.1.call-update) | async-done | bytes 4718608 | tf_op jit(solution)/shard_map/all_gather | solution.py:34
  177.6 12.0 copy.38
  189.6 0.0 copy-done.1
  189.6 13.1 %reshape.38 = f32[12,1536,64]{1,2,0:T(8,128)} reshape(f32[12,32,48,64]{2,1,3,0:T(8,128)} %copy.38) | data formatting | bytes 9437184 | tf_op jit(solution)/shard_map/reshape | solution.py:39
  202.7 12.7 %gather_fusion = f32[48,1536,64]{1,2,0:T(8,128)} fusion(f32[12,1536,64]{1,2,0:T(8,128)} %reshape.38, s32[1024]{0:T(1024)S(1)} %pad_clamp_fusion), kind=kCustom, calls=%fused_computation | custom fusion | bytes 37748928 | tf_op jit(solution)/shard_map/jit(_take)/gather | solution.py:46
  215.4 13.2 %select_multiply_fusion = f32[8,6,1536,64]{2,3,1,0:T(8,128)} fusion(f32[8,6,1536,64]{2,3,1,0:T(8,128)} %bitcast.84, f32[8,6]{1,0:T(8,128)S(1)} %copy.40, pred[8,6]{1,0:T(8,128)(4,1)S(1)} %copy.36), kind=kLoop, calls=%fused_computation.18 | loop fusion | flops 9437184 | bytes 37748976 | tf_op jit(solution)/shard_map/mul | solution.py:46
  228.6 6.5 all-to-all-start
  235.1 0.0 reduce-scatter.2.cloned.1.call-start
  235.1 0.0 copy-done.3
  235.1 0.2 dynamic-slice_reduce_fusion
  235.2 0.1 reshape.40
  235.3 0.2 fusion.14
  235.5 204.6 %all-to-all-done = f32[8,6,1536,64]{2,3,1,0:T(8,128)} async-done(((f32[8,6,1536,64]{2,3,1,0:T(8,128)}), f32[8,6,1536,64]{2,3,1,0:T(8,128)}, u32[]{:S(2)}, u32[]{:S(2)}) %all-to-all-start) | async-done | bytes 18874400 | tf_op jit(solution)/shard_map/all_to_all | solution.py:47
  440.1 12.6 %copy.41 = f32[6,1536,8,64]{1,3,2,0:T(8,128)} copy(f32[6,1536,8,64]{1,3,0,2:T(8,128)} %bitcast.12) | data formatting | bytes 37748736 | tf_op jit(solution)/shard_map/transpose | solution.py:48
  452.7 359.6 %while.10 = (s32[]{:T(128)}, f32[3,2,1536,512]{2,3,1,0:T(8,128)}, f32[3,2,1536,512]{2,3,1,0:T(8,128)}, pred[3]{0:T(512)(128)(4,1)S(1)}, f32[3,1536,1536]{2,1,0:T...) while((s32[]{:T(128)}, f32[3,2,1536,512]{2,3,1,0:T(8,128)}, ...), condition=%wide.region_1.2_spmd, body=%wide.region_0.1_spmd.sunk | while | flops 43498340352 | bytes 179310272 | solution.py:58
  473.0 8.1 dynamic-slice_bitcast_fusion.16
  481.0 9.6 copy.64
  490.7 0.6 dynamic_slice.36
  491.3 22.7 %convolution_multiply_fusion.3 = f32[1536,1536]{1,0:T(8,128)S(1)} fusion(f32[1536,1536]{0,1:T(8,128)} %copy.64, pred[]{:T(512)} %bitcast.83, f32[3,2,1536,512]{2,3,1,0:T(8,128)} %get-tuple-element.113, s32[]{:T(128)} %get-tuple-element.101, s32[]{:T(128)S(6)} %add.38, f32[3,1536,1536]{2,1,0:T(8,128)} %get-tuple-element.115), kind=kOutput, calls=%fused_computation.1.clone.1 | convolution fusion | flops 14504951808 | bytes 34605060 | tf_op jit(solution)/shard_map/while/body/eval_jaxpr/dot_general | solution.py:8
  513.9 0.0 copy-start
  513.9 3.6 copy-done
  517.5 17.0 %convolution_bitcast_fusion.2 = f32[1,1536,512]{2,1,0:T(8,128)S(1)} fusion(f32[1536,1536]{1,0:T(8,128)S(1)} %convolution_multiply_fusion.3, f32[3,2,1536,512]{2,3,1,0:T(8,128)} %get-tuple-element.113, s32[]{:T(128)} %get-tuple-element.101, s32[]{:T(128)S(6)} %add.38), kind=kOutput, calls=%fused_computation.9.clone.1 | convolution fusion | flops 14495514624 | bytes 15729156 | tf_op jit(solution)/shard_map/while/body/eval_jaxpr/dot_general | solution.py:16
  535.1 32.9 %fusion.22 = f32[1,1536,512]{2,1,0:T(8,128)S(1)} fusion(f32[1536,1536]{1,0:T(8,128)} %copy-done, f32[3,2,1536,512]{2,3,1,0:T(8,128)} %get-tuple-element.113, s32[]{:T(128)} %get-tuple-element.101, f32[]{:T(128)S(6)} %select_n.45), kind=kOutput, calls=%fused_computation.8.clone.1 | convolution fusion | flops 14496301056 | bytes 15729156 | tf_op jit(solution)/shard_map/while/body/eval_jaxpr/dot_general | solution.py:19
  568.0 3.3 maximum_bitcast_fusion.2
  571.3 6.6 copy.65
  577.9 5.8 constant_dynamic-update-slice_fusion.2
  583.7 8.1 dynamic-slice_bitcast_fusion.16
  591.8 9.6 copy.64
  601.4 0.6 dynamic_slice.36
  602.0 22.7 %convolution_multiply_fusion.3 = f32[1536,1536]{1,0:T(8,128)S(1)} fusion(f32[1536,1536]{0,1:T(8,128)} %copy.64, pred[]{:T(512)} %bitcast.83, f32[3,2,1536,512]{2,3,1,0:T(8,128)} %get-tuple-element.113, s32[]{:T(128)} %get-tuple-element.101, s32[]{:T(128)S(6)} %add.38, f32[3,1536,1536]{2,1,0:T(8,128)} %get-tuple-element.115), kind=kOutput, calls=%fused_computation.1.clone.1 | convolution fusion | flops 14504951808 | bytes 34605060 | tf_op jit(solution)/shard_map/while/body/eval_jaxpr/dot_general | solution.py:8
  624.7 3.6 copy-done
  628.3 17.0 %convolution_bitcast_fusion.2 = f32[1,1536,512]{2,1,0:T(8,128)S(1)} fusion(f32[1536,1536]{1,0:T(8,128)S(1)} %convolution_multiply_fusion.3, f32[3,2,1536,512]{2,3,1,0:T(8,128)} %get-tuple-element.113, s32[]{:T(128)} %get-tuple-element.101, s32[]{:T(128)S(6)} %add.38), kind=kOutput, calls=%fused_computation.9.clone.1 | convolution fusion | flops 14495514624 | bytes 15729156 | tf_op jit(solution)/shard_map/while/body/eval_jaxpr/dot_general | solution.py:16
  645.8 32.9 %fusion.22 = f32[1,1536,512]{2,1,0:T(8,128)S(1)} fusion(f32[1536,1536]{1,0:T(8,128)} %copy-done, f32[3,2,1536,512]{2,3,1,0:T(8,128)} %get-tuple-element.113, s32[]{:T(128)} %get-tuple-element.101, f32[]{:T(128)S(6)} %select_n.45), kind=kOutput, calls=%fused_computation.8.clone.1 | convolution fusion | flops 14496301056 | bytes 15729156 | tf_op jit(solution)/shard_map/while/body/eval_jaxpr/dot_general | solution.py:19
  678.8 3.3 maximum_bitcast_fusion.2
  682.0 6.6 copy.65
  688.6 5.9 constant_dynamic-update-slice_fusion.2
  694.6 8.1 dynamic-slice_bitcast_fusion.16
  702.6 9.6 copy.64
  712.2 0.6 dynamic_slice.36
  712.8 22.7 %convolution_multiply_fusion.3 = f32[1536,1536]{1,0:T(8,128)S(1)} fusion(f32[1536,1536]{0,1:T(8,128)} %copy.64, pred[]{:T(512)} %bitcast.83, f32[3,2,1536,512]{2,3,1,0:T(8,128)} %get-tuple-element.113, s32[]{:T(128)} %get-tuple-element.101, s32[]{:T(128)S(6)} %add.38, f32[3,1536,1536]{2,1,0:T(8,128)} %get-tuple-element.115), kind=kOutput, calls=%fused_computation.1.clone.1 | convolution fusion | flops 14504951808 | bytes 34605060 | tf_op jit(solution)/shard_map/while/body/eval_jaxpr/dot_general | solution.py:8
  735.5 3.6 copy-done
  739.1 17.0 %convolution_bitcast_fusion.2 = f32[1,1536,512]{2,1,0:T(8,128)S(1)} fusion(f32[1536,1536]{1,0:T(8,128)S(1)} %convolution_multiply_fusion.3, f32[3,2,1536,512]{2,3,1,0:T(8,128)} %get-tuple-element.113, s32[]{:T(128)} %get-tuple-element.101, s32[]{:T(128)S(6)} %add.38), kind=kOutput, calls=%fused_computation.9.clone.1 | convolution fusion | flops 14495514624 | bytes 15729156 | tf_op jit(solution)/shard_map/while/body/eval_jaxpr/dot_general | solution.py:16
  756.7 32.9 %fusion.22 = f32[1,1536,512]{2,1,0:T(8,128)S(1)} fusion(f32[1536,1536]{1,0:T(8,128)} %copy-done, f32[3,2,1536,512]{2,3,1,0:T(8,128)} %get-tuple-element.113, s32[]{:T(128)} %get-tuple-element.101, f32[]{:T(128)S(6)} %select_n.45), kind=kOutput, calls=%fused_computation.8.clone.1 | convolution fusion | flops 14496301056 | bytes 15729156 | tf_op jit(solution)/shard_map/while/body/eval_jaxpr/dot_general | solution.py:19
  789.6 3.3 maximum_bitcast_fusion.2
  792.9 6.6 copy.65
  799.4 5.9 constant_dynamic-update-slice_fusion.2
  812.3 12.6 %copy.44 = f32[8,6,1536,64]{2,3,1,0:T(8,128)} copy(f32[8,6,1536,64]{2,3,0,1:T(8,128)} %bitcast.86) | data formatting | bytes 37748736 | tf_op jit(solution)/shard_map/transpose | solution.py:59
  824.9 210.8 %all_to_all.10 = f32[8,6,1536,64]{2,3,1,0:T(8,128)S(1)} all-to-all(f32[8,6,1536,64]{2,3,1,0:T(8,128)} %copy.44), channel_id=1, replica_groups=mesh['grp'=4,'band'=8] {'band'}, dimensions={0} | all-to-all | bytes 37748736 | tf_op jit(solution)/shard_map/all_to_all | solution.py:60
  1035.6 0.0 copy-done.2
  1035.6 15.3 %fusion.8 = f32[12,1536,64]{1,0,2:T(8,128)} fusion(f32[8,6,1536,64]{2,3,1,0:T(8,128)S(1)} %all_to_all.10, s32[8,6]{0,1:T(8,128)S(1)} %copy-done.2), kind=kOutput, calls=%fused_computation.19 | convolution fusion | flops 679477824 | bytes 23593152 | tf_op jit(solution)/shard_map/srk,srpc->kpc/dot_general | solution.py:64
  1050.9 11.0 reshape.57
  1061.9 12.2 copy.47
  1074.2 0.0 reduce-scatter.2.cloned.1.call-update
  1074.2 158.7 %reduce-scatter.2.cloned.1.call-done = f32[12,1,8,48,64]{4,3,2,0,1:T(8,128)} async-done(((f32[12,4,8,48,64]{4,3,2,0,1:T(8,128)}), f32[12,1,8,48,64]{4,3,2,0,1:T(8,128)}) %reduce-scatter.2.cloned.1.call-update) | async-done | bytes 1179664 | tf_op jit(solution)/shard_map/reduce_scatter | solution.py:66
  1232.9 1.9 copy.48
  1234.8 1.7 copy.49
  (9 shorter events, 0.0 us)
Async XLA Ops:
  6.5 171.0 %all-gather.2.cloned.1.call-start = ((), (), s32[]{:S(2)}) async-start(), calls=%async_computation.3 | async-start | bytes 11796480 | tf_op jit(solution)/shard_map/all_gather | solution.py:34
  10.2 179.4 %copy-start.1 = (s32[8,6]{0,1:T(8,128)}, s32[8,6]{0,1:T(8,128)S(1)}, u32[]{:S(2)}) copy-start(s32[8,6]{0,1:T(8,128)S(1)} %get-tuple-element.59) | copy-start | bytes 580
  228.6 6.5 copy-start.3
  228.6 211.5 %all-to-all-start = ((f32[8,6,1536,64]{2,3,1,0:T(8,128)}), f32[8,6,1536,64]{2,3,1,0:T(8,128)}, u32[]{:S(2)}, u32[]{:S(2)}) async-start(f32[8,6,1536,64]{2,3,1,0:T(8,128)} %select_multiply_fusion), calls=%async_computation | async-start | bytes 37748736 | tf_op jit(solution)/shard_map/all_to_all | solution.py:47
  235.1 997.8 %reduce-scatter.2.cloned.1.call-start = ((), (), s32[]{:S(2)}) async-start(), calls=%async_computation.4 | async-start | bytes 11796480 | tf_op jit(solution)/shard_map/reduce_scatter | solution.py:66
  513.9 3.6 copy-start
  624.7 3.6 copy-start
  735.5 3.6 copy-start
  824.9 210.8 %copy-start.2 = (s32[8,6]{0,1:T(8,128)S(1)}, s32[8,6]{0,1:T(8,128)}, u32[]{:S(2)}) copy-start(s32[8,6]{0,1:T(8,128)} %copy-done.1) | copy-start | bytes 580
Sparse Core Ops, SparseCore 0:
  9.5 167.9 all-gather.1
  1074.3 158.5 reduce-scatter.1

commit v2 on v1

v2 whole, which is shorter than its diff:
```python
import jax
import jax.numpy as jnp
from jax import lax
from jax.sharding import PartitionSpec as P

PRECISION = lax.Precision.HIGH


def slot_work(first_block, second_block, coulomb_tile, diagonal):
    density = jnp.dot(
        first_block, second_block.T, precision=PRECISION, preferred_element_type=jnp.float32
    )
    symmetric = jnp.where(diagonal, 0.5 * (coulomb_tile + coulomb_tile.T), coulomb_tile)
    kernel = density * symmetric
    onto_first = jnp.dot(kernel, second_block, precision=PRECISION, preferred_element_type=jnp.float32)
    onto_second = jnp.dot(kernel.T, first_block, precision=PRECISION, preferred_element_type=jnp.float32)
    onto_second = onto_second * jnp.where(diagonal, 0.0, 1.0)
    return jnp.stack([onto_first, onto_second], 0)


def body(orbitals, requests, coulomb):
    group_count = lax.axis_size("grp")
    band_count = lax.axis_size("band")
    devices = group_count * band_count
    blk = coulomb.shape[1]
    col_width = orbitals.shape[1]
    orbital_width = col_width * band_count
    piece_rows = blk // devices
    slot_count = coulomb.shape[0]
    copies = jnp.broadcast_to(orbitals[None], (group_count,) + orbitals.shape)
    all_points = lax.all_to_all(copies, "grp", split_axis=0, concat_axis=0, tiled=True)
    block_count = all_points.shape[0] * all_points.shape[1] // (devices * piece_rows)
    blocks = (
        all_points.reshape(devices, block_count, piece_rows, col_width)
        .transpose(1, 0, 2, 3)
        .reshape(block_count, blk, col_width)
    )
    group_index = lax.axis_index("grp")
    band_index = lax.axis_index("band")
    group_requests = lax.dynamic_slice_in_dim(requests, group_index * band_count, band_count, 0)
    live = (group_requests >= 0).astype(jnp.float32)
    own_pairs = lax.dynamic_index_in_dim(group_requests, band_index, 0, keepdims=False)
    returned = []
    for slot in range(slot_count):
        wanted = group_requests[:, 2 * slot : 2 * slot + 2]
        outgoing = jnp.take(blocks, jnp.maximum(wanted, 0), axis=0)
        outgoing = outgoing * live[:, 2 * slot : 2 * slot + 2, None, None]
        arrived = lax.all_to_all(outgoing, "band", split_axis=0, concat_axis=0, tiled=True)
        pair_rows = arrived.transpose(1, 2, 0, 3).reshape(2, blk, orbital_width)
        diagonal = own_pairs[2 * slot] == own_pairs[2 * slot + 1]
        result = slot_work(pair_rows[0], pair_rows[1], coulomb[slot], diagonal)
        outbound = result.reshape(2, blk, band_count, col_width).transpose(2, 0, 1, 3)
        returned.append(lax.all_to_all(outbound, "band", split_axis=0, concat_axis=0, tiled=True))
    returned = jnp.concatenate(returned, axis=1)
    one_hot = (
        group_requests[:, :, None] == jnp.arange(block_count, dtype=jnp.int32)[None, None, :]
    ).astype(jnp.float32)
    summed = jnp.einsum("srk,srpc->kpc", one_hot, returned, precision=lax.Precision.HIGHEST)
    summed = summed.reshape(block_count, group_count, band_count, piece_rows, col_width)
    summed = summed.transpose(1, 0, 2, 3, 4)
    parts = lax.all_to_all(summed, "grp", split_axis=0, concat_axis=0, tiled=True)
    mine = parts.sum(axis=0).transpose(1, 0, 2, 3)
    return mine.reshape(band_count * block_count * piece_rows, col_width)


def solution(mesh):
    placed = (P("grp", "band"), P(), P(("grp", "band"), None, None))
    return jax.shard_map(
        body, mesh=mesh, in_specs=placed, out_specs=P("grp", "band"), check_vma=False
    )
```

time: 1250 us -> 837 us (0.67)
  waiting for transfers between devices: 530 us -> 305 us
  matrix products: 233 us -> 110 us
  blocking collectives: 211 us -> 111 us
  starting transfers between devices: 6.46 us -> 40.7 us
  loops' own time: 29 us -> 0 us
  other arithmetic: 24 us -> 44.1 us
  local copies, waits for them, and re-layouts: 196 us -> 215 us
    all_to_all x0 -> x4, waiting for transfers between devices: none -> 189 us  [the longest x1 104 us: body(): lax.all_to_all(copies, 'grp', split_axis=0, concat_axis=0, tiled=True)]
    all_gather x1 -> x0, waiting for transfers between devices: 167 us -> none  [body(): all_points = lax.all_gather(orbitals, 'grp', axis=0, tiled=True)]
    reduce_scatter x1 -> x0, waiting for transfers between devices: 159 us -> none  [body(): mine = lax.psum_scatter(summed, 'grp', scatter_dimension=1, tiled=True)]
    dot_general x9, matrix products: 218 us -> 97.2 us  [the longest x3 39.7 us: slot_work(): jnp.dot(first_block, second_block.T, precision=PRECISION, preferred_eleme...]
    all_to_all x1, blocking collectives: 211 us -> 111 us  [body(): lax.all_to_all(summed, 'grp', split_axis=0, concat_axis=0, tiled=True)]
    all_to_all x1 -> x3, waiting for transfers between devices: 205 us -> 115 us  [body(): lax.all_to_all(outgoing, 'band', split_axis=0, concat_axis=0, tiled=True)]
    all_to_all x0 -> x8, local copies, waits for them, and re-layouts: none -> 46.1 us  [the longest x3 27.2 us: body(): lax.all_to_all(outbound, 'band', split_axis=0, concat_axis=0, tiled=True)]
    dynamic_update_slice x6 -> x0, local copies, waits for them, and re-layouts: 37.4 us -> none  [body(): results = lax.map(per_slot, (fetched, coulomb, diagonal))]
  transfers between devices with their start and end apart: 3 -> 7, of which waited for: 3 -> 6; matrix products, arithmetic and copies ran while one was open for 0% -> 26% of each run, Pallas kernels for 0% -> 0%
where the time goes in v2:
time: 837 us; the launch traced here: 829 us
  waiting for transfers between devices  305 us (36%)
  local copies, waits for them, and re-layouts  215 us (26%)
  blocking collectives  111 us (13%)
  matrix products  110 us (13%)
  other arithmetic  44.1 us (5%)
  starting transfers between devices  40.7 us (5%)
    all_to_all x3, waiting for transfers between devices, body(): lax.all_to_all(outgoing, 'band', split_axis=0, concat_axis=0, tiled=True)  115 us
    all_to_all x1, blocking collectives, body(): lax.all_to_all(summed, 'grp', split_axis=0, concat_axis=0, tiled=True)  111 us
    all_to_all x1, waiting for transfers between devices, body(): lax.all_to_all(copies, 'grp', split_axis=0, concat_axis=0, tiled=True)  104 us
    all_to_all x3, waiting for transfers between devices, body(): lax.all_to_all(outbound, 'band', split_axis=0, concat_axis=0, tiled=True)  85.2 us
    squeeze x4, local copies, waits for them, and re-layouts, body(): result = slot_work(pair_rows[0], pair_rows[1], coulomb[slot], diagonal)  48.6 us
    dot_general x3, matrix products, slot_work(): jnp.dot(first_block, second_block.T, precision=PRECISION, preferred_eleme...  39.7 us
    dot_general x3, matrix products, slot_work(): jnp.dot(kernel, second_block, precision=PRECISION, preferred_element_type...  32.4 us
    all_to_all x3, local copies, waits for them, and re-layouts, body(): lax.all_to_all(outbound, 'band', split_axis=0, concat_axis=0, tiled=True)  27.2 us
  transfers between devices with their start and end apart: 7, of which 6 were waited for; matrix products, arithmetic and copies ran while one was open for 26% of the time, Pallas kernels for 0%

profile of v2, /device:TPU:2, one launch (start us, length us, event | category | flops | bytes accessed | tf_op | source)
XLA Modules:
  0.0 829.3 jit_solution(12527199113737379650)
XLA Ops:
  0.0 4.1 broadcast_in_dim.11
  4.1 5.0 all-to-all-start
  9.5 104.2 %all-to-all-done = f32[4,4608,64]{1,2,0:T(8,128)} async-done(((f32[4,4608,64]{1,2,0:T(8,128)}), f32[4,4608,64]{1,2,0:T(8,128)}, u32[]{:S(2)}, u32[]{:S(2)}) %all-to-all-start) | async-done | bytes 4718624 | tf_op jit(solution)/shard_map/all_to_all | solution.py:31
  113.8 7.6 copy.40
  121.4 12.0 %copy.41 = f32[12,32,48,64]{2,1,3,0:T(8,128)} copy(f32[12,32,48,64]{3,2,0,1:T(8,128)} %bitcast.158) | data formatting | bytes 9437184 | tf_op jit(solution)/shard_map/transpose | solution.py:35
  133.3 13.1 %reshape.101 = f32[12,1536,64]{1,2,0:T(8,128)} reshape(f32[12,32,48,64]{2,1,3,0:T(8,128)} %copy.41) | data formatting | bytes 9437184 | tf_op jit(solution)/shard_map/reshape | solution.py:36
  146.4 5.9 gather_fusion
  152.4 6.3 select_multiply_fusion.2
  158.7 5.1 all-to-all-start.1
  164.1 5.9 gather_fusion.1
  170.0 6.4 select_multiply_fusion.1
  176.4 57.6 %all-to-all-done.1 = f32[8,2,1536,64]{2,3,1,0:T(8,128)} async-done(((f32[8,2,1536,64]{2,3,1,0:T(8,128)}), f32[8,2,1536,64]{2,3,1,0:T(8,128)}, u32[]{:S(2)}, u32[]{:S(2)}) %all-to-all-start.1) | async-done | bytes 6291488 | tf_op jit(solution)/shard_map/all_to_all | solution.py:48
  234.0 6.1 all-to-all-start.3
  240.5 5.9 gather_fusion.2
  246.4 6.3 select_multiply_fusion
  252.7 57.7 %all-to-all-done.3 = f32[8,2,1536,64]{2,3,1,0:T(8,128)} async-done(((f32[8,2,1536,64]{2,3,1,0:T(8,128)}), f32[8,2,1536,64]{2,3,1,0:T(8,128)}, u32[]{:S(2)}, u32[]{:S(2)}) %all-to-all-start.3) | async-done | bytes 6291488 | tf_op jit(solution)/shard_map/all_to_all | solution.py:48
  310.3 6.4 all-to-all-start.5
  316.8 19.8 %slice_bitcast_fusion.2 = (f32[1536,1536]{1,0:T(8,128)}, f32[1536,1536]{1,0:T(8,128)}, f32[1536,1536]{1,0:T(8,128)}) fusion(f32[3,1536,1536]{2,1,0:T(8,128)} %param.7), kind=kLoop, calls=%fused_computation.29 | loop fusion | bytes 56623104 | tf_op jit(solution)/shard_map/squeeze | solution.py:51
  336.6 9.6 %copy.45 = f32[1536,1536]{0,1:T(8,128)} copy(f32[1536,1536]{1,0:T(8,128)} %get-tuple-element.8) | data formatting | bytes 18874368 | tf_op jit(solution)/shard_map/squeeze | solution.py:51
  348.0 3.6 copy.75
  351.6 2.0 slice.102
  353.6 1.1 copy-done
  354.7 13.3 %fusion.20 = f32[1536,1536]{1,0:T(8,128)} fusion(f32[1536,1536]{0,1:T(8,128)S(1)} %copy-done, pred[]{:T(512)} %bitcast.8, f32[2,1536,8,64]{1,3,2,0:T(8,128)S(1)} %bitcast.160, f32[3,1536,1536]{2,1,0:T(8,128)} %param.7), kind=kOutput, calls=%fused_computation.26 | convolution fusion | flops 7257194496 | bytes 34603008 | tf_op jit(solution)/shard_map/dot_general | solution.py:10
  368.0 10.8 %fusion.24 = f32[1,1536,8,64]{1,3,2,0:T(8,128)S(1)} fusion(f32[1536,1536]{1,0:T(8,128)} %fusion.20, f32[2,1536,8,64]{1,3,2,0:T(8,128)S(1)} %bitcast.161), kind=kOutput, calls=%fused_computation.43 | convolution fusion | flops 7247757312 | bytes 15728640 | tf_op jit(solution)/shard_map/dot_general | solution.py:15
  378.8 8.4 %convolution_multiply_fusion.2 = f32[1536,512]{0,1:T(8,128)S(1)} fusion(f32[1536,1536]{1,0:T(8,128)S(1)} %copy-done.9, f32[1536,512]{0,1:T(8,128)S(1)} %bitcast.170, f32[]{:T(128)S(6)} %select_n.54), kind=kOutput, calls=%fused_computation.42 | convolution fusion | flops 7248543744 | bytes 15728644 | tf_op jit(solution)/shard_map/dot_general | solution.py:16
  387.2 0.6 maximum_bitcast_fusion
  387.8 3.1 copy.46
  390.9 5.2 all-to-all-start.2
  396.1 9.6 %copy.51 = f32[1536,1536]{0,1:T(8,128)} copy(f32[1536,1536]{1,0:T(8,128)} %get-tuple-element.10) | data formatting | bytes 18874368 | tf_op jit(solution)/shard_map/squeeze | solution.py:51
  406.9 3.6 copy.74
  410.5 2.0 slice.104
  412.6 1.0 copy-done.2
  413.5 13.1 %fusion.15 = f32[1536,1536]{1,0:T(8,128)} fusion(f32[1536,1536]{0,1:T(8,128)S(1)} %copy-done.2, pred[]{:T(512)} %bitcast.24, f32[2,1536,8,64]{1,3,2,0:T(8,128)S(1)} %bitcast.163, f32[3,1536,1536]{2,1,0:T(8,128)} %param.7), kind=kOutput, calls=%fused_computation.20 | convolution fusion | flops 7257194496 | bytes 34603008 | tf_op jit(solution)/shard_map/dot_general | solution.py:10
  426.7 10.7 %fusion.27 = f32[1,1536,8,64]{1,3,2,0:T(8,128)S(1)} fusion(f32[1536,1536]{1,0:T(8,128)} %fusion.15, f32[2,1536,8,64]{1,3,2,0:T(8,128)S(1)} %bitcast.164), kind=kOutput, calls=%fused_computation.44 | convolution fusion | flops 7247757312 | bytes 15728640 | tf_op jit(solution)/shard_map/dot_general | solution.py:15
  437.4 8.4 %convolution_multiply_fusion.1 = f32[1536,512]{0,1:T(8,128)S(1)} fusion(f32[1536,1536]{1,0:T(8,128)S(1)} %copy-done.10, f32[1536,512]{0,1:T(8,128)S(1)} %bitcast.171, f32[]{:T(128)S(6)} %select_n.57), kind=kOutput, calls=%fused_computation.41 | convolution fusion | flops 7248543744 | bytes 15728644 | tf_op jit(solution)/shard_map/dot_general | solution.py:16
  445.8 0.6 maximum_bitcast_fusion.1
  446.4 3.0 copy.52
  449.4 16.8 %all-to-all-done.2 = f32[8,2,1536,64]{2,3,1,0:T(8,128)} async-done(((f32[8,2,1536,64]{2,3,1,0:T(8,128)}), f32[8,2,1536,64]{2,3,1,0:T(8,128)}, u32[]{:S(2)}, u32[]{:S(2)}) %all-to-all-start.2) | async-done | bytes 6291488 | tf_op jit(solution)/shard_map/all_to_all | solution.py:53
  466.2 6.4 all-to-all-start.4
  472.7 9.6 %copy.57 = f32[1536,1536]{0,1:T(8,128)} copy(f32[1536,1536]{1,0:T(8,128)} %get-tuple-element.9) | data formatting | bytes 18874368 | tf_op jit(solution)/shard_map/squeeze | solution.py:51
  483.5 3.6 copy.73
  487.1 2.0 slice.106
  489.1 1.0 copy-done.1
  490.2 13.3 %fusion.10 = f32[1536,1536]{1,0:T(8,128)} fusion(f32[1536,1536]{0,1:T(8,128)S(1)} %copy-done.1, pred[]{:T(512)} %bitcast.40, f32[2,1536,8,64]{1,3,2,0:T(8,128)S(1)} %bitcast.166, f32[3,1536,1536]{2,1,0:T(8,128)} %param.7), kind=kOutput, calls=%fused_computation.14 | convolution fusion | flops 7257194496 | bytes 34603008 | tf_op jit(solution)/shard_map/dot_general | solution.py:10
  503.4 10.9 %fusion.30 = f32[1,1536,8,64]{1,3,2,0:T(8,128)S(1)} fusion(f32[1536,1536]{1,0:T(8,128)} %fusion.10, f32[2,1536,8,64]{1,3,2,0:T(8,128)S(1)} %bitcast.167), kind=kOutput, calls=%fused_computation.45 | convolution fusion | flops 7247757312 | bytes 15728640 | tf_op jit(solution)/shard_map/dot_general | solution.py:15
  514.4 8.4 %convolution_multiply_fusion = f32[1536,512]{0,1:T(8,128)S(1)} fusion(f32[1536,1536]{1,0:T(8,128)S(1)} %copy-done.11, f32[1536,512]{0,1:T(8,128)S(1)} %bitcast.172, f32[]{:T(128)S(6)} %select_n.60), kind=kOutput, calls=%fused_computation.40 | convolution fusion | flops 7248543744 | bytes 15728644 | tf_op jit(solution)/shard_map/dot_general | solution.py:16
  523.4 3.0 copy.58
  526.4 16.4 %all-to-all-done.4 = f32[8,2,1536,64]{2,3,1,0:T(8,128)} async-done(((f32[8,2,1536,64]{2,3,1,0:T(8,128)}), f32[8,2,1536,64]{2,3,1,0:T(8,128)}, u32[]{:S(2)}, u32[]{:S(2)}) %all-to-all-start.4) | async-done | bytes 6291488 | tf_op jit(solution)/shard_map/all_to_all | solution.py:53
  542.8 6.4 all-to-all-start.6
  549.2 9.1 %copy.59 = f32[8,2,1536,64]{2,0,1,3:T(8,128)} copy(f32[8,2,1536,64]{2,3,1,0:T(8,128)} %all-to-all-done.2) | data formatting | bytes 12582912 | tf_op jit(solution)/shard_map/all_to_all | solution.py:53
  558.3 9.1 %copy.60 = f32[8,2,1536,64]{2,0,1,3:T(8,128)} copy(f32[8,2,1536,64]{2,3,1,0:T(8,128)} %all-to-all-done.4) | data formatting | bytes 12582912 | tf_op jit(solution)/shard_map/all_to_all | solution.py:53
  567.4 51.9 %all-to-all-done.6 = f32[8,2,1536,64]{2,3,1,0:T(8,128)} async-done(((f32[8,2,1536,64]{2,3,1,0:T(8,128)}), f32[8,2,1536,64]{2,3,1,0:T(8,128)}, u32[]{:S(2)}, u32[]{:S(2)}) %all-to-all-start.6) | async-done | bytes 6291488 | tf_op jit(solution)/shard_map/all_to_all | solution.py:53
  619.4 9.0 %copy.61 = f32[8,2,1536,64]{2,0,1,3:T(8,128)} copy(f32[8,2,1536,64]{2,3,1,0:T(8,128)} %all-to-all-done.6) | data formatting | bytes 12582912 | tf_op jit(solution)/shard_map/all_to_all | solution.py:53
  628.4 12.4 %fusion.21 = f32[12,1536,64]{1,0,2:T(8,128)} fusion(f32[8,2,1536,64]{2,0,1,3:T(8,128)} %copy.61, f32[8,2,1536,64]{2,0,1,3:T(8,128)} %copy.60, f32[8,2,1536,64]{2,0,1,3:T(8,128)} %copy.59, s32[8,6]{0,1:T(8,128)S(1)} %copy-done.7), kind=kOutput, calls=%fused_computation.39 | convolution fusion | flops 688915008 | bytes 23593152 | tf_op jit(solution)/shard_map/srk,srpc->kpc/dot_general | solution.py:58
  640.8 7.6 copy.62
  648.4 10.6 %reshape.108 = f32[12,4,8,48,64]{3,2,1,4,0:T(8,128)} reshape(f32[12,1536,64]{1,2,0:T(8,128)} %copy.62) | data formatting | bytes 9437184 | tf_op jit(solution)/shard_map/reshape | solution.py:59
  659.0 11.7 %copy.63 = f32[4,12,8,48,64]{4,3,2,1,0:T(8,128)} copy(f32[4,12,8,48,64]{3,2,0,4,1:T(8,128)} %bitcast.157) | data formatting | bytes 9437184 | tf_op jit(solution)/shard_map/transpose | solution.py:60
  670.7 9.3 %reshape.160 = f32[4,1,294912]{2,1,0:T(1,128)} reshape(f32[4,12,8,48,64]{4,3,2,1,0:T(8,128)} %copy.63) | data formatting | bytes 9437184
  680.0 111.1 %all_to_all.40 = f32[4,1,294912]{2,1,0:T(1,128)} all-to-all(f32[4,1,294912]{2,1,0:T(1,128)} %reshape.160), channel_id=1, replica_groups=mesh['grp'=4,'band'=8] {'grp'}, dimensions={0} | all-to-all | bytes 9437184 | tf_op jit(solution)/shard_map/all_to_all | solution.py:61
  791.7 16.9 %reduce = f32[4,294912]{1,0:T(4,128)} reduce(f32[4,1,294912]{2,1,0:T(1,128)} %all_to_all.40, f32[]{:T(128)} %broadcast.74), dimensions={1}, to_apply=%all_to_all.31.reduce_sub_computation | reduce | bytes 9437188 | tf_op jit(solution)/shard_map/all_to_all | solution.py:61
  808.6 10.3 %reshape.161 = f32[4,12,8,48,64]{4,3,2,1,0:T(8,128)} reshape(f32[4,294912]{1,0:T(4,128)} %reduce) | data formatting | bytes 9437184
  818.9 6.3 reduce_sum.9
  825.3 1.9 copy.65
  827.2 1.7 copy.66
  (45 shorter events, 3.0 us)
Async XLA Ops:
  0.0 9.1 %copy-start.8 = (s32[32,6]{0,1:T(8,128)S(1)}, s32[32,6]{0,1:T(8,128)}, u32[]{:S(2)}) copy-start(s32[32,6]{0,1:T(8,128)} %param.6) | copy-start | bytes 2308
  4.1 109.7 %all-to-all-start = ((f32[4,4608,64]{1,2,0:T(8,128)}), f32[4,4608,64]{1,2,0:T(8,128)}, u32[]{:S(2)}, u32[]{:S(2)}) async-start(f32[4,4608,64]{1,2,0:T(8,128)} %broadcast_in_dim.11), calls=%async_computation | async-start | bytes 9437184 | tf_op jit(solution)/shard_map/all_to_all | solution.py:31
  9.2 112.2 %copy-start.6 = (s32[8,6]{0,1:T(8,128)}, s32[8,6]{0,1:T(8,128)S(1)}, u32[]{:S(2)}) copy-start(s32[8,6]{0,1:T(8,128)S(1)} %get-tuple-element.7) | copy-start | bytes 580
  158.7 75.3 %all-to-all-start.1 = ((f32[8,2,1536,64]{2,3,1,0:T(8,128)}), f32[8,2,1536,64]{2,3,1,0:T(8,128)}, u32[]{:S(2)}, u32[]{:S(2)}) async-start(f32[8,2,1536,64]{2,3,1,0:T(8,128)} %select_multiply_fusion.2), calls=%async_computation.1 | async-start | bytes 12582912 | tf_op jit(solution)/shard_map/all_to_all | solution.py:48
  234.0 76.3 %all-to-all-start.3 = ((f32[8,2,1536,64]{2,3,1,0:T(8,128)}), f32[8,2,1536,64]{2,3,1,0:T(8,128)}, u32[]{:S(2)}, u32[]{:S(2)}) async-start(f32[8,2,1536,64]{2,3,1,0:T(8,128)} %select_multiply_fusion.1), calls=%async_computation.3 | async-start | bytes 12582912 | tf_op jit(solution)/shard_map/all_to_all | solution.py:48
  310.3 80.5 %all-to-all-start.5 = ((f32[8,2,1536,64]{2,3,1,0:T(8,128)}), f32[8,2,1536,64]{2,3,1,0:T(8,128)}, u32[]{:S(2)}, u32[]{:S(2)}) async-start(f32[8,2,1536,64]{2,3,1,0:T(8,128)} %select_multiply_fusion), calls=%async_computation.5 | async-start | bytes 12582912 | tf_op jit(solution)/shard_map/all_to_all | solution.py:48
  348.0 6.6 copy-start
  368.0 10.8 %copy-start.3 = (f32[1,1536,8,64]{1,3,2,0:T(8,128)S(1)}, f32[1,1536,8,64]{1,3,2,0:T(8,128)}, u32[]{:S(2)}) copy-start(f32[1,1536,8,64]{1,3,2,0:T(8,128)} %slice.102) | copy-start | bytes 9437188
  368.0 10.8 %copy-start.9 = (f32[1536,1536]{1,0:T(8,128)S(1)}, f32[1536,1536]{1,0:T(8,128)}, u32[]{:S(2)}) copy-start(f32[1536,1536]{1,0:T(8,128)} %fusion.20) | copy-start | bytes 28311556
  390.9 75.4 %all-to-all-start.2 = ((f32[8,2,1536,64]{2,3,1,0:T(8,128)}), f32[8,2,1536,64]{2,3,1,0:T(8,128)}, u32[]{:S(2)}, u32[]{:S(2)}) async-start(f32[8,2,1536,64]{2,3,1,0:T(8,128)} %copy.46), calls=%async_computation.2 | async-start | bytes 12582912 | tf_op jit(solution)/shard_map/all_to_all | solution.py:53
  406.9 6.6 copy-start.2
  426.7 10.7 %copy-start.4 = (f32[1,1536,8,64]{1,3,2,0:T(8,128)S(1)}, f32[1,1536,8,64]{1,3,2,0:T(8,128)}, u32[]{:S(2)}) copy-start(f32[1,1536,8,64]{1,3,2,0:T(8,128)} %slice.104) | copy-start | bytes 9437188
  426.7 10.7 %copy-start.10 = (f32[1536,1536]{1,0:T(8,128)S(1)}, f32[1536,1536]{1,0:T(8,128)}, u32[]{:S(2)}) copy-start(f32[1536,1536]{1,0:T(8,128)} %fusion.15) | copy-start | bytes 28311556
  466.2 76.6 %all-to-all-start.4 = ((f32[8,2,1536,64]{2,3,1,0:T(8,128)}), f32[8,2,1536,64]{2,3,1,0:T(8,128)}, u32[]{:S(2)}, u32[]{:S(2)}) async-start(f32[8,2,1536,64]{2,3,1,0:T(8,128)} %copy.52), calls=%async_computation.4 | async-start | bytes 12582912 | tf_op jit(solution)/shard_map/all_to_all | solution.py:53
  483.5 6.6 copy-start.1
  503.4 10.9 %copy-start.5 = (f32[1,1536,8,64]{1,3,2,0:T(8,128)S(1)}, f32[1,1536,8,64]{1,3,2,0:T(8,128)}, u32[]{:S(2)}) copy-start(f32[1,1536,8,64]{1,3,2,0:T(8,128)} %slice.106) | copy-start | bytes 9437188
  503.4 11.0 %copy-start.11 = (f32[1536,1536]{1,0:T(8,128)S(1)}, f32[1536,1536]{1,0:T(8,128)}, u32[]{:S(2)}) copy-start(f32[1536,1536]{1,0:T(8,128)} %fusion.10) | copy-start | bytes 28311556
  542.8 76.5 %all-to-all-start.6 = ((f32[8,2,1536,64]{2,3,1,0:T(8,128)}), f32[8,2,1536,64]{2,3,1,0:T(8,128)}, u32[]{:S(2)}, u32[]{:S(2)}) async-start(f32[8,2,1536,64]{2,3,1,0:T(8,128)} %copy.58), calls=%async_computation.6 | async-start | bytes 12582912 | tf_op jit(solution)/shard_map/all_to_all | solution.py:53
  567.4 60.9 %copy-start.7 = (s32[8,6]{0,1:T(8,128)S(1)}, s32[8,6]{0,1:T(8,128)}, u32[]{:S(2)}) copy-start(s32[8,6]{0,1:T(8,128)} %copy-done.6) | copy-start | bytes 580

commit v3 on v2

v3 whole, which is shorter than its diff:
```python
import jax
import jax.numpy as jnp
from jax import lax
from jax.sharding import PartitionSpec as P

PRECISION = lax.Precision.HIGH
EXACT = lax.Precision.HIGHEST


def body(orbitals, requests, coulomb):
    group_count = lax.axis_size("grp")
    band_count = lax.axis_size("band")
    devices = group_count * band_count
    blk = coulomb.shape[1]
    col_width = orbitals.shape[1]
    piece_rows = blk // devices
    slot_count = coulomb.shape[0]
    block_count = orbitals.shape[0] // (band_count * piece_rows)
    copies = jnp.broadcast_to(orbitals[None], (group_count,) + orbitals.shape)
    all_points = lax.all_to_all(copies, "grp", split_axis=0, concat_axis=0, tiled=True)
    all_points = all_points.reshape(group_count, band_count, block_count, piece_rows, col_width)
    group_index = lax.axis_index("grp")
    band_index = lax.axis_index("band")
    group_requests = lax.dynamic_slice_in_dim(requests, group_index * band_count, band_count, 0)
    one_hot = (
        group_requests[:, :, None] == jnp.arange(block_count, dtype=jnp.int32)[None, None, :]
    ).astype(jnp.float32)
    own_pairs = lax.dynamic_index_in_dim(group_requests, band_index, 0, keepdims=False)
    summed = None
    for slot in range(slot_count):
        pick = one_hot[:, 2 * slot : 2 * slot + 2]
        outgoing = jnp.einsum("rqk,gjkpc->rqgjpc", pick, all_points, precision=EXACT)
        arrived = lax.all_to_all(outgoing, "band", split_axis=0, concat_axis=0, tiled=True)
        arrived = arrived.reshape(band_count, 2, blk, col_width)
        first, second = arrived[:, 0], arrived[:, 1]
        density = jnp.einsum("sic,sjc->ij", first, second, precision=PRECISION)
        kernel = density * coulomb[slot]
        onto_first = jnp.einsum("ij,sjc->sic", kernel, second, precision=PRECISION)
        onto_second = jnp.einsum("ij,sic->sjc", kernel, first, precision=PRECISION)
        scale = jnp.where(own_pairs[2 * slot] == own_pairs[2 * slot + 1], 0.5, 1.0)
        outbound = jnp.stack([onto_first, onto_second], axis=1) * scale
        returned = lax.all_to_all(outbound, "band", split_axis=0, concat_axis=0, tiled=True)
        returned = returned.reshape(band_count, 2, group_count, band_count, piece_rows, col_width)
        part = jnp.einsum("sqk,sqgjpc->gjkpc", pick, returned, precision=EXACT)
        summed = part if summed is None else summed + part
    parts = lax.all_to_all(summed, "grp", split_axis=0, concat_axis=0, tiled=True)
    mine = parts.sum(axis=0)
    return mine.reshape(band_count * block_count * piece_rows, col_width)


def solution(mesh):
    placed = (P("grp", "band"), P(), P(("grp", "band"), None, None))
    return jax.shard_map(
        body, mesh=mesh, in_specs=placed, out_specs=P("grp", "band"), check_vma=False
    )
```

time: 837 us -> 919 us (1.098)
  matrix products: 110 us -> 274 us
  waiting for transfers between devices: 305 us -> 193 us
  other arithmetic: 44.1 us -> 89.7 us
  local copies, waits for them, and re-layouts: 215 us -> 199 us
    dot_general x10 -> x15, matrix products: 110 us -> 274 us  [the longest x3 95.8 us: body(): onto_first = jnp.einsum('ij,sjc->sic', kernel, second, precision=PRECISION)]
    unnamed x26 -> x20, local copies, waits for them, and re-layouts: 22.7 us -> 94.2 us
    all_to_all x0 -> x3, other arithmetic: none -> 59.3 us  [body(): lax.all_to_all(outgoing, 'band', split_axis=0, concat_axis=0, tiled=True)]
    all_to_all x3, waiting for transfers between devices: 85.2 us -> 26.7 us  [body(): lax.all_to_all(outbound, 'band', split_axis=0, concat_axis=0, tiled=True)]
    all_to_all x3, waiting for transfers between devices: 115 us -> 62.2 us  [body(): lax.all_to_all(outgoing, 'band', split_axis=0, concat_axis=0, tiled=True)]
    squeeze x4 -> x0, local copies, waits for them, and re-layouts: 48.6 us -> none  [body(): result = slot_work(pair_rows[0], pair_rows[1], coulomb[slot], diagonal)]
    transpose x6 -> x0, local copies, waits for them, and re-layouts: 34.7 us -> none  [the longest x1 12 us: body(): blocks = all_points.reshape(devices, block_count, piece_rows, col_width)....]
    all_to_all x4 -> x0, local copies, waits for them, and re-layouts: 27.7 us -> none  [the longest x3 27.2 us: body(): lax.all_to_all(outbound, 'band', split_axis=0, concat_axis=0, tiled=True)]
  transfers between devices with their start and end apart: 7 -> 7, of which waited for: 6 -> 4; matrix products, arithmetic and copies ran while one was open for 26% -> 47% of each run, Pallas kernels for 0% -> 0%
where the time goes in v3:
time: 919 us; the launch traced here: 910 us
  matrix products  274 us (30%)
  local copies, waits for them, and re-layouts  199 us (22%)
  waiting for transfers between devices  193 us (21%)
  blocking collectives  111 us (12%)
  other arithmetic  89.7 us (10%)
  starting transfers between devices  38.7 us (4%)
    all_to_all x1, blocking collectives, body(): lax.all_to_all(summed, 'grp', split_axis=0, concat_axis=0, tiled=True)  111 us
    all_to_all x1, waiting for transfers between devices, body(): lax.all_to_all(copies, 'grp', split_axis=0, concat_axis=0, tiled=True)  105 us
    dot_general x3, matrix products, body(): onto_first = jnp.einsum('ij,sjc->sic', kernel, second, precision=PRECISION)  95.8 us
    unnamed x20, local copies, waits for them, and re-layouts  94.2 us
    dot_general x3, matrix products, body(): density = jnp.einsum('sic,sjc->ij', first, second, precision=PRECISION)  65.4 us
    all_to_all x3, waiting for transfers between devices, body(): lax.all_to_all(outgoing, 'band', split_axis=0, concat_axis=0, tiled=True)  62.2 us
    all_to_all x3, other arithmetic, body(): lax.all_to_all(outgoing, 'band', split_axis=0, concat_axis=0, tiled=True)  59.3 us
    dot_general x3, matrix products, body(): jnp.einsum('rqk,gjkpc->rqgjpc', pick, all_points, precision=EXACT)  44.7 us
  transfers between devices with their start and end apart: 7, of which 4 were waited for; matrix products, arithmetic and copies ran while one was open for 47% of the time, Pallas kernels for 0%

profile of v3, /device:TPU:2, one launch (start us, length us, event | category | flops | bytes accessed | tf_op | source)
XLA Modules:
  0.0 909.7 jit_solution(2030223642507071753)
XLA Ops:
  0.0 4.1 broadcast_in_dim.2
  4.1 4.9 all-to-all-start
  9.0 0.1 constant_dynamic-slice_fusion.1
  9.1 0.1 iota_compare_fusion
  9.2 104.5 %all-to-all-done = f32[4,4608,64]{1,2,0:T(8,128)} async-done(((f32[4,4608,64]{1,2,0:T(8,128)}), f32[4,4608,64]{1,2,0:T(8,128)}, u32[]{:S(2)}, u32[]{:S(2)}) %all-to-all-start) | async-done | bytes 4718624 | tf_op jit(solution)/shard_map/all_to_all | solution.py:20
  113.7 7.6 copy.51
  121.3 14.9 %fusion.1 = f32[8,2,4,8,48,64]{5,0,4,3,2,1:T(8,128)} fusion(f32[4,8,12,48,64]{4,3,2,1,0:T(8,128)} %bitcast.176, pred[8,6,12]{2,0,1:T(8,128)(4,1)S(1)} %iota_compare_fusion), kind=kOutput, calls=%fused_computation.3 | convolution fusion | flops 226492416 | bytes 11012096 | tf_op jit(solution)/shard_map/rqk,gjkpc->rqgjpc/dot_general | solution.py:32
  136.2 11.5 %copy.67 = f32[8,2,4,8,48,64]{5,4,3,2,1,0:T(8,128)} copy(f32[8,2,4,8,48,64]{5,0,4,3,2,1:T(8,128)} %fusion.1) | data formatting | bytes 12582912 | tf_op jit(solution)/shard_map/rqk,gjkpc->rqgjpc/dot_general | solution.py:32
  147.8 12.6 %reshape.77 = f32[8,1,196608]{2,1,0:T(1,128)} reshape(f32[8,2,4,8,48,64]{5,4,3,2,1,0:T(8,128)} %copy.67) | data formatting | bytes 12582912
  160.4 5.4 all-to-all-start.5
  165.8 14.9 %fusion.5 = f32[8,2,4,8,48,64]{5,0,4,3,2,1:T(8,128)} fusion(f32[4,8,12,48,64]{4,3,2,1,0:T(8,128)} %bitcast.177, pred[8,6,12]{2,0,1:T(8,128)(4,1)S(1)} %iota_compare_fusion), kind=kOutput, calls=%fused_computation.7 | convolution fusion | flops 226492416 | bytes 11012096 | tf_op jit(solution)/shard_map/rqk,gjkpc->rqgjpc/dot_general | solution.py:32
  180.7 11.5 %copy.53 = f32[8,2,4,8,48,64]{5,4,3,2,1,0:T(8,128)} copy(f32[8,2,4,8,48,64]{5,0,4,3,2,1:T(8,128)} %fusion.5) | data formatting | bytes 12582912 | tf_op jit(solution)/shard_map/rqk,gjkpc->rqgjpc/dot_general | solution.py:32
  192.2 12.6 %reshape.75 = f32[8,1,196608]{2,1,0:T(1,128)} reshape(f32[8,2,4,8,48,64]{5,4,3,2,1,0:T(8,128)} %copy.53) | data formatting | bytes 12582912
  204.9 31.1 %all-to-all-done.5 = f32[8,1,196608]{2,1,0:T(1,128)} async-done(((f32[8,1,196608]{2,1,0:T(1,128)}), f32[8,1,196608]{2,1,0:T(1,128)}, u32[]{:S(2)}, u32[]{:S(2)}) %all-to-all-start.5) | async-done | bytes 6291488 | tf_op jit(solution)/shard_map/all_to_all | solution.py:33
  235.9 6.6 all-to-all-start.1
  242.6 14.9 %fusion.3 = f32[8,2,4,8,48,64]{5,0,4,3,2,1:T(8,128)} fusion(f32[4,8,12,48,64]{4,3,2,1,0:T(8,128)} %bitcast.178, pred[8,6,12]{2,0,1:T(8,128)(4,1)S(1)} %iota_compare_fusion), kind=kOutput, calls=%fused_computation.5 | convolution fusion | flops 226492416 | bytes 11012096 | tf_op jit(solution)/shard_map/rqk,gjkpc->rqgjpc/dot_general | solution.py:32
  257.5 11.5 %copy.60 = f32[8,2,4,8,48,64]{5,4,3,2,1,0:T(8,128)} copy(f32[8,2,4,8,48,64]{5,0,4,3,2,1:T(8,128)} %fusion.3) | data formatting | bytes 12582912 | tf_op jit(solution)/shard_map/rqk,gjkpc->rqgjpc/dot_general | solution.py:32
  269.0 12.6 %reshape.73 = f32[8,1,196608]{2,1,0:T(1,128)} reshape(f32[8,2,4,8,48,64]{5,4,3,2,1,0:T(8,128)} %copy.60) | data formatting | bytes 12582912
  281.6 31.1 %all-to-all-done.1 = f32[8,1,196608]{2,1,0:T(1,128)} async-done(((f32[8,1,196608]{2,1,0:T(1,128)}), f32[8,1,196608]{2,1,0:T(1,128)}, u32[]{:S(2)}, u32[]{:S(2)}) %all-to-all-start.1) | async-done | bytes 6291488 | tf_op jit(solution)/shard_map/all_to_all | solution.py:33
  312.7 6.4 all-to-all-start.3
  319.2 0.1 constant_dynamic-slice_fusion
  319.2 0.6 fusion.54
  321.2 0.5 broadcast.2
  321.7 19.8 %reduce.1 = f32[8,196608]{1,0:T(8,128)} reduce(f32[8,1,196608]{2,1,0:T(1,128)} %all-to-all-done.1, f32[]{:T(128)} %broadcast.2), dimensions={1}, to_apply=%all_to_all.25.reduce_sub_computation | reduce | bytes 12582916 | tf_op jit(solution)/shard_map/all_to_all | solution.py:33
  341.5 12.2 %reshape.76 = f32[8,2,4,8,48,64]{5,4,3,2,1,0:T(8,128)} reshape(f32[8,196608]{1,0:T(8,128)} %reduce.1) | data formatting | bytes 12582912
  353.7 21.9 %bitcast_multiply_fusion.2 = f32[1536,1536]{1,0:T(8,128)S(1)} fusion(f32[3,1536,1536]{2,1,0:T(8,128)} %param.5, f32[8,2,1536,64]{3,2,1,0:T(8,128)} %bitcast.181), kind=kOutput, calls=%fused_computation.26 | convolution fusion | flops 7250116608 | bytes 25165824 | tf_op jit(solution)/shard_map/sic,sjc->ij/dot_general | solution.py:36
  375.6 9.0 fusion.22
  384.6 31.8 %fusion.31 = f32[8,1,1536,64]{2,3,0,1:T(8,128)} fusion(f32[1536,1536]{1,0:T(8,128)S(1)} %bitcast_multiply_fusion.2, f32[8,2,1536,64]{3,2,1,0:T(8,128)S(1)} %bitcast.183), kind=kOutput, calls=%fused_computation.39 | convolution fusion | flops 7247757312 | bytes 18874368 | tf_op jit(solution)/shard_map/ij,sjc->sic/dot_general | solution.py:38
  416.4 2.7 maximum_multiply_fusion
  419.1 3.0 copy.57
  422.2 0.0 all-to-all-done.3
  422.2 5.2 all-to-all-start.2
  428.6 19.8 %reduce = f32[8,196608]{1,0:T(8,128)} reduce(f32[8,1,196608]{2,1,0:T(1,128)} %all-to-all-done.3, f32[]{:T(128)} %broadcast.2), dimensions={1}, to_apply=%all_to_all.27.reduce_sub_computation | reduce | bytes 12582916 | tf_op jit(solution)/shard_map/all_to_all | solution.py:33
  448.4 12.2 %reshape.74 = f32[8,2,4,8,48,64]{5,4,3,2,1,0:T(8,128)} reshape(f32[8,196608]{1,0:T(8,128)} %reduce) | data formatting | bytes 12582912
  460.7 21.6 %bitcast_multiply_fusion.1 = f32[1536,1536]{1,0:T(8,128)S(1)} fusion(f32[3,1536,1536]{2,1,0:T(8,128)} %param.5, f32[8,2,1536,64]{3,2,1,0:T(8,128)} %bitcast.184), kind=kOutput, calls=%fused_computation.21 | convolution fusion | flops 7250116608 | bytes 25165824 | tf_op jit(solution)/shard_map/sic,sjc->ij/dot_general | solution.py:36
  482.3 9.0 fusion.25
  491.3 32.1 %fusion.34 = f32[8,1,1536,64]{2,3,0,1:T(8,128)} fusion(f32[1536,1536]{1,0:T(8,128)S(1)} %bitcast_multiply_fusion.1, f32[8,2,1536,64]{3,2,1,0:T(8,128)S(1)} %bitcast.186), kind=kOutput, calls=%fused_computation.40 | convolution fusion | flops 7247757312 | bytes 18874368 | tf_op jit(solution)/shard_map/ij,sjc->sic/dot_general | solution.py:38
  523.4 2.7 maximum_multiply_fusion.1
  526.1 3.1 copy.64
  529.2 0.0 all-to-all-done.2
  529.2 4.9 all-to-all-start.4
  535.4 19.8 %reduce.2 = f32[8,196608]{1,0:T(8,128)} reduce(f32[8,1,196608]{2,1,0:T(1,128)} %all-to-all-done.5, f32[]{:T(128)} %broadcast.2), dimensions={1}, to_apply=%all_to_all.29.reduce_sub_computation | reduce | bytes 12582916 | tf_op jit(solution)/shard_map/all_to_all | solution.py:33
  555.2 12.2 %reshape.78 = f32[8,2,4,8,48,64]{5,4,3,2,1,0:T(8,128)} reshape(f32[8,196608]{1,0:T(8,128)} %reduce.2) | data formatting | bytes 12582912
  567.4 21.9 %bitcast_multiply_fusion = f32[1536,1536]{1,0:T(8,128)S(1)} fusion(f32[3,1536,1536]{2,1,0:T(8,128)} %param.5, f32[8,2,1536,64]{3,2,1,0:T(8,128)} %bitcast.187), kind=kOutput, calls=%fused_computation.16 | convolution fusion | flops 7250116608 | bytes 25165824 | tf_op jit(solution)/shard_map/sic,sjc->ij/dot_general | solution.py:36
  589.3 9.0 fusion.28
  598.3 31.9 %fusion.37 = f32[8,1,1536,64]{2,3,0,1:T(8,128)} fusion(f32[1536,1536]{1,0:T(8,128)S(1)} %bitcast_multiply_fusion, f32[8,2,1536,64]{3,2,1,0:T(8,128)S(1)} %bitcast.189), kind=kOutput, calls=%fused_computation.41 | convolution fusion | flops 7247757312 | bytes 18874368 | tf_op jit(solution)/shard_map/ij,sjc->sic/dot_general | solution.py:38
  630.2 2.7 maximum_multiply_fusion.2
  632.9 3.1 copy.71
  635.9 0.0 all-to-all-done.4
  635.9 5.2 all-to-all-start.6
  641.1 11.3 %copy.89 = f32[8,2,1536,64]{3,0,1,2:T(8,128)} copy(f32[8,2,1536,64]{2,3,1,0:T(8,128)} %all-to-all-done.2) | data formatting | bytes 12582912 | tf_op jit(solution)/shard_map/reshape | solution.py:43
  652.5 11.3 %copy.93 = f32[8,2,1536,64]{3,0,1,2:T(8,128)} copy(f32[8,2,1536,64]{2,3,1,0:T(8,128)} %all-to-all-done.4) | data formatting | bytes 12582912 | tf_op jit(solution)/shard_map/reshape | solution.py:43
  663.8 11.8 %fusion.45 = f32[4,8,48,64,12,1]{3,4,5,2,1,0:T(8,128)} fusion(f32[8,2,4,8,48,64]{5,0,1,4,3,2:T(8,128)} %bitcast.179, pred[8,6,12]{2,0,1:T(8,128)(4,1)S(1)} %iota_compare_fusion), kind=kOutput, calls=%fused_computation.48 | convolution fusion | flops 226492416 | bytes 11012096 | tf_op jit(solution)/shard_map/sqk,sqgjpc->gjkpc/dot_general | solution.py:44
  675.6 9.0 fusion.42
  684.6 26.7 %all-to-all-done.6 = f32[8,2,1536,64]{2,3,1,0:T(8,128)} async-done(((f32[8,2,1536,64]{2,3,1,0:T(8,128)}), f32[8,2,1536,64]{2,3,1,0:T(8,128)}, u32[]{:S(2)}, u32[]{:S(2)}) %all-to-all-start.6) | async-done | bytes 6291488 | tf_op jit(solution)/shard_map/all_to_all | solution.py:42
  711.3 11.3 %copy.97 = f32[8,2,1536,64]{3,0,1,2:T(8,128)} copy(f32[8,2,1536,64]{2,3,1,0:T(8,128)} %all-to-all-done.6) | data formatting | bytes 12582912 | tf_op jit(solution)/shard_map/reshape | solution.py:43
  722.6 20.1 %fusion = f32[4,8,12,48,64]{4,2,3,1,0:T(8,128)} fusion(f32[4,8,48,64,12,1]{3,4,5,2,1,0:T(8,128)} %fusion.42, f32[4,8,48,64,12,1]{3,4,5,2,1,0:T(8,128)} %fusion.45, f32[8,2,4,8,48,64]{5,0,1,4,3,2:T(8,128)} %bitcast.190, pred[8,6,12]{2,0,1:T(8,128)(4,1)S(1)} %iota_compare_fusion), kind=kOutput, calls=%fused_computation.1 | convolution fusion | flops 228851712 | bytes 20449280 | tf_op jit(solution)/shard_map/sqk,sqgjpc->gjkpc/dot_general | solution.py:44
  742.7 12.1 %copy.73 = f32[4,8,12,48,64]{4,3,2,1,0:T(8,128)} copy(f32[4,8,12,48,64]{4,2,3,1,0:T(8,128)} %fusion) | data formatting | bytes 9437184 | tf_op jit(solution)/shard_map/add | solution.py:45
  754.8 9.4 %reshape.79 = f32[4,1,294912]{2,1,0:T(1,128)} reshape(f32[4,8,12,48,64]{4,3,2,1,0:T(8,128)} %copy.73) | data formatting | bytes 9437184
  764.2 111.1 %all_to_all.40 = f32[4,1,294912]{2,1,0:T(1,128)} all-to-all(f32[4,1,294912]{2,1,0:T(1,128)} %reshape.79), channel_id=1, replica_groups=mesh['grp'=4,'band'=8] {'grp'}, dimensions={0} | all-to-all | bytes 9437184 | tf_op jit(solution)/shard_map/all_to_all | solution.py:46
  875.3 17.3 %reduce.3 = f32[4,294912]{1,0:T(4,128)} reduce(f32[4,1,294912]{2,1,0:T(1,128)} %all_to_all.40, f32[]{:T(128)} %broadcast.2), dimensions={1}, to_apply=%all_to_all.31.reduce_sub_computation | reduce | bytes 9437188 | tf_op jit(solution)/shard_map/all_to_all | solution.py:46
  892.5 10.3 %reshape.80 = f32[4,8,12,48,64]{4,3,2,1,0:T(8,128)} reshape(f32[4,294912]{1,0:T(4,128)} %reduce.3) | data formatting | bytes 9437184
  902.8 4.9 reduce_sum.9
  907.7 1.7 copy.76
  (12 shorter events, 0.0 us)
Async XLA Ops:
  0.0 9.0 copy-start
  4.1 109.7 %all-to-all-start = ((f32[4,4608,64]{1,2,0:T(8,128)}), f32[4,4608,64]{1,2,0:T(8,128)}, u32[]{:S(2)}, u32[]{:S(2)}) async-start(f32[4,4608,64]{1,2,0:T(8,128)} %broadcast_in_dim.2), calls=%async_computation | async-start | bytes 9437184 | tf_op jit(solution)/shard_map/all_to_all | solution.py:20
  160.4 75.6 %all-to-all-start.5 = ((f32[8,1,196608]{2,1,0:T(1,128)}), f32[8,1,196608]{2,1,0:T(1,128)}, u32[]{:S(2)}, u32[]{:S(2)}) async-start(f32[8,1,196608]{2,1,0:T(1,128)} %reshape.77), calls=%async_computation.5 | async-start | bytes 12582912 | tf_op jit(solution)/shard_map/all_to_all | solution.py:33
  235.9 76.8 %all-to-all-start.1 = ((f32[8,1,196608]{2,1,0:T(1,128)}), f32[8,1,196608]{2,1,0:T(1,128)}, u32[]{:S(2)}, u32[]{:S(2)}) async-start(f32[8,1,196608]{2,1,0:T(1,128)} %reshape.75), calls=%async_computation.1 | async-start | bytes 12582912 | tf_op jit(solution)/shard_map/all_to_all | solution.py:33
  312.7 109.5 %all-to-all-start.3 = ((f32[8,1,196608]{2,1,0:T(1,128)}), f32[8,1,196608]{2,1,0:T(1,128)}, u32[]{:S(2)}, u32[]{:S(2)}) async-start(f32[8,1,196608]{2,1,0:T(1,128)} %reshape.73), calls=%async_computation.3 | async-start | bytes 12582912 | tf_op jit(solution)/shard_map/all_to_all | solution.py:33
  353.7 21.9 %copy-start.3 = (f32[8,2,4,8,48,64]{5,4,3,2,1,0:T(8,128)S(1)}, f32[8,2,4,8,48,64]{5,4,3,2,1,0:T(8,128)}, u32[]{:S(2)}) copy-start(f32[8,2,4,8,48,64]{5,4,3,2,1,0:T(8,128)} %reshape.76) | copy-start | bytes 18874372
  422.2 107.0 %all-to-all-start.2 = ((f32[8,2,1536,64]{2,3,1,0:T(8,128)}), f32[8,2,1536,64]{2,3,1,0:T(8,128)}, u32[]{:S(2)}, u32[]{:S(2)}) async-start(f32[8,2,1536,64]{2,3,1,0:T(8,128)} %copy.57), calls=%async_computation.2 | async-start | bytes 12582912 | tf_op jit(solution)/shard_map/all_to_all | solution.py:42
  460.7 21.7 %copy-start.4 = (f32[8,2,4,8,48,64]{5,4,3,2,1,0:T(8,128)S(1)}, f32[8,2,4,8,48,64]{5,4,3,2,1,0:T(8,128)}, u32[]{:S(2)}) copy-start(f32[8,2,4,8,48,64]{5,4,3,2,1,0:T(8,128)} %reshape.74) | copy-start | bytes 18874372
  529.2 106.8 %all-to-all-start.4 = ((f32[8,2,1536,64]{2,3,1,0:T(8,128)}), f32[8,2,1536,64]{2,3,1,0:T(8,128)}, u32[]{:S(2)}, u32[]{:S(2)}) async-start(f32[8,2,1536,64]{2,3,1,0:T(8,128)} %copy.64), calls=%async_computation.4 | async-start | bytes 12582912 | tf_op jit(solution)/shard_map/all_to_all | solution.py:42
  567.4 21.9 %copy-start.5 = (f32[8,2,4,8,48,64]{5,4,3,2,1,0:T(8,128)S(1)}, f32[8,2,4,8,48,64]{5,4,3,2,1,0:T(8,128)}, u32[]{:S(2)}) copy-start(f32[8,2,4,8,48,64]{5,4,3,2,1,0:T(8,128)} %reshape.78) | copy-start | bytes 18874372
  635.9 75.3 %all-to-all-start.6 = ((f32[8,2,1536,64]{2,3,1,0:T(8,128)}), f32[8,2,1536,64]{2,3,1,0:T(8,128)}, u32[]{:S(2)}, u32[]{:S(2)}) async-start(f32[8,2,1536,64]{2,3,1,0:T(8,128)} %copy.71), calls=%async_computation.6 | async-start | bytes 12582912 | tf_op jit(solution)/shard_map/all_to_all | solution.py:42
  663.8 11.8 %copy-start.2 = (f32[8,2,1536,64]{3,0,1,2:T(8,128)S(1)}, f32[8,2,1536,64]{3,0,1,2:T(8,128)}, u32[]{:S(2)}) copy-start(f32[8,2,1536,64]{3,0,1,2:T(8,128)} %copy.93) | copy-start | bytes 18874372
  892.5 16.9 %copy-start.1 = (s32[32,6]{0,1:T(8,128)S(1)}, s32[32,6]{0,1:T(8,128)}, u32[]{:S(2)}) copy-start(s32[32,6]{0,1:T(8,128)} %param.4) | copy-start | bytes 2308

commit v4 on v2

--- a/solution.py
+++ b/solution.py
@@ -10,12 +10,11 @@
     density = jnp.dot(
         first_block, second_block.T, precision=PRECISION, preferred_element_type=jnp.float32
     )
-    symmetric = jnp.where(diagonal, 0.5 * (coulomb_tile + coulomb_tile.T), coulomb_tile)
-    kernel = density * symmetric
+    kernel = density * coulomb_tile
     onto_first = jnp.dot(kernel, second_block, precision=PRECISION, preferred_element_type=jnp.float32)
     onto_second = jnp.dot(kernel.T, first_block, precision=PRECISION, preferred_element_type=jnp.float32)
-    onto_second = onto_second * jnp.where(diagonal, 0.0, 1.0)
-    return jnp.stack([onto_first, onto_second], 0)
+    scale = jnp.where(diagonal, 0.5, 1.0)
+    return jnp.stack([onto_first, onto_second], 0) * scale
 
 
 def body(orbitals, requests, coulomb):

time: 837 us -> 834 us (level)
  waiting for transfers between devices: 305 us -> 373 us
  local copies, waits for them, and re-layouts: 215 us -> 157 us
  matrix products: 110 us -> 95.3 us
    squeeze x4 -> x0, local copies, waits for them, and re-layouts: 48.6 us -> none  [body(): result = slot_work(pair_rows[0], pair_rows[1], coulomb[slot], diagonal)]
    all_to_all x3, waiting for transfers between devices: 85.2 us -> 120 us  [body(): lax.all_to_all(outbound, 'band', split_axis=0, concat_axis=0, tiled=True)]
    all_to_all x3, waiting for transfers between devices: 115 us -> 148 us  [body(): lax.all_to_all(outgoing, 'band', split_axis=0, concat_axis=0, tiled=True)]
    dot_general x3, matrix products: 32.4 us -> 22.5 us  [slot_work(): jnp.dot(kernel, second_block, precision=PRECISION, preferred_element_type...]
    unnamed x26 -> x8, local copies, waits for them, and re-layouts: 22.7 us -> 19.6 us
  transfers between devices with their start and end apart: 7 -> 7, of which waited for: 6 -> 7; matrix products, arithmetic and copies ran while one was open for 26% -> 18% of each run, Pallas kernels for 0% -> 0%
where the time goes in v4:
time: 834 us; the launch traced here: 826 us
  waiting for transfers between devices  373 us (45%)
  local copies, waits for them, and re-layouts  157 us (19%)
  blocking collectives  111 us (13%)
  matrix products  95.3 us (11%)
  other arithmetic  44.4 us (5%)
  starting transfers between devices  41.3 us (5%)
    all_to_all x3, waiting for transfers between devices, body(): lax.all_to_all(outgoing, 'band', split_axis=0, concat_axis=0, tiled=True)  148 us
    all_to_all x3, waiting for transfers between devices, body(): lax.all_to_all(outbound, 'band', split_axis=0, concat_axis=0, tiled=True)  120 us
    all_to_all x1, blocking collectives, body(): lax.all_to_all(summed, 'grp', split_axis=0, concat_axis=0, tiled=True)  111 us
    all_to_all x1, waiting for transfers between devices, body(): lax.all_to_all(copies, 'grp', split_axis=0, concat_axis=0, tiled=True)  104 us
    dot_general x3, matrix products, slot_work(): jnp.dot(first_block, second_block.T, precision=PRECISION, preferred_eleme...  36.3 us
    all_to_all x3, local copies, waits for them, and re-layouts, body(): lax.all_to_all(outbound, 'band', split_axis=0, concat_axis=0, tiled=True)  27.2 us
    dot_general x3, matrix products, slot_work(): jnp.dot(kernel.T, first_block, precision=PRECISION, preferred_element_typ...  24.1 us
    dot_general x3, matrix products, slot_work(): jnp.dot(kernel, second_block, precision=PRECISION, preferred_element_type...  22.5 us
  transfers between devices with their start and end apart: 7, of which 7 were waited for; matrix products, arithmetic and copies ran while one was open for 18% of the time, Pallas kernels for 0%

profile of v4, /device:TPU:2, one launch (start us, length us, event | category | flops | bytes accessed | tf_op | source)
XLA Modules:
  0.0 826.2 jit_solution(14515839127205263711)
XLA Ops:
  0.0 4.1 broadcast_in_dim.11
  4.1 5.0 all-to-all-start
  9.1 0.1 copy.33
  9.2 0.1 reshape.164
  9.3 0.1 copy.30
  9.4 0.1 copy.34
  9.5 104.2 %all-to-all-done = f32[4,4608,64]{1,2,0:T(8,128)} async-done(((f32[4,4608,64]{1,2,0:T(8,128)}), f32[4,4608,64]{1,2,0:T(8,128)}, u32[]{:S(2)}, u32[]{:S(2)}) %all-to-all-start) | async-done | bytes 4718624 | tf_op jit(solution)/shard_map/all_to_all | solution.py:30
  113.7 7.6 copy.31
  121.3 12.0 %copy.32 = f32[12,32,48,64]{2,1,3,0:T(8,128)} copy(f32[12,32,48,64]{3,2,0,1:T(8,128)} %bitcast.155) | data formatting | bytes 9437184 | tf_op jit(solution)/shard_map/transpose | solution.py:34
  133.3 13.1 %reshape.125 = f32[12,1536,64]{1,2,0:T(8,128)} reshape(f32[12,32,48,64]{2,1,3,0:T(8,128)} %copy.32) | data formatting | bytes 9437184 | tf_op jit(solution)/shard_map/reshape | solution.py:35
  146.4 6.0 gather_fusion
  152.3 6.3 select_multiply_fusion.2
  158.7 5.2 all-to-all-start.1
  164.0 0.1 copy.37
  164.2 5.9 gather_fusion.1
  170.1 6.4 select_multiply_fusion.1
  176.5 57.6 %all-to-all-done.1 = f32[8,2,1536,64]{2,3,1,0:T(8,128)} async-done(((f32[8,2,1536,64]{2,3,1,0:T(8,128)}), f32[8,2,1536,64]{2,3,1,0:T(8,128)}, u32[]{:S(2)}, u32[]{:S(2)}) %all-to-all-start.1) | async-done | bytes 6291488 | tf_op jit(solution)/shard_map/all_to_all | solution.py:47
  234.1 6.2 all-to-all-start.3
  240.4 0.1 copy.42
  240.6 6.0 gather_fusion.2
  246.6 6.3 select_multiply_fusion
  252.9 57.5 %all-to-all-done.3 = f32[8,2,1536,64]{2,3,1,0:T(8,128)} async-done(((f32[8,2,1536,64]{2,3,1,0:T(8,128)}), f32[8,2,1536,64]{2,3,1,0:T(8,128)}, u32[]{:S(2)}, u32[]{:S(2)}) %all-to-all-start.3) | async-done | bytes 6291488 | tf_op jit(solution)/shard_map/all_to_all | solution.py:47
  310.4 6.4 all-to-all-start.5
  317.0 0.6 fusion.70
  318.8 3.4 copy.63
  322.2 12.1 %bitcast_multiply_fusion.2 = f32[1536,1536]{1,0:T(8,128)S(1)} fusion(f32[3,1536,1536]{2,1,0:T(8,128)} %param.7, f32[2,1536,8,64]{1,3,2,0:T(8,128)S(1)} %bitcast.158), kind=kOutput, calls=%fused_computation.23 | convolution fusion | flops 7250116608 | bytes 25165824 | tf_op jit(solution)/shard_map/dot_general | solution.py:10
  334.2 7.5 fusion.24
  341.7 8.2 fusion.27
  350.0 0.7 fusion.18
  350.6 3.1 copy.36
  353.8 33.3 %all-to-all-done.5 = f32[8,2,1536,64]{2,3,1,0:T(8,128)} async-done(((f32[8,2,1536,64]{2,3,1,0:T(8,128)}), f32[8,2,1536,64]{2,3,1,0:T(8,128)}, u32[]{:S(2)}, u32[]{:S(2)}) %all-to-all-start.5) | async-done | bytes 6291488 | tf_op jit(solution)/shard_map/all_to_all | solution.py:47
  387.0 6.2 all-to-all-start.2
  394.6 3.4 copy.62
  398.0 12.0 %bitcast_multiply_fusion.1 = f32[1536,1536]{1,0:T(8,128)S(1)} fusion(f32[3,1536,1536]{2,1,0:T(8,128)} %param.7, f32[2,1536,8,64]{1,3,2,0:T(8,128)S(1)} %bitcast.161), kind=kOutput, calls=%fused_computation.18 | convolution fusion | flops 7250116608 | bytes 25165824 | tf_op jit(solution)/shard_map/dot_general | solution.py:10
  409.9 7.5 fusion.30
  417.5 8.0 fusion.33
  425.4 0.7 fusion.19
  426.1 3.1 copy.41
  429.1 34.3 %all-to-all-done.2 = f32[8,2,1536,64]{2,3,1,0:T(8,128)} async-done(((f32[8,2,1536,64]{2,3,1,0:T(8,128)}), f32[8,2,1536,64]{2,3,1,0:T(8,128)}, u32[]{:S(2)}, u32[]{:S(2)}) %all-to-all-start.2) | async-done | bytes 6291488 | tf_op jit(solution)/shard_map/all_to_all | solution.py:52
  463.4 6.2 all-to-all-start.4
  471.0 3.4 copy.61
  474.4 12.3 %bitcast_multiply_fusion = f32[1536,1536]{1,0:T(8,128)S(1)} fusion(f32[3,1536,1536]{2,1,0:T(8,128)} %param.7, f32[2,1536,8,64]{1,3,2,0:T(8,128)S(1)} %bitcast.164), kind=kOutput, calls=%fused_computation.13 | convolution fusion | flops 7250116608 | bytes 25165824 | tf_op jit(solution)/shard_map/dot_general | solution.py:10
  486.7 7.5 fusion.36
  494.2 7.9 fusion.39
  502.1 0.7 fusion.20
  502.8 3.1 copy.46
  505.9 33.9 %all-to-all-done.4 = f32[8,2,1536,64]{2,3,1,0:T(8,128)} async-done(((f32[8,2,1536,64]{2,3,1,0:T(8,128)}), f32[8,2,1536,64]{2,3,1,0:T(8,128)}, u32[]{:S(2)}, u32[]{:S(2)}) %all-to-all-start.4) | async-done | bytes 6291488 | tf_op jit(solution)/shard_map/all_to_all | solution.py:52
  539.8 6.2 all-to-all-start.6
  546.0 9.1 %copy.47 = f32[8,2,1536,64]{2,0,1,3:T(8,128)} copy(f32[8,2,1536,64]{2,3,1,0:T(8,128)} %all-to-all-done.2) | data formatting | bytes 12582912 | tf_op jit(solution)/shard_map/all_to_all | solution.py:52
  555.1 9.0 %copy.48 = f32[8,2,1536,64]{2,0,1,3:T(8,128)} copy(f32[8,2,1536,64]{2,3,1,0:T(8,128)} %all-to-all-done.4) | data formatting | bytes 12582912 | tf_op jit(solution)/shard_map/all_to_all | solution.py:52
  564.1 52.1 %all-to-all-done.6 = f32[8,2,1536,64]{2,3,1,0:T(8,128)} async-done(((f32[8,2,1536,64]{2,3,1,0:T(8,128)}), f32[8,2,1536,64]{2,3,1,0:T(8,128)}, u32[]{:S(2)}, u32[]{:S(2)}) %all-to-all-start.6) | async-done | bytes 6291488 | tf_op jit(solution)/shard_map/all_to_all | solution.py:52
  616.2 9.1 %copy.49 = f32[8,2,1536,64]{2,0,1,3:T(8,128)} copy(f32[8,2,1536,64]{2,3,1,0:T(8,128)} %all-to-all-done.6) | data formatting | bytes 12582912 | tf_op jit(solution)/shard_map/all_to_all | solution.py:52
  625.2 12.4 %fusion.21 = f32[12,1536,64]{1,0,2:T(8,128)} fusion(f32[8,2,1536,64]{2,0,1,3:T(8,128)} %copy.49, f32[8,2,1536,64]{2,0,1,3:T(8,128)} %copy.48, f32[8,2,1536,64]{2,0,1,3:T(8,128)} %copy.47, s32[8,6]{0,1:T(8,128)S(1)} %copy-done.1), kind=kOutput, calls=%fused_computation.36 | convolution fusion | flops 688915008 | bytes 23593152 | tf_op jit(solution)/shard_map/srk,srpc->kpc/dot_general | solution.py:57
  637.7 7.6 copy.50
  645.3 10.6 %reshape.132 = f32[12,4,8,48,64]{3,2,1,4,0:T(8,128)} reshape(f32[12,1536,64]{1,2,0:T(8,128)} %copy.50) | data formatting | bytes 9437184 | tf_op jit(solution)/shard_map/reshape | solution.py:58
  655.9 11.6 %copy.51 = f32[4,12,8,48,64]{4,3,2,1,0:T(8,128)} copy(f32[4,12,8,48,64]{3,2,0,4,1:T(8,128)} %bitcast.154) | data formatting | bytes 9437184 | tf_op jit(solution)/shard_map/transpose | solution.py:59
  667.6 9.3 %reshape.184 = f32[4,1,294912]{2,1,0:T(1,128)} reshape(f32[4,12,8,48,64]{4,3,2,1,0:T(8,128)} %copy.51) | data formatting | bytes 9437184
  676.9 111.1 %all_to_all.40 = f32[4,1,294912]{2,1,0:T(1,128)} all-to-all(f32[4,1,294912]{2,1,0:T(1,128)} %reshape.184), channel_id=1, replica_groups=mesh['grp'=4,'band'=8] {'grp'}, dimensions={0} | all-to-all | bytes 9437184 | tf_op jit(solution)/shard_map/all_to_all | solution.py:60
  788.0 0.5 broadcast.70
  788.5 16.9 %reduce = f32[4,294912]{1,0:T(4,128)} reduce(f32[4,1,294912]{2,1,0:T(1,128)} %all_to_all.40, f32[]{:T(128)} %broadcast.70), dimensions={1}, to_apply=%all_to_all.31.reduce_sub_computation | reduce | bytes 9437188 | tf_op jit(solution)/shard_map/all_to_all | solution.py:60
  805.5 10.3 %reshape.185 = f32[4,12,8,48,64]{4,3,2,1,0:T(8,128)} reshape(f32[4,294912]{1,0:T(4,128)} %reduce) | data formatting | bytes 9437184
  815.8 6.4 reduce_sum.9
  822.1 1.9 copy.53
  824.0 1.7 copy.54
  (20 shorter events, 0.7 us)
Async XLA Ops:
  0.0 9.0 %copy-start.2 = (s32[32,6]{0,1:T(8,128)S(1)}, s32[32,6]{0,1:T(8,128)}, u32[]{:S(2)}) copy-start(s32[32,6]{0,1:T(8,128)} %param.6) | copy-start | bytes 2308
  4.1 109.7 %all-to-all-start = ((f32[4,4608,64]{1,2,0:T(8,128)}), f32[4,4608,64]{1,2,0:T(8,128)}, u32[]{:S(2)}, u32[]{:S(2)}) async-start(f32[4,4608,64]{1,2,0:T(8,128)} %broadcast_in_dim.11), calls=%async_computation | async-start | bytes 9437184 | tf_op jit(solution)/shard_map/all_to_all | solution.py:30
  9.1 112.2 %copy-start = (s32[8,6]{0,1:T(8,128)}, s32[8,6]{0,1:T(8,128)S(1)}, u32[]{:S(2)}) copy-start(s32[8,6]{0,1:T(8,128)S(1)} %get-tuple-element.7) | copy-start | bytes 580
  158.7 75.4 %all-to-all-start.1 = ((f32[8,2,1536,64]{2,3,1,0:T(8,128)}), f32[8,2,1536,64]{2,3,1,0:T(8,128)}, u32[]{:S(2)}, u32[]{:S(2)}) async-start(f32[8,2,1536,64]{2,3,1,0:T(8,128)} %select_multiply_fusion.2), calls=%async_computation.1 | async-start | bytes 12582912 | tf_op jit(solution)/shard_map/all_to_all | solution.py:47
  234.1 76.4 %all-to-all-start.3 = ((f32[8,2,1536,64]{2,3,1,0:T(8,128)}), f32[8,2,1536,64]{2,3,1,0:T(8,128)}, u32[]{:S(2)}, u32[]{:S(2)}) async-start(f32[8,2,1536,64]{2,3,1,0:T(8,128)} %select_multiply_fusion.1), calls=%async_computation.3 | async-start | bytes 12582912 | tf_op jit(solution)/shard_map/all_to_all | solution.py:47
  310.4 76.6 %all-to-all-start.5 = ((f32[8,2,1536,64]{2,3,1,0:T(8,128)}), f32[8,2,1536,64]{2,3,1,0:T(8,128)}, u32[]{:S(2)}, u32[]{:S(2)}) async-start(f32[8,2,1536,64]{2,3,1,0:T(8,128)} %select_multiply_fusion), calls=%async_computation.5 | async-start | bytes 12582912 | tf_op jit(solution)/shard_map/all_to_all | solution.py:47
  387.0 76.4 %all-to-all-start.2 = ((f32[8,2,1536,64]{2,3,1,0:T(8,128)}), f32[8,2,1536,64]{2,3,1,0:T(8,128)}, u32[]{:S(2)}, u32[]{:S(2)}) async-start(f32[8,2,1536,64]{2,3,1,0:T(8,128)} %copy.36), calls=%async_computation.2 | async-start | bytes 12582912 | tf_op jit(solution)/shard_map/all_to_all | solution.py:52
  463.4 76.4 %all-to-all-start.4 = ((f32[8,2,1536,64]{2,3,1,0:T(8,128)}), f32[8,2,1536,64]{2,3,1,0:T(8,128)}, u32[]{:S(2)}, u32[]{:S(2)}) async-start(f32[8,2,1536,64]{2,3,1,0:T(8,128)} %copy.41), calls=%async_computation.4 | async-start | bytes 12582912 | tf_op jit(solution)/shard_map/all_to_all | solution.py:52
  539.8 76.4 %all-to-all-start.6 = ((f32[8,2,1536,64]{2,3,1,0:T(8,128)}), f32[8,2,1536,64]{2,3,1,0:T(8,128)}, u32[]{:S(2)}, u32[]{:S(2)}) async-start(f32[8,2,1536,64]{2,3,1,0:T(8,128)} %copy.46), calls=%async_computation.6 | async-start | bytes 12582912 | tf_op jit(solution)/shard_map/all_to_all | solution.py:52
  564.1 61.1 %copy-start.1 = (s32[8,6]{0,1:T(8,128)S(1)}, s32[8,6]{0,1:T(8,128)}, u32[]{:S(2)}) copy-start(s32[8,6]{0,1:T(8,128)} %copy-done) | copy-start | bytes 580

commit v5 on v4

--- a/solution.py
+++ b/solution.py
@@ -17,6 +17,37 @@
     return jnp.stack([onto_first, onto_second], 0) * scale
 
 
+def line_gather(x, axis, count):
+    index = lax.axis_index(axis)
+    spare = jnp.zeros((count + 1,) + x.shape, x.dtype)
+    spare = lax.dynamic_update_index_in_dim(spare, x, index, 0)
+    rightward, leftward = x, x
+    for step in range(1, count):
+        rightward = lax.ppermute(rightward, axis, [(i, i + 1) for i in range(step - 1, count - 1)])
+        leftward = lax.ppermute(leftward, axis, [(i + 1, i) for i in range(0, count - step)])
+        from_left = jnp.where(index >= step, index - step, count)
+        from_right = jnp.where(index + step < count, index + step, count)
+        spare = lax.dynamic_update_index_in_dim(spare, rightward, from_left, 0)
+        spare = lax.dynamic_update_index_in_dim(spare, leftward, from_right, 0)
+    return spare[:count]
+
+
+def line_reduce(parts, axis, count):
+    index = lax.axis_index(axis)
+
+    def part_for(target):
+        return lax.dynamic_index_in_dim(parts, jnp.clip(target, 0, count - 1), 0, keepdims=False)
+
+    rightward = jnp.zeros(parts.shape[1:], parts.dtype)
+    leftward = jnp.zeros(parts.shape[1:], parts.dtype)
+    for step in range(1, count):
+        send_right = rightward + part_for(index + count - step)
+        send_left = leftward + part_for(index - count + step)
+        rightward = lax.ppermute(send_right, axis, [(i, i + 1) for i in range(0, step)])
+        leftward = lax.ppermute(send_left, axis, [(i, i - 1) for i in range(count - step, count)])
+    return part_for(index) + rightward + leftward
+
+
 def body(orbitals, requests, coulomb):
     group_count = lax.axis_size("grp")
     band_count = lax.axis_size("band")
@@ -26,8 +57,7 @@
     orbital_width = col_width * band_count
     piece_rows = blk // devices
     slot_count = coulomb.shape[0]
-    copies = jnp.broadcast_to(orbitals[None], (group_count,) + orbitals.shape)
-    all_points = lax.all_to_all(copies, "grp", split_axis=0, concat_axis=0, tiled=True)
+    all_points = line_gather(orbitals, "grp", group_count)
     block_count = all_points.shape[0] * all_points.shape[1] // (devices * piece_rows)
     blocks = (
         all_points.reshape(devices, block_count, piece_rows, col_width)
@@ -57,8 +87,7 @@
     summed = jnp.einsum("srk,srpc->kpc", one_hot, returned, precision=lax.Precision.HIGHEST)
     summed = summed.reshape(block_count, group_count, band_count, piece_rows, col_width)
     summed = summed.transpose(1, 0, 2, 3, 4)
-    parts = lax.all_to_all(summed, "grp", split_axis=0, concat_axis=0, tiled=True)
-    mine = parts.sum(axis=0).transpose(1, 0, 2, 3)
+    mine = line_reduce(summed, "grp", group_count).transpose(1, 0, 2, 3)
     return mine.reshape(band_count * block_count * piece_rows, col_width)
 
 

time: 834 us -> 860 us (1.031)
  blocking collectives: 111 us -> 0 us
  waiting for transfers between devices: 373 us -> 447 us
  local copies, waits for them, and re-layouts: 157 us -> 187 us
  starting transfers between devices: 41.3 us -> 68.3 us
    ppermute x0 -> x12, waiting for transfers between devices: none -> 179 us  [the longest x3 115 us: line_reduce(): lax.ppermute(send_right, axis, [(i, i + 1) for i in range(0, step)])]
    all_to_all x1 -> x0, blocking collectives: 111 us -> none  [body(): lax.all_to_all(summed, 'grp', split_axis=0, concat_axis=0, tiled=True)]
    all_to_all x1 -> x0, waiting for transfers between devices: 104 us -> none  [body(): lax.all_to_all(copies, 'grp', split_axis=0, concat_axis=0, tiled=True)]
    another operation x0 -> x8, local copies, waits for them, and re-layouts: none -> 37.3 us
    ppermute x0 -> x12, starting transfers between devices: none -> 31.8 us  [the longest x3 14.5 us: line_reduce(): lax.ppermute(send_right, axis, [(i, i + 1) for i in range(0, step)])]
    unnamed x8 -> x23, local copies, waits for them, and re-layouts: 19.6 us -> 1.87 us
    all_to_all x1 -> x0, other arithmetic: 16.9 us -> none  [body(): lax.all_to_all(summed, 'grp', split_axis=0, concat_axis=0, tiled=True)]
    add x0 -> x4, other arithmetic: none -> 15 us  [the longest x2 8.16 us: line_reduce(): send_right = rightward + part_for(index + count - step)]
  transfers between devices with their start and end apart: 7 -> 18, of which waited for: 7 -> 13; matrix products, arithmetic and copies ran while one was open for 18% -> 25% of each run, Pallas kernels for 0% -> 0%
where the time goes in v5:
time: 860 us; the launch traced here: 844 us
  waiting for transfers between devices  447 us (52%)
  local copies, waits for them, and re-layouts  187 us (22%)
  matrix products  94.9 us (11%)
  starting transfers between devices  68.3 us (8%)
  other arithmetic  42.1 us (5%)
    all_to_all x3, waiting for transfers between devices, body(): lax.all_to_all(outgoing, 'band', split_axis=0, concat_axis=0, tiled=True)  149 us
    all_to_all x3, waiting for transfers between devices, body(): lax.all_to_all(outbound, 'band', split_axis=0, concat_axis=0, tiled=True)  120 us
    ppermute x3, waiting for transfers between devices, line_reduce(): lax.ppermute(send_right, axis, [(i, i + 1) for i in range(0, step)])  115 us
    ppermute x3, waiting for transfers between devices, line_gather(): lax.ppermute(leftward, axis, [(i + 1, i) for i in range(0, count - step)])  45.9 us
    another operation x8, local copies, waits for them, and re-layouts  37.3 us
    dot_general x3, matrix products, slot_work(): jnp.dot(first_block, second_block.T, precision=PRECISION, preferred_eleme...  35.8 us
    all_to_all x3, local copies, waits for them, and re-layouts, body(): lax.all_to_all(outbound, 'band', split_axis=0, concat_axis=0, tiled=True)  27.2 us
    dot_general x3, matrix products, slot_work(): jnp.dot(kernel.T, first_block, precision=PRECISION, preferred_element_typ...  24.2 us
  transfers between devices with their start and end apart: 18, of which 13 were waited for; matrix products, arithmetic and copies ran while one was open for 25% of the time, Pallas kernels for 0%

profile of v5, /device:TPU:2, one launch (start us, length us, event | category | flops | bytes accessed | tf_op | source)
XLA Modules:
  0.0 843.9 jit_solution(6944774770718904467)
XLA Ops:
  0.0 4.6 collective-permute-start
  13.6 5.1 broadcast_in_dim.39
  20.3 8.7 %collective-permute-done = f32[4608,64]{0,1:T(8,128)} collective-permute-done((f32[4608,64]{0,1:T(8,128)}, f32[4608,64]{0,1:T(8,128)}, u32[]{:S(2)}, u32[]{:S(2)}) %collective-permute-start) | collective-permute-done | bytes 1179680 | tf_op jit(solution)/shard_map/ppermute | solution.py:26
  42.9 24.2 %collective-permute-done.3 = f32[4608,64]{0,1:T(8,128)} collective-permute-done((f32[4608,64]{0,1:T(8,128)S(1)}, f32[4608,64]{0,1:T(8,128)}, u32[]{:S(2)}, u32[]{:S(2)}) %collective-permute-start.3) | collective-permute-done | bytes 1179680 | tf_op jit(solution)/shard_map/ppermute | solution.py:27
  75.2 21.7 %collective-permute-done.5 = f32[4608,64]{0,1:T(8,128)S(1)} collective-permute-done((f32[4608,64]{0,1:T(8,128)}, f32[4608,64]{0,1:T(8,128)S(1)}, u32[]{:S(2)}, u32[]{:S(2)}) %collective-permute-start.5) | collective-permute-done | bytes 1179680 | tf_op jit(solution)/shard_map/ppermute | solution.py:27
  99.4 7.9 slice.106
  107.3 12.0 %copy.37 = f32[12,32,48,64]{2,1,3,0:T(8,128)} copy(f32[12,32,48,64]{3,2,0,1:T(8,128)} %bitcast.183) | data formatting | bytes 9437184 | tf_op jit(solution)/shard_map/transpose | solution.py:64
  119.3 13.0 %reshape.138 = f32[12,1536,64]{1,2,0:T(8,128)} reshape(f32[12,32,48,64]{2,1,3,0:T(8,128)} %copy.37) | data formatting | bytes 9437184 | tf_op jit(solution)/shard_map/reshape | solution.py:65
  132.3 5.9 gather_fusion
  138.3 6.4 select_multiply_fusion.2
  144.6 5.3 all-to-all-start
  150.3 5.9 gather_fusion.1
  156.2 6.3 select_multiply_fusion.1
  162.6 57.6 %all-to-all-done = f32[8,2,1536,64]{2,3,1,0:T(8,128)} async-done(((f32[8,2,1536,64]{2,3,1,0:T(8,128)}), f32[8,2,1536,64]{2,3,1,0:T(8,128)}, u32[]{:S(2)}, u32[]{:S(2)}) %all-to-all-start) | async-done | bytes 6291488 | tf_op jit(solution)/shard_map/all_to_all | solution.py:77
  220.1 6.1 all-to-all-start.2
  226.6 6.0 gather_fusion.2
  232.6 6.4 select_multiply_fusion
  239.0 57.5 %all-to-all-done.2 = f32[8,2,1536,64]{2,3,1,0:T(8,128)} async-done(((f32[8,2,1536,64]{2,3,1,0:T(8,128)}), f32[8,2,1536,64]{2,3,1,0:T(8,128)}, u32[]{:S(2)}, u32[]{:S(2)}) %all-to-all-start.2) | async-done | bytes 6291488 | tf_op jit(solution)/shard_map/all_to_all | solution.py:77
  296.5 6.6 all-to-all-start.4
  305.1 3.4 copy.71
  308.5 11.8 %bitcast_multiply_fusion.2 = f32[1536,1536]{1,0:T(8,128)S(1)} fusion(f32[3,1536,1536]{2,1,0:T(8,128)} %param.7, f32[2,1536,8,64]{1,3,2,0:T(8,128)S(1)} %bitcast.185), kind=kOutput, calls=%fused_computation.23 | convolution fusion | flops 7250116608 | bytes 25165824 | tf_op jit(solution)/shard_map/dot_general | solution.py:10
  320.3 7.5 fusion.24
  327.8 7.9 fusion.27
  336.4 3.2 copy.41
  339.5 33.7 %all-to-all-done.4 = f32[8,2,1536,64]{2,3,1,0:T(8,128)} async-done(((f32[8,2,1536,64]{2,3,1,0:T(8,128)}), f32[8,2,1536,64]{2,3,1,0:T(8,128)}, u32[]{:S(2)}, u32[]{:S(2)}) %all-to-all-start.4) | async-done | bytes 6291488 | tf_op jit(solution)/shard_map/all_to_all | solution.py:77
  373.2 6.2 all-to-all-start.1
  380.7 3.4 copy.70
  384.1 12.0 %bitcast_multiply_fusion.1 = f32[1536,1536]{1,0:T(8,128)S(1)} fusion(f32[3,1536,1536]{2,1,0:T(8,128)} %param.7, f32[2,1536,8,64]{1,3,2,0:T(8,128)S(1)} %bitcast.188), kind=kOutput, calls=%fused_computation.18 | convolution fusion | flops 7250116608 | bytes 25165824 | tf_op jit(solution)/shard_map/dot_general | solution.py:10
  396.1 7.5 fusion.30
  403.6 8.2 fusion.33
  415.5 34.0 %all-to-all-done.1 = f32[8,2,1536,64]{2,3,1,0:T(8,128)} async-done(((f32[8,2,1536,64]{2,3,1,0:T(8,128)}), f32[8,2,1536,64]{2,3,1,0:T(8,128)}, u32[]{:S(2)}, u32[]{:S(2)}) %all-to-all-start.1) | async-done | bytes 6291488 | tf_op jit(solution)/shard_map/all_to_all | solution.py:82
  449.6 6.1 all-to-all-start.3
  457.0 3.4 copy.69
  460.3 12.0 %bitcast_multiply_fusion = f32[1536,1536]{1,0:T(8,128)S(1)} fusion(f32[3,1536,1536]{2,1,0:T(8,128)} %param.7, f32[2,1536,8,64]{1,3,2,0:T(8,128)S(1)} %bitcast.191), kind=kOutput, calls=%fused_computation.13 | convolution fusion | flops 7250116608 | bytes 25165824 | tf_op jit(solution)/shard_map/dot_general | solution.py:10
  472.3 7.5 fusion.36
  479.8 8.2 fusion.39
  488.7 3.2 copy.51
  491.8 34.1 %all-to-all-done.3 = f32[8,2,1536,64]{2,3,1,0:T(8,128)} async-done(((f32[8,2,1536,64]{2,3,1,0:T(8,128)}), f32[8,2,1536,64]{2,3,1,0:T(8,128)}, u32[]{:S(2)}, u32[]{:S(2)}) %all-to-all-start.3) | async-done | bytes 6291488 | tf_op jit(solution)/shard_map/all_to_all | solution.py:82
  525.9 6.2 all-to-all-start.5
  532.1 9.0 %copy.52 = f32[8,2,1536,64]{2,0,1,3:T(8,128)} copy(f32[8,2,1536,64]{2,3,1,0:T(8,128)} %all-to-all-done.1) | data formatting | bytes 12582912 | tf_op jit(solution)/shard_map/all_to_all | solution.py:82
  541.1 9.1 %copy.53 = f32[8,2,1536,64]{2,0,1,3:T(8,128)} copy(f32[8,2,1536,64]{2,3,1,0:T(8,128)} %all-to-all-done.3) | data formatting | bytes 12582912 | tf_op jit(solution)/shard_map/all_to_all | solution.py:82
  550.2 52.1 %all-to-all-done.5 = f32[8,2,1536,64]{2,3,1,0:T(8,128)} async-done(((f32[8,2,1536,64]{2,3,1,0:T(8,128)}), f32[8,2,1536,64]{2,3,1,0:T(8,128)}, u32[]{:S(2)}, u32[]{:S(2)}) %all-to-all-start.5) | async-done | bytes 6291488 | tf_op jit(solution)/shard_map/all_to_all | solution.py:82
  602.3 9.1 %copy.54 = f32[8,2,1536,64]{2,0,1,3:T(8,128)} copy(f32[8,2,1536,64]{2,3,1,0:T(8,128)} %all-to-all-done.5) | data formatting | bytes 12582912 | tf_op jit(solution)/shard_map/all_to_all | solution.py:82
  611.3 12.4 %fusion.21 = f32[12,1536,64]{1,0,2:T(8,128)} fusion(f32[8,2,1536,64]{2,0,1,3:T(8,128)} %copy.54, f32[8,2,1536,64]{2,0,1,3:T(8,128)} %copy.53, f32[8,2,1536,64]{2,0,1,3:T(8,128)} %copy.52, s32[8,6]{0,1:T(8,128)S(1)} %copy-done.3), kind=kOutput, calls=%fused_computation.36 | convolution fusion | flops 688915008 | bytes 23593152 | tf_op jit(solution)/shard_map/srk,srpc->kpc/dot_general | solution.py:87
  623.8 7.6 copy.55
  631.4 10.7 %reshape.145 = f32[12,4,8,48,64]{3,2,1,4,0:T(8,128)} reshape(f32[12,1536,64]{1,2,0:T(8,128)} %copy.55) | data formatting | bytes 9437184 | tf_op jit(solution)/shard_map/reshape | solution.py:88
  642.1 14.5 %constant_dynamic-slice_fusion.6 = (f32[12,1,8,48,64]{3,2,1,4,0:T(8,128)S(1)}, f32[12,1,8,48,64]{3,2,1,4,0:T(8,128)}, f32[12,1,8,48,64]{3,2,1,4,0:T(8,128)}, f32...) fusion(f32[12,4,8,48,64]{3,2,1,4,0:T(8,128)} %reshape.145, ...), kind=kLoop, calls=%fused_computation.93 | loop fusion | bytes 16515100 | tf_op jit(solution)/shard_map/dynamic-slice
  656.6 3.4 copy.57
  662.9 3.4 copy.60
  668.4 3.4 copy.58
  671.7 3.4 copy.61
  675.1 37.5 %collective-permute-done.6 = f32[12,8,48,64]{3,2,1,0:T(8,128)} collective-permute-done((f32[12,8,48,64]{3,2,1,0:T(8,128)}, f32[12,8,48,64]{3,2,1,0:T(8,128)}, u32[]{:S(2)}, u32[]{:S(2)}) %collective-permute-start.6) | collective-permute-done | bytes 1179680 | tf_op jit(solution)/shard_map/ppermute | solution.py:46
  712.6 4.1 bitcast_add_fusion.3
  716.7 5.8 collective-permute-start.7
  722.5 3.4 bitcast_add_fusion.1
  728.0 3.6 copy.59
  731.6 3.4 copy.62
  735.0 36.4 %collective-permute-done.7 = f32[12,8,48,64]{3,2,1,0:T(8,128)} collective-permute-done((f32[12,8,48,64]{3,2,1,0:T(8,128)}, f32[12,8,48,64]{3,2,1,0:T(8,128)}, u32[]{:S(2)}, u32[]{:S(2)}) %collective-permute-start.7) | collective-permute-done | bytes 1179680 | tf_op jit(solution)/shard_map/ppermute | solution.py:46
  771.4 4.0 bitcast_add_fusion.2
  775.5 5.8 collective-permute-start.8
  781.3 3.4 bitcast_add_fusion
  788.2 41.0 %collective-permute-done.8 = f32[12,8,48,64]{3,2,1,0:T(8,128)} collective-permute-done((f32[12,8,48,64]{3,2,1,0:T(8,128)}, f32[12,8,48,64]{3,2,1,0:T(8,128)}, u32[]{:S(2)}, u32[]{:S(2)}) %collective-permute-start.8) | collective-permute-done | bytes 1179680 | tf_op jit(solution)/shard_map/ppermute | solution.py:46
  829.2 9.0 %collective-permute-done.11 = f32[12,8,48,64]{3,2,1,0:T(8,128)} collective-permute-done((f32[12,8,48,64]{3,2,1,0:T(8,128)}, f32[12,8,48,64]{3,2,1,0:T(8,128)}, u32[]{:S(2)}, u32[]{:S(2)}) %collective-permute-start.11) | collective-permute-done | bytes 1179680 | tf_op jit(solution)/shard_map/ppermute | solution.py:47
  838.2 3.5 fusion.67
  (78 shorter events, 54.0 us)
Async XLA Ops:
  0.0 29.0 %collective-permute-start = (f32[4608,64]{0,1:T(8,128)}, f32[4608,64]{0,1:T(8,128)}, u32[]{:S(2)}, u32[]{:S(2)}) collective-permute-start(f32[4608,64]{0,1:T(8,128)} %param.5), channel_id=1, source_target_pairs={{0,8},{8,16},{16,24},{1,9},{9,17},{17,25},{2,10},{10,18},{18,26},{... | collective-permute-start | bytes 3538952 | tf_op jit(solution)/shard_map/ppermute | solution.py:26
  4.6 29.5 %collective-permute-start.1 = (f32[4608,64]{0,1:T(8,128)}, f32[4608,64]{0,1:T(8,128)S(1)}, u32[]{:S(2)}, u32[]{:S(2)}) collective-permute-start(f32[4608,64]{0,1:T(8,128)} %param.5), channel_id=1, source_target_pairs={{8,0},{16,8},{24,16},{9,1},{17,9},{25,17},{10,2},{18,10},{26,18},{... | collective-permute-start | bytes 3538952 | tf_op jit(solution)/shard_map/ppermute | solution.py:27
  8.5 0.6 copy-start.2
  30.8 7.0 collective-permute-start.2
  34.9 32.2 %collective-permute-start.3 = (f32[4608,64]{0,1:T(8,128)S(1)}, f32[4608,64]{0,1:T(8,128)}, u32[]{:S(2)}, u32[]{:S(2)}) collective-permute-start(f32[4608,64]{0,1:T(8,128)S(1)} %collective-permute-done.1), channel_id=1, source_target_pairs={{8,0},{16,8},{9,1},{17,9},{10,2},{18,10},{11,3},{19,11},{12,4},{20... | collective-permute-start | bytes 3538952 | tf_op jit(solution)/shard_map/ppermute | solution.py:27
  39.7 32.2 %collective-permute-start.4 = (f32[4608,64]{0,1:T(8,128)}, f32[4608,64]{0,1:T(8,128)}, u32[]{:S(2)}, u32[]{:S(2)}) collective-permute-start(f32[4608,64]{0,1:T(8,128)} %collective-permute-done.2), channel_id=1, source_target_pairs={{16,24},{17,25},{18,26},{19,27},{20,28},{21,29},{22,30},{23,31}} | collective-permute-start | bytes 3538952 | tf_op jit(solution)/shard_map/ppermute | solution.py:26
  68.9 28.0 %collective-permute-start.5 = (f32[4608,64]{0,1:T(8,128)}, f32[4608,64]{0,1:T(8,128)S(1)}, u32[]{:S(2)}, u32[]{:S(2)}) collective-permute-start(f32[4608,64]{0,1:T(8,128)} %collective-permute-done.3), channel_id=1, source_target_pairs={{8,0},{9,1},{10,2},{11,3},{12,4},{13,5},{14,6},{15,7}} | collective-permute-start | bytes 3538952 | tf_op jit(solution)/shard_map/ppermute | solution.py:27
  132.3 5.9 copy-start.8
  144.6 5.3 copy-start.6
  144.6 5.5 copy-start.10
  144.6 5.6 copy-start.7
  144.6 75.5 %all-to-all-start = ((f32[8,2,1536,64]{2,3,1,0:T(8,128)}), f32[8,2,1536,64]{2,3,1,0:T(8,128)}, u32[]{:S(2)}, u32[]{:S(2)}) async-start(f32[8,2,1536,64]{2,3,1,0:T(8,128)} %select_multiply_fusion.2), calls=%async_computation | async-start | bytes 12582912 | tf_op jit(solution)/shard_map/all_to_all | solution.py:77
  162.6 63.9 %copy-start.9 = (pred[8,2]{0,1:T(4,128)(4,1)S(1)}, pred[8,2]{0,1:T(4,128)(4,1)}, u32[]{:S(2)}) copy-start(pred[8,2]{0,1:T(4,128)(4,1)} %get-tuple-element.23) | copy-start | bytes 52
  162.6 64.0 %copy-start.5 = (f32[8,2]{0,1:T(2,128)S(1)}, f32[8,2]{0,1:T(2,128)}, u32[]{:S(2)}) copy-start(f32[8,2]{0,1:T(2,128)} %get-tuple-element.25) | copy-start | bytes 196
  220.1 76.3 %all-to-all-start.2 = ((f32[8,2,1536,64]{2,3,1,0:T(8,128)}), f32[8,2,1536,64]{2,3,1,0:T(8,128)}, u32[]{:S(2)}, u32[]{:S(2)}) async-start(f32[8,2,1536,64]{2,3,1,0:T(8,128)} %select_multiply_fusion.1), calls=%async_computation.2 | async-start | bytes 12582912 | tf_op jit(solution)/shard_map/all_to_all | solution.py:77
  239.0 64.1 %copy-start.4 = (s32[32,6]{0,1:T(8,128)S(1)}, s32[32,6]{0,1:T(8,128)}, u32[]{:S(2)}) copy-start(s32[32,6]{0,1:T(8,128)} %param.6) | copy-start | bytes 2308
  296.5 76.7 %all-to-all-start.4 = ((f32[8,2,1536,64]{2,3,1,0:T(8,128)}), f32[8,2,1536,64]{2,3,1,0:T(8,128)}, u32[]{:S(2)}, u32[]{:S(2)}) async-start(f32[8,2,1536,64]{2,3,1,0:T(8,128)} %select_multiply_fusion), calls=%async_computation.4 | async-start | bytes 12582912 | tf_op jit(solution)/shard_map/all_to_all | solution.py:77
  373.2 76.4 %all-to-all-start.1 = ((f32[8,2,1536,64]{2,3,1,0:T(8,128)}), f32[8,2,1536,64]{2,3,1,0:T(8,128)}, u32[]{:S(2)}, u32[]{:S(2)}) async-start(f32[8,2,1536,64]{2,3,1,0:T(8,128)} %copy.41), calls=%async_computation.1 | async-start | bytes 12582912 | tf_op jit(solution)/shard_map/all_to_all | solution.py:82
  449.6 76.3 %all-to-all-start.3 = ((f32[8,2,1536,64]{2,3,1,0:T(8,128)}), f32[8,2,1536,64]{2,3,1,0:T(8,128)}, u32[]{:S(2)}, u32[]{:S(2)}) async-start(f32[8,2,1536,64]{2,3,1,0:T(8,128)} %copy.46), calls=%async_computation.3 | async-start | bytes 12582912 | tf_op jit(solution)/shard_map/all_to_all | solution.py:82
  525.9 76.4 %all-to-all-start.5 = ((f32[8,2,1536,64]{2,3,1,0:T(8,128)}), f32[8,2,1536,64]{2,3,1,0:T(8,128)}, u32[]{:S(2)}, u32[]{:S(2)}) async-start(f32[8,2,1536,64]{2,3,1,0:T(8,128)} %copy.51), calls=%async_computation.5 | async-start | bytes 12582912 | tf_op jit(solution)/shard_map/all_to_all | solution.py:82
  550.2 61.2 %copy-start.3 = (s32[8,6]{0,1:T(8,128)S(1)}, s32[8,6]{0,1:T(8,128)}, u32[]{:S(2)}) copy-start(s32[8,6]{0,1:T(8,128)} %copy-done.2) | copy-start | bytes 580
  660.0 52.6 %collective-permute-start.6 = (f32[12,8,48,64]{3,2,1,0:T(8,128)}, f32[12,8,48,64]{3,2,1,0:T(8,128)}, u32[]{:S(2)}, u32[]{:S(2)}) collective-permute-start(f32[12,8,48,64]{3,2,1,0:T(8,128)} %bitcast.195), channel_id=1, source_target_pairs={{0,8},{1,9},{2,10},{3,11},{4,12},{5,13},{6,14},{7,15}} | collective-permute-start | bytes 3538952 | tf_op jit(solution)/shard_map/ppermute | solution.py:46
  666.3 56.3 %collective-permute-start.9 = (f32[12,8,48,64]{3,2,1,0:T(8,128)}, f32[12,8,48,64]{3,2,1,0:T(8,128)}, u32[]{:S(2)}, u32[]{:S(2)}) collective-permute-start(f32[12,8,48,64]{3,2,1,0:T(8,128)} %bitcast.194), channel_id=1, source_target_pairs={{24,16},{25,17},{26,18},{27,19},{28,20},{29,21},{30,22},{31,23}} | collective-permute-start | bytes 3538952 | tf_op jit(solution)/shard_map/ppermute | solution.py:47
  675.1 47.5 %copy-start = (f32[12,1,8,48,64]{4,3,2,0,1:T(8,128)S(1)}, f32[12,1,8,48,64]{4,3,2,0,1:T(8,128)}, u32[]{:S(2)}) copy-start(f32[12,1,8,48,64]{4,3,2,0,1:T(8,128)} %copy.61) | copy-start | bytes 3538948
  716.7 54.7 %collective-permute-start.7 = (f32[12,8,48,64]{3,2,1,0:T(8,128)}, f32[12,8,48,64]{3,2,1,0:T(8,128)}, u32[]{:S(2)}, u32[]{:S(2)}) collective-permute-start(f32[12,8,48,64]{3,2,1,0:T(8,128)} %bitcast_add_fusion.3), channel_id=1, source_target_pairs={{0,8},{8,16},{1,9},{9,17},{2,10},{10,18},{3,11},{11,19},{4,12},{12... | collective-permute-start | bytes 3538952 | tf_op jit(solution)/shard_map/ppermute | solution.py:46
  726.0 55.3 %collective-permute-start.10 = (f32[12,8,48,64]{3,2,1,0:T(8,128)}, f32[12,8,48,64]{3,2,1,0:T(8,128)}, u32[]{:S(2)}, u32[]{:S(2)}) collective-permute-start(f32[12,8,48,64]{3,2,1,0:T(8,128)} %bitcast_add_fusion.1), channel_id=1, source_target_pairs={{16,8},{24,16},{17,9},{25,17},{18,10},{26,18},{19,11},{27,19},{20,... | collective-permute-start | bytes 3538952 | tf_op jit(solution)/shard_map/ppermute | solution.py:47
  735.0 46.2 %copy-start.1 = (f32[12,1,8,48,64]{4,3,2,0,1:T(8,128)S(1)}, f32[12,1,8,48,64]{4,3,2,0,1:T(8,128)}, u32[]{:S(2)}) copy-start(f32[12,1,8,48,64]{4,3,2,0,1:T(8,128)} %copy.62) | copy-start | bytes 3538948
  775.5 53.8 %collective-permute-start.8 = (f32[12,8,48,64]{3,2,1,0:T(8,128)}, f32[12,8,48,64]{3,2,1,0:T(8,128)}, u32[]{:S(2)}, u32[]{:S(2)}) collective-permute-start(f32[12,8,48,64]{3,2,1,0:T(8,128)} %bitcast_add_fusion.2), channel_id=1, source_target_pairs={{0,8},{8,16},{16,24},{1,9},{9,17},{17,25},{2,10},{10,18},{18,26},{... | collective-permute-start | bytes 3538952 | tf_op jit(solution)/shard_map/ppermute | solution.py:46
  784.7 53.5 %collective-permute-start.11 = (f32[12,8,48,64]{3,2,1,0:T(8,128)}, f32[12,8,48,64]{3,2,1,0:T(8,128)}, u32[]{:S(2)}, u32[]{:S(2)}) collective-permute-start(f32[12,8,48,64]{3,2,1,0:T(8,128)} %bitcast_add_fusion), channel_id=1, source_target_pairs={{8,0},{16,8},{24,16},{9,1},{17,9},{25,17},{10,2},{18,10},{26,18},{... | collective-permute-start | bytes 3538952 | tf_op jit(solution)/shard_map/ppermute | solution.py:47

commit v6 on v5

--- a/solution.py
+++ b/solution.py
@@ -53,17 +53,13 @@
     band_count = lax.axis_size("band")
     devices = group_count * band_count
     blk = coulomb.shape[1]
-    col_width = orbitals.shape[1]
-    orbital_width = col_width * band_count
+    orbital_width = orbitals.shape[1] * band_count
     piece_rows = blk // devices
     slot_count = coulomb.shape[0]
-    all_points = line_gather(orbitals, "grp", group_count)
-    block_count = all_points.shape[0] * all_points.shape[1] // (devices * piece_rows)
-    blocks = (
-        all_points.reshape(devices, block_count, piece_rows, col_width)
-        .transpose(1, 0, 2, 3)
-        .reshape(block_count, blk, col_width)
-    )
+    block_count = orbitals.shape[0] // (band_count * piece_rows)
+    own_rows = lax.all_to_all(orbitals, "band", split_axis=0, concat_axis=1, tiled=True)
+    pieces = line_gather(own_rows, "grp", group_count)
+    pieces = pieces.reshape(group_count, block_count, piece_rows, orbital_width)
     group_index = lax.axis_index("grp")
     band_index = lax.axis_index("band")
     group_requests = lax.dynamic_slice_in_dim(requests, group_index * band_count, band_count, 0)
@@ -72,23 +68,24 @@
     returned = []
     for slot in range(slot_count):
         wanted = group_requests[:, 2 * slot : 2 * slot + 2]
-        outgoing = jnp.take(blocks, jnp.maximum(wanted, 0), axis=0)
-        outgoing = outgoing * live[:, 2 * slot : 2 * slot + 2, None, None]
+        outgoing = jnp.take(pieces, jnp.maximum(wanted, 0), axis=1)
+        outgoing = outgoing * live[None, :, 2 * slot : 2 * slot + 2, None, None]
+        outgoing = outgoing.transpose(1, 2, 0, 3, 4)
         arrived = lax.all_to_all(outgoing, "band", split_axis=0, concat_axis=0, tiled=True)
-        pair_rows = arrived.transpose(1, 2, 0, 3).reshape(2, blk, orbital_width)
+        pair_rows = arrived.transpose(1, 2, 0, 3, 4).reshape(2, blk, orbital_width)
         diagonal = own_pairs[2 * slot] == own_pairs[2 * slot + 1]
         result = slot_work(pair_rows[0], pair_rows[1], coulomb[slot], diagonal)
-        outbound = result.reshape(2, blk, band_count, col_width).transpose(2, 0, 1, 3)
+        outbound = result.reshape(2, group_count, band_count, piece_rows, orbital_width)
+        outbound = outbound.transpose(2, 0, 1, 3, 4)
         returned.append(lax.all_to_all(outbound, "band", split_axis=0, concat_axis=0, tiled=True))
     returned = jnp.concatenate(returned, axis=1)
     one_hot = (
         group_requests[:, :, None] == jnp.arange(block_count, dtype=jnp.int32)[None, None, :]
     ).astype(jnp.float32)
-    summed = jnp.einsum("srk,srpc->kpc", one_hot, returned, precision=lax.Precision.HIGHEST)
-    summed = summed.reshape(block_count, group_count, band_count, piece_rows, col_width)
-    summed = summed.transpose(1, 0, 2, 3, 4)
-    mine = line_reduce(summed, "grp", group_count).transpose(1, 0, 2, 3)
-    return mine.reshape(band_count * block_count * piece_rows, col_width)
+    summed = jnp.einsum("srk,srgpn->gkpn", one_hot, returned, precision=lax.Precision.HIGHEST)
+    parts = lax.all_to_all(summed, "grp", split_axis=0, concat_axis=0, tiled=True)
+    home_rows = parts.sum(axis=0).reshape(block_count * piece_rows, orbital_width)
+    return lax.all_to_all(home_rows, "band", split_axis=1, concat_axis=0, tiled=True)
 
 
 def solution(mesh):

time: 860 us -> 760 us (0.88)
  waiting for transfers between devices: 447 us -> 291 us
  blocking collectives: 0 us -> 149 us
  local copies, waits for them, and re-layouts: 187 us -> 120 us
  starting transfers between devices: 68.3 us -> 47.5 us
  matrix products: 94.9 us -> 111 us
  other arithmetic: 42.1 us -> 26.4 us
    all_to_all x0 -> x3, blocking collectives: none -> 149 us  [the longest x1 108 us: body(): lax.all_to_all(summed, 'grp', split_axis=0, concat_axis=0, tiled=True)]
    ppermute x6 -> x0, waiting for transfers between devices: 124 us -> none  [the longest x3 115 us: line_reduce(): lax.ppermute(send_right, axis, [(i, i + 1) for i in range(0, step)])]
    another operation x8 -> x0, local copies, waits for them, and re-layouts: 37.3 us -> none
    all_to_all x3, waiting for transfers between devices: 120 us -> 87.8 us  [body(): lax.all_to_all(outbound, 'band', split_axis=0, concat_axis=0, tiled=True)]
    reshape x3 -> x0, local copies, waits for them, and re-layouts: 25.4 us -> none  [the longest x1 13 us: body(): blocks = all_points.reshape(devices, block_count, piece_rows, col_width)....]
    dot_general x1 -> x3, local copies, waits for them, and re-layouts: 7.61 us -> 28.8 us  [slot_work(): jnp.dot(kernel.T, first_block, precision=PRECISION, preferred_element_typ...]
    ppermute x6 -> x0, starting transfers between devices: 20 us -> none  [the longest x3 14.5 us: line_reduce(): lax.ppermute(send_right, axis, [(i, i + 1) for i in range(0, step)])]
    mul x3 -> x0, other arithmetic: 19 us -> none  [body(): outgoing = outgoing * live[:, 2 * slot:2 * slot + 2, None, None]]
  transfers between devices with their start and end apart: 18 -> 12, of which waited for: 13 -> 10; matrix products, arithmetic and copies ran while one was open for 25% -> 27% of each run, Pallas kernels for 0% -> 0%
where the time goes in v6:
time: 760 us; the launch traced here: 750 us
  waiting for transfers between devices  291 us (38%)
  blocking collectives  149 us (20%)
  local copies, waits for them, and re-layouts  120 us (16%)
  matrix products  111 us (15%)
  starting transfers between devices  47.5 us (6%)
  other arithmetic  26.4 us (3%)
    all_to_all x3, waiting for transfers between devices, body(): lax.all_to_all(outgoing, 'band', split_axis=0, concat_axis=0, tiled=True)  130 us
    all_to_all x1, blocking collectives, body(): lax.all_to_all(summed, 'grp', split_axis=0, concat_axis=0, tiled=True)  108 us
    all_to_all x3, waiting for transfers between devices, body(): lax.all_to_all(outbound, 'band', split_axis=0, concat_axis=0, tiled=True)  87.8 us
    ppermute x3, waiting for transfers between devices, line_gather(): lax.ppermute(leftward, axis, [(i + 1, i) for i in range(0, count - step)])  49.7 us
    dot_general x3, matrix products, slot_work(): jnp.dot(first_block, second_block.T, precision=PRECISION, preferred_eleme...  39.5 us
    dot_general x3, matrix products, slot_work(): jnp.dot(kernel, second_block, precision=PRECISION, preferred_element_type...  35.6 us
    dot_general x3, local copies, waits for them, and re-layouts, slot_work(): jnp.dot(kernel.T, first_block, precision=PRECISION, preferred_element_typ...  28.8 us
    all_to_all x3, local copies, waits for them, and re-layouts, body(): lax.all_to_all(outbound, 'band', split_axis=0, concat_axis=0, tiled=True)  27.2 us
  transfers between devices with their start and end apart: 12, of which 10 were waited for; matrix products, arithmetic and copies ran while one was open for 27% of the time, Pallas kernels for 0%

profile of v6, /device:TPU:2, one launch (start us, length us, event | category | flops | bytes accessed | tf_op | source)
XLA Modules:
  0.0 749.6 jit_solution(12543547398660307386)
XLA Ops:
  0.0 1.7 all_to_all.49
  2.0 20.8 %all_to_all.73 = f32[8,576,64]{1,2,0:T(8,128)S(1)} all-to-all(f32[8,576,64]{1,2,0:T(8,128)S(1)} %copy.60), channel_id=1, replica_groups=mesh['grp'=4,'band'=8] {'band'}, dimensions={0} | all-to-all | bytes 2359296 | tf_op jit(solution)/shard_map/all_to_all | solution.py:60
  23.1 4.5 collective-permute-start
  27.7 1.3 collective-permute-start.1
  28.9 23.0 %collective-permute-done = f32[576,512]{1,0:T(8,128)} collective-permute-done((f32[576,512]{1,0:T(8,128)S(1)}, f32[576,512]{1,0:T(8,128)}, u32[]{:S(2)}, u32[]{:S(2)}) %collective-permute-start) | collective-permute-done | bytes 1179680 | tf_op jit(solution)/shard_map/ppermute | solution.py:26
  51.9 1.7 collective-permute-start.2
  53.6 3.5 collective-permute-done.1
  57.2 1.3 collective-permute-start.3
  61.2 25.0 %collective-permute-done.3 = f32[576,512]{1,0:T(8,128)} collective-permute-done((f32[576,512]{1,0:T(8,128)}, f32[576,512]{1,0:T(8,128)}, u32[]{:S(2)}, u32[]{:S(2)}) %collective-permute-start.3) | collective-permute-done | bytes 1179680 | tf_op jit(solution)/shard_map/ppermute | solution.py:27
  86.2 1.3 collective-permute-start.5
  87.4 1.4 bitcast_dynamic-update-slice_fusion.5
  88.8 1.4 bitcast_dynamic-update-slice_fusion.4
  90.2 1.4 bitcast_dynamic-update-slice_fusion.3
  91.5 1.4 bitcast_dynamic-update-slice_fusion.2
  93.0 21.1 %collective-permute-done.5 = f32[576,512]{1,0:T(8,128)S(1)} collective-permute-done((f32[576,512]{1,0:T(8,128)}, f32[576,512]{1,0:T(8,128)S(1)}, u32[]{:S(2)}, u32[]{:S(2)}) %collective-permute-start.5) | collective-permute-done | bytes 1179680 | tf_op jit(solution)/shard_map/ppermute | solution.py:27
  114.2 2.7 slice.106
  116.9 5.9 gather_fusion
  122.8 6.9 fusion.11
  129.7 4.7 all-to-all-start.1
  134.8 5.9 gather_fusion.1
  140.7 6.9 fusion.10
  147.6 56.1 %all-to-all-done.1 = f32[8,2,4,48,512]{4,3,2,1,0:T(8,128)} async-done(((f32[8,2,4,48,512]{4,3,2,1,0:T(8,128)}), f32[8,2,4,48,512]{4,3,2,1,0:T(8,128)}, u32[]{:S(2)}, u32[]{:S(2)}) %all-to-all-start.1) | async-done | bytes 6291488 | tf_op jit(solution)/shard_map/all_to_all | solution.py:74
  203.7 6.2 all-to-all-start.3
  210.2 5.9 gather_fusion.2
  216.1 6.9 fusion.9
  223.0 57.0 %all-to-all-done.3 = f32[8,2,4,48,512]{4,3,2,1,0:T(8,128)} async-done(((f32[8,2,4,48,512]{4,3,2,1,0:T(8,128)}), f32[8,2,4,48,512]{4,3,2,1,0:T(8,128)}, u32[]{:S(2)}, u32[]{:S(2)}) %all-to-all-start.3) | async-done | bytes 6291488 | tf_op jit(solution)/shard_map/all_to_all | solution.py:74
  280.0 6.5 all-to-all-start.5
  288.4 3.6 fusion.19
  292.6 13.2 %convolution_multiply_fusion.2 = f32[1536,1536]{1,0:T(8,128)} fusion(f32[1536,512]{1,0:T(8,128)S(1)} %bitcast.150, f32[1536,512]{1,0:T(8,128)S(1)} %bitcast.159, f32[3,1536,1536]{2,1,0:T(8,128)} %param.7), kind=kOutput, calls=%fused_computation.11 | convolution fusion | flops 7250116608 | bytes 25165824 | tf_op jit(solution)/shard_map/dot_general | solution.py:10
  305.8 9.6 %copy.68 = f32[1536,1536]{1,0:T(8,128)} copy(f32[1536,1536]{0,1:T(8,128)} %bitcast.144) | data formatting | bytes 18874368 | tf_op jit(solution)/shard_map/dot_general | solution.py:15
  315.4 12.0 %convolution_bitcast_fusion.5 = f32[1,4,8,48,512]{4,3,2,1,0:T(8,128)S(1)} fusion(f32[4,8,48,1536]{3,2,1,0:T(8,128)} %bitcast.145, f32[1536,512,1,1]{1,0,3,2:T(8,128)} %bitcast.160), kind=kOutput, calls=%fused_computation.30 | convolution fusion | flops 7247757312 | bytes 15728640 | tf_op jit(solution)/shard_map/dot_general | solution.py:14
  327.4 8.0 %convolution_bitcast_fusion.4 = f32[1,4,8,48,512]{4,3,2,1,0:T(8,128)S(1)} fusion(f32[4,8,48,1536]{3,2,1,0:T(8,128)S(1)} %bitcast.167, f32[1536,512,1,1]{1,0,3,2:T(8,128)S(1)} %bitcast.151), kind=kOutput, calls=%fused_computation.29 | convolution fusion | flops 7247757312 | bytes 15728640 | tf_op jit(solution)/shard_map/dot_general | solution.py:15
  335.4 0.9 fusion.6
  336.3 3.3 copy.69
  339.6 17.1 %all-to-all-done.5 = f32[8,2,4,48,512]{4,3,2,1,0:T(8,128)} async-done(((f32[8,2,4,48,512]{4,3,2,1,0:T(8,128)}), f32[8,2,4,48,512]{4,3,2,1,0:T(8,128)}, u32[]{:S(2)}, u32[]{:S(2)}) %all-to-all-start.5) | async-done | bytes 6291488 | tf_op jit(solution)/shard_map/all_to_all | solution.py:74
  356.7 6.4 all-to-all-start.2
  364.4 3.6 fusion.20
  368.6 13.2 %convolution_multiply_fusion.1 = f32[1536,1536]{1,0:T(8,128)} fusion(f32[1536,512]{1,0:T(8,128)S(1)} %bitcast.152, f32[1536,512]{1,0:T(8,128)S(1)} %bitcast.161, f32[3,1536,1536]{2,1,0:T(8,128)} %param.7), kind=kOutput, calls=%fused_computation.10 | convolution fusion | flops 7250116608 | bytes 25165824 | tf_op jit(solution)/shard_map/dot_general | solution.py:10
  381.8 9.6 %copy.75 = f32[1536,1536]{1,0:T(8,128)} copy(f32[1536,1536]{0,1:T(8,128)} %bitcast.146) | data formatting | bytes 18874368 | tf_op jit(solution)/shard_map/dot_general | solution.py:15
  391.4 11.7 %convolution_bitcast_fusion.3 = f32[1,4,8,48,512]{4,3,2,1,0:T(8,128)S(1)} fusion(f32[4,8,48,1536]{3,2,1,0:T(8,128)} %bitcast.147, f32[1536,512,1,1]{1,0,3,2:T(8,128)} %bitcast.162), kind=kOutput, calls=%fused_computation.28 | convolution fusion | flops 7247757312 | bytes 15728640 | tf_op jit(solution)/shard_map/dot_general | solution.py:14
  403.1 8.0 %convolution_bitcast_fusion.2 = f32[1,4,8,48,512]{4,3,2,1,0:T(8,128)S(1)} fusion(f32[4,8,48,1536]{3,2,1,0:T(8,128)S(1)} %bitcast.168, f32[1536,512,1,1]{1,0,3,2:T(8,128)S(1)} %bitcast.153), kind=kOutput, calls=%fused_computation.27 | convolution fusion | flops 7247757312 | bytes 15728640 | tf_op jit(solution)/shard_map/dot_general | solution.py:15
  411.1 0.9 fusion.7
  412.0 3.3 copy.76
  415.3 18.0 %all-to-all-done.2 = f32[8,2,4,48,512]{4,3,2,1,0:T(8,128)} async-done(((f32[8,2,4,48,512]{4,3,2,1,0:T(8,128)}), f32[8,2,4,48,512]{4,3,2,1,0:T(8,128)}, u32[]{:S(2)}, u32[]{:S(2)}) %all-to-all-start.2) | async-done | bytes 6291488 | tf_op jit(solution)/shard_map/all_to_all | solution.py:80
  433.3 6.5 all-to-all-start.4
  441.1 3.6 fusion.21
  445.3 13.2 %convolution_multiply_fusion = f32[1536,1536]{1,0:T(8,128)} fusion(f32[1536,512]{1,0:T(8,128)S(1)} %bitcast.154, f32[1536,512]{1,0:T(8,128)S(1)} %bitcast.163, f32[3,1536,1536]{2,1,0:T(8,128)} %param.7), kind=kOutput, calls=%fused_computation.9 | convolution fusion | flops 7250116608 | bytes 25165824 | tf_op jit(solution)/shard_map/dot_general | solution.py:10
  458.4 9.6 %copy.82 = f32[1536,1536]{1,0:T(8,128)} copy(f32[1536,1536]{0,1:T(8,128)} %bitcast.148) | data formatting | bytes 18874368 | tf_op jit(solution)/shard_map/dot_general | solution.py:15
  468.0 11.9 %convolution_bitcast_fusion.1 = f32[1,4,8,48,512]{4,3,2,1,0:T(8,128)S(1)} fusion(f32[4,8,48,1536]{3,2,1,0:T(8,128)} %bitcast.149, f32[1536,512,1,1]{1,0,3,2:T(8,128)} %bitcast.164), kind=kOutput, calls=%fused_computation.26 | convolution fusion | flops 7247757312 | bytes 15728640 | tf_op jit(solution)/shard_map/dot_general | solution.py:14
  480.0 8.0 %convolution_bitcast_fusion = f32[1,4,8,48,512]{4,3,2,1,0:T(8,128)S(1)} fusion(f32[4,8,48,1536]{3,2,1,0:T(8,128)S(1)} %bitcast.169, f32[1536,512,1,1]{1,0,3,2:T(8,128)S(1)} %bitcast.155), kind=kOutput, calls=%fused_computation.25 | convolution fusion | flops 7247757312 | bytes 15728640 | tf_op jit(solution)/shard_map/dot_general | solution.py:15
  488.8 3.3 copy.83
  492.2 17.7 %all-to-all-done.4 = f32[8,2,4,48,512]{4,3,2,1,0:T(8,128)} async-done(((f32[8,2,4,48,512]{4,3,2,1,0:T(8,128)}), f32[8,2,4,48,512]{4,3,2,1,0:T(8,128)}, u32[]{:S(2)}, u32[]{:S(2)}) %all-to-all-start.4) | async-done | bytes 6291488 | tf_op jit(solution)/shard_map/all_to_all | solution.py:80
  509.9 6.4 all-to-all-start.6
  516.3 9.1 %copy.84 = f32[8,2,4,48,512]{4,0,1,3,2:T(8,128)} copy(f32[8,2,4,48,512]{4,3,2,1,0:T(8,128)} %all-to-all-done.2) | data formatting | bytes 12582912 | tf_op jit(solution)/shard_map/all_to_all | solution.py:80
  525.4 9.1 %copy.85 = f32[8,2,4,48,512]{4,0,1,3,2:T(8,128)} copy(f32[8,2,4,48,512]{4,3,2,1,0:T(8,128)} %all-to-all-done.4) | data formatting | bytes 12582912 | tf_op jit(solution)/shard_map/all_to_all | solution.py:80
  534.4 52.0 %all-to-all-done.6 = f32[8,2,4,48,512]{4,3,2,1,0:T(8,128)} async-done(((f32[8,2,4,48,512]{4,3,2,1,0:T(8,128)}), f32[8,2,4,48,512]{4,3,2,1,0:T(8,128)}, u32[]{:S(2)}, u32[]{:S(2)}) %all-to-all-start.6) | async-done | bytes 6291488 | tf_op jit(solution)/shard_map/all_to_all | solution.py:80
  586.4 9.0 %copy.86 = f32[8,2,4,48,512]{4,0,1,3,2:T(8,128)} copy(f32[8,2,4,48,512]{4,3,2,1,0:T(8,128)} %all-to-all-done.6) | data formatting | bytes 12582912 | tf_op jit(solution)/shard_map/all_to_all | solution.py:80
  595.5 12.4 %fusion.12 = f32[4,12,48,512]{3,1,2,0:T(8,128)} fusion(f32[8,2,4,48,512]{4,0,1,3,2:T(8,128)} %copy.86, f32[8,2,4,48,512]{4,0,1,3,2:T(8,128)} %copy.85, f32[8,2,4,48,512]{4,0,1,3,2:T(8,128)} %copy.84, s32[8,6]{0,1:T(8,128)S(1)} %copy-done.7), kind=kOutput, calls=%fused_computation.24 | convolution fusion | flops 688915008 | bytes 23593152 | tf_op jit(solution)/shard_map/srk,srgpn->gkpn/dot_general | solution.py:85
  607.9 5.5 copy.87
  613.4 108.3 %all_to_all.74 = f32[4,12,48,512]{3,2,1,0:T(8,128)} all-to-all(f32[4,12,48,512]{3,2,1,0:T(8,128)S(1)} %copy.87), channel_id=1, replica_groups=mesh['grp'=4,'band'=8] {'grp'}, dimensions={0} | all-to-all | bytes 9437184 | tf_op jit(solution)/shard_map/all_to_all | solution.py:86
  721.7 3.0 reduce_sum.9
  725.2 2.0 copy.90
  727.2 20.0 %all_to_all.75 = f32[576,8,64]{0,2,1:T(8,128)S(1)} all-to-all(f32[576,8,64]{0,2,1:T(8,128)} %copy.90), channel_id=1, replica_groups=mesh['grp'=4,'band'=8] {'band'}, dimensions={1} | all-to-all | bytes 2359296 | tf_op jit(solution)/shard_map/all_to_all | solution.py:88
  748.0 1.3 all_to_all.63
  (58 shorter events, 8.8 us)
Async XLA Ops:
  0.0 58.5 %copy-start.8 = (s32[32,6]{0,1:T(8,128)S(1)}, s32[32,6]{0,1:T(8,128)}, u32[]{:S(2)}) copy-start(s32[32,6]{0,1:T(8,128)} %param.6) | copy-start | bytes 2308
  23.1 28.8 %collective-permute-start = (f32[576,512]{1,0:T(8,128)S(1)}, f32[576,512]{1,0:T(8,128)}, u32[]{:S(2)}, u32[]{:S(2)}) collective-permute-start(f32[576,512]{1,0:T(8,128)S(1)} %copy.62), channel_id=1, source_target_pairs={{0,8},{8,16},{16,24},{1,9},{9,17},{17,25},{2,10},{10,18},{18,26},{... | collective-permute-start | bytes 3538952 | tf_op jit(solution)/shard_map/ppermute | solution.py:26
  27.7 29.5 %collective-permute-start.1 = (f32[576,512]{1,0:T(8,128)S(1)}, f32[576,512]{1,0:T(8,128)}, u32[]{:S(2)}, u32[]{:S(2)}) collective-permute-start(f32[576,512]{1,0:T(8,128)S(1)} %copy.62), channel_id=1, source_target_pairs={{8,0},{16,8},{24,16},{9,1},{17,9},{25,17},{10,2},{18,10},{26,18},{... | collective-permute-start | bytes 3538952 | tf_op jit(solution)/shard_map/ppermute | solution.py:27
  51.9 7.6 %collective-permute-start.2 = (f32[576,512]{1,0:T(8,128)}, f32[576,512]{1,0:T(8,128)}, u32[]{:S(2)}, u32[]{:S(2)}) collective-permute-start(f32[576,512]{1,0:T(8,128)} %collective-permute-done), channel_id=1, source_target_pairs={{8,16},{16,24},{9,17},{17,25},{10,18},{18,26},{11,19},{19,27},{12,... | collective-permute-start | bytes 3538952 | tf_op jit(solution)/shard_map/ppermute | solution.py:26
  57.2 29.0 %collective-permute-start.3 = (f32[576,512]{1,0:T(8,128)}, f32[576,512]{1,0:T(8,128)}, u32[]{:S(2)}, u32[]{:S(2)}) collective-permute-start(f32[576,512]{1,0:T(8,128)} %collective-permute-done.1), channel_id=1, source_target_pairs={{8,0},{16,8},{9,1},{17,9},{10,2},{18,10},{11,3},{19,11},{12,4},{20... | collective-permute-start | bytes 3538952 | tf_op jit(solution)/shard_map/ppermute | solution.py:27
  58.6 0.6 copy-start.6
  59.6 33.3 %collective-permute-start.4 = (f32[576,512]{1,0:T(8,128)}, f32[576,512]{1,0:T(8,128)S(1)}, u32[]{:S(2)}, u32[]{:S(2)}) collective-permute-start(f32[576,512]{1,0:T(8,128)} %collective-permute-done.2), channel_id=1, source_target_pairs={{16,24},{17,25},{18,26},{19,27},{20,28},{21,29},{22,30},{23,31}} | collective-permute-start | bytes 3538952 | tf_op jit(solution)/shard_map/ppermute | solution.py:26
  86.2 28.0 %collective-permute-start.5 = (f32[576,512]{1,0:T(8,128)}, f32[576,512]{1,0:T(8,128)S(1)}, u32[]{:S(2)}, u32[]{:S(2)}) collective-permute-start(f32[576,512]{1,0:T(8,128)} %collective-permute-done.3), channel_id=1, source_target_pairs={{8,0},{9,1},{10,2},{11,3},{12,4},{13,5},{14,6},{15,7}} | collective-permute-start | bytes 3538952 | tf_op jit(solution)/shard_map/ppermute | solution.py:27
  129.7 74.0 %all-to-all-start.1 = ((f32[8,2,4,48,512]{4,3,2,1,0:T(8,128)}), f32[8,2,4,48,512]{4,3,2,1,0:T(8,128)}, u32[]{:S(2)}, u32[]{:S(2)}) async-start(f32[8,2,4,48,512]{4,3,2,1,0:T(8,128)} %fusion.11), calls=%async_computation.1 | async-start | bytes 12582912 | tf_op jit(solution)/shard_map/all_to_all | solution.py:74
  203.7 76.4 %all-to-all-start.3 = ((f32[8,2,4,48,512]{4,3,2,1,0:T(8,128)}), f32[8,2,4,48,512]{4,3,2,1,0:T(8,128)}, u32[]{:S(2)}, u32[]{:S(2)}) async-start(f32[8,2,4,48,512]{4,3,2,1,0:T(8,128)} %fusion.10), calls=%async_computation.3 | async-start | bytes 12582912 | tf_op jit(solution)/shard_map/all_to_all | solution.py:74
  280.0 76.7 %all-to-all-start.5 = ((f32[8,2,4,48,512]{4,3,2,1,0:T(8,128)}), f32[8,2,4,48,512]{4,3,2,1,0:T(8,128)}, u32[]{:S(2)}, u32[]{:S(2)}) async-start(f32[8,2,4,48,512]{4,3,2,1,0:T(8,128)} %fusion.9), calls=%async_computation.5 | async-start | bytes 12582912 | tf_op jit(solution)/shard_map/all_to_all | solution.py:74
  292.6 13.2 %copy-start = (f32[1,4,8,48,512]{4,3,2,1,0:T(8,128)}, f32[1,4,8,48,512]{4,3,2,1,0:T(8,128)S(1)}, u32[]{:S(2)}) copy-start(f32[1,4,8,48,512]{4,3,2,1,0:T(8,128)S(1)} %copy.67) | copy-start | bytes 9437188
  315.4 12.0 %copy-start.3 = (f32[1536,1536]{1,0:T(8,128)S(1)}, f32[1536,1536]{1,0:T(8,128)}, u32[]{:S(2)}) copy-start(f32[1536,1536]{1,0:T(8,128)} %copy.68) | copy-start | bytes 28311556
  356.7 76.6 %all-to-all-start.2 = ((f32[8,2,4,48,512]{4,3,2,1,0:T(8,128)}), f32[8,2,4,48,512]{4,3,2,1,0:T(8,128)}, u32[]{:S(2)}, u32[]{:S(2)}) async-start(f32[8,2,4,48,512]{4,3,2,1,0:T(8,128)} %copy.69), calls=%async_computation.2 | async-start | bytes 12582912 | tf_op jit(solution)/shard_map/all_to_all | solution.py:80
  368.6 13.2 %copy-start.1 = (f32[1,4,8,48,512]{4,3,2,1,0:T(8,128)}, f32[1,4,8,48,512]{4,3,2,1,0:T(8,128)S(1)}, u32[]{:S(2)}) copy-start(f32[1,4,8,48,512]{4,3,2,1,0:T(8,128)S(1)} %copy.74) | copy-start | bytes 9437188
  391.4 11.7 %copy-start.4 = (f32[1536,1536]{1,0:T(8,128)S(1)}, f32[1536,1536]{1,0:T(8,128)}, u32[]{:S(2)}) copy-start(f32[1536,1536]{1,0:T(8,128)} %copy.75) | copy-start | bytes 28311556
  433.3 76.6 %all-to-all-start.4 = ((f32[8,2,4,48,512]{4,3,2,1,0:T(8,128)}), f32[8,2,4,48,512]{4,3,2,1,0:T(8,128)}, u32[]{:S(2)}, u32[]{:S(2)}) async-start(f32[8,2,4,48,512]{4,3,2,1,0:T(8,128)} %copy.76), calls=%async_computation.4 | async-start | bytes 12582912 | tf_op jit(solution)/shard_map/all_to_all | solution.py:80
  445.3 13.2 %copy-start.2 = (f32[1,4,8,48,512]{4,3,2,1,0:T(8,128)}, f32[1,4,8,48,512]{4,3,2,1,0:T(8,128)S(1)}, u32[]{:S(2)}) copy-start(f32[1,4,8,48,512]{4,3,2,1,0:T(8,128)S(1)} %copy.81) | copy-start | bytes 9437188
  468.0 11.9 %copy-start.5 = (f32[1536,1536]{1,0:T(8,128)S(1)}, f32[1536,1536]{1,0:T(8,128)}, u32[]{:S(2)}) copy-start(f32[1536,1536]{1,0:T(8,128)} %copy.82) | copy-start | bytes 28311556
  509.9 76.5 %all-to-all-start.6 = ((f32[8,2,4,48,512]{4,3,2,1,0:T(8,128)}), f32[8,2,4,48,512]{4,3,2,1,0:T(8,128)}, u32[]{:S(2)}, u32[]{:S(2)}) async-start(f32[8,2,4,48,512]{4,3,2,1,0:T(8,128)} %copy.83), calls=%async_computation.6 | async-start | bytes 12582912 | tf_op jit(solution)/shard_map/all_to_all | solution.py:80
  534.4 61.1 %copy-start.7 = (s32[8,6]{0,1:T(8,128)S(1)}, s32[8,6]{0,1:T(8,128)}, u32[]{:S(2)}) copy-start(s32[8,6]{0,1:T(8,128)} %copy-done.6) | copy-start | bytes 580

commit v7 on v6

--- a/solution.py
+++ b/solution.py
@@ -83,8 +83,7 @@
         group_requests[:, :, None] == jnp.arange(block_count, dtype=jnp.int32)[None, None, :]
     ).astype(jnp.float32)
     summed = jnp.einsum("srk,srgpn->gkpn", one_hot, returned, precision=lax.Precision.HIGHEST)
-    parts = lax.all_to_all(summed, "grp", split_axis=0, concat_axis=0, tiled=True)
-    home_rows = parts.sum(axis=0).reshape(block_count * piece_rows, orbital_width)
+    home_rows = line_reduce(summed, "grp", group_count).reshape(block_count * piece_rows, orbital_width)
     return lax.all_to_all(home_rows, "band", split_axis=1, concat_axis=0, tiled=True)
 
 

time: 760 us -> 743 us (0.978)
  blocking collectives: 149 us -> 40.8 us
  waiting for transfers between devices: 291 us -> 364 us
  starting transfers between devices: 47.5 us -> 61.6 us
    all_to_all x1 -> x0, blocking collectives: 108 us -> none  [body(): lax.all_to_all(summed, 'grp', split_axis=0, concat_axis=0, tiled=True)]
    ppermute x0 -> x6, waiting for transfers between devices: none -> 73.1 us  [the longest x3 68.1 us: line_reduce(): lax.ppermute(send_right, axis, [(i, i + 1) for i in range(0, step)])]
    ppermute x0 -> x6, starting transfers between devices: none -> 13.7 us  [the longest x3 10.6 us: line_reduce(): lax.ppermute(send_right, axis, [(i, i + 1) for i in range(0, step)])]
  transfers between devices with their start and end apart: 12 -> 18, of which waited for: 10 -> 14; matrix products, arithmetic and copies ran while one was open for 27% -> 28% of each run, Pallas kernels for 0% -> 0%
where the time goes in v7:
time: 743 us; the launch traced here: 733 us
  waiting for transfers between devices  364 us (49%)
  local copies, waits for them, and re-layouts  123 us (17%)
  matrix products  111 us (15%)
  starting transfers between devices  61.6 us (8%)
  blocking collectives  40.8 us (5%)
  other arithmetic  27.4 us (4%)
    all_to_all x3, waiting for transfers between devices, body(): lax.all_to_all(outgoing, 'band', split_axis=0, concat_axis=0, tiled=True)  130 us
    all_to_all x3, waiting for transfers between devices, body(): lax.all_to_all(outbound, 'band', split_axis=0, concat_axis=0, tiled=True)  88 us
    ppermute x3, waiting for transfers between devices, line_reduce(): lax.ppermute(send_right, axis, [(i, i + 1) for i in range(0, step)])  68.1 us
    ppermute x3, waiting for transfers between devices, line_gather(): lax.ppermute(leftward, axis, [(i + 1, i) for i in range(0, count - step)])  49.6 us
    dot_general x3, matrix products, slot_work(): jnp.dot(first_block, second_block.T, precision=PRECISION, preferred_eleme...  39.6 us
    dot_general x3, matrix products, slot_work(): jnp.dot(kernel, second_block, precision=PRECISION, preferred_element_type...  34.9 us
    dot_general x3, local copies, waits for them, and re-layouts, slot_work(): jnp.dot(kernel.T, first_block, precision=PRECISION, preferred_element_typ...  28.8 us
    all_to_all x3, local copies, waits for them, and re-layouts, body(): lax.all_to_all(outbound, 'band', split_axis=0, concat_axis=0, tiled=True)  27.2 us
  transfers between devices with their start and end apart: 18, of which 14 were waited for; matrix products, arithmetic and copies ran while one was open for 28% of the time, Pallas kernels for 0%

profile of v7, /device:TPU:2, one launch (start us, length us, event | category | flops | bytes accessed | tf_op | source)
XLA Modules:
  0.0 732.5 jit_solution(1199439657434776636)
XLA Ops:
  0.0 1.7 all_to_all.46
  2.0 20.8 %all_to_all.68 = f32[8,576,64]{1,2,0:T(8,128)S(1)} all-to-all(f32[8,576,64]{1,2,0:T(8,128)S(1)} %copy.105), channel_id=1, replica_groups=mesh['grp'=4,'band'=8] {'band'}, dimensions={0} | all-to-all | bytes 2359296 | tf_op jit(solution)/shard_map/all_to_all | solution.py:60
  23.1 4.5 collective-permute-start
  29.0 23.0 %collective-permute-done = f32[576,512]{1,0:T(8,128)} collective-permute-done((f32[576,512]{1,0:T(8,128)S(1)}, f32[576,512]{1,0:T(8,128)}, u32[]{:S(2)}, u32[]{:S(2)}) %collective-permute-start) | collective-permute-done | bytes 1179680 | tf_op jit(solution)/shard_map/ppermute | solution.py:26
  51.9 1.7 collective-permute-start.2
  53.6 3.6 collective-permute-done.1
  61.2 25.0 %collective-permute-done.3 = f32[576,512]{1,0:T(8,128)} collective-permute-done((f32[576,512]{1,0:T(8,128)}, f32[576,512]{1,0:T(8,128)}, u32[]{:S(2)}, u32[]{:S(2)}) %collective-permute-start.3) | collective-permute-done | bytes 1179680 | tf_op jit(solution)/shard_map/ppermute | solution.py:27
  87.4 1.4 bitcast_dynamic-update-slice_fusion.5
  88.8 1.4 bitcast_dynamic-update-slice_fusion.4
  90.2 1.4 bitcast_dynamic-update-slice_fusion.3
  91.5 1.4 bitcast_dynamic-update-slice_fusion.2
  93.0 21.1 %collective-permute-done.5 = f32[576,512]{1,0:T(8,128)S(1)} collective-permute-done((f32[576,512]{1,0:T(8,128)}, f32[576,512]{1,0:T(8,128)S(1)}, u32[]{:S(2)}, u32[]{:S(2)}) %collective-permute-start.5) | collective-permute-done | bytes 1179680 | tf_op jit(solution)/shard_map/ppermute | solution.py:27
  114.2 2.7 slice.106
  116.9 5.9 gather_fusion
  122.8 6.9 fusion.11
  129.7 4.7 all-to-all-start.1
  134.7 6.0 gather_fusion.1
  140.7 6.9 fusion.10
  147.6 56.1 %all-to-all-done.1 = f32[8,2,4,48,512]{4,3,2,1,0:T(8,128)} async-done(((f32[8,2,4,48,512]{4,3,2,1,0:T(8,128)}), f32[8,2,4,48,512]{4,3,2,1,0:T(8,128)}, u32[]{:S(2)}, u32[]{:S(2)}) %all-to-all-start.1) | async-done | bytes 6291488 | tf_op jit(solution)/shard_map/all_to_all | solution.py:74
  203.6 6.2 all-to-all-start.3
  210.2 5.9 gather_fusion.2
  216.1 7.0 fusion.9
  223.0 57.0 %all-to-all-done.3 = f32[8,2,4,48,512]{4,3,2,1,0:T(8,128)} async-done(((f32[8,2,4,48,512]{4,3,2,1,0:T(8,128)}), f32[8,2,4,48,512]{4,3,2,1,0:T(8,128)}, u32[]{:S(2)}, u32[]{:S(2)}) %all-to-all-start.3) | async-done | bytes 6291488 | tf_op jit(solution)/shard_map/all_to_all | solution.py:74
  280.0 6.7 all-to-all-start.5
  288.7 3.6 fusion.25
  292.9 13.2 %convolution_multiply_fusion.2 = f32[1536,1536]{1,0:T(8,128)} fusion(f32[1536,512]{1,0:T(8,128)S(1)} %bitcast.188, f32[1536,512]{1,0:T(8,128)S(1)} %bitcast.197, f32[3,1536,1536]{2,1,0:T(8,128)} %param.7), kind=kOutput, calls=%fused_computation.11 | convolution fusion | flops 7250116608 | bytes 25165824 | tf_op jit(solution)/shard_map/dot_general | solution.py:10
  306.1 9.6 %copy.113 = f32[1536,1536]{1,0:T(8,128)} copy(f32[1536,1536]{0,1:T(8,128)} %bitcast.182) | data formatting | bytes 18874368 | tf_op jit(solution)/shard_map/dot_general | solution.py:15
  315.7 11.6 %convolution_bitcast_fusion.5 = f32[1,4,8,48,512]{4,3,2,1,0:T(8,128)S(1)} fusion(f32[4,8,48,1536]{3,2,1,0:T(8,128)} %bitcast.183, f32[1536,512,1,1]{1,0,3,2:T(8,128)} %bitcast.198), kind=kOutput, calls=%fused_computation.30 | convolution fusion | flops 7247757312 | bytes 15728640 | tf_op jit(solution)/shard_map/dot_general | solution.py:14
  327.4 8.0 %convolution_bitcast_fusion.4 = f32[1,4,8,48,512]{4,3,2,1,0:T(8,128)S(1)} fusion(f32[4,8,48,1536]{3,2,1,0:T(8,128)S(1)} %bitcast.205, f32[1536,512,1,1]{1,0,3,2:T(8,128)S(1)} %bitcast.189), kind=kOutput, calls=%fused_computation.29 | convolution fusion | flops 7247757312 | bytes 15728640 | tf_op jit(solution)/shard_map/dot_general | solution.py:15
  336.2 3.3 copy.114
  339.5 17.4 %all-to-all-done.5 = f32[8,2,4,48,512]{4,3,2,1,0:T(8,128)} async-done(((f32[8,2,4,48,512]{4,3,2,1,0:T(8,128)}), f32[8,2,4,48,512]{4,3,2,1,0:T(8,128)}, u32[]{:S(2)}, u32[]{:S(2)}) %all-to-all-start.5) | async-done | bytes 6291488 | tf_op jit(solution)/shard_map/all_to_all | solution.py:74
  356.9 6.5 all-to-all-start.2
  364.7 3.6 fusion.26
  368.9 13.2 %convolution_multiply_fusion.1 = f32[1536,1536]{1,0:T(8,128)} fusion(f32[1536,512]{1,0:T(8,128)S(1)} %bitcast.190, f32[1536,512]{1,0:T(8,128)S(1)} %bitcast.199, f32[3,1536,1536]{2,1,0:T(8,128)} %param.7), kind=kOutput, calls=%fused_computation.10 | convolution fusion | flops 7250116608 | bytes 25165824 | tf_op jit(solution)/shard_map/dot_general | solution.py:10
  382.1 9.6 %copy.120 = f32[1536,1536]{1,0:T(8,128)} copy(f32[1536,1536]{0,1:T(8,128)} %bitcast.184) | data formatting | bytes 18874368 | tf_op jit(solution)/shard_map/dot_general | solution.py:15
  391.7 11.7 %convolution_bitcast_fusion.3 = f32[1,4,8,48,512]{4,3,2,1,0:T(8,128)S(1)} fusion(f32[4,8,48,1536]{3,2,1,0:T(8,128)} %bitcast.185, f32[1536,512,1,1]{1,0,3,2:T(8,128)} %bitcast.200), kind=kOutput, calls=%fused_computation.28 | convolution fusion | flops 7247757312 | bytes 15728640 | tf_op jit(solution)/shard_map/dot_general | solution.py:14
  403.4 8.0 %convolution_bitcast_fusion.2 = f32[1,4,8,48,512]{4,3,2,1,0:T(8,128)S(1)} fusion(f32[4,8,48,1536]{3,2,1,0:T(8,128)S(1)} %bitcast.206, f32[1536,512,1,1]{1,0,3,2:T(8,128)S(1)} %bitcast.191), kind=kOutput, calls=%fused_computation.27 | convolution fusion | flops 7247757312 | bytes 15728640 | tf_op jit(solution)/shard_map/dot_general | solution.py:15
  412.3 3.3 copy.121
  415.6 17.9 %all-to-all-done.2 = f32[8,2,4,48,512]{4,3,2,1,0:T(8,128)} async-done(((f32[8,2,4,48,512]{4,3,2,1,0:T(8,128)}), f32[8,2,4,48,512]{4,3,2,1,0:T(8,128)}, u32[]{:S(2)}, u32[]{:S(2)}) %all-to-all-start.2) | async-done | bytes 6291488 | tf_op jit(solution)/shard_map/all_to_all | solution.py:80
  433.5 6.7 all-to-all-start.4
  441.4 3.6 fusion.27
  445.6 13.2 %convolution_multiply_fusion = f32[1536,1536]{1,0:T(8,128)} fusion(f32[1536,512]{1,0:T(8,128)S(1)} %bitcast.192, f32[1536,512]{1,0:T(8,128)S(1)} %bitcast.201, f32[3,1536,1536]{2,1,0:T(8,128)} %param.7), kind=kOutput, calls=%fused_computation.9 | convolution fusion | flops 7250116608 | bytes 25165824 | tf_op jit(solution)/shard_map/dot_general | solution.py:10
  458.8 9.6 %copy.127 = f32[1536,1536]{1,0:T(8,128)} copy(f32[1536,1536]{0,1:T(8,128)} %bitcast.186) | data formatting | bytes 18874368 | tf_op jit(solution)/shard_map/dot_general | solution.py:15
  468.4 11.6 %convolution_bitcast_fusion.1 = f32[1,4,8,48,512]{4,3,2,1,0:T(8,128)S(1)} fusion(f32[4,8,48,1536]{3,2,1,0:T(8,128)} %bitcast.187, f32[1536,512,1,1]{1,0,3,2:T(8,128)} %bitcast.202), kind=kOutput, calls=%fused_computation.26 | convolution fusion | flops 7247757312 | bytes 15728640 | tf_op jit(solution)/shard_map/dot_general | solution.py:14
  480.0 8.0 %convolution_bitcast_fusion = f32[1,4,8,48,512]{4,3,2,1,0:T(8,128)S(1)} fusion(f32[4,8,48,1536]{3,2,1,0:T(8,128)S(1)} %bitcast.207, f32[1536,512,1,1]{1,0,3,2:T(8,128)S(1)} %bitcast.193), kind=kOutput, calls=%fused_computation.25 | convolution fusion | flops 7247757312 | bytes 15728640 | tf_op jit(solution)/shard_map/dot_general | solution.py:15
  488.9 3.3 copy.128
  492.2 18.2 %all-to-all-done.4 = f32[8,2,4,48,512]{4,3,2,1,0:T(8,128)} async-done(((f32[8,2,4,48,512]{4,3,2,1,0:T(8,128)}), f32[8,2,4,48,512]{4,3,2,1,0:T(8,128)}, u32[]{:S(2)}, u32[]{:S(2)}) %all-to-all-start.4) | async-done | bytes 6291488 | tf_op jit(solution)/shard_map/all_to_all | solution.py:80
  510.4 6.4 all-to-all-start.6
  516.8 9.1 %copy.129 = f32[8,2,4,48,512]{4,0,1,3,2:T(8,128)} copy(f32[8,2,4,48,512]{4,3,2,1,0:T(8,128)} %all-to-all-done.2) | data formatting | bytes 12582912 | tf_op jit(solution)/shard_map/all_to_all | solution.py:80
  525.9 9.1 %copy.130 = f32[8,2,4,48,512]{4,0,1,3,2:T(8,128)} copy(f32[8,2,4,48,512]{4,3,2,1,0:T(8,128)} %all-to-all-done.4) | data formatting | bytes 12582912 | tf_op jit(solution)/shard_map/all_to_all | solution.py:80
  535.0 52.0 %all-to-all-done.6 = f32[8,2,4,48,512]{4,3,2,1,0:T(8,128)} async-done(((f32[8,2,4,48,512]{4,3,2,1,0:T(8,128)}), f32[8,2,4,48,512]{4,3,2,1,0:T(8,128)}, u32[]{:S(2)}, u32[]{:S(2)}) %all-to-all-start.6) | async-done | bytes 6291488 | tf_op jit(solution)/shard_map/all_to_all | solution.py:80
  586.9 9.0 %copy.131 = f32[8,2,4,48,512]{4,0,1,3,2:T(8,128)} copy(f32[8,2,4,48,512]{4,3,2,1,0:T(8,128)} %all-to-all-done.6) | data formatting | bytes 12582912 | tf_op jit(solution)/shard_map/all_to_all | solution.py:80
  596.0 12.4 %fusion.12 = f32[4,48,512,12]{2,3,1,0:T(8,128)} fusion(f32[8,2,4,48,512]{4,0,1,3,2:T(8,128)} %copy.131, f32[8,2,4,48,512]{4,0,1,3,2:T(8,128)} %copy.130, f32[8,2,4,48,512]{4,0,1,3,2:T(8,128)} %copy.129, s32[8,6]{0,1:T(8,128)S(1)} %copy-done.7), kind=kOutput, calls=%fused_computation.24 | convolution fusion | flops 688915008 | bytes 23593152 | tf_op jit(solution)/shard_map/srk,srgpn->gkpn/dot_general | solution.py:85
  608.4 6.8 constant_dynamic-slice_fusion.4
  615.9 1.7 collective-permute-start.6
  619.1 23.9 %collective-permute-done.6 = f32[12,48,512]{2,1,0:T(8,128)S(1)} collective-permute-done((f32[12,48,512]{2,1,0:T(8,128)S(1)}, f32[12,48,512]{2,1,0:T(8,128)S(1)}, u32[]{:S(2)}, u32[]{:S(2)}) %collective-permute-start.6) | collective-permute-done | bytes 1179680 | tf_op jit(solution)/shard_map/ppermute | solution.py:46
  643.7 4.5 collective-permute-start.7
  649.7 23.0 %collective-permute-done.7 = f32[12,48,512]{2,1,0:T(8,128)S(1)} collective-permute-done((f32[12,48,512]{2,1,0:T(8,128)S(1)}, f32[12,48,512]{2,1,0:T(8,128)S(1)}, u32[]{:S(2)}, u32[]{:S(2)}) %collective-permute-start.7) | collective-permute-done | bytes 1179680 | tf_op jit(solution)/shard_map/ppermute | solution.py:46
  673.5 4.5 collective-permute-start.8
  678.7 1.6 collective-permute-start.11
  680.3 21.2 %collective-permute-done.8 = f32[12,48,512]{2,1,0:T(8,128)S(1)} collective-permute-done((f32[12,48,512]{2,1,0:T(8,128)S(1)}, f32[12,48,512]{2,1,0:T(8,128)S(1)}, u32[]{:S(2)}, u32[]{:S(2)}) %collective-permute-start.8) | collective-permute-done | bytes 1179680 | tf_op jit(solution)/shard_map/ppermute | solution.py:46
  701.6 5.0 collective-permute-done.11
  707.9 2.0 copy.139
  709.9 20.0 %all_to_all.69 = f32[576,8,64]{0,2,1:T(8,128)S(1)} all-to-all(f32[576,8,64]{0,2,1:T(8,128)} %copy.139), channel_id=1, replica_groups=mesh['grp'=4,'band'=8] {'band'}, dimensions={1} | all-to-all | bytes 2359296 | tf_op jit(solution)/shard_map/all_to_all | solution.py:87
  (75 shorter events, 22.5 us)
Async XLA Ops:
  2.0 56.5 %copy-start.8 = (s32[32,6]{0,1:T(8,128)S(1)}, s32[32,6]{0,1:T(8,128)}, u32[]{:S(2)}) copy-start(s32[32,6]{0,1:T(8,128)} %param.6) | copy-start | bytes 2308
  23.1 28.8 %collective-permute-start = (f32[576,512]{1,0:T(8,128)S(1)}, f32[576,512]{1,0:T(8,128)}, u32[]{:S(2)}, u32[]{:S(2)}) collective-permute-start(f32[576,512]{1,0:T(8,128)S(1)} %copy.107), channel_id=1, source_target_pairs={{0,8},{8,16},{16,24},{1,9},{9,17},{17,25},{2,10},{10,18},{18,26},{... | collective-permute-start | bytes 3538952 | tf_op jit(solution)/shard_map/ppermute | solution.py:26
  27.7 29.5 %collective-permute-start.1 = (f32[576,512]{1,0:T(8,128)S(1)}, f32[576,512]{1,0:T(8,128)}, u32[]{:S(2)}, u32[]{:S(2)}) collective-permute-start(f32[576,512]{1,0:T(8,128)S(1)} %copy.107), channel_id=1, source_target_pairs={{8,0},{16,8},{24,16},{9,1},{17,9},{25,17},{10,2},{18,10},{26,18},{... | collective-permute-start | bytes 3538952 | tf_op jit(solution)/shard_map/ppermute | solution.py:27
  51.9 7.7 %collective-permute-start.2 = (f32[576,512]{1,0:T(8,128)}, f32[576,512]{1,0:T(8,128)}, u32[]{:S(2)}, u32[]{:S(2)}) collective-permute-start(f32[576,512]{1,0:T(8,128)} %collective-permute-done), channel_id=1, source_target_pairs={{8,16},{16,24},{9,17},{17,25},{10,18},{18,26},{11,19},{19,27},{12,... | collective-permute-start | bytes 3538952 | tf_op jit(solution)/shard_map/ppermute | solution.py:26
  57.2 29.0 %collective-permute-start.3 = (f32[576,512]{1,0:T(8,128)}, f32[576,512]{1,0:T(8,128)}, u32[]{:S(2)}, u32[]{:S(2)}) collective-permute-start(f32[576,512]{1,0:T(8,128)} %collective-permute-done.1), channel_id=1, source_target_pairs={{8,0},{16,8},{9,1},{17,9},{10,2},{18,10},{11,3},{19,11},{12,4},{20... | collective-permute-start | bytes 3538952 | tf_op jit(solution)/shard_map/ppermute | solution.py:27
  58.6 0.6 copy-start.6
  59.6 33.3 %collective-permute-start.4 = (f32[576,512]{1,0:T(8,128)}, f32[576,512]{1,0:T(8,128)S(1)}, u32[]{:S(2)}, u32[]{:S(2)}) collective-permute-start(f32[576,512]{1,0:T(8,128)} %collective-permute-done.2), channel_id=1, source_target_pairs={{16,24},{17,25},{18,26},{19,27},{20,28},{21,29},{22,30},{23,31}} | collective-permute-start | bytes 3538952 | tf_op jit(solution)/shard_map/ppermute | solution.py:26
  86.1 27.9 %collective-permute-start.5 = (f32[576,512]{1,0:T(8,128)}, f32[576,512]{1,0:T(8,128)S(1)}, u32[]{:S(2)}, u32[]{:S(2)}) collective-permute-start(f32[576,512]{1,0:T(8,128)} %collective-permute-done.3), channel_id=1, source_target_pairs={{8,0},{9,1},{10,2},{11,3},{12,4},{13,5},{14,6},{15,7}} | collective-permute-start | bytes 3538952 | tf_op jit(solution)/shard_map/ppermute | solution.py:27
  129.7 74.0 %all-to-all-start.1 = ((f32[8,2,4,48,512]{4,3,2,1,0:T(8,128)}), f32[8,2,4,48,512]{4,3,2,1,0:T(8,128)}, u32[]{:S(2)}, u32[]{:S(2)}) async-start(f32[8,2,4,48,512]{4,3,2,1,0:T(8,128)} %fusion.11), calls=%async_computation.1 | async-start | bytes 12582912 | tf_op jit(solution)/shard_map/all_to_all | solution.py:74
  203.6 76.4 %all-to-all-start.3 = ((f32[8,2,4,48,512]{4,3,2,1,0:T(8,128)}), f32[8,2,4,48,512]{4,3,2,1,0:T(8,128)}, u32[]{:S(2)}, u32[]{:S(2)}) async-start(f32[8,2,4,48,512]{4,3,2,1,0:T(8,128)} %fusion.10), calls=%async_computation.3 | async-start | bytes 12582912 | tf_op jit(solution)/shard_map/all_to_all | solution.py:74
  280.0 76.9 %all-to-all-start.5 = ((f32[8,2,4,48,512]{4,3,2,1,0:T(8,128)}), f32[8,2,4,48,512]{4,3,2,1,0:T(8,128)}, u32[]{:S(2)}, u32[]{:S(2)}) async-start(f32[8,2,4,48,512]{4,3,2,1,0:T(8,128)} %fusion.9), calls=%async_computation.5 | async-start | bytes 12582912 | tf_op jit(solution)/shard_map/all_to_all | solution.py:74
  292.9 13.2 %copy-start = (f32[1,4,8,48,512]{4,3,2,1,0:T(8,128)}, f32[1,4,8,48,512]{4,3,2,1,0:T(8,128)S(1)}, u32[]{:S(2)}) copy-start(f32[1,4,8,48,512]{4,3,2,1,0:T(8,128)S(1)} %copy.112) | copy-start | bytes 9437188
  315.7 11.6 %copy-start.3 = (f32[1536,1536]{1,0:T(8,128)S(1)}, f32[1536,1536]{1,0:T(8,128)}, u32[]{:S(2)}) copy-start(f32[1536,1536]{1,0:T(8,128)} %copy.113) | copy-start | bytes 28311556
  356.9 76.6 %all-to-all-start.2 = ((f32[8,2,4,48,512]{4,3,2,1,0:T(8,128)}), f32[8,2,4,48,512]{4,3,2,1,0:T(8,128)}, u32[]{:S(2)}, u32[]{:S(2)}) async-start(f32[8,2,4,48,512]{4,3,2,1,0:T(8,128)} %copy.114), calls=%async_computation.2 | async-start | bytes 12582912 | tf_op jit(solution)/shard_map/all_to_all | solution.py:80
  368.9 13.2 %copy-start.1 = (f32[1,4,8,48,512]{4,3,2,1,0:T(8,128)}, f32[1,4,8,48,512]{4,3,2,1,0:T(8,128)S(1)}, u32[]{:S(2)}) copy-start(f32[1,4,8,48,512]{4,3,2,1,0:T(8,128)S(1)} %copy.119) | copy-start | bytes 9437188
  391.7 11.7 %copy-start.4 = (f32[1536,1536]{1,0:T(8,128)S(1)}, f32[1536,1536]{1,0:T(8,128)}, u32[]{:S(2)}) copy-start(f32[1536,1536]{1,0:T(8,128)} %copy.120) | copy-start | bytes 28311556
  433.5 76.8 %all-to-all-start.4 = ((f32[8,2,4,48,512]{4,3,2,1,0:T(8,128)}), f32[8,2,4,48,512]{4,3,2,1,0:T(8,128)}, u32[]{:S(2)}, u32[]{:S(2)}) async-start(f32[8,2,4,48,512]{4,3,2,1,0:T(8,128)} %copy.121), calls=%async_computation.4 | async-start | bytes 12582912 | tf_op jit(solution)/shard_map/all_to_all | solution.py:80
  445.6 13.2 %copy-start.2 = (f32[1,4,8,48,512]{4,3,2,1,0:T(8,128)}, f32[1,4,8,48,512]{4,3,2,1,0:T(8,128)S(1)}, u32[]{:S(2)}) copy-start(f32[1,4,8,48,512]{4,3,2,1,0:T(8,128)S(1)} %copy.126) | copy-start | bytes 9437188
  468.4 11.6 %copy-start.5 = (f32[1536,1536]{1,0:T(8,128)S(1)}, f32[1536,1536]{1,0:T(8,128)}, u32[]{:S(2)}) copy-start(f32[1536,1536]{1,0:T(8,128)} %copy.127) | copy-start | bytes 28311556
  510.4 76.6 %all-to-all-start.6 = ((f32[8,2,4,48,512]{4,3,2,1,0:T(8,128)}), f32[8,2,4,48,512]{4,3,2,1,0:T(8,128)}, u32[]{:S(2)}, u32[]{:S(2)}) async-start(f32[8,2,4,48,512]{4,3,2,1,0:T(8,128)} %copy.128), calls=%async_computation.6 | async-start | bytes 12582912 | tf_op jit(solution)/shard_map/all_to_all | solution.py:80
  535.0 61.0 %copy-start.7 = (s32[8,6]{0,1:T(8,128)S(1)}, s32[8,6]{0,1:T(8,128)}, u32[]{:S(2)}) copy-start(s32[8,6]{0,1:T(8,128)} %copy-done.6) | copy-start | bytes 580
  615.9 27.1 %collective-permute-start.6 = (f32[12,48,512]{2,1,0:T(8,128)S(1)}, f32[12,48,512]{2,1,0:T(8,128)S(1)}, u32[]{:S(2)}, u32[]{:S(2)}) collective-permute-start(f32[12,48,512]{2,1,0:T(8,128)S(1)} %copy.133), channel_id=1, source_target_pairs={{0,8},{1,9},{2,10},{3,11},{4,12},{5,13},{6,14},{7,15}} | collective-permute-start | bytes 3538952 | tf_op jit(solution)/shard_map/ppermute | solution.py:46
  618.3 29.9 %collective-permute-start.9 = (f32[12,48,512]{2,1,0:T(8,128)S(1)}, f32[12,48,512]{2,1,0:T(8,128)S(1)}, u32[]{:S(2)}, u32[]{:S(2)}) collective-permute-start(f32[12,48,512]{2,1,0:T(8,128)S(1)} %copy.136), channel_id=1, source_target_pairs={{24,16},{25,17},{26,18},{27,19},{28,20},{29,21},{30,22},{31,23}} | collective-permute-start | bytes 3538952 | tf_op jit(solution)/shard_map/ppermute | solution.py:47
  643.7 29.0 %collective-permute-start.7 = (f32[12,48,512]{2,1,0:T(8,128)S(1)}, f32[12,48,512]{2,1,0:T(8,128)S(1)}, u32[]{:S(2)}, u32[]{:S(2)}) collective-permute-start(f32[12,48,512]{2,1,0:T(8,128)S(1)} %fusion.18), channel_id=1, source_target_pairs={{0,8},{8,16},{1,9},{9,17},{2,10},{10,18},{3,11},{11,19},{4,12},{12... | collective-permute-start | bytes 3538952 | tf_op jit(solution)/shard_map/ppermute | solution.py:46
  649.0 29.0 %collective-permute-start.10 = (f32[12,48,512]{2,1,0:T(8,128)S(1)}, f32[12,48,512]{2,1,0:T(8,128)S(1)}, u32[]{:S(2)}, u32[]{:S(2)}) collective-permute-start(f32[12,48,512]{2,1,0:T(8,128)S(1)} %fusion.16), channel_id=1, source_target_pairs={{16,8},{24,16},{17,9},{25,17},{18,10},{26,18},{19,11},{27,19},{20,... | collective-permute-start | bytes 3538952 | tf_op jit(solution)/shard_map/ppermute | solution.py:47
  673.5 28.1 %collective-permute-start.8 = (f32[12,48,512]{2,1,0:T(8,128)S(1)}, f32[12,48,512]{2,1,0:T(8,128)S(1)}, u32[]{:S(2)}, u32[]{:S(2)}) collective-permute-start(f32[12,48,512]{2,1,0:T(8,128)S(1)} %fusion.17), channel_id=1, source_target_pairs={{0,8},{8,16},{16,24},{1,9},{9,17},{17,25},{2,10},{10,18},{18,26},{... | collective-permute-start | bytes 3538952 | tf_op jit(solution)/shard_map/ppermute | solution.py:46
  678.7 27.8 %collective-permute-start.11 = (f32[12,48,512]{2,1,0:T(8,128)S(1)}, f32[12,48,512]{2,1,0:T(8,128)S(1)}, u32[]{:S(2)}, u32[]{:S(2)}) collective-permute-start(f32[12,48,512]{2,1,0:T(8,128)S(1)} %fusion.15), channel_id=1, source_target_pairs={{8,0},{16,8},{24,16},{9,1},{17,9},{25,17},{10,2},{18,10},{26,18},{... | collective-permute-start | bytes 3538952 | tf_op jit(solution)/shard_map/ppermute | solution.py:47

commit v8 on v7

v8 whole, which is shorter than its diff:
```python
import jax
import jax.numpy as jnp
from jax import lax
from jax.sharding import PartitionSpec as P

PRECISION = lax.Precision.HIGH


def band_exchange(outgoing):
    return lax.all_to_all(outgoing, "band", split_axis=0, concat_axis=0, tiled=True)


def line_gather(x, axis, count, riders=()):
    index = lax.axis_index(axis)
    spare = jnp.zeros((count + 1,) + x.shape, x.dtype)
    spare = lax.dynamic_update_index_in_dim(spare, x, index, 0)
    rightward, leftward = x, x
    carried = []
    for step in range(1, count):
        rider = step - 1 < len(riders)
        if rider:
            rightward, leftward, load = lax.optimization_barrier((rightward, leftward, riders[step - 1]))
        rightward = lax.ppermute(rightward, axis, [(i, i + 1) for i in range(step - 1, count - 1)])
        leftward = lax.ppermute(leftward, axis, [(i + 1, i) for i in range(0, count - step)])
        if rider:
            rightward, leftward, load = lax.optimization_barrier((rightward, leftward, band_exchange(load)))
            carried.append(load)
        from_left = jnp.where(index >= step, index - step, count)
        from_right = jnp.where(index + step < count, index + step, count)
        spare = lax.dynamic_update_index_in_dim(spare, rightward, from_left, 0)
        spare = lax.dynamic_update_index_in_dim(spare, leftward, from_right, 0)
    carried += [band_exchange(load) for load in riders[len(carried):]]
    return spare[:count], carried


def line_reduce(parts, axis, count, riders=()):
    index = lax.axis_index(axis)

    def part_for(target):
        return lax.dynamic_index_in_dim(parts, jnp.clip(target, 0, count - 1), 0, keepdims=False)

    rightward = jnp.zeros(parts.shape[1:], parts.dtype)
    leftward = jnp.zeros(parts.shape[1:], parts.dtype)
    carried = []
    for step in range(1, count):
        send_right = rightward + part_for(index + count - step)
        send_left = leftward + part_for(index - count + step)
        rider = step - 1 < len(riders)
        if rider:
            send_right, send_left, load = lax.optimization_barrier((send_right, send_left, riders[step - 1]))
        rightward = lax.ppermute(send_right, axis, [(i, i + 1) for i in range(0, step)])
        leftward = lax.ppermute(send_left, axis, [(i, i - 1) for i in range(count - step, count)])
        if rider:
            rightward, leftward, load = lax.optimization_barrier((rightward, leftward, band_exchange(load)))
            carried.append(load)
    carried += [band_exchange(load) for load in riders[len(carried):]]
    return part_for(index) + rightward + leftward, carried


def body(orbitals, requests, coulomb):
    group_count = lax.axis_size("grp")
    band_count = lax.axis_size("band")
    devices = group_count * band_count
    blk = coulomb.shape[1]
    orbital_width = orbitals.shape[1] * band_count
    half = orbital_width // 2
    piece_rows = blk // devices
    slot_count = coulomb.shape[0]
    block_count = orbitals.shape[0] // (band_count * piece_rows)
    own_rows = lax.all_to_all(orbitals, "band", split_axis=0, concat_axis=1, tiled=True)
    group_index = lax.axis_index("grp")
    band_index = lax.axis_index("band")
    group_requests = lax.dynamic_slice_in_dim(requests, group_index * band_count, band_count, 0)
    live = (group_requests >= 0).astype(jnp.float32)
    own_pairs = lax.dynamic_index_in_dim(group_requests, band_index, 0, keepdims=False)
    one_hot = (
        group_requests[:, :, None] == jnp.arange(block_count, dtype=jnp.int32)[None, None, :]
    ).astype(jnp.float32)

    def requested(pieces, slot):
        wanted = group_requests[:, 2 * slot : 2 * slot + 2]
        mask = live[None, :, 2 * slot : 2 * slot + 2, None, None]
        outgoing = jnp.take(pieces, jnp.maximum(wanted, 0), axis=1) * mask
        return outgoing.transpose(1, 2, 0, 3, 4)

    def shape_pieces(gathered):
        return gathered.reshape(group_count, block_count, piece_rows, half)

    first_pieces = shape_pieces(line_gather(own_rows[:, :half], "grp", group_count)[0])
    first_loads = [requested(first_pieces, slot) for slot in range(slot_count)]
    second_pieces, first_arrived = line_gather(own_rows[:, half:], "grp", group_count, first_loads)
    second_pieces = shape_pieces(second_pieces)
    second_arrived = [band_exchange(requested(second_pieces, slot)) for slot in range(slot_count)]
    returned = [[], []]
    held = []
    for slot in range(slot_count):
        rows = [
            arrived.transpose(1, 2, 0, 3, 4).reshape(2, blk, half)
            for arrived in (first_arrived[slot], second_arrived[slot])
        ]
        density = sum(
            jnp.dot(r[0], r[1].T, precision=PRECISION, preferred_element_type=jnp.float32) for r in rows
        )
        kernel = density * coulomb[slot]
        scale = jnp.where(own_pairs[2 * slot] == own_pairs[2 * slot + 1], 0.5, 1.0)
        for h in range(2):
            onto_first = jnp.dot(kernel, rows[h][1], precision=PRECISION, preferred_element_type=jnp.float32)
            onto_second = jnp.dot(kernel.T, rows[h][0], precision=PRECISION, preferred_element_type=jnp.float32)
            outbound = (jnp.stack([onto_first, onto_second], 0) * scale).reshape(
                2, group_count, band_count, piece_rows, half
            )
            outbound = outbound.transpose(2, 0, 1, 3, 4)
            if h == 0:
                returned[0].append(band_exchange(outbound))
            else:
                held.append(outbound)

    def sum_blocks(returned):
        gathered = jnp.concatenate(returned, axis=1)
        return jnp.einsum("srk,srgpn->gkpn", one_hot, gathered, precision=lax.Precision.HIGHEST)

    first_home, second_returned = line_reduce(sum_blocks(returned[0]), "grp", group_count, held)
    second_home, _ = line_reduce(sum_blocks(second_returned), "grp", group_count)
    home_rows = jnp.concatenate([first_home, second_home], axis=-1).reshape(
        block_count * piece_rows, orbital_width
    )
    return lax.all_to_all(home_rows, "band", split_axis=1, concat_axis=0, tiled=True)


def solution(mesh):
    placed = (P("grp", "band"), P(), P(("grp", "band"), None, None))
    return jax.shard_map(
        body, mesh=mesh, in_specs=placed, out_specs=P("grp", "band"), check_vma=False
    )
```

time: 743 us -> 733 us (0.987)
  waiting for transfers between devices: 364 us -> 231 us
  starting transfers between devices: 61.6 us -> 116 us
  local copies, waits for them, and re-layouts: 123 us -> 153 us
  other arithmetic: 27.4 us -> 46.2 us
  matrix products: 111 us -> 129 us
    all_to_all x6 -> x12, waiting for transfers between devices: 218 us -> 125 us  [band_exchange(): lax.all_to_all(outgoing, 'band', split_axis=0, concat_axis=0, tiled=True)]
    all_to_all x6 -> x12, starting transfers between devices: 37.2 us -> 67.3 us  [band_exchange(): lax.all_to_all(outgoing, 'band', split_axis=0, concat_axis=0, tiled=True)]
    optimization_barrier x0 -> x14, local copies, waits for them, and re-layouts: none -> 27.1 us  [the longest x3 14.7 us: line_reduce(): lax.optimization_barrier((rightward, leftward, band_exchange(load)))]
    ppermute x3 -> x6, waiting for transfers between devices: 68.1 us -> 41.8 us  [line_reduce(): lax.ppermute(send_right, axis, [(i, i + 1) for i in range(0, step)])]
    dot_general x10 -> x20, matrix products: 111 us -> 129 us  [the longest x6 52 us: body(): jnp.dot(r[0], r[1].T, precision=PRECISION, preferred_element_type=jnp.flo...]
    unnamed x18 -> x128, local copies, waits for them, and re-layouts: 0.26 us -> 13.4 us
    all_to_all x3, local copies, waits for them, and re-layouts: 27.2 us -> 14.6 us  [band_exchange(): lax.all_to_all(outgoing, 'band', split_axis=0, concat_axis=0, tiled=True)]
    ppermute x3 -> x6, waiting for transfers between devices: 23 us -> 11.7 us  [line_gather(): lax.ppermute(rightward, axis, [(i, i + 1) for i in range(step - 1, count...]
  transfers between devices with their start and end apart: 18 -> 36, of which waited for: 14 -> 24; matrix products, arithmetic and copies ran while one was open for 28% -> 35% of each run, Pallas kernels for 0% -> 0%
where the time goes in v8:
time: 733 us; the launch traced here: 721 us
  waiting for transfers between devices  231 us (32%)
  local copies, waits for them, and re-layouts  153 us (21%)
  matrix products  129 us (18%)
  starting transfers between devices  116 us (16%)
  other arithmetic  46.2 us (6%)
  blocking collectives  40.8 us (6%)
    all_to_all x12, waiting for transfers between devices, band_exchange(): lax.all_to_all(outgoing, 'band', split_axis=0, concat_axis=0, tiled=True)  125 us
    all_to_all x12, starting transfers between devices, band_exchange(): lax.all_to_all(outgoing, 'band', split_axis=0, concat_axis=0, tiled=True)  67.3 us
    dot_general x6, matrix products, body(): jnp.dot(r[0], r[1].T, precision=PRECISION, preferred_element_type=jnp.flo...  52 us
    ppermute x6, waiting for transfers between devices, line_gather(): lax.ppermute(leftward, axis, [(i + 1, i) for i in range(0, count - step)])  46.2 us
    dot_general x6, matrix products, body(): jnp.dot(kernel, rows[h][1], precision=PRECISION, preferred_element_type=j...  42.2 us
    ppermute x6, waiting for transfers between devices, line_reduce(): lax.ppermute(send_right, axis, [(i, i + 1) for i in range(0, step)])  41.8 us
    dot_general x3, local copies, waits for them, and re-layouts, body(): jnp.dot(kernel.T, rows[h][0], precision=PRECISION, preferred_element_type...  29 us
    dot_general x6, matrix products, body(): jnp.dot(kernel.T, rows[h][0], precision=PRECISION, preferred_element_type...  27.5 us
  transfers between devices with their start and end apart: 36, of which 24 were waited for; matrix products, arithmetic and copies ran while one was open for 35% of the time, Pallas kernels for 0%

profile of v8, /device:TPU:2, one launch (start us, length us, event | category | flops | bytes accessed | tf_op | source)
XLA Modules:
  0.0 720.7 jit_solution(10450717688236952612)
XLA Ops:
  2.0 20.8 %all_to_all.98 = f32[8,576,64]{1,2,0:T(8,128)S(1)} all-to-all(f32[8,576,64]{1,2,0:T(8,128)S(1)} %copy.177), channel_id=1, replica_groups=mesh['grp'=4,'band'=8] {'band'}, dimensions={0} | all-to-all | bytes 2359296 | tf_op jit(solution)/shard_map/all_to_all | solution.py:70
  30.9 10.4 %collective-permute-done = f32[576,256]{1,0:T(8,128)S(1)} collective-permute-done((f32[576,256]{1,0:T(8,128)}, f32[576,256]{1,0:T(8,128)S(1)}, u32[]{:S(2)}, u32[]{:S(2)}) %collective-permute-start) | collective-permute-done | bytes 589856 | tf_op jit(solution)/shard_map/ppermute | solution.py:23
  49.0 14.5 %collective-permute-done.3 = f32[576,256]{1,0:T(8,128)S(1)} collective-permute-done((f32[576,256]{1,0:T(8,128)}, f32[576,256]{1,0:T(8,128)S(1)}, u32[]{:S(2)}, u32[]{:S(2)}) %collective-permute-start.3) | collective-permute-done | bytes 589856 | tf_op jit(solution)/shard_map/ppermute | solution.py:24
  66.0 12.8 %collective-permute-done.5 = f32[576,256]{1,0:T(8,128)S(1)} collective-permute-done((f32[576,256]{1,0:T(8,128)S(1)}, f32[576,256]{1,0:T(8,128)S(1)}, u32[]{:S(2)}, u32[]{:S(2)}) %collective-permute-start.5) | collective-permute-done | bytes 589856 | tf_op jit(solution)/shard_map/ppermute | solution.py:24
  81.5 4.0 fusion.26
  85.5 4.5 all-to-all-start.1
  93.5 4.6 collective-permute-start.6
  103.3 4.1 fusion.25
  110.0 15.6 %all-to-all-done.1 = f32[8,2,4,48,256]{4,3,2,1,0:T(8,128)} async-done(((f32[8,2,4,48,256]{4,3,2,1,0:T(8,128)}), f32[8,2,4,48,256]{4,3,2,1,0:T(8,128)}, u32[]{:S(2)}, u32[]{:S(2)}) %all-to-all-start.1) | async-done | bytes 3145760 | tf_op jit(solution)/shard_map/all_to_all | solution.py:10
  125.6 5.9 all-to-all-start.2
  146.0 4.4 collective-permute-done.9
  150.4 17.6 %all-to-all-done.2 = f32[8,2,4,48,256]{4,3,2,1,0:T(8,128)} async-done(((f32[8,2,4,48,256]{4,3,2,1,0:T(8,128)}), f32[8,2,4,48,256]{4,3,2,1,0:T(8,128)}, u32[]{:S(2)}, u32[]{:S(2)}) %all-to-all-start.2) | async-done | bytes 3145760 | tf_op jit(solution)/shard_map/all_to_all | solution.py:10
  168.0 5.1 all-to-all-start.3
  183.3 11.5 %collective-permute-done.11 = f32[576,256]{1,0:T(8,128)} collective-permute-done((f32[576,256]{1,0:T(8,128)}, f32[576,256]{1,0:T(8,128)}, u32[]{:S(2)}, u32[]{:S(2)}) %collective-permute-start.11) | collective-permute-done | bytes 589856 | tf_op jit(solution)/shard_map/ppermute | solution.py:24
  194.8 14.7 %all-to-all-done.3 = f32[8,2,4,48,256]{4,3,2,1,0:T(8,128)S(1)} async-done(((f32[8,2,4,48,256]{4,3,2,1,0:T(8,128)}), f32[8,2,4,48,256]{4,3,2,1,0:T(8,128)S(1)}, u32[]{:S(2)}, u32[]{:S(2)}) %all-to-all-start.3) | async-done | bytes 3145760 | tf_op jit(solution)/shard_map/all_to_all | solution.py:10
  221.9 6.0 all-to-all-start.8
  239.0 25.4 %all-to-all-done.8 = f32[8,2,4,48,256]{4,3,2,1,0:T(8,128)} async-done(((f32[8,2,4,48,256]{4,3,2,1,0:T(8,128)}), f32[8,2,4,48,256]{4,3,2,1,0:T(8,128)}, u32[]{:S(2)}, u32[]{:S(2)}) %all-to-all-start.8) | async-done | bytes 3145760 | tf_op jit(solution)/shard_map/all_to_all | solution.py:10
  264.4 6.1 all-to-all-start.6
  273.0 6.4 fusion.54
  283.3 6.4 fusion.55
  298.2 6.4 fusion.56
  306.9 6.3 all-to-all-start.4
  319.0 9.7 %fusion = f32[1536,1536]{1,0:T(8,128)} fusion(f32[1536,1536]{1,0:T(8,128)S(1)} %copy-done.3, f32[1536,256]{1,0:T(8,128)S(1)} %bitcast.353, f32[1536,256]{1,0:T(8,128)S(1)} %bitcast.355, f32[3,1536,1536]{2,1,0:T(8,128)} %param.7), kind=kOutput, calls=%fused_computation.7 | convolution fusion | flops 3628597248 | bytes 31457280 | tf_op jit(solution)/shard_map/dot_general | solution.py:102
  328.7 9.6 %copy.215 = f32[1536,1536]{1,0:T(8,128)} copy(f32[1536,1536]{0,1:T(8,128)} %bitcast.316) | data formatting | bytes 18874368 | tf_op jit(solution)/shard_map/dot_general | solution.py:108
  338.3 6.9 convolution_bitcast_fusion.7
  345.3 4.0 convolution_bitcast_fusion.6
  351.7 4.6 all-to-all-start.9
  358.8 11.8 %fusion.2 = f32[1536,1536]{1,0:T(8,128)} fusion(f32[1536,1536]{1,0:T(8,128)} %fusion.54, f32[1536,256]{1,0:T(8,128)S(1)} %bitcast.363, f32[1536,256]{1,0:T(8,128)S(1)} %bitcast.361, f32[3,1536,1536]{2,1,0:T(8,128)} %param.7), kind=kOutput, calls=%fused_computation.11 | convolution fusion | flops 3628597248 | bytes 31457280 | tf_op jit(solution)/shard_map/dot_general | solution.py:102
  370.6 9.7 %copy.199 = f32[1536,1536]{1,0:T(8,128)} copy(f32[1536,1536]{0,1:T(8,128)} %bitcast.322) | data formatting | bytes 18874368 | tf_op jit(solution)/shard_map/dot_general | solution.py:108
  380.3 7.0 convolution_bitcast_fusion.11
  387.3 4.1 convolution_bitcast_fusion.10
  393.8 5.1 all-to-all-start.5
  401.2 11.3 %fusion.1 = f32[1536,1536]{1,0:T(8,128)} fusion(f32[1536,1536]{1,0:T(8,128)} %fusion.55, f32[1536,256]{1,0:T(8,128)S(1)} %bitcast.357, f32[1536,256]{1,0:T(8,128)S(1)} %bitcast.359, f32[3,1536,1536]{2,1,0:T(8,128)} %param.7), kind=kOutput, calls=%fused_computation.9 | convolution fusion | flops 3628597248 | bytes 31457280 | tf_op jit(solution)/shard_map/dot_general | solution.py:102
  412.5 9.7 %copy.207 = f32[1536,1536]{1,0:T(8,128)} copy(f32[1536,1536]{0,1:T(8,128)} %bitcast.319) | data formatting | bytes 18874368 | tf_op jit(solution)/shard_map/dot_general | solution.py:108
  422.2 7.0 convolution_bitcast_fusion.9
  429.2 4.1 convolution_bitcast_fusion.8
  435.6 5.5 all-to-all-start.7
  441.2 6.9 convolution_bitcast_fusion.5
  448.1 7.3 %convolution_bitcast_fusion.4 = f32[1,4,8,48,256]{4,3,2,1,0:T(8,128)S(1)} fusion(f32[4,8,48,1536]{3,2,1,0:T(8,128)} %bitcast.333, f32[1536,256,1,1]{1,0,3,2:T(8,128)S(1)} %bitcast.364), kind=kOutput, calls=%fused_computation.55 | convolution fusion | flops 3623878656 | bytes 12582912 | tf_op jit(solution)/shard_map/dot_general | solution.py:108
  457.4 5.3 copy.219
  462.7 5.4 copy.217
  468.1 9.6 %all-to-all-done.7 = f32[8,2,4,48,256]{4,3,2,1,0:T(8,128)} async-done(((f32[8,2,4,48,256]{4,3,2,1,0:T(8,128)}), f32[8,2,4,48,256]{4,3,2,1,0:T(8,128)}, u32[]{:S(2)}, u32[]{:S(2)}) %all-to-all-start.7) | async-done | bytes 3145760 | tf_op jit(solution)/shard_map/all_to_all | solution.py:10
  490.6 6.2 all-to-all-start.10
  496.9 7.4 %convolution_bitcast_fusion.3 = f32[1,4,8,48,256]{4,3,2,1,0:T(8,128)S(1)} fusion(f32[4,8,48,1536]{3,2,1,0:T(8,128)} %bitcast.321, f32[1536,256,1,1]{1,0,3,2:T(8,128)} %bitcast.360), kind=kOutput, calls=%fused_computation.54 | convolution fusion | flops 3623878656 | bytes 12582912 | tf_op jit(solution)/shard_map/dot_general | solution.py:107
  508.9 4.0 convolution_bitcast_fusion.2
  515.0 6.0 collective-permute-done.12
  521.0 12.3 %all-to-all-done.10 = f32[8,2,4,48,256]{4,3,2,1,0:T(8,128)} async-done(((f32[8,2,4,48,256]{4,3,2,1,0:T(8,128)}), f32[8,2,4,48,256]{4,3,2,1,0:T(8,128)}, u32[]{:S(2)}, u32[]{:S(2)}) %all-to-all-start.10) | async-done | bytes 3145760 | tf_op jit(solution)/shard_map/all_to_all | solution.py:10
  538.6 6.1 all-to-all-start.11
  544.8 7.0 convolution_bitcast_fusion.1
  556.3 4.1 convolution_bitcast_fusion
  562.4 6.0 collective-permute-done.14
  568.4 12.8 %all-to-all-done.11 = f32[8,2,4,48,256]{4,3,2,1,0:T(8,128)} async-done(((f32[8,2,4,48,256]{4,3,2,1,0:T(8,128)}), f32[8,2,4,48,256]{4,3,2,1,0:T(8,128)}, u32[]{:S(2)}, u32[]{:S(2)}) %all-to-all-start.11) | async-done | bytes 3145760 | tf_op jit(solution)/shard_map/all_to_all | solution.py:10
  586.5 5.9 all-to-all-start.12
  596.6 5.4 collective-permute-start.16
  602.0 5.4 copy.235
  607.4 5.4 copy.236
  613.8 15.1 %all-to-all-done.12 = f32[8,2,4,48,256]{4,3,2,1,0:T(8,128)} async-done(((f32[8,2,4,48,256]{4,3,2,1,0:T(8,128)}), f32[8,2,4,48,256]{4,3,2,1,0:T(8,128)}, u32[]{:S(2)}, u32[]{:S(2)}) %all-to-all-start.12) | async-done | bytes 3145760 | tf_op jit(solution)/shard_map/all_to_all | solution.py:10
  640.8 11.8 %collective-permute-done.18 = f32[12,48,256]{2,1,0:T(8,128)S(1)} collective-permute-done((f32[12,48,256]{2,1,0:T(8,128)S(1)}, f32[12,48,256]{2,1,0:T(8,128)S(1)}, u32[]{:S(2)}, u32[]{:S(2)}) %collective-permute-start.18) | collective-permute-done | bytes 589856 | tf_op jit(solution)/shard_map/ppermute | solution.py:51
  653.0 4.4 collective-permute-start.19
  658.7 10.7 %collective-permute-done.19 = f32[12,48,256]{2,1,0:T(8,128)S(1)} collective-permute-done((f32[12,48,256]{2,1,0:T(8,128)S(1)}, f32[12,48,256]{2,1,0:T(8,128)S(1)}, u32[]{:S(2)}, u32[]{:S(2)}) %collective-permute-start.19) | collective-permute-done | bytes 589856 | tf_op jit(solution)/shard_map/ppermute | solution.py:51
  670.6 5.2 collective-permute-start.20
  680.2 6.3 collective-permute-done.20
  686.5 6.1 collective-permute-done.23
  698.2 20.0 %all_to_all.99 = f32[576,8,64]{0,2,1:T(8,128)S(1)} all-to-all(f32[576,8,64]{0,2,1:T(8,128)} %copy.247), channel_id=1, replica_groups=mesh['grp'=4,'band'=8] {'band'}, dimensions={1} | all-to-all | bytes 2359296 | tf_op jit(solution)/shard_map/all_to_all | solution.py:127
  (282 shorter events, 183.6 us)
Async XLA Ops:
  24.8 16.4 %collective-permute-start = (f32[576,256]{1,0:T(8,128)}, f32[576,256]{1,0:T(8,128)S(1)}, u32[]{:S(2)}, u32[]{:S(2)}) collective-permute-start(f32[576,256]{1,0:T(8,128)} %copy.180), channel_id=1, source_target_pairs={{0,8},{8,16},{16,24},{1,9},{9,17},{17,25},{2,10},{10,18},{18,26},{... | collective-permute-start | bytes 1769480 | tf_op jit(solution)/shard_map/ppermute | solution.py:23
  28.4 18.7 %copy-start.45 = (s32[8,6]{0,1:T(8,128)}, s32[8,6]{0,1:T(8,128)S(1)}, u32[]{:S(2)}) copy-start(s32[8,6]{0,1:T(8,128)S(1)} %get-tuple-element.79) | copy-start | bytes 580
  28.4 17.1 %collective-permute-start.1 = (f32[576,256]{1,0:T(8,128)}, f32[576,256]{1,0:T(8,128)}, u32[]{:S(2)}, u32[]{:S(2)}) collective-permute-start(f32[576,256]{1,0:T(8,128)} %copy.180), channel_id=1, source_target_pairs={{8,0},{16,8},{24,16},{9,1},{17,9},{25,17},{10,2},{18,10},{26,18},{... | collective-permute-start | bytes 1769480 | tf_op jit(solution)/shard_map/ppermute | solution.py:24
  41.2 5.9 collective-permute-start.2
  43.3 38.2 %copy-start.52 = (pred[8,2]{1,0:T(8,128)(4,1)}, pred[8,2]{1,0:T(8,128)(4,1)S(1)}, u32[]{:S(2)}) copy-start(pred[8,2]{1,0:T(8,128)(4,1)S(1)} %copy.178) | copy-start | bytes 52
  45.5 18.0 %collective-permute-start.3 = (f32[576,256]{1,0:T(8,128)}, f32[576,256]{1,0:T(8,128)S(1)}, u32[]{:S(2)}, u32[]{:S(2)}) collective-permute-start(f32[576,256]{1,0:T(8,128)} %collective-permute-done.1), channel_id=1, source_target_pairs={{8,0},{16,8},{9,1},{17,9},{10,2},{18,10},{11,3},{19,11},{12,4},{20... | collective-permute-start | bytes 1769480 | tf_op jit(solution)/shard_map/ppermute | solution.py:24
  47.1 18.8 %collective-permute-start.4 = (f32[576,256]{1,0:T(8,128)}, f32[576,256]{1,0:T(8,128)S(1)}, u32[]{:S(2)}, u32[]{:S(2)}) collective-permute-start(f32[576,256]{1,0:T(8,128)} %collective-permute-done.2), channel_id=1, source_target_pairs={{16,24},{17,25},{18,26},{19,27},{20,28},{21,29},{22,30},{23,31}} | collective-permute-start | bytes 1769480 | tf_op jit(solution)/shard_map/ppermute | solution.py:23
  63.5 15.4 %collective-permute-start.5 = (f32[576,256]{1,0:T(8,128)S(1)}, f32[576,256]{1,0:T(8,128)S(1)}, u32[]{:S(2)}, u32[]{:S(2)}) collective-permute-start(f32[576,256]{1,0:T(8,128)S(1)} %collective-permute-done.3), channel_id=1, source_target_pairs={{8,0},{9,1},{10,2},{11,3},{12,4},{13,5},{14,6},{15,7}} | collective-permute-start | bytes 1769480 | tf_op jit(solution)/shard_map/ppermute | solution.py:24
  85.5 12.6 %copy-start.57 = (pred[8,2]{0,1:T(4,128)(4,1)S(1)}, pred[8,2]{0,1:T(4,128)(4,1)}, u32[]{:S(2)}) copy-start(pred[8,2]{0,1:T(4,128)(4,1)} %get-tuple-element.115) | copy-start | bytes 52
  85.5 40.1 %all-to-all-start.1 = ((f32[8,2,4,48,256]{4,3,2,1,0:T(8,128)}), f32[8,2,4,48,256]{4,3,2,1,0:T(8,128)}, u32[]{:S(2)}, u32[]{:S(2)}) async-start(f32[8,2,4,48,256]{4,3,2,1,0:T(8,128)} %fusion.26), calls=%async_computation.1 | async-start | bytes 6291456 | tf_op jit(solution)/shard_map/all_to_all | solution.py:10
  92.2 16.5 %collective-permute-start.7 = (f32[576,256]{1,0:T(8,128)}, f32[576,256]{1,0:T(8,128)S(1)}, u32[]{:S(2)}, u32[]{:S(2)}) collective-permute-start(f32[576,256]{1,0:T(8,128)} %copy.185), channel_id=1, source_target_pairs={{8,0},{16,8},{24,16},{9,1},{17,9},{25,17},{10,2},{18,10},{26,18},{... | collective-permute-start | bytes 1769480 | tf_op jit(solution)/shard_map/ppermute | solution.py:24
  93.5 16.5 %collective-permute-start.6 = (f32[576,256]{1,0:T(8,128)}, f32[576,256]{1,0:T(8,128)S(1)}, u32[]{:S(2)}, u32[]{:S(2)}) collective-permute-start(f32[576,256]{1,0:T(8,128)} %copy.184), channel_id=1, source_target_pairs={{0,8},{8,16},{16,24},{1,9},{9,17},{17,25},{2,10},{10,18},{18,26},{... | collective-permute-start | bytes 1769480 | tf_op jit(solution)/shard_map/ppermute | solution.py:23
  107.4 26.9 %copy-start.56 = (pred[8,2]{0,1:T(4,128)(4,1)S(1)}, pred[8,2]{0,1:T(4,128)(4,1)}, u32[]{:S(2)}) copy-start(pred[8,2]{0,1:T(4,128)(4,1)} %get-tuple-element.114) | copy-start | bytes 52
  108.7 24.3 %copy-start.40 = (f32[576,256]{1,0:T(8,128)}, f32[576,256]{1,0:T(8,128)S(1)}, u32[]{:S(2)}) copy-start(f32[576,256]{1,0:T(8,128)S(1)} %collective-permute-done.7) | copy-start | bytes 1769476
  110.0 21.5 %copy-start.42 = (f32[576,256]{1,0:T(8,128)}, f32[576,256]{1,0:T(8,128)S(1)}, u32[]{:S(2)}) copy-start(f32[576,256]{1,0:T(8,128)S(1)} %collective-permute-done.6) | copy-start | bytes 1769476
  125.6 42.4 %all-to-all-start.2 = ((f32[8,2,4,48,256]{4,3,2,1,0:T(8,128)}), f32[8,2,4,48,256]{4,3,2,1,0:T(8,128)}, u32[]{:S(2)}, u32[]{:S(2)}) async-start(f32[8,2,4,48,256]{4,3,2,1,0:T(8,128)} %fusion.25), calls=%async_computation.2 | async-start | bytes 6291456 | tf_op jit(solution)/shard_map/all_to_all | solution.py:10
  131.5 14.5 %collective-permute-start.8 = (f32[576,256]{1,0:T(8,128)S(1)}, f32[576,256]{1,0:T(8,128)}, u32[]{:S(2)}, u32[]{:S(2)}) collective-permute-start(f32[576,256]{1,0:T(8,128)S(1)} %collective-permute-done.6), channel_id=1, source_target_pairs={{8,16},{16,24},{9,17},{17,25},{10,18},{18,26},{11,19},{19,27},{12,... | collective-permute-start | bytes 1769480 | tf_op jit(solution)/shard_map/ppermute | solution.py:23
  133.0 17.4 %collective-permute-start.9 = (f32[576,256]{1,0:T(8,128)S(1)}, f32[576,256]{1,0:T(8,128)}, u32[]{:S(2)}, u32[]{:S(2)}) collective-permute-start(f32[576,256]{1,0:T(8,128)S(1)} %collective-permute-done.7), channel_id=1, source_target_pairs={{8,0},{16,8},{9,1},{17,9},{10,2},{18,10},{11,3},{19,11},{12,4},{20... | collective-permute-start | bytes 1769480 | tf_op jit(solution)/shard_map/ppermute | solution.py:24
  168.0 41.5 %all-to-all-start.3 = ((f32[8,2,4,48,256]{4,3,2,1,0:T(8,128)}), f32[8,2,4,48,256]{4,3,2,1,0:T(8,128)S(1)}, u32[]{:S(2)}, u32[]{:S(2)}) async-start(f32[8,2,4,48,256]{4,3,2,1,0:T(8,128)} %fusion.24), calls=%async_computation.3 | async-start | bytes 6291456 | tf_op jit(solution)/shard_map/all_to_all | solution.py:10
  176.5 4.3 collective-permute-start.10
  177.2 17.6 %collective-permute-start.11 = (f32[576,256]{1,0:T(8,128)}, f32[576,256]{1,0:T(8,128)}, u32[]{:S(2)}, u32[]{:S(2)}) collective-permute-start(f32[576,256]{1,0:T(8,128)} %collective-permute-done.9), channel_id=1, source_target_pairs={{8,0},{9,1},{10,2},{11,3},{12,4},{13,5},{14,6},{15,7}} | collective-permute-start | bytes 1769480 | tf_op jit(solution)/shard_map/ppermute | solution.py:24
  221.9 10.6 %copy-start.48 = (s32[1024]{0:T(1024)S(1)}, s32[1024]{0:T(1024)}, u32[]{:S(2)}) copy-start(s32[1024]{0:T(1024)} %copy-done.47) | copy-start | bytes 12292
  221.9 42.5 %all-to-all-start.8 = ((f32[8,2,4,48,256]{4,3,2,1,0:T(8,128)}), f32[8,2,4,48,256]{4,3,2,1,0:T(8,128)}, u32[]{:S(2)}, u32[]{:S(2)}) async-start(f32[8,2,4,48,256]{4,3,2,1,0:T(8,128)} %fusion.21), calls=%async_computation.8 | async-start | bytes 6291456 | tf_op jit(solution)/shard_map/all_to_all | solution.py:10
  264.4 42.6 %all-to-all-start.6 = ((f32[8,2,4,48,256]{4,3,2,1,0:T(8,128)}), f32[8,2,4,48,256]{4,3,2,1,0:T(8,128)}, u32[]{:S(2)}, u32[]{:S(2)}) async-start(f32[8,2,4,48,256]{4,3,2,1,0:T(8,128)} %fusion.22), calls=%async_computation.6 | async-start | bytes 6291456 | tf_op jit(solution)/shard_map/all_to_all | solution.py:10
  306.9 44.7 %all-to-all-start.4 = ((f32[8,2,4,48,256]{4,3,2,1,0:T(8,128)}), f32[8,2,4,48,256]{4,3,2,1,0:T(8,128)}, u32[]{:S(2)}, u32[]{:S(2)}) async-start(f32[8,2,4,48,256]{4,3,2,1,0:T(8,128)} %fusion.23), calls=%async_computation.4 | async-start | bytes 6291456 | tf_op jit(solution)/shard_map/all_to_all | solution.py:10
  315.7 13.0 %copy-start.18 = (f32[1,4,8,48,256]{4,3,2,1,0:T(8,128)}, f32[1,4,8,48,256]{4,3,2,1,0:T(8,128)S(1)}, u32[]{:S(2)}) copy-start(f32[1,4,8,48,256]{4,3,2,1,0:T(8,128)S(1)} %copy.214) | copy-start | bytes 4718596
  315.8 12.9 %copy-start.16 = (f32[1,4,8,48,256]{4,3,2,1,0:T(8,128)}, f32[1,4,8,48,256]{4,3,2,1,0:T(8,128)S(1)}, u32[]{:S(2)}) copy-start(f32[1,4,8,48,256]{4,3,2,1,0:T(8,128)S(1)} %copy.213) | copy-start | bytes 4718596
  351.7 42.1 %all-to-all-start.9 = ((f32[8,2,4,48,256]{4,3,2,1,0:T(8,128)}), f32[8,2,4,48,256]{4,3,2,1,0:T(8,128)}, u32[]{:S(2)}, u32[]{:S(2)}) async-start(f32[8,2,4,48,256]{4,3,2,1,0:T(8,128)} %copy.216), calls=%async_computation.9 | async-start | bytes 6291456 | tf_op jit(solution)/shard_map/all_to_all | solution.py:10
  358.6 12.0 %copy-start.21 = (f32[1,4,8,48,256]{4,3,2,1,0:T(8,128)}, f32[1,4,8,48,256]{4,3,2,1,0:T(8,128)S(1)}, u32[]{:S(2)}) copy-start(f32[1,4,8,48,256]{4,3,2,1,0:T(8,128)S(1)} %copy.198) | copy-start | bytes 4718596
  358.7 11.8 %copy-start.23 = (f32[1,4,8,48,256]{4,3,2,1,0:T(8,128)}, f32[1,4,8,48,256]{4,3,2,1,0:T(8,128)S(1)}, u32[]{:S(2)}) copy-start(f32[1,4,8,48,256]{4,3,2,1,0:T(8,128)S(1)} %copy.197) | copy-start | bytes 4718596
  370.6 9.7 %copy-start.15 = (f32[1,4,8,48,256]{4,3,2,1,0:T(8,128)S(1)}, f32[1,4,8,48,256]{4,3,2,1,0:T(8,128)}, u32[]{:S(2)}) copy-start(f32[1,4,8,48,256]{4,3,2,1,0:T(8,128)} %copy-done.14) | copy-start | bytes 4718596
  393.8 41.8 %all-to-all-start.5 = ((f32[8,2,4,48,256]{4,3,2,1,0:T(8,128)}), f32[8,2,4,48,256]{4,3,2,1,0:T(8,128)}, u32[]{:S(2)}, u32[]{:S(2)}) async-start(f32[8,2,4,48,256]{4,3,2,1,0:T(8,128)} %copy.200), calls=%async_computation.5 | async-start | bytes 6291456 | tf_op jit(solution)/shard_map/all_to_all | solution.py:10
  401.1 11.4 %copy-start.20 = (f32[1,4,8,48,256]{4,3,2,1,0:T(8,128)}, f32[1,4,8,48,256]{4,3,2,1,0:T(8,128)S(1)}, u32[]{:S(2)}) copy-start(f32[1,4,8,48,256]{4,3,2,1,0:T(8,128)S(1)} %copy.206) | copy-start | bytes 4718596
  412.5 9.7 %copy-start.13 = (f32[1,4,8,48,256]{4,3,2,1,0:T(8,128)S(1)}, f32[1,4,8,48,256]{4,3,2,1,0:T(8,128)}, u32[]{:S(2)}) copy-start(f32[1,4,8,48,256]{4,3,2,1,0:T(8,128)} %copy-done.12) | copy-start | bytes 4718596
  422.2 7.0 copy-start.9
  435.6 42.0 %all-to-all-start.7 = ((f32[8,2,4,48,256]{4,3,2,1,0:T(8,128)}), f32[8,2,4,48,256]{4,3,2,1,0:T(8,128)}, u32[]{:S(2)}, u32[]{:S(2)}) async-start(f32[8,2,4,48,256]{4,3,2,1,0:T(8,128)} %copy.208), calls=%async_computation.7 | async-start | bytes 6291456 | tf_op jit(solution)/shard_map/all_to_all | solution.py:10
  462.7 18.8 %copy-start.46 = (s32[8,6]{0,1:T(8,128)S(1)}, s32[8,6]{0,1:T(8,128)}, u32[]{:S(2)}) copy-start(s32[8,6]{0,1:T(8,128)} %copy-done.45) | copy-start | bytes 580
  490.6 18.2 %slice-start.3 = ((s8[9437184]{0:T(1024)(128)(4,1)}), s8[1048576]{0:T(1024)(128)(4,1)S(1)}, s32[]{:S(2)}) async-start(s8[9437184]{0:T(1024)(128)(4,1)} %bitcast.330), calls=%async_computation.17 | async-start | bytes 2097152
  490.6 42.7 %all-to-all-start.10 = ((f32[8,2,4,48,256]{4,3,2,1,0:T(8,128)}), f32[8,2,4,48,256]{4,3,2,1,0:T(8,128)}, u32[]{:S(2)}, u32[]{:S(2)}) async-start(f32[8,2,4,48,256]{4,3,2,1,0:T(8,128)} %copy.222), calls=%async_computation.10 | async-start | bytes 6291456 | tf_op jit(solution)/shard_map/all_to_all | solution.py:10
  496.9 7.5 %copy-start.38 = (f32[12,48,256]{2,0,1:T(8,128)S(1)}, f32[12,48,256]{2,0,1:T(8,128)}, u32[]{:S(2)}) copy-start(f32[12,48,256]{2,0,1:T(8,128)} %get-tuple-element.60) | copy-start | bytes 1769476
  496.9 7.9 %copy-start.37 = (f32[12,48,256]{2,0,1:T(8,128)S(1)}, f32[12,48,256]{2,0,1:T(8,128)}, u32[]{:S(2)}) copy-start(f32[12,48,256]{2,0,1:T(8,128)} %get-tuple-element.61) | copy-start | bytes 1769476
  496.9 12.0 %slice-start.4 = ((s8[9437184]{0:T(1024)(128)(4,1)}), s8[4194304]{0:T(1024)(128)(4,1)S(1)}, s32[]{:S(2)}) async-start(s8[9437184]{0:T(1024)(128)(4,1)} %bitcast.330), calls=%async_computation.18 | async-start | bytes 8388608
  496.9 12.0 %slice-start.5 = ((s8[9437184]{0:T(1024)(128)(4,1)}), s8[4194304]{0:T(1024)(128)(4,1)S(1)}, s32[]{:S(2)}) async-start(s8[9437184]{0:T(1024)(128)(4,1)} %bitcast.330), calls=%async_computation.19 | async-start | bytes 8388608
  505.1 9.9 %collective-permute-start.13 = (f32[12,48,256]{2,1,0:T(8,128)S(1)}, f32[12,48,256]{2,1,0:T(8,128)}, u32[]{:S(2)}, u32[]{:S(2)}) collective-permute-start(f32[12,48,256]{2,1,0:T(8,128)S(1)} %copy.221), channel_id=1, source_target_pairs={{24,16},{25,17},{26,18},{27,19},{28,20},{29,21},{30,22},{31,23}} | collective-permute-start | bytes 1769480 | tf_op jit(solution)/shard_map/ppermute | solution.py:52
  506.6 14.4 %collective-permute-start.12 = (f32[12,48,256]{2,1,0:T(8,128)S(1)}, f32[12,48,256]{2,1,0:T(8,128)}, u32[]{:S(2)}, u32[]{:S(2)}) collective-permute-start(f32[12,48,256]{2,1,0:T(8,128)S(1)} %copy.220), channel_id=1, source_target_pairs={{0,8},{1,9},{2,10},{3,11},{4,12},{5,13},{6,14},{7,15}} | collective-permute-start | bytes 1769480 | tf_op jit(solution)/shard_map/ppermute | solution.py:51
  512.9 20.4 %copy-start.5 = (f32[4,48,256,12]{2,3,1,0:T(8,128)S(1)}, f32[4,48,256,12]{2,3,1,0:T(8,128)}, u32[]{:S(2)}) copy-start(f32[4,48,256,12]{2,3,1,0:T(8,128)} %copy-done.4) | copy-start | bytes 7077892
  538.6 17.6 %slice-start = ((s8[9437184]{0:T(1024)(128)(4,1)}), s8[1048576]{0:T(1024)(128)(4,1)S(1)}, s32[]{:S(2)}) async-start(s8[9437184]{0:T(1024)(128)(4,1)} %bitcast.326), calls=%async_computation.14 | async-start | bytes 2097152
  538.6 42.6 %all-to-all-start.11 = ((f32[8,2,4,48,256]{4,3,2,1,0:T(8,128)}), f32[8,2,4,48,256]{4,3,2,1,0:T(8,128)}, u32[]{:S(2)}, u32[]{:S(2)}) async-start(f32[8,2,4,48,256]{4,3,2,1,0:T(8,128)} %copy.227), calls=%async_computation.11 | async-start | bytes 6291456 | tf_op jit(solution)/shard_map/all_to_all | solution.py:10
  544.7 7.0 copy-start.36
  544.7 7.4 %copy-start.35 = (f32[12,48,256]{2,0,1:T(8,128)S(1)}, f32[12,48,256]{2,0,1:T(8,128)}, u32[]{:S(2)}) copy-start(f32[12,48,256]{2,0,1:T(8,128)} %get-tuple-element.66) | copy-start | bytes 1769476
  544.7 11.5 %slice-start.1 = ((s8[9437184]{0:T(1024)(128)(4,1)}), s8[4194304]{0:T(1024)(128)(4,1)S(1)}, s32[]{:S(2)}) async-start(s8[9437184]{0:T(1024)(128)(4,1)} %bitcast.326), calls=%async_computation.15 | async-start | bytes 8388608
  544.8 11.5 %slice-start.2 = ((s8[9437184]{0:T(1024)(128)(4,1)}), s8[4194304]{0:T(1024)(128)(4,1)S(1)}, s32[]{:S(2)}) async-start(s8[9437184]{0:T(1024)(128)(4,1)} %bitcast.326), calls=%async_computation.16 | async-start | bytes 8388608
  552.5 9.9 %collective-permute-start.15 = (f32[12,48,256]{2,1,0:T(8,128)S(1)}, f32[12,48,256]{2,1,0:T(8,128)}, u32[]{:S(2)}, u32[]{:S(2)}) collective-permute-start(f32[12,48,256]{2,1,0:T(8,128)S(1)} %copy.226), channel_id=1, source_target_pairs={{16,8},{24,16},{17,9},{25,17},{18,10},{26,18},{19,11},{27,19},{20,... | collective-permute-start | bytes 1769480 | tf_op jit(solution)/shard_map/ppermute | solution.py:52
  554.0 14.4 %collective-permute-start.14 = (f32[12,48,256]{2,1,0:T(8,128)S(1)}, f32[12,48,256]{2,1,0:T(8,128)}, u32[]{:S(2)}, u32[]{:S(2)}) collective-permute-start(f32[12,48,256]{2,1,0:T(8,128)S(1)} %copy.225), channel_id=1, source_target_pairs={{0,8},{8,16},{1,9},{9,17},{2,10},{10,18},{3,11},{11,19},{4,12},{12... | collective-permute-start | bytes 1769480 | tf_op jit(solution)/shard_map/ppermute | solution.py:51
  560.4 20.9 %copy-start.6 = (f32[4,48,256,12]{2,3,1,0:T(8,128)S(1)}, f32[4,48,256,12]{2,3,1,0:T(8,128)}, u32[]{:S(2)}) copy-start(f32[4,48,256,12]{2,3,1,0:T(8,128)} %copy-done.4) | copy-start | bytes 7077892
  586.5 42.4 %all-to-all-start.12 = ((f32[8,2,4,48,256]{4,3,2,1,0:T(8,128)}), f32[8,2,4,48,256]{4,3,2,1,0:T(8,128)}, u32[]{:S(2)}, u32[]{:S(2)}) async-start(f32[8,2,4,48,256]{4,3,2,1,0:T(8,128)} %copy.232), calls=%async_computation.12 | async-start | bytes 6291456 | tf_op jit(solution)/shard_map/all_to_all | solution.py:10
  595.3 17.5 %collective-permute-start.17 = (f32[12,48,256]{2,1,0:T(8,128)S(1)}, f32[12,48,256]{2,1,0:T(8,128)}, u32[]{:S(2)}, u32[]{:S(2)}) collective-permute-start(f32[12,48,256]{2,1,0:T(8,128)S(1)} %copy.231), channel_id=1, source_target_pairs={{8,0},{16,8},{24,16},{9,1},{17,9},{25,17},{10,2},{18,10},{26,18},{... | collective-permute-start | bytes 1769480 | tf_op jit(solution)/shard_map/ppermute | solution.py:52
  596.6 17.2 %collective-permute-start.16 = (f32[12,48,256]{2,1,0:T(8,128)S(1)}, f32[12,48,256]{2,1,0:T(8,128)}, u32[]{:S(2)}, u32[]{:S(2)}) collective-permute-start(f32[12,48,256]{2,1,0:T(8,128)S(1)} %copy.230), channel_id=1, source_target_pairs={{0,8},{8,16},{16,24},{1,9},{9,17},{17,25},{2,10},{10,18},{18,26},{... | collective-permute-start | bytes 1769480 | tf_op jit(solution)/shard_map/ppermute | solution.py:51
  638.2 14.4 %collective-permute-start.18 = (f32[12,48,256]{2,1,0:T(8,128)S(1)}, f32[12,48,256]{2,1,0:T(8,128)S(1)}, u32[]{:S(2)}, u32[]{:S(2)}) collective-permute-start(f32[12,48,256]{2,1,0:T(8,128)S(1)} %copy.238), channel_id=1, source_target_pairs={{0,8},{1,9},{2,10},{3,11},{4,12},{5,13},{6,14},{7,15}} | collective-permute-start | bytes 1769480 | tf_op jit(solution)/shard_map/ppermute | solution.py:51
  640.1 17.3 %collective-permute-start.21 = (f32[12,48,256]{2,1,0:T(8,128)S(1)}, f32[12,48,256]{2,1,0:T(8,128)S(1)}, u32[]{:S(2)}, u32[]{:S(2)}) collective-permute-start(f32[12,48,256]{2,1,0:T(8,128)S(1)} %copy.242), channel_id=1, source_target_pairs={{24,16},{25,17},{26,18},{27,19},{28,20},{29,21},{30,22},{31,23}} | collective-permute-start | bytes 1769480 | tf_op jit(solution)/shard_map/ppermute | solution.py:52
  653.0 16.5 %collective-permute-start.19 = (f32[12,48,256]{2,1,0:T(8,128)S(1)}, f32[12,48,256]{2,1,0:T(8,128)S(1)}, u32[]{:S(2)}, u32[]{:S(2)}) collective-permute-start(f32[12,48,256]{2,1,0:T(8,128)S(1)} %fusion.38), channel_id=1, source_target_pairs={{0,8},{8,16},{1,9},{9,17},{2,10},{10,18},{3,11},{11,19},{4,12},{12... | collective-permute-start | bytes 1769480 | tf_op jit(solution)/shard_map/ppermute | solution.py:51
  657.8 18.1 %collective-permute-start.22 = (f32[12,48,256]{2,1,0:T(8,128)S(1)}, f32[12,48,256]{2,1,0:T(8,128)S(1)}, u32[]{:S(2)}, u32[]{:S(2)}) collective-permute-start(f32[12,48,256]{2,1,0:T(8,128)S(1)} %fusion.36), channel_id=1, source_target_pairs={{16,8},{24,16},{17,9},{25,17},{18,10},{26,18},{19,11},{27,19},{20,... | collective-permute-start | bytes 1769480 | tf_op jit(solution)/shard_map/ppermute | solution.py:52
  670.6 15.9 %collective-permute-start.20 = (f32[12,48,256]{2,1,0:T(8,128)}, f32[12,48,256]{2,1,0:T(8,128)}, u32[]{:S(2)}, u32[]{:S(2)}) collective-permute-start(f32[12,48,256]{2,1,0:T(8,128)} %fusion.37), channel_id=1, source_target_pairs={{0,8},{8,16},{16,24},{1,9},{9,17},{17,25},{2,10},{10,18},{18,26},{... | collective-permute-start | bytes 1769480 | tf_op jit(solution)/shard_map/ppermute | solution.py:51
  677.0 15.6 %collective-permute-start.23 = (f32[12,48,256]{2,1,0:T(8,128)}, f32[12,48,256]{2,1,0:T(8,128)}, u32[]{:S(2)}, u32[]{:S(2)}) collective-permute-start(f32[12,48,256]{2,1,0:T(8,128)} %fusion.35), channel_id=1, source_target_pairs={{8,0},{16,8},{24,16},{9,1},{17,9},{25,17},{10,2},{18,10},{26,18},{... | collective-permute-start | bytes 1769480 | tf_op jit(solution)/shard_map/ppermute | solution.py:52
  (36 other events, 138.9 us)

commit v9 on v8

--- a/solution.py
+++ b/solution.py
@@ -67,7 +67,13 @@
     piece_rows = blk // devices
     slot_count = coulomb.shape[0]
     block_count = orbitals.shape[0] // (band_count * piece_rows)
-    own_rows = lax.all_to_all(orbitals, "band", split_axis=0, concat_axis=1, tiled=True)
+    col_half = orbitals.shape[1] // 2
+    own_rows = [
+        lax.all_to_all(
+            orbitals[:, h * col_half : (h + 1) * col_half], "band", split_axis=0, concat_axis=1, tiled=True
+        )
+        for h in range(2)
+    ]
     group_index = lax.axis_index("grp")
     band_index = lax.axis_index("band")
     group_requests = lax.dynamic_slice_in_dim(requests, group_index * band_count, band_count, 0)
@@ -86,9 +92,9 @@
     def shape_pieces(gathered):
         return gathered.reshape(group_count, block_count, piece_rows, half)
 
-    first_pieces = shape_pieces(line_gather(own_rows[:, :half], "grp", group_count)[0])
+    first_pieces = shape_pieces(line_gather(own_rows[0], "grp", group_count)[0])
     first_loads = [requested(first_pieces, slot) for slot in range(slot_count)]
-    second_pieces, first_arrived = line_gather(own_rows[:, half:], "grp", group_count, first_loads)
+    second_pieces, first_arrived = line_gather(own_rows[1], "grp", group_count, first_loads)
     second_pieces = shape_pieces(second_pieces)
     second_arrived = [band_exchange(requested(second_pieces, slot)) for slot in range(slot_count)]
     returned = [[], []]
@@ -121,10 +127,13 @@
 
     first_home, second_returned = line_reduce(sum_blocks(returned[0]), "grp", group_count, held)
     second_home, _ = line_reduce(sum_blocks(second_returned), "grp", group_count)
-    home_rows = jnp.concatenate([first_home, second_home], axis=-1).reshape(
-        block_count * piece_rows, orbital_width
-    )
-    return lax.all_to_all(home_rows, "band", split_axis=1, concat_axis=0, tiled=True)
+    home = [
+        lax.all_to_all(
+            rows.reshape(block_count * piece_rows, half), "band", split_axis=1, concat_axis=0, tiled=True
+        )
+        for rows in (first_home, second_home)
+    ]
+    return jnp.concatenate(home, axis=1)
 
 
 def solution(mesh):

time: 733 us -> 723 us (0.986)
  blocking collectives: 40.8 us -> 13.7 us
  starting transfers between devices: 116 us -> 129 us
    all_to_all x2 -> x1, blocking collectives: 40.8 us -> 13.7 us  [body(): lax.all_to_all(orbitals[:, h * col_half:(h + 1) * col_half], 'band', spli...]
    all_to_all x0 -> x3, starting transfers between devices: none -> 12.6 us  [the longest x2 7.69 us: body(): lax.all_to_all(rows.reshape(block_count * piece_rows, half), 'band', spli...]
    all_to_all x0 -> x3, waiting for transfers between devices: none -> 8.06 us  [the longest x2 8.06 us: body(): lax.all_to_all(rows.reshape(block_count * piece_rows, half), 'band', spli...]
    ppermute x6, waiting for transfers between devices: 41.8 us -> 34.4 us  [line_reduce(): lax.ppermute(send_right, axis, [(i, i + 1) for i in range(0, step)])]
  transfers between devices with their start and end apart: 36 -> 39, of which waited for: 24 -> 23; matrix products, arithmetic and copies ran while one was open for 35% -> 38% of each run, Pallas kernels for 0% -> 0%
where the time goes in v9:
time: 723 us; the launch traced here: 710 us
  waiting for transfers between devices  229 us (32%)
  local copies, waits for them, and re-layouts  155 us (21%)
  starting transfers between devices  129 us (18%)
  matrix products  129 us (18%)
  other arithmetic  48.3 us (7%)
  blocking collectives  13.7 us (2%)
    all_to_all x12, waiting for transfers between devices, band_exchange(): lax.all_to_all(outgoing, 'band', split_axis=0, concat_axis=0, tiled=True)  125 us
    all_to_all x12, starting transfers between devices, band_exchange(): lax.all_to_all(outgoing, 'band', split_axis=0, concat_axis=0, tiled=True)  67.3 us
    ppermute x6, waiting for transfers between devices, line_gather(): lax.ppermute(leftward, axis, [(i + 1, i) for i in range(0, count - step)])  53.1 us
    dot_general x6, matrix products, body(): jnp.dot(r[0], r[1].T, precision=PRECISION, preferred_element_type=jnp.flo...  52.4 us
    dot_general x6, matrix products, body(): jnp.dot(kernel, rows[h][1], precision=PRECISION, preferred_element_type=j...  42.2 us
    ppermute x6, waiting for transfers between devices, line_reduce(): lax.ppermute(send_right, axis, [(i, i + 1) for i in range(0, step)])  34.4 us
    dot_general x3, local copies, waits for them, and re-layouts, body(): jnp.dot(kernel.T, rows[h][0], precision=PRECISION, preferred_element_type...  29.2 us
    dot_general x6, matrix products, body(): jnp.dot(kernel.T, rows[h][0], precision=PRECISION, preferred_element_type...  27.5 us
  transfers between devices with their start and end apart: 39, of which 23 were waited for; matrix products, arithmetic and copies ran while one was open for 38% of the time, Pallas kernels for 0%

profile of v9, /device:TPU:2, one launch (start us, length us, event | category | flops | bytes accessed | tf_op | source)
XLA Modules:
  0.0 710.3 jit_solution(11833351102165132574)
XLA Ops:
  1.7 13.7 %all_to_all.136 = f32[8,576,32]{1,2,0:T(8,128)S(1)} all-to-all(f32[8,576,32]{1,2,0:T(8,128)S(1)} %copy.186), channel_id=1, replica_groups=mesh['grp'=4,'band'=8] {'band'}, dimensions={0} | all-to-all | bytes 1179648 | tf_op jit(solution)/shard_map/all_to_all | solution.py:72
  16.5 4.3 collective-permute-start
  22.0 4.9 all-to-all-start
  35.4 9.0 %collective-permute-done.1 = f32[576,256]{1,0:T(8,128)S(1)} collective-permute-done((f32[576,256]{1,0:T(8,128)}, f32[576,256]{1,0:T(8,128)S(1)}, u32[]{:S(2)}, u32[]{:S(2)}) %collective-permute-start.1) | collective-permute-done | bytes 589856 | tf_op jit(solution)/shard_map/ppermute | solution.py:24
  47.9 12.9 %collective-permute-done.3 = f32[576,256]{1,0:T(8,128)S(1)} collective-permute-done((f32[576,256]{1,0:T(8,128)S(1)}, f32[576,256]{1,0:T(8,128)S(1)}, u32[]{:S(2)}, u32[]{:S(2)}) %collective-permute-start.3) | collective-permute-done | bytes 589856 | tf_op jit(solution)/shard_map/ppermute | solution.py:24
  63.4 13.0 %collective-permute-done.5 = f32[576,256]{1,0:T(8,128)S(1)} collective-permute-done((f32[576,256]{1,0:T(8,128)S(1)}, f32[576,256]{1,0:T(8,128)S(1)}, u32[]{:S(2)}, u32[]{:S(2)}) %collective-permute-start.5) | collective-permute-done | bytes 589856 | tf_op jit(solution)/shard_map/ppermute | solution.py:24
  83.0 5.2 all-to-all-start.2
  91.6 4.6 collective-permute-start.6
  101.3 4.1 fusion.25
  109.1 15.6 %all-to-all-done.2 = f32[8,2,4,48,256]{4,3,2,1,0:T(8,128)} async-done(((f32[8,2,4,48,256]{4,3,2,1,0:T(8,128)}), f32[8,2,4,48,256]{4,3,2,1,0:T(8,128)}, u32[]{:S(2)}, u32[]{:S(2)}) %all-to-all-start.2) | async-done | bytes 3145760 | tf_op jit(solution)/shard_map/all_to_all | solution.py:10
  124.7 5.9 all-to-all-start.3
  141.2 4.1 fusion.24
  145.3 4.1 collective-permute-done.9
  149.4 17.6 %all-to-all-done.3 = f32[8,2,4,48,256]{4,3,2,1,0:T(8,128)} async-done(((f32[8,2,4,48,256]{4,3,2,1,0:T(8,128)}), f32[8,2,4,48,256]{4,3,2,1,0:T(8,128)}, u32[]{:S(2)}, u32[]{:S(2)}) %all-to-all-start.3) | async-done | bytes 3145760 | tf_op jit(solution)/shard_map/all_to_all | solution.py:10
  167.1 5.1 all-to-all-start.4
  182.3 11.6 %collective-permute-done.11 = f32[576,256]{1,0:T(8,128)} collective-permute-done((f32[576,256]{1,0:T(8,128)}, f32[576,256]{1,0:T(8,128)}, u32[]{:S(2)}, u32[]{:S(2)}) %collective-permute-start.11) | collective-permute-done | bytes 589856 | tf_op jit(solution)/shard_map/ppermute | solution.py:24
  193.9 14.6 %all-to-all-done.4 = f32[8,2,4,48,256]{4,3,2,1,0:T(8,128)S(1)} async-done(((f32[8,2,4,48,256]{4,3,2,1,0:T(8,128)}), f32[8,2,4,48,256]{4,3,2,1,0:T(8,128)S(1)}, u32[]{:S(2)}, u32[]{:S(2)}) %all-to-all-start.4) | async-done | bytes 3145760 | tf_op jit(solution)/shard_map/all_to_all | solution.py:10
  217.1 4.1 fusion.21
  221.1 6.0 all-to-all-start.9
  234.1 4.1 fusion.22
  238.2 25.4 %all-to-all-done.9 = f32[8,2,4,48,256]{4,3,2,1,0:T(8,128)} async-done(((f32[8,2,4,48,256]{4,3,2,1,0:T(8,128)}), f32[8,2,4,48,256]{4,3,2,1,0:T(8,128)}, u32[]{:S(2)}, u32[]{:S(2)}) %all-to-all-start.9) | async-done | bytes 3145760 | tf_op jit(solution)/shard_map/all_to_all | solution.py:10
  263.6 6.2 all-to-all-start.7
  272.2 6.5 fusion.57
  282.7 6.5 fusion.58
  297.7 6.6 fusion.59
  306.2 6.4 all-to-all-start.5
  318.4 9.6 %fusion = f32[1536,1536]{1,0:T(8,128)} fusion(f32[1536,1536]{1,0:T(8,128)S(1)} %copy-done.3, f32[1536,256]{1,0:T(8,128)S(1)} %bitcast.365, f32[1536,256]{1,0:T(8,128)S(1)} %bitcast.367, f32[3,1536,1536]{2,1,0:T(8,128)} %param.7), kind=kOutput, calls=%fused_computation.7 | convolution fusion | flops 3628597248 | bytes 31457280 | tf_op jit(solution)/shard_map/dot_general | solution.py:108
  328.0 9.6 %copy.223 = f32[1536,1536]{1,0:T(8,128)} copy(f32[1536,1536]{0,1:T(8,128)} %bitcast.328) | data formatting | bytes 18874368 | tf_op jit(solution)/shard_map/dot_general | solution.py:114
  337.6 6.9 convolution_bitcast_fusion.7
  351.0 4.6 all-to-all-start.10
  358.1 11.9 %fusion.2 = f32[1536,1536]{1,0:T(8,128)} fusion(f32[1536,1536]{1,0:T(8,128)} %fusion.57, f32[1536,256]{1,0:T(8,128)S(1)} %bitcast.375, f32[1536,256]{1,0:T(8,128)S(1)} %bitcast.373, f32[3,1536,1536]{2,1,0:T(8,128)} %param.7), kind=kOutput, calls=%fused_computation.11 | convolution fusion | flops 3628597248 | bytes 31457280 | tf_op jit(solution)/shard_map/dot_general | solution.py:108
  370.0 9.7 %copy.207 = f32[1536,1536]{1,0:T(8,128)} copy(f32[1536,1536]{0,1:T(8,128)} %bitcast.334) | data formatting | bytes 18874368 | tf_op jit(solution)/shard_map/dot_general | solution.py:114
  379.7 7.0 convolution_bitcast_fusion.11
  393.0 5.1 all-to-all-start.6
  400.6 11.4 %fusion.1 = f32[1536,1536]{1,0:T(8,128)} fusion(f32[1536,1536]{1,0:T(8,128)} %fusion.58, f32[1536,256]{1,0:T(8,128)S(1)} %bitcast.369, f32[1536,256]{1,0:T(8,128)S(1)} %bitcast.371, f32[3,1536,1536]{2,1,0:T(8,128)} %param.7), kind=kOutput, calls=%fused_computation.9 | convolution fusion | flops 3628597248 | bytes 31457280 | tf_op jit(solution)/shard_map/dot_general | solution.py:108
  411.9 9.8 %copy.215 = f32[1536,1536]{1,0:T(8,128)} copy(f32[1536,1536]{0,1:T(8,128)} %bitcast.331) | data formatting | bytes 18874368 | tf_op jit(solution)/shard_map/dot_general | solution.py:114
  421.8 7.0 convolution_bitcast_fusion.9
  435.1 5.4 all-to-all-start.8
  440.5 6.9 convolution_bitcast_fusion.5
  447.4 7.3 %convolution_bitcast_fusion.4 = f32[1,4,8,48,256]{4,3,2,1,0:T(8,128)S(1)} fusion(f32[4,8,48,1536]{3,2,1,0:T(8,128)} %bitcast.345, f32[1536,256,1,1]{1,0,3,2:T(8,128)S(1)} %bitcast.376), kind=kOutput, calls=%fused_computation.54 | convolution fusion | flops 3623878656 | bytes 12582912 | tf_op jit(solution)/shard_map/dot_general | solution.py:114
  456.7 5.3 copy.227
  462.1 5.3 copy.225
  467.4 9.6 %all-to-all-done.8 = f32[8,2,4,48,256]{4,3,2,1,0:T(8,128)} async-done(((f32[8,2,4,48,256]{4,3,2,1,0:T(8,128)}), f32[8,2,4,48,256]{4,3,2,1,0:T(8,128)}, u32[]{:S(2)}, u32[]{:S(2)}) %all-to-all-start.8) | async-done | bytes 3145760 | tf_op jit(solution)/shard_map/all_to_all | solution.py:10
  490.2 6.2 all-to-all-start.11
  496.5 7.4 %convolution_bitcast_fusion.3 = f32[1,4,8,48,256]{4,3,2,1,0:T(8,128)S(1)} fusion(f32[4,8,48,1536]{3,2,1,0:T(8,128)} %bitcast.333, f32[1536,256,1,1]{1,0,3,2:T(8,128)} %bitcast.372), kind=kOutput, calls=%fused_computation.53 | convolution fusion | flops 3623878656 | bytes 12582912 | tf_op jit(solution)/shard_map/dot_general | solution.py:113
  514.5 6.1 collective-permute-done.12
  520.6 12.2 %all-to-all-done.11 = f32[8,2,4,48,256]{4,3,2,1,0:T(8,128)} async-done(((f32[8,2,4,48,256]{4,3,2,1,0:T(8,128)}), f32[8,2,4,48,256]{4,3,2,1,0:T(8,128)}, u32[]{:S(2)}, u32[]{:S(2)}) %all-to-all-start.11) | async-done | bytes 3145760 | tf_op jit(solution)/shard_map/all_to_all | solution.py:10
  538.2 6.1 all-to-all-start.12
  544.3 7.0 convolution_bitcast_fusion.1
  555.9 4.1 convolution_bitcast_fusion
  562.1 5.9 collective-permute-done.14
  568.0 12.8 %all-to-all-done.12 = f32[8,2,4,48,256]{4,3,2,1,0:T(8,128)} async-done(((f32[8,2,4,48,256]{4,3,2,1,0:T(8,128)}), f32[8,2,4,48,256]{4,3,2,1,0:T(8,128)}, u32[]{:S(2)}, u32[]{:S(2)}) %all-to-all-start.12) | async-done | bytes 3145760 | tf_op jit(solution)/shard_map/all_to_all | solution.py:10
  586.1 5.1 all-to-all-start.13
  595.4 5.4 collective-permute-start.16
  600.8 5.5 copy.244
  606.3 5.4 copy.245
  612.6 15.0 %all-to-all-done.13 = f32[8,2,4,48,256]{4,3,2,1,0:T(8,128)S(1)} async-done(((f32[8,2,4,48,256]{4,3,2,1,0:T(8,128)}), f32[8,2,4,48,256]{4,3,2,1,0:T(8,128)S(1)}, u32[]{:S(2)}, u32[]{:S(2)}) %all-to-all-start.13) | async-done | bytes 3145760 | tf_op jit(solution)/shard_map/all_to_all | solution.py:10
  637.4 11.8 %collective-permute-done.18 = f32[12,48,256]{2,1,0:T(8,128)S(1)} collective-permute-done((f32[12,48,256]{2,1,0:T(8,128)S(1)}, f32[12,48,256]{2,1,0:T(8,128)S(1)}, u32[]{:S(2)}, u32[]{:S(2)}) %collective-permute-start.18) | collective-permute-done | bytes 589856 | tf_op jit(solution)/shard_map/ppermute | solution.py:51
  649.6 5.0 collective-permute-start.19
  655.7 10.6 %collective-permute-done.19 = f32[12,48,256]{2,1,0:T(8,128)S(1)} collective-permute-done((f32[12,48,256]{2,1,0:T(8,128)S(1)}, f32[12,48,256]{2,1,0:T(8,128)S(1)}, u32[]{:S(2)}, u32[]{:S(2)}) %collective-permute-start.19) | collective-permute-done | bytes 589856 | tf_op jit(solution)/shard_map/ppermute | solution.py:51
  667.5 5.2 collective-permute-start.20
  680.7 4.1 all-to-all-start.14
  684.9 4.5 collective-permute-done.23
  700.4 8.1 %all-to-all-done.15 = f32[576,8,32]{0,2,1:T(8,128)S(1)} async-done(((f32[576,8,32]{0,2,1:T(8,128)}), f32[576,8,32]{0,2,1:T(8,128)S(1)}, u32[]{:S(2)}, u32[]{:S(2)}) %all-to-all-start.15) | async-done | bytes 589856 | tf_op jit(solution)/shard_map/all_to_all | solution.py:131
  (298 shorter events, 197.0 us)
Async XLA Ops:
  1.7 25.2 %copy-start.53 = (s32[32,6]{0,1:T(8,128)S(1)}, s32[32,6]{0,1:T(8,128)}, u32[]{:S(2)}) copy-start(s32[32,6]{0,1:T(8,128)} %param.6) | copy-start | bytes 2308
  16.5 16.3 %collective-permute-start = (f32[576,256]{1,0:T(8,128)}, f32[576,256]{1,0:T(8,128)}, u32[]{:S(2)}, u32[]{:S(2)}) collective-permute-start(f32[576,256]{1,0:T(8,128)} %copy.188), channel_id=1, source_target_pairs={{0,8},{8,16},{16,24},{1,9},{9,17},{17,25},{2,10},{10,18},{18,26},{... | collective-permute-start | bytes 1769480 | tf_op jit(solution)/shard_map/ppermute | solution.py:23
  22.0 61.1 %all-to-all-start = ((f32[8,576,32]{1,2,0:T(8,128)}), f32[8,576,32]{1,2,0:T(8,128)S(1)}, u32[]{:S(2)}, u32[]{:S(2)}) async-start(f32[8,576,32]{1,2,0:T(8,128)} %copy.184), calls=%async_computation | async-start | bytes 1310720 | tf_op jit(solution)/shard_map/all_to_all | solution.py:72
  26.9 20.2 %copy-start.48 = (s32[8,6]{0,1:T(8,128)}, s32[8,6]{0,1:T(8,128)S(1)}, u32[]{:S(2)}) copy-start(s32[8,6]{0,1:T(8,128)S(1)} %get-tuple-element.79) | copy-start | bytes 580
  26.9 17.5 %collective-permute-start.1 = (f32[576,256]{1,0:T(8,128)}, f32[576,256]{1,0:T(8,128)S(1)}, u32[]{:S(2)}, u32[]{:S(2)}) collective-permute-start(f32[576,256]{1,0:T(8,128)} %copy.188), channel_id=1, source_target_pairs={{8,0},{16,8},{24,16},{9,1},{17,9},{25,17},{10,2},{18,10},{26,18},{... | collective-permute-start | bytes 1769480 | tf_op jit(solution)/shard_map/ppermute | solution.py:24
  32.8 14.4 %collective-permute-start.2 = (f32[576,256]{1,0:T(8,128)}, f32[576,256]{1,0:T(8,128)}, u32[]{:S(2)}, u32[]{:S(2)}) collective-permute-start(f32[576,256]{1,0:T(8,128)} %collective-permute-done), channel_id=1, source_target_pairs={{8,16},{16,24},{9,17},{17,25},{10,18},{18,26},{11,19},{19,27},{12,... | collective-permute-start | bytes 1769480 | tf_op jit(solution)/shard_map/ppermute | solution.py:23
  35.0 44.1 %copy-start.55 = (pred[8,2]{1,0:T(8,128)(4,1)}, pred[8,2]{1,0:T(8,128)(4,1)S(1)}, u32[]{:S(2)}) copy-start(pred[8,2]{1,0:T(8,128)(4,1)S(1)} %copy.185) | copy-start | bytes 52
  44.4 16.4 %collective-permute-start.3 = (f32[576,256]{1,0:T(8,128)S(1)}, f32[576,256]{1,0:T(8,128)S(1)}, u32[]{:S(2)}, u32[]{:S(2)}) collective-permute-start(f32[576,256]{1,0:T(8,128)S(1)} %collective-permute-done.1), channel_id=1, source_target_pairs={{8,0},{16,8},{9,1},{17,9},{10,2},{18,10},{11,3},{19,11},{12,4},{20... | collective-permute-start | bytes 1769480 | tf_op jit(solution)/shard_map/ppermute | solution.py:24
  47.2 16.2 %collective-permute-start.4 = (f32[576,256]{1,0:T(8,128)}, f32[576,256]{1,0:T(8,128)S(1)}, u32[]{:S(2)}, u32[]{:S(2)}) collective-permute-start(f32[576,256]{1,0:T(8,128)} %collective-permute-done.2), channel_id=1, source_target_pairs={{16,24},{17,25},{18,26},{19,27},{20,28},{21,29},{22,30},{23,31}} | collective-permute-start | bytes 1769480 | tf_op jit(solution)/shard_map/ppermute | solution.py:23
  60.9 15.5 %collective-permute-start.5 = (f32[576,256]{1,0:T(8,128)S(1)}, f32[576,256]{1,0:T(8,128)S(1)}, u32[]{:S(2)}, u32[]{:S(2)}) collective-permute-start(f32[576,256]{1,0:T(8,128)S(1)} %collective-permute-done.3), channel_id=1, source_target_pairs={{8,0},{9,1},{10,2},{11,3},{12,4},{13,5},{14,6},{15,7}} | collective-permute-start | bytes 1769480 | tf_op jit(solution)/shard_map/ppermute | solution.py:24
  83.0 13.2 %copy-start.60 = (pred[8,2]{0,1:T(4,128)(4,1)S(1)}, pred[8,2]{0,1:T(4,128)(4,1)}, u32[]{:S(2)}) copy-start(pred[8,2]{0,1:T(4,128)(4,1)} %get-tuple-element.115) | copy-start | bytes 52
  83.0 41.7 %all-to-all-start.2 = ((f32[8,2,4,48,256]{4,3,2,1,0:T(8,128)}), f32[8,2,4,48,256]{4,3,2,1,0:T(8,128)}, u32[]{:S(2)}, u32[]{:S(2)}) async-start(f32[8,2,4,48,256]{4,3,2,1,0:T(8,128)} %fusion.26), calls=%async_computation.2 | async-start | bytes 6291456 | tf_op jit(solution)/shard_map/all_to_all | solution.py:10
  90.3 17.5 %collective-permute-start.7 = (f32[576,256]{1,0:T(8,128)}, f32[576,256]{1,0:T(8,128)S(1)}, u32[]{:S(2)}, u32[]{:S(2)}) collective-permute-start(f32[576,256]{1,0:T(8,128)} %copy.193), channel_id=1, source_target_pairs={{8,0},{16,8},{24,16},{9,1},{17,9},{25,17},{10,2},{18,10},{26,18},{... | collective-permute-start | bytes 1769480 | tf_op jit(solution)/shard_map/ppermute | solution.py:24
  91.6 17.5 %collective-permute-start.6 = (f32[576,256]{1,0:T(8,128)}, f32[576,256]{1,0:T(8,128)S(1)}, u32[]{:S(2)}, u32[]{:S(2)}) collective-permute-start(f32[576,256]{1,0:T(8,128)} %copy.192), channel_id=1, source_target_pairs={{0,8},{8,16},{16,24},{1,9},{9,17},{17,25},{2,10},{10,18},{18,26},{... | collective-permute-start | bytes 1769480 | tf_op jit(solution)/shard_map/ppermute | solution.py:23
  105.4 28.0 %copy-start.59 = (pred[8,2]{0,1:T(4,128)(4,1)S(1)}, pred[8,2]{0,1:T(4,128)(4,1)}, u32[]{:S(2)}) copy-start(pred[8,2]{0,1:T(4,128)(4,1)} %get-tuple-element.114) | copy-start | bytes 52
  107.8 24.3 %copy-start.43 = (f32[576,256]{1,0:T(8,128)}, f32[576,256]{1,0:T(8,128)S(1)}, u32[]{:S(2)}) copy-start(f32[576,256]{1,0:T(8,128)S(1)} %collective-permute-done.7) | copy-start | bytes 1769476
  109.1 21.5 %copy-start.45 = (f32[576,256]{1,0:T(8,128)}, f32[576,256]{1,0:T(8,128)S(1)}, u32[]{:S(2)}) copy-start(f32[576,256]{1,0:T(8,128)S(1)} %collective-permute-done.6) | copy-start | bytes 1769476
  124.7 42.4 %all-to-all-start.3 = ((f32[8,2,4,48,256]{4,3,2,1,0:T(8,128)}), f32[8,2,4,48,256]{4,3,2,1,0:T(8,128)}, u32[]{:S(2)}, u32[]{:S(2)}) async-start(f32[8,2,4,48,256]{4,3,2,1,0:T(8,128)} %fusion.25), calls=%async_computation.3 | async-start | bytes 6291456 | tf_op jit(solution)/shard_map/all_to_all | solution.py:10
  130.6 14.7 %collective-permute-start.8 = (f32[576,256]{1,0:T(8,128)S(1)}, f32[576,256]{1,0:T(8,128)}, u32[]{:S(2)}, u32[]{:S(2)}) collective-permute-start(f32[576,256]{1,0:T(8,128)S(1)} %collective-permute-done.6), channel_id=1, source_target_pairs={{8,16},{16,24},{9,17},{17,25},{10,18},{18,26},{11,19},{19,27},{12,... | collective-permute-start | bytes 1769480 | tf_op jit(solution)/shard_map/ppermute | solution.py:23
  132.1 17.4 %collective-permute-start.9 = (f32[576,256]{1,0:T(8,128)S(1)}, f32[576,256]{1,0:T(8,128)}, u32[]{:S(2)}, u32[]{:S(2)}) collective-permute-start(f32[576,256]{1,0:T(8,128)S(1)} %collective-permute-done.7), channel_id=1, source_target_pairs={{8,0},{16,8},{9,1},{17,9},{10,2},{18,10},{11,3},{19,11},{12,4},{20... | collective-permute-start | bytes 1769480 | tf_op jit(solution)/shard_map/ppermute | solution.py:24
  167.1 41.5 %all-to-all-start.4 = ((f32[8,2,4,48,256]{4,3,2,1,0:T(8,128)}), f32[8,2,4,48,256]{4,3,2,1,0:T(8,128)S(1)}, u32[]{:S(2)}, u32[]{:S(2)}) async-start(f32[8,2,4,48,256]{4,3,2,1,0:T(8,128)} %fusion.24), calls=%async_computation.4 | async-start | bytes 6291456 | tf_op jit(solution)/shard_map/all_to_all | solution.py:10
  175.6 4.3 collective-permute-start.10
  176.3 17.6 %collective-permute-start.11 = (f32[576,256]{1,0:T(8,128)}, f32[576,256]{1,0:T(8,128)}, u32[]{:S(2)}, u32[]{:S(2)}) collective-permute-start(f32[576,256]{1,0:T(8,128)} %collective-permute-done.9), channel_id=1, source_target_pairs={{8,0},{9,1},{10,2},{11,3},{12,4},{13,5},{14,6},{15,7}} | collective-permute-start | bytes 1769480 | tf_op jit(solution)/shard_map/ppermute | solution.py:24
  221.1 10.5 %copy-start.51 = (s32[1024]{0:T(1024)S(1)}, s32[1024]{0:T(1024)}, u32[]{:S(2)}) copy-start(s32[1024]{0:T(1024)} %copy-done.50) | copy-start | bytes 12292
  221.1 42.5 %all-to-all-start.9 = ((f32[8,2,4,48,256]{4,3,2,1,0:T(8,128)}), f32[8,2,4,48,256]{4,3,2,1,0:T(8,128)}, u32[]{:S(2)}, u32[]{:S(2)}) async-start(f32[8,2,4,48,256]{4,3,2,1,0:T(8,128)} %fusion.21), calls=%async_computation.9 | async-start | bytes 6291456 | tf_op jit(solution)/shard_map/all_to_all | solution.py:10
  263.6 42.6 %all-to-all-start.7 = ((f32[8,2,4,48,256]{4,3,2,1,0:T(8,128)}), f32[8,2,4,48,256]{4,3,2,1,0:T(8,128)}, u32[]{:S(2)}, u32[]{:S(2)}) async-start(f32[8,2,4,48,256]{4,3,2,1,0:T(8,128)} %fusion.22), calls=%async_computation.7 | async-start | bytes 6291456 | tf_op jit(solution)/shard_map/all_to_all | solution.py:10
  306.2 44.7 %all-to-all-start.5 = ((f32[8,2,4,48,256]{4,3,2,1,0:T(8,128)}), f32[8,2,4,48,256]{4,3,2,1,0:T(8,128)}, u32[]{:S(2)}, u32[]{:S(2)}) async-start(f32[8,2,4,48,256]{4,3,2,1,0:T(8,128)} %fusion.23), calls=%async_computation.5 | async-start | bytes 6291456 | tf_op jit(solution)/shard_map/all_to_all | solution.py:10
  315.0 12.9 %copy-start.17 = (f32[1,4,8,48,256]{4,3,2,1,0:T(8,128)}, f32[1,4,8,48,256]{4,3,2,1,0:T(8,128)S(1)}, u32[]{:S(2)}) copy-start(f32[1,4,8,48,256]{4,3,2,1,0:T(8,128)S(1)} %copy.222) | copy-start | bytes 4718596
  315.2 12.8 %copy-start.15 = (f32[1,4,8,48,256]{4,3,2,1,0:T(8,128)}, f32[1,4,8,48,256]{4,3,2,1,0:T(8,128)S(1)}, u32[]{:S(2)}) copy-start(f32[1,4,8,48,256]{4,3,2,1,0:T(8,128)S(1)} %copy.221) | copy-start | bytes 4718596
  351.0 42.1 %all-to-all-start.10 = ((f32[8,2,4,48,256]{4,3,2,1,0:T(8,128)}), f32[8,2,4,48,256]{4,3,2,1,0:T(8,128)}, u32[]{:S(2)}, u32[]{:S(2)}) async-start(f32[8,2,4,48,256]{4,3,2,1,0:T(8,128)} %copy.224), calls=%async_computation.10 | async-start | bytes 6291456 | tf_op jit(solution)/shard_map/all_to_all | solution.py:10
  357.9 12.0 %copy-start.20 = (f32[1,4,8,48,256]{4,3,2,1,0:T(8,128)}, f32[1,4,8,48,256]{4,3,2,1,0:T(8,128)S(1)}, u32[]{:S(2)}) copy-start(f32[1,4,8,48,256]{4,3,2,1,0:T(8,128)S(1)} %copy.206) | copy-start | bytes 4718596
  358.1 11.9 %copy-start.22 = (f32[1,4,8,48,256]{4,3,2,1,0:T(8,128)}, f32[1,4,8,48,256]{4,3,2,1,0:T(8,128)S(1)}, u32[]{:S(2)}) copy-start(f32[1,4,8,48,256]{4,3,2,1,0:T(8,128)S(1)} %copy.205) | copy-start | bytes 4718596
  393.0 42.0 %all-to-all-start.6 = ((f32[8,2,4,48,256]{4,3,2,1,0:T(8,128)}), f32[8,2,4,48,256]{4,3,2,1,0:T(8,128)}, u32[]{:S(2)}, u32[]{:S(2)}) async-start(f32[8,2,4,48,256]{4,3,2,1,0:T(8,128)} %copy.208), calls=%async_computation.6 | async-start | bytes 6291456 | tf_op jit(solution)/shard_map/all_to_all | solution.py:10
  400.4 11.5 %copy-start.19 = (f32[1,4,8,48,256]{4,3,2,1,0:T(8,128)}, f32[1,4,8,48,256]{4,3,2,1,0:T(8,128)S(1)}, u32[]{:S(2)}) copy-start(f32[1,4,8,48,256]{4,3,2,1,0:T(8,128)S(1)} %copy.214) | copy-start | bytes 4718596
  411.9 9.8 %copy-start.12 = (f32[1,4,8,48,256]{4,3,2,1,0:T(8,128)S(1)}, f32[1,4,8,48,256]{4,3,2,1,0:T(8,128)}, u32[]{:S(2)}) copy-start(f32[1,4,8,48,256]{4,3,2,1,0:T(8,128)} %copy-done.11) | copy-start | bytes 4718596
  435.1 41.9 %all-to-all-start.8 = ((f32[8,2,4,48,256]{4,3,2,1,0:T(8,128)}), f32[8,2,4,48,256]{4,3,2,1,0:T(8,128)}, u32[]{:S(2)}, u32[]{:S(2)}) async-start(f32[8,2,4,48,256]{4,3,2,1,0:T(8,128)} %copy.216), calls=%async_computation.8 | async-start | bytes 6291456 | tf_op jit(solution)/shard_map/all_to_all | solution.py:10
  462.1 18.8 %copy-start.49 = (s32[8,6]{0,1:T(8,128)S(1)}, s32[8,6]{0,1:T(8,128)}, u32[]{:S(2)}) copy-start(s32[8,6]{0,1:T(8,128)} %copy-done.48) | copy-start | bytes 580
  490.2 18.3 %slice-start.3 = ((s8[9437184]{0:T(1024)(128)(4,1)}), s8[1048576]{0:T(1024)(128)(4,1)S(1)}, s32[]{:S(2)}) async-start(s8[9437184]{0:T(1024)(128)(4,1)} %bitcast.342), calls=%async_computation.19 | async-start | bytes 2097152
  490.2 42.7 %all-to-all-start.11 = ((f32[8,2,4,48,256]{4,3,2,1,0:T(8,128)}), f32[8,2,4,48,256]{4,3,2,1,0:T(8,128)}, u32[]{:S(2)}, u32[]{:S(2)}) async-start(f32[8,2,4,48,256]{4,3,2,1,0:T(8,128)} %copy.231), calls=%async_computation.11 | async-start | bytes 6291456 | tf_op jit(solution)/shard_map/all_to_all | solution.py:10
  496.4 12.0 %slice-start.4 = ((s8[9437184]{0:T(1024)(128)(4,1)}), s8[4194304]{0:T(1024)(128)(4,1)S(1)}, s32[]{:S(2)}) async-start(s8[9437184]{0:T(1024)(128)(4,1)} %bitcast.342), calls=%async_computation.20 | async-start | bytes 8388608
  496.4 12.0 %slice-start.5 = ((s8[9437184]{0:T(1024)(128)(4,1)}), s8[4194304]{0:T(1024)(128)(4,1)S(1)}, s32[]{:S(2)}) async-start(s8[9437184]{0:T(1024)(128)(4,1)} %bitcast.342), calls=%async_computation.21 | async-start | bytes 8388608
  504.6 9.9 %collective-permute-start.13 = (f32[12,48,256]{2,1,0:T(8,128)S(1)}, f32[12,48,256]{2,1,0:T(8,128)}, u32[]{:S(2)}, u32[]{:S(2)}) collective-permute-start(f32[12,48,256]{2,1,0:T(8,128)S(1)} %copy.230), channel_id=1, source_target_pairs={{24,16},{25,17},{26,18},{27,19},{28,20},{29,21},{30,22},{31,23}} | collective-permute-start | bytes 1769480 | tf_op jit(solution)/shard_map/ppermute | solution.py:52
  506.1 14.5 %collective-permute-start.12 = (f32[12,48,256]{2,1,0:T(8,128)S(1)}, f32[12,48,256]{2,1,0:T(8,128)}, u32[]{:S(2)}, u32[]{:S(2)}) collective-permute-start(f32[12,48,256]{2,1,0:T(8,128)S(1)} %copy.229), channel_id=1, source_target_pairs={{0,8},{1,9},{2,10},{3,11},{4,12},{5,13},{6,14},{7,15}} | collective-permute-start | bytes 1769480 | tf_op jit(solution)/shard_map/ppermute | solution.py:51
  512.5 20.4 %copy-start.5 = (f32[4,48,256,12]{2,3,1,0:T(8,128)S(1)}, f32[4,48,256,12]{2,3,1,0:T(8,128)}, u32[]{:S(2)}) copy-start(f32[4,48,256,12]{2,3,1,0:T(8,128)} %copy-done.4) | copy-start | bytes 7077892
  538.2 17.7 %slice-start = ((s8[9437184]{0:T(1024)(128)(4,1)}), s8[1048576]{0:T(1024)(128)(4,1)S(1)}, s32[]{:S(2)}) async-start(s8[9437184]{0:T(1024)(128)(4,1)} %bitcast.338), calls=%async_computation.16 | async-start | bytes 2097152
  538.2 42.6 %all-to-all-start.12 = ((f32[8,2,4,48,256]{4,3,2,1,0:T(8,128)}), f32[8,2,4,48,256]{4,3,2,1,0:T(8,128)}, u32[]{:S(2)}, u32[]{:S(2)}) async-start(f32[8,2,4,48,256]{4,3,2,1,0:T(8,128)} %copy.236), calls=%async_computation.12 | async-start | bytes 6291456 | tf_op jit(solution)/shard_map/all_to_all | solution.py:10
  544.3 11.6 %slice-start.1 = ((s8[9437184]{0:T(1024)(128)(4,1)}), s8[4194304]{0:T(1024)(128)(4,1)S(1)}, s32[]{:S(2)}) async-start(s8[9437184]{0:T(1024)(128)(4,1)} %bitcast.338), calls=%async_computation.17 | async-start | bytes 8388608
  544.3 11.6 %slice-start.2 = ((s8[9437184]{0:T(1024)(128)(4,1)}), s8[4194304]{0:T(1024)(128)(4,1)S(1)}, s32[]{:S(2)}) async-start(s8[9437184]{0:T(1024)(128)(4,1)} %bitcast.338), calls=%async_computation.18 | async-start | bytes 8388608
  552.0 10.1 %collective-permute-start.15 = (f32[12,48,256]{2,1,0:T(8,128)S(1)}, f32[12,48,256]{2,1,0:T(8,128)}, u32[]{:S(2)}, u32[]{:S(2)}) collective-permute-start(f32[12,48,256]{2,1,0:T(8,128)S(1)} %copy.235), channel_id=1, source_target_pairs={{16,8},{24,16},{17,9},{25,17},{18,10},{26,18},{19,11},{27,19},{20,... | collective-permute-start | bytes 1769480 | tf_op jit(solution)/shard_map/ppermute | solution.py:52
  553.5 14.5 %collective-permute-start.14 = (f32[12,48,256]{2,1,0:T(8,128)S(1)}, f32[12,48,256]{2,1,0:T(8,128)}, u32[]{:S(2)}, u32[]{:S(2)}) collective-permute-start(f32[12,48,256]{2,1,0:T(8,128)S(1)} %copy.234), channel_id=1, source_target_pairs={{0,8},{8,16},{1,9},{9,17},{2,10},{10,18},{3,11},{11,19},{4,12},{12... | collective-permute-start | bytes 1769480 | tf_op jit(solution)/shard_map/ppermute | solution.py:51
  560.0 20.8 %copy-start.6 = (f32[4,48,256,12]{2,3,1,0:T(8,128)S(1)}, f32[4,48,256,12]{2,3,1,0:T(8,128)}, u32[]{:S(2)}) copy-start(f32[4,48,256,12]{2,3,1,0:T(8,128)} %copy-done.4) | copy-start | bytes 7077892
  586.1 41.5 %all-to-all-start.13 = ((f32[8,2,4,48,256]{4,3,2,1,0:T(8,128)}), f32[8,2,4,48,256]{4,3,2,1,0:T(8,128)S(1)}, u32[]{:S(2)}, u32[]{:S(2)}) async-start(f32[8,2,4,48,256]{4,3,2,1,0:T(8,128)} %copy.241), calls=%async_computation.13 | async-start | bytes 6291456 | tf_op jit(solution)/shard_map/all_to_all | solution.py:10
  594.1 17.6 %collective-permute-start.17 = (f32[12,48,256]{2,1,0:T(8,128)S(1)}, f32[12,48,256]{2,1,0:T(8,128)S(1)}, u32[]{:S(2)}, u32[]{:S(2)}) collective-permute-start(f32[12,48,256]{2,1,0:T(8,128)S(1)} %copy.240), channel_id=1, source_target_pairs={{8,0},{16,8},{24,16},{9,1},{17,9},{25,17},{10,2},{18,10},{26,18},{... | collective-permute-start | bytes 1769480 | tf_op jit(solution)/shard_map/ppermute | solution.py:52
  595.4 17.2 %collective-permute-start.16 = (f32[12,48,256]{2,1,0:T(8,128)S(1)}, f32[12,48,256]{2,1,0:T(8,128)}, u32[]{:S(2)}, u32[]{:S(2)}) collective-permute-start(f32[12,48,256]{2,1,0:T(8,128)S(1)} %copy.239), channel_id=1, source_target_pairs={{0,8},{8,16},{16,24},{1,9},{9,17},{17,25},{2,10},{10,18},{18,26},{... | collective-permute-start | bytes 1769480 | tf_op jit(solution)/shard_map/ppermute | solution.py:51
  634.9 14.4 %collective-permute-start.18 = (f32[12,48,256]{2,1,0:T(8,128)S(1)}, f32[12,48,256]{2,1,0:T(8,128)S(1)}, u32[]{:S(2)}, u32[]{:S(2)}) collective-permute-start(f32[12,48,256]{2,1,0:T(8,128)S(1)} %copy.248), channel_id=1, source_target_pairs={{0,8},{1,9},{2,10},{3,11},{4,12},{5,13},{6,14},{7,15}} | collective-permute-start | bytes 1769480 | tf_op jit(solution)/shard_map/ppermute | solution.py:51
  636.7 17.9 %collective-permute-start.21 = (f32[12,48,256]{2,1,0:T(8,128)S(1)}, f32[12,48,256]{2,1,0:T(8,128)S(1)}, u32[]{:S(2)}, u32[]{:S(2)}) collective-permute-start(f32[12,48,256]{2,1,0:T(8,128)S(1)} %copy.251), channel_id=1, source_target_pairs={{24,16},{25,17},{26,18},{27,19},{28,20},{29,21},{30,22},{31,23}} | collective-permute-start | bytes 1769480 | tf_op jit(solution)/shard_map/ppermute | solution.py:52
  649.6 25.5 %copy-start.37 = (f32[1,48,256,12]{2,3,1,0:T(8,128)S(1)}, f32[1,48,256,12]{2,3,1,0:T(8,128)}, u32[]{:S(2)}) copy-start(f32[1,48,256,12]{2,3,1,0:T(8,128)} %get-tuple-element.80) | copy-start | bytes 1769476
  649.6 25.5 %copy-start.42 = (f32[12,48,256]{2,1,0:T(8,128)S(1)}, f32[12,48,256]{2,1,0:T(8,128)}, u32[]{:S(2)}) copy-start(f32[12,48,256]{2,1,0:T(8,128)} %copy-done.41) | copy-start | bytes 1769476
  649.6 16.6 %collective-permute-start.19 = (f32[12,48,256]{2,1,0:T(8,128)S(1)}, f32[12,48,256]{2,1,0:T(8,128)S(1)}, u32[]{:S(2)}, u32[]{:S(2)}) collective-permute-start(f32[12,48,256]{2,1,0:T(8,128)S(1)} %fusion.36), channel_id=1, source_target_pairs={{0,8},{8,16},{1,9},{9,17},{2,10},{10,18},{3,11},{11,19},{4,12},{12... | collective-permute-start | bytes 1769480 | tf_op jit(solution)/shard_map/ppermute | solution.py:51
  655.0 17.7 %collective-permute-start.22 = (f32[12,48,256]{2,1,0:T(8,128)S(1)}, f32[12,48,256]{2,1,0:T(8,128)S(1)}, u32[]{:S(2)}, u32[]{:S(2)}) collective-permute-start(f32[12,48,256]{2,1,0:T(8,128)S(1)} %fusion.34), channel_id=1, source_target_pairs={{16,8},{24,16},{17,9},{25,17},{18,10},{26,18},{19,11},{27,19},{20,... | collective-permute-start | bytes 1769480 | tf_op jit(solution)/shard_map/ppermute | solution.py:52
  667.5 17.4 %collective-permute-start.20 = (f32[12,48,256]{2,1,0:T(8,128)}, f32[12,48,256]{2,1,0:T(8,128)}, u32[]{:S(2)}, u32[]{:S(2)}) collective-permute-start(f32[12,48,256]{2,1,0:T(8,128)} %fusion.35), channel_id=1, source_target_pairs={{0,8},{8,16},{16,24},{1,9},{9,17},{17,25},{2,10},{10,18},{18,26},{... | collective-permute-start | bytes 1769480 | tf_op jit(solution)/shard_map/ppermute | solution.py:51
  673.8 15.6 %collective-permute-start.23 = (f32[12,48,256]{2,1,0:T(8,128)}, f32[12,48,256]{2,1,0:T(8,128)}, u32[]{:S(2)}, u32[]{:S(2)}) collective-permute-start(f32[12,48,256]{2,1,0:T(8,128)} %fusion.33), channel_id=1, source_target_pairs={{8,0},{16,8},{24,16},{9,1},{17,9},{25,17},{10,2},{18,10},{26,18},{... | collective-permute-start | bytes 1769480 | tf_op jit(solution)/shard_map/ppermute | solution.py:52
  680.7 14.5 %all-to-all-start.14 = ((f32[576,8,32]{0,2,1:T(8,128)}), f32[576,8,32]{0,2,1:T(8,128)}, u32[]{:S(2)}, u32[]{:S(2)}) async-start(f32[576,8,32]{0,2,1:T(8,128)} %copy.271), calls=%async_computation.14 | async-start | bytes 1310720 | tf_op jit(solution)/shard_map/all_to_all | solution.py:131
  695.2 13.2 %all-to-all-start.15 = ((f32[576,8,32]{0,2,1:T(8,128)}), f32[576,8,32]{0,2,1:T(8,128)S(1)}, u32[]{:S(2)}, u32[]{:S(2)}) async-start(f32[576,8,32]{0,2,1:T(8,128)} %copy.272), calls=%async_computation.15 | async-start | bytes 1310720 | tf_op jit(solution)/shard_map/all_to_all | solution.py:131
  (42 other events, 182.8 us)

commit v10 on v9

--- a/solution.py
+++ b/solution.py
@@ -96,9 +96,11 @@
     first_loads = [requested(first_pieces, slot) for slot in range(slot_count)]
     second_pieces, first_arrived = line_gather(own_rows[1], "grp", group_count, first_loads)
     second_pieces = shape_pieces(second_pieces)
-    second_arrived = [band_exchange(requested(second_pieces, slot)) for slot in range(slot_count)]
+    second_loads = [requested(second_pieces, slot) for slot in range(slot_count)]
+    second_arrived = [band_exchange(load) for load in second_loads[:2]]
     returned = [[], []]
     held = []
+    waiting = []
     for slot in range(slot_count):
         rows = [
             arrived.transpose(1, 2, 0, 3, 4).reshape(2, blk, half)
@@ -109,17 +111,23 @@
         )
         kernel = density * coulomb[slot]
         scale = jnp.where(own_pairs[2 * slot] == own_pairs[2 * slot + 1], 0.5, 1.0)
+        outbound = []
         for h in range(2):
             onto_first = jnp.dot(kernel, rows[h][1], precision=PRECISION, preferred_element_type=jnp.float32)
             onto_second = jnp.dot(kernel.T, rows[h][0], precision=PRECISION, preferred_element_type=jnp.float32)
-            outbound = (jnp.stack([onto_first, onto_second], 0) * scale).reshape(
+            terms = (jnp.stack([onto_first, onto_second], 0) * scale).reshape(
                 2, group_count, band_count, piece_rows, half
             )
-            outbound = outbound.transpose(2, 0, 1, 3, 4)
-            if h == 0:
-                returned[0].append(band_exchange(outbound))
-            else:
-                held.append(outbound)
+            outbound.append(terms.transpose(2, 0, 1, 3, 4))
+        held.append(outbound[1])
+        if slot + 2 < slot_count:
+            load, outbound[0] = lax.optimization_barrier((second_loads[slot + 2], outbound[0]))
+            second_arrived.append(band_exchange(load))
+        if waiting:
+            waiting[0], outbound[0] = lax.optimization_barrier((waiting[0], outbound[0]))
+            returned[0].append(band_exchange(waiting.pop()))
+        waiting.append(outbound[0])
+    returned[0].append(band_exchange(waiting.pop()))
 
     def sum_blocks(returned):
         gathered = jnp.concatenate(returned, axis=1)

time: 723 us -> 749 us (1.036)
  waiting for transfers between devices: 229 us -> 259 us
  starting transfers between devices: 129 us -> 121 us
    all_to_all x12, waiting for transfers between devices: 125 us -> 148 us  [band_exchange(): lax.all_to_all(outgoing, 'band', split_axis=0, concat_axis=0, tiled=True)]
    dot_general x6, matrix products: 42.2 us -> 24.4 us  [body(): jnp.dot(kernel, rows[h][1], precision=PRECISION, preferred_element_type=j...]
    dot_general x6, matrix products: 27.5 us -> 42.3 us  [body(): jnp.dot(kernel.T, rows[h][0], precision=PRECISION, preferred_element_type...]
    optimization_barrier x0 -> x3, local copies, waits for them, and re-layouts: none -> 7.67 us  [body(): lax.optimization_barrier((waiting[0], outbound[0]))]
  transfers between devices with their start and end apart: 39 -> 39, of which waited for: 23 -> 24; matrix products, arithmetic and copies ran while one was open for 38% -> 38% of each run, Pallas kernels for 0% -> 0%
where the time goes in v10:
time: 749 us; the launch traced here: 737 us
  waiting for transfers between devices  259 us (35%)
  local copies, waits for them, and re-layouts  159 us (21%)
  matrix products  131 us (17%)
  starting transfers between devices  121 us (16%)
  other arithmetic  47.6 us (6%)
  blocking collectives  13.7 us (2%)
    all_to_all x12, waiting for transfers between devices, band_exchange(): lax.all_to_all(outgoing, 'band', split_axis=0, concat_axis=0, tiled=True)  148 us
    all_to_all x12, starting transfers between devices, band_exchange(): lax.all_to_all(outgoing, 'band', split_axis=0, concat_axis=0, tiled=True)  64.5 us
    dot_general x6, matrix products, body(): jnp.dot(r[0], r[1].T, precision=PRECISION, preferred_element_type=jnp.flo...  57.5 us
    ppermute x6, waiting for transfers between devices, line_gather(): lax.ppermute(leftward, axis, [(i + 1, i) for i in range(0, count - step)])  55.7 us
    dot_general x6, matrix products, body(): jnp.dot(kernel.T, rows[h][0], precision=PRECISION, preferred_element_type...  42.3 us
    ppermute x6, waiting for transfers between devices, line_reduce(): lax.ppermute(send_right, axis, [(i, i + 1) for i in range(0, step)])  34.8 us
    dot_general x3, local copies, waits for them, and re-layouts, body(): jnp.dot(kernel.T, rows[h][0], precision=PRECISION, preferred_element_type...  29.1 us
    dot_general x6, matrix products, body(): jnp.dot(kernel, rows[h][1], precision=PRECISION, preferred_element_type=j...  24.4 us
  transfers between devices with their start and end apart: 39, of which 24 were waited for; matrix products, arithmetic and copies ran while one was open for 38% of the time, Pallas kernels for 0%

profile of v10, /device:TPU:2, one launch (start us, length us, event | category | flops | bytes accessed | tf_op | source)
XLA Modules:
  0.0 737.2 jit_solution(11296756464918792672)
XLA Ops:
  1.7 13.7 %all_to_all.136 = f32[8,576,32]{1,2,0:T(8,128)S(1)} all-to-all(f32[8,576,32]{1,2,0:T(8,128)S(1)} %copy.188), channel_id=1, replica_groups=mesh['grp'=4,'band'=8] {'band'}, dimensions={0} | all-to-all | bytes 1179648 | tf_op jit(solution)/shard_map/all_to_all | solution.py:72
  16.5 4.3 collective-permute-start
  21.9 4.9 all-to-all-start
  35.3 9.0 %collective-permute-done.1 = f32[576,256]{1,0:T(8,128)S(1)} collective-permute-done((f32[576,256]{1,0:T(8,128)}, f32[576,256]{1,0:T(8,128)S(1)}, u32[]{:S(2)}, u32[]{:S(2)}) %collective-permute-start.1) | collective-permute-done | bytes 589856 | tf_op jit(solution)/shard_map/ppermute | solution.py:24
  47.9 12.9 %collective-permute-done.3 = f32[576,256]{1,0:T(8,128)S(1)} collective-permute-done((f32[576,256]{1,0:T(8,128)S(1)}, f32[576,256]{1,0:T(8,128)S(1)}, u32[]{:S(2)}, u32[]{:S(2)}) %collective-permute-start.3) | collective-permute-done | bytes 589856 | tf_op jit(solution)/shard_map/ppermute | solution.py:24
  63.3 13.0 %collective-permute-done.5 = f32[576,256]{1,0:T(8,128)S(1)} collective-permute-done((f32[576,256]{1,0:T(8,128)S(1)}, f32[576,256]{1,0:T(8,128)S(1)}, u32[]{:S(2)}, u32[]{:S(2)}) %collective-permute-start.5) | collective-permute-done | bytes 589856 | tf_op jit(solution)/shard_map/ppermute | solution.py:24
  83.0 5.2 all-to-all-start.2
  96.7 4.1 fusion.25
  104.0 5.9 collective-permute-done.7
  109.9 14.8 %all-to-all-done.2 = f32[8,2,4,48,256]{4,3,2,1,0:T(8,128)} async-done(((f32[8,2,4,48,256]{4,3,2,1,0:T(8,128)}), f32[8,2,4,48,256]{4,3,2,1,0:T(8,128)}, u32[]{:S(2)}, u32[]{:S(2)}) %all-to-all-start.2) | async-done | bytes 3145760 | tf_op jit(solution)/shard_map/all_to_all | solution.py:10
  124.7 5.9 all-to-all-start.3
  139.7 4.1 fusion.24
  143.8 4.8 collective-permute-done.9
  148.7 18.4 %all-to-all-done.3 = f32[8,2,4,48,256]{4,3,2,1,0:T(8,128)} async-done(((f32[8,2,4,48,256]{4,3,2,1,0:T(8,128)}), f32[8,2,4,48,256]{4,3,2,1,0:T(8,128)}, u32[]{:S(2)}, u32[]{:S(2)}) %all-to-all-start.3) | async-done | bytes 3145760 | tf_op jit(solution)/shard_map/all_to_all | solution.py:10
  167.1 5.1 all-to-all-start.4
  192.2 10.0 %collective-permute-done.11 = f32[576,256]{1,0:T(8,128)} collective-permute-done((f32[576,256]{1,0:T(8,128)}, f32[576,256]{1,0:T(8,128)}, u32[]{:S(2)}, u32[]{:S(2)}) %collective-permute-start.11) | collective-permute-done | bytes 589856 | tf_op jit(solution)/shard_map/ppermute | solution.py:24
  202.2 6.4 all-to-all-done.4
  221.1 6.2 all-to-all-start.5
  227.3 9.4 %fusion.57 = f32[1536,1536]{1,0:T(8,128)} fusion(f32[1536,256]{1,0:T(8,128)} %bitcast.357, f32[1536,256]{1,0:T(8,128)} %bitcast.363), kind=kOutput, calls=%fused_computation.132 | convolution fusion | flops 3623878656 | bytes 12582912 | tf_op jit(solution)/shard_map/dot_general | solution.py:110
  240.7 6.5 fusion.58
  261.7 6.5 fusion.59
  268.2 5.0 all-to-all-start.6
  275.6 11.9 %fusion.2 = f32[1536,1536]{1,0:T(8,128)} fusion(f32[1536,1536]{1,0:T(8,128)} %fusion.57, f32[1536,256]{1,0:T(8,128)S(1)} %bitcast.377, f32[1536,256]{1,0:T(8,128)S(1)} %bitcast.375, f32[3,1536,1536]{2,1,0:T(8,128)} %param.7), kind=kOutput, calls=%fused_computation.11 | convolution fusion | flops 3628597248 | bytes 31457280 | tf_op jit(solution)/shard_map/dot_general | solution.py:110
  287.4 9.7 %copy.209 = f32[1536,1536]{1,0:T(8,128)} copy(f32[1536,1536]{0,1:T(8,128)} %bitcast.333) | data formatting | bytes 18874368 | tf_op jit(solution)/shard_map/dot_general | solution.py:117
  297.2 7.0 convolution_bitcast_fusion.10
  304.1 7.2 convolution_bitcast_fusion.4
  311.4 4.1 convolution_bitcast_fusion.11
  315.5 4.1 convolution_bitcast_fusion.5
  326.6 4.7 all-to-all-start.8
  331.3 11.4 %fusion.1 = f32[1536,1536]{1,0:T(8,128)} fusion(f32[1536,1536]{1,0:T(8,128)} %fusion.58, f32[1536,256]{1,0:T(8,128)} %bitcast.373, f32[1536,256]{1,0:T(8,128)S(1)} %bitcast.371, f32[3,1536,1536]{2,1,0:T(8,128)} %param.7), kind=kOutput, calls=%fused_computation.9 | convolution fusion | flops 3628597248 | bytes 31457280 | tf_op jit(solution)/shard_map/dot_general | solution.py:110
  342.7 9.8 %copy.216 = f32[1536,1536]{1,0:T(8,128)} copy(f32[1536,1536]{0,1:T(8,128)} %bitcast.338) | data formatting | bytes 18874368 | tf_op jit(solution)/shard_map/dot_general | solution.py:117
  352.5 7.0 convolution_bitcast_fusion.8
  359.5 7.3 convolution_bitcast_fusion.2
  366.9 4.1 convolution_bitcast_fusion.9
  370.9 4.1 convolution_bitcast_fusion.3
  380.4 4.9 all-to-all-start.7
  387.7 11.9 %fusion = f32[1536,1536]{1,0:T(8,128)} fusion(f32[1536,1536]{1,0:T(8,128)} %fusion.59, f32[1536,256]{1,0:T(8,128)S(1)} %bitcast.369, f32[1536,256]{1,0:T(8,128)S(1)} %bitcast.367, f32[3,1536,1536]{2,1,0:T(8,128)} %param.7), kind=kOutput, calls=%fused_computation.7 | convolution fusion | flops 3628597248 | bytes 31457280 | tf_op jit(solution)/shard_map/dot_general | solution.py:110
  399.6 9.6 %copy.222 = f32[1536,1536]{1,0:T(8,128)} copy(f32[1536,1536]{0,1:T(8,128)} %bitcast.328) | data formatting | bytes 18874368 | tf_op jit(solution)/shard_map/dot_general | solution.py:117
  409.2 6.9 convolution_bitcast_fusion.6
  416.2 4.1 convolution_bitcast_fusion.7
  422.5 4.4 all-to-all-start.10
  430.7 32.6 %all-to-all-done.10 = f32[8,2,4,48,256]{4,3,2,1,0:T(8,128)S(1)} async-done(((f32[8,2,4,48,256]{4,3,2,1,0:T(8,128)}), f32[8,2,4,48,256]{4,3,2,1,0:T(8,128)S(1)}, u32[]{:S(2)}, u32[]{:S(2)}) %all-to-all-start.10) | async-done | bytes 3145760 | tf_op jit(solution)/shard_map/all_to_all | solution.py:10
  463.3 6.1 all-to-all-start.9
  469.4 5.5 copy.225
  478.4 27.4 %all-to-all-done.9 = f32[8,2,4,48,256]{4,3,2,1,0:T(8,128)} async-done(((f32[8,2,4,48,256]{4,3,2,1,0:T(8,128)}), f32[8,2,4,48,256]{4,3,2,1,0:T(8,128)}, u32[]{:S(2)}, u32[]{:S(2)}) %all-to-all-start.9) | async-done | bytes 3145760 | tf_op jit(solution)/shard_map/all_to_all | solution.py:10
  519.0 5.9 all-to-all-start.11
  533.4 8.5 %collective-permute-done.12 = f32[12,48,256]{2,1,0:T(8,128)} collective-permute-done((f32[12,48,256]{2,1,0:T(8,128)}, f32[12,48,256]{2,1,0:T(8,128)}, u32[]{:S(2)}, u32[]{:S(2)}) %collective-permute-start.12) | collective-permute-done | bytes 589856 | tf_op jit(solution)/shard_map/ppermute | solution.py:51
  541.9 19.4 %all-to-all-done.11 = f32[8,2,4,48,256]{4,3,2,1,0:T(8,128)} async-done(((f32[8,2,4,48,256]{4,3,2,1,0:T(8,128)}), f32[8,2,4,48,256]{4,3,2,1,0:T(8,128)}, u32[]{:S(2)}, u32[]{:S(2)}) %all-to-all-start.11) | async-done | bytes 3145760 | tf_op jit(solution)/shard_map/all_to_all | solution.py:10
  566.6 6.1 all-to-all-start.12
  572.7 7.0 convolution_bitcast_fusion
  584.3 4.1 convolution_bitcast_fusion.1
  590.5 4.2 collective-permute-done.14
  594.7 14.5 %all-to-all-done.12 = f32[8,2,4,48,256]{4,3,2,1,0:T(8,128)} async-done(((f32[8,2,4,48,256]{4,3,2,1,0:T(8,128)}), f32[8,2,4,48,256]{4,3,2,1,0:T(8,128)}, u32[]{:S(2)}, u32[]{:S(2)}) %all-to-all-start.12) | async-done | bytes 3145760 | tf_op jit(solution)/shard_map/all_to_all | solution.py:10
  614.5 5.1 all-to-all-start.13
  625.7 5.4 copy.244
  631.1 5.4 copy.245
  641.2 14.7 %all-to-all-done.13 = f32[8,2,4,48,256]{4,3,2,1,0:T(8,128)S(1)} async-done(((f32[8,2,4,48,256]{4,3,2,1,0:T(8,128)}), f32[8,2,4,48,256]{4,3,2,1,0:T(8,128)S(1)}, u32[]{:S(2)}, u32[]{:S(2)}) %all-to-all-start.13) | async-done | bytes 3145760 | tf_op jit(solution)/shard_map/all_to_all | solution.py:10
  667.2 11.5 %collective-permute-done.18 = f32[12,48,256]{2,1,0:T(8,128)S(1)} collective-permute-done((f32[12,48,256]{2,1,0:T(8,128)S(1)}, f32[12,48,256]{2,1,0:T(8,128)S(1)}, u32[]{:S(2)}, u32[]{:S(2)}) %collective-permute-start.18) | collective-permute-done | bytes 589856 | tf_op jit(solution)/shard_map/ppermute | solution.py:51
  679.1 4.4 collective-permute-start.19
  686.0 9.6 %collective-permute-done.19 = f32[12,48,256]{2,1,0:T(8,128)S(1)} collective-permute-done((f32[12,48,256]{2,1,0:T(8,128)S(1)}, f32[12,48,256]{2,1,0:T(8,128)S(1)}, u32[]{:S(2)}, u32[]{:S(2)}) %collective-permute-start.19) | collective-permute-done | bytes 589856 | tf_op jit(solution)/shard_map/ppermute | solution.py:51
  696.8 5.2 collective-permute-start.20
  707.6 4.1 all-to-all-start.14
  720.7 4.9 all-to-all-start.15
  727.3 8.1 %all-to-all-done.15 = f32[576,8,32]{0,2,1:T(8,128)S(1)} async-done(((f32[576,8,32]{0,2,1:T(8,128)}), f32[576,8,32]{0,2,1:T(8,128)S(1)}, u32[]{:S(2)}, u32[]{:S(2)}) %all-to-all-start.15) | async-done | bytes 589856 | tf_op jit(solution)/shard_map/all_to_all | solution.py:139
  (295 shorter events, 202.5 us)
Async XLA Ops:
  1.7 25.2 %copy-start.51 = (s32[32,6]{0,1:T(8,128)S(1)}, s32[32,6]{0,1:T(8,128)}, u32[]{:S(2)}) copy-start(s32[32,6]{0,1:T(8,128)} %param.6) | copy-start | bytes 2308
  16.5 16.3 %collective-permute-start = (f32[576,256]{1,0:T(8,128)}, f32[576,256]{1,0:T(8,128)}, u32[]{:S(2)}, u32[]{:S(2)}) collective-permute-start(f32[576,256]{1,0:T(8,128)} %copy.190), channel_id=1, source_target_pairs={{0,8},{8,16},{16,24},{1,9},{9,17},{17,25},{2,10},{10,18},{18,26},{... | collective-permute-start | bytes 1769480 | tf_op jit(solution)/shard_map/ppermute | solution.py:23
  21.9 61.1 %all-to-all-start = ((f32[8,576,32]{1,2,0:T(8,128)}), f32[8,576,32]{1,2,0:T(8,128)S(1)}, u32[]{:S(2)}, u32[]{:S(2)}) async-start(f32[8,576,32]{1,2,0:T(8,128)} %copy.185), calls=%async_computation | async-start | bytes 1310720 | tf_op jit(solution)/shard_map/all_to_all | solution.py:72
  26.9 20.2 %copy-start.46 = (s32[8,6]{0,1:T(8,128)}, s32[8,6]{0,1:T(8,128)S(1)}, u32[]{:S(2)}) copy-start(s32[8,6]{0,1:T(8,128)S(1)} %get-tuple-element.91) | copy-start | bytes 580
  26.9 17.5 %collective-permute-start.1 = (f32[576,256]{1,0:T(8,128)}, f32[576,256]{1,0:T(8,128)S(1)}, u32[]{:S(2)}, u32[]{:S(2)}) collective-permute-start(f32[576,256]{1,0:T(8,128)} %copy.190), channel_id=1, source_target_pairs={{8,0},{16,8},{24,16},{9,1},{17,9},{25,17},{10,2},{18,10},{26,18},{... | collective-permute-start | bytes 1769480 | tf_op jit(solution)/shard_map/ppermute | solution.py:24
  32.7 14.4 %collective-permute-start.2 = (f32[576,256]{1,0:T(8,128)}, f32[576,256]{1,0:T(8,128)}, u32[]{:S(2)}, u32[]{:S(2)}) collective-permute-start(f32[576,256]{1,0:T(8,128)} %collective-permute-done), channel_id=1, source_target_pairs={{8,16},{16,24},{9,17},{17,25},{10,18},{18,26},{11,19},{19,27},{12,... | collective-permute-start | bytes 1769480 | tf_op jit(solution)/shard_map/ppermute | solution.py:23
  35.1 43.9 %copy-start.52 = (pred[8,2]{1,0:T(8,128)(4,1)}, pred[8,2]{1,0:T(8,128)(4,1)S(1)}, u32[]{:S(2)}) copy-start(pred[8,2]{1,0:T(8,128)(4,1)S(1)} %copy.187) | copy-start | bytes 52
  44.4 16.4 %collective-permute-start.3 = (f32[576,256]{1,0:T(8,128)S(1)}, f32[576,256]{1,0:T(8,128)S(1)}, u32[]{:S(2)}, u32[]{:S(2)}) collective-permute-start(f32[576,256]{1,0:T(8,128)S(1)} %collective-permute-done.1), channel_id=1, source_target_pairs={{8,0},{16,8},{9,1},{17,9},{10,2},{18,10},{11,3},{19,11},{12,4},{20... | collective-permute-start | bytes 1769480 | tf_op jit(solution)/shard_map/ppermute | solution.py:24
  47.1 16.2 %collective-permute-start.4 = (f32[576,256]{1,0:T(8,128)}, f32[576,256]{1,0:T(8,128)S(1)}, u32[]{:S(2)}, u32[]{:S(2)}) collective-permute-start(f32[576,256]{1,0:T(8,128)} %collective-permute-done.2), channel_id=1, source_target_pairs={{16,24},{17,25},{18,26},{19,27},{20,28},{21,29},{22,30},{23,31}} | collective-permute-start | bytes 1769480 | tf_op jit(solution)/shard_map/ppermute | solution.py:23
  60.8 15.5 %collective-permute-start.5 = (f32[576,256]{1,0:T(8,128)S(1)}, f32[576,256]{1,0:T(8,128)S(1)}, u32[]{:S(2)}, u32[]{:S(2)}) collective-permute-start(f32[576,256]{1,0:T(8,128)S(1)} %collective-permute-done.3), channel_id=1, source_target_pairs={{8,0},{9,1},{10,2},{11,3},{12,4},{13,5},{14,6},{15,7}} | collective-permute-start | bytes 1769480 | tf_op jit(solution)/shard_map/ppermute | solution.py:24
  83.0 8.6 %copy-start.33 = (f32[8,576,32]{1,2,0:T(8,128)}, f32[8,576,32]{1,2,0:T(8,128)S(1)}, u32[]{:S(2)}) copy-start(f32[8,576,32]{1,2,0:T(8,128)S(1)} %all-to-all-done) | copy-start | bytes 1769476
  83.0 41.7 %all-to-all-start.2 = ((f32[8,2,4,48,256]{4,3,2,1,0:T(8,128)}), f32[8,2,4,48,256]{4,3,2,1,0:T(8,128)}, u32[]{:S(2)}, u32[]{:S(2)}) async-start(f32[8,2,4,48,256]{4,3,2,1,0:T(8,128)} %fusion.26), calls=%async_computation.2 | async-start | bytes 6291456 | tf_op jit(solution)/shard_map/all_to_all | solution.py:10
  89.3 14.8 %collective-permute-start.6 = (f32[576,256]{1,0:T(8,128)}, f32[576,256]{1,0:T(8,128)}, u32[]{:S(2)}, u32[]{:S(2)}) collective-permute-start(f32[576,256]{1,0:T(8,128)} %copy.194), channel_id=1, source_target_pairs={{0,8},{8,16},{16,24},{1,9},{9,17},{17,25},{2,10},{10,18},{18,26},{... | collective-permute-start | bytes 1769480 | tf_op jit(solution)/shard_map/ppermute | solution.py:23
  92.6 17.3 %collective-permute-start.7 = (f32[576,256]{1,0:T(8,128)}, f32[576,256]{1,0:T(8,128)S(1)}, u32[]{:S(2)}, u32[]{:S(2)}) collective-permute-start(f32[576,256]{1,0:T(8,128)} %copy.195), channel_id=1, source_target_pairs={{8,0},{16,8},{24,16},{9,1},{17,9},{25,17},{10,2},{18,10},{26,18},{... | collective-permute-start | bytes 1769480 | tf_op jit(solution)/shard_map/ppermute | solution.py:24
  109.9 21.3 %copy-start.41 = (f32[576,256]{1,0:T(8,128)}, f32[576,256]{1,0:T(8,128)S(1)}, u32[]{:S(2)}) copy-start(f32[576,256]{1,0:T(8,128)S(1)} %collective-permute-done.7) | copy-start | bytes 1769476
  124.7 42.3 %all-to-all-start.3 = ((f32[8,2,4,48,256]{4,3,2,1,0:T(8,128)}), f32[8,2,4,48,256]{4,3,2,1,0:T(8,128)}, u32[]{:S(2)}, u32[]{:S(2)}) async-start(f32[8,2,4,48,256]{4,3,2,1,0:T(8,128)} %fusion.25), calls=%async_computation.3 | async-start | bytes 6291456 | tf_op jit(solution)/shard_map/all_to_all | solution.py:10
  130.6 13.2 %collective-permute-start.8 = (f32[576,256]{1,0:T(8,128)}, f32[576,256]{1,0:T(8,128)S(1)}, u32[]{:S(2)}, u32[]{:S(2)}) collective-permute-start(f32[576,256]{1,0:T(8,128)} %collective-permute-done.6), channel_id=1, source_target_pairs={{8,16},{16,24},{9,17},{17,25},{10,18},{18,26},{11,19},{19,27},{12,... | collective-permute-start | bytes 1769480 | tf_op jit(solution)/shard_map/ppermute | solution.py:23
  131.3 17.4 %collective-permute-start.9 = (f32[576,256]{1,0:T(8,128)S(1)}, f32[576,256]{1,0:T(8,128)}, u32[]{:S(2)}, u32[]{:S(2)}) collective-permute-start(f32[576,256]{1,0:T(8,128)S(1)} %collective-permute-done.7), channel_id=1, source_target_pairs={{8,0},{16,8},{9,1},{17,9},{10,2},{18,10},{11,3},{19,11},{12,4},{20... | collective-permute-start | bytes 1769480 | tf_op jit(solution)/shard_map/ppermute | solution.py:24
  143.8 23.3 %copy-start.43 = (f32[576,256]{1,0:T(8,128)}, f32[576,256]{1,0:T(8,128)S(1)}, u32[]{:S(2)}) copy-start(f32[576,256]{1,0:T(8,128)S(1)} %collective-permute-done.8) | copy-start | bytes 1769476
  167.1 41.5 %all-to-all-start.4 = ((f32[8,2,4,48,256]{4,3,2,1,0:T(8,128)}), f32[8,2,4,48,256]{4,3,2,1,0:T(8,128)S(1)}, u32[]{:S(2)}, u32[]{:S(2)}) async-start(f32[8,2,4,48,256]{4,3,2,1,0:T(8,128)} %fusion.24), calls=%async_computation.4 | async-start | bytes 6291456 | tf_op jit(solution)/shard_map/all_to_all | solution.py:10
  183.9 5.8 collective-permute-start.10
  184.6 17.6 %collective-permute-start.11 = (f32[576,256]{1,0:T(8,128)}, f32[576,256]{1,0:T(8,128)}, u32[]{:S(2)}, u32[]{:S(2)}) collective-permute-start(f32[576,256]{1,0:T(8,128)} %collective-permute-done.9), channel_id=1, source_target_pairs={{8,0},{9,1},{10,2},{11,3},{12,4},{13,5},{14,6},{15,7}} | collective-permute-start | bytes 1769480 | tf_op jit(solution)/shard_map/ppermute | solution.py:24
  221.1 47.1 %all-to-all-start.5 = ((f32[8,2,4,48,256]{4,3,2,1,0:T(8,128)}), f32[8,2,4,48,256]{4,3,2,1,0:T(8,128)}, u32[]{:S(2)}, u32[]{:S(2)}) async-start(f32[8,2,4,48,256]{4,3,2,1,0:T(8,128)} %fusion.22), calls=%async_computation.5 | async-start | bytes 6291456 | tf_op jit(solution)/shard_map/all_to_all | solution.py:10
  268.2 54.8 %all-to-all-start.6 = ((f32[8,2,4,48,256]{4,3,2,1,0:T(8,128)}), f32[8,2,4,48,256]{4,3,2,1,0:T(8,128)}, u32[]{:S(2)}, u32[]{:S(2)}) async-start(f32[8,2,4,48,256]{4,3,2,1,0:T(8,128)} %fusion.21), calls=%async_computation.6 | async-start | bytes 6291456 | tf_op jit(solution)/shard_map/all_to_all | solution.py:10
  275.4 12.0 %copy-start.20 = (f32[1,4,8,48,256]{4,3,2,1,0:T(8,128)}, f32[1,4,8,48,256]{4,3,2,1,0:T(8,128)S(1)}, u32[]{:S(2)}) copy-start(f32[1,4,8,48,256]{4,3,2,1,0:T(8,128)S(1)} %copy.207) | copy-start | bytes 4718596
  275.6 11.9 %copy-start.18 = (f32[1,4,8,48,256]{4,3,2,1,0:T(8,128)}, f32[1,4,8,48,256]{4,3,2,1,0:T(8,128)S(1)}, u32[]{:S(2)}) copy-start(f32[1,4,8,48,256]{4,3,2,1,0:T(8,128)S(1)} %copy.208) | copy-start | bytes 4718596
  287.4 9.7 %copy-start.3 = (f32[1,4,8,48,256]{4,3,2,1,0:T(8,128)S(1)}, f32[1,4,8,48,256]{4,3,2,1,0:T(8,128)}, u32[]{:S(2)}) copy-start(f32[1,4,8,48,256]{4,3,2,1,0:T(8,128)} %copy.203) | copy-start | bytes 4718596
  297.1 14.2 %slice-start.3 = ((s8[9437184]{0:T(1024)(128)(4,1)}), s8[4194304]{0:T(1024)(128)(4,1)S(1)}, s32[]{:S(2)}) async-start(s8[9437184]{0:T(1024)(128)(4,1)} %bitcast.334), calls=%async_computation.19 | async-start | bytes 8388608
  297.1 14.2 %slice-start.4 = ((s8[9437184]{0:T(1024)(128)(4,1)}), s8[4194304]{0:T(1024)(128)(4,1)S(1)}, s32[]{:S(2)}) async-start(s8[9437184]{0:T(1024)(128)(4,1)} %bitcast.334), calls=%async_computation.20 | async-start | bytes 8388608
  326.6 53.8 %all-to-all-start.8 = ((f32[8,2,4,48,256]{4,3,2,1,0:T(8,128)}), f32[8,2,4,48,256]{4,3,2,1,0:T(8,128)}, u32[]{:S(2)}, u32[]{:S(2)}) async-start(f32[8,2,4,48,256]{4,3,2,1,0:T(8,128)} %fusion.23), calls=%async_computation.8 | async-start | bytes 6291456 | tf_op jit(solution)/shard_map/all_to_all | solution.py:10
  342.7 9.8 %copy-start.5 = (f32[1,4,8,48,256]{4,3,2,1,0:T(8,128)S(1)}, f32[1,4,8,48,256]{4,3,2,1,0:T(8,128)}, u32[]{:S(2)}) copy-start(f32[1,4,8,48,256]{4,3,2,1,0:T(8,128)} %copy-done.4) | copy-start | bytes 4718596
  352.5 14.3 %slice-start.6 = ((s8[9437184]{0:T(1024)(128)(4,1)}), s8[4194304]{0:T(1024)(128)(4,1)S(1)}, s32[]{:S(2)}) async-start(s8[9437184]{0:T(1024)(128)(4,1)} %bitcast.339), calls=%async_computation.22 | async-start | bytes 8388608
  352.5 14.3 %slice-start.7 = ((s8[9437184]{0:T(1024)(128)(4,1)}), s8[4194304]{0:T(1024)(128)(4,1)S(1)}, s32[]{:S(2)}) async-start(s8[9437184]{0:T(1024)(128)(4,1)} %bitcast.339), calls=%async_computation.23 | async-start | bytes 8388608
  380.4 42.1 %all-to-all-start.7 = ((f32[8,2,4,48,256]{4,3,2,1,0:T(8,128)}), f32[8,2,4,48,256]{4,3,2,1,0:T(8,128)}, u32[]{:S(2)}, u32[]{:S(2)}) async-start(f32[8,2,4,48,256]{4,3,2,1,0:T(8,128)} %copy.217), calls=%async_computation.7 | async-start | bytes 6291456 | tf_op jit(solution)/shard_map/all_to_all | solution.py:10
  387.6 12.0 %copy-start.13 = (f32[1,4,8,48,256]{4,3,2,1,0:T(8,128)}, f32[1,4,8,48,256]{4,3,2,1,0:T(8,128)S(1)}, u32[]{:S(2)}) copy-start(f32[1,4,8,48,256]{4,3,2,1,0:T(8,128)S(1)} %copy.220) | copy-start | bytes 4718596
  387.7 11.9 %copy-start.11 = (f32[1,4,8,48,256]{4,3,2,1,0:T(8,128)}, f32[1,4,8,48,256]{4,3,2,1,0:T(8,128)S(1)}, u32[]{:S(2)}) copy-start(f32[1,4,8,48,256]{4,3,2,1,0:T(8,128)S(1)} %copy.221) | copy-start | bytes 4718596
  422.5 40.8 %all-to-all-start.10 = ((f32[8,2,4,48,256]{4,3,2,1,0:T(8,128)}), f32[8,2,4,48,256]{4,3,2,1,0:T(8,128)S(1)}, u32[]{:S(2)}, u32[]{:S(2)}) async-start(f32[8,2,4,48,256]{4,3,2,1,0:T(8,128)} %copy.224), calls=%async_computation.10 | async-start | bytes 6291456 | tf_op jit(solution)/shard_map/all_to_all | solution.py:10
  463.3 42.6 %all-to-all-start.9 = ((f32[8,2,4,48,256]{4,3,2,1,0:T(8,128)}), f32[8,2,4,48,256]{4,3,2,1,0:T(8,128)}, u32[]{:S(2)}, u32[]{:S(2)}) async-start(f32[8,2,4,48,256]{4,3,2,1,0:T(8,128)} %copy.223), calls=%async_computation.9 | async-start | bytes 6291456 | tf_op jit(solution)/shard_map/all_to_all | solution.py:10
  474.8 34.9 %copy-start.47 = (s32[8,6]{0,1:T(8,128)S(1)}, s32[8,6]{0,1:T(8,128)}, u32[]{:S(2)}) copy-start(s32[8,6]{0,1:T(8,128)} %copy-done.46) | copy-start | bytes 580
  513.2 48.1 %copy-start.1 = (f32[4,48,256,12]{2,3,1,0:T(8,128)}, f32[4,48,256,12]{2,3,1,0:T(8,128)S(1)}, u32[]{:S(2)}) copy-start(f32[4,48,256,12]{2,3,1,0:T(8,128)S(1)} %fusion.30) | copy-start | bytes 7077892
  519.0 42.4 %all-to-all-start.11 = ((f32[8,2,4,48,256]{4,3,2,1,0:T(8,128)}), f32[8,2,4,48,256]{4,3,2,1,0:T(8,128)}, u32[]{:S(2)}, u32[]{:S(2)}) async-start(f32[8,2,4,48,256]{4,3,2,1,0:T(8,128)} %copy.231), calls=%async_computation.11 | async-start | bytes 6291456 | tf_op jit(solution)/shard_map/all_to_all | solution.py:10
  527.1 14.8 %collective-permute-start.12 = (f32[12,48,256]{2,1,0:T(8,128)}, f32[12,48,256]{2,1,0:T(8,128)}, u32[]{:S(2)}, u32[]{:S(2)}) collective-permute-start(f32[12,48,256]{2,1,0:T(8,128)} %copy.229), channel_id=1, source_target_pairs={{0,8},{1,9},{2,10},{3,11},{4,12},{5,13},{6,14},{7,15}} | collective-permute-start | bytes 1769480 | tf_op jit(solution)/shard_map/ppermute | solution.py:51
  531.7 10.2 %collective-permute-start.13 = (f32[12,48,256]{2,1,0:T(8,128)}, f32[12,48,256]{2,1,0:T(8,128)}, u32[]{:S(2)}, u32[]{:S(2)}) collective-permute-start(f32[12,48,256]{2,1,0:T(8,128)} %copy.230), channel_id=1, source_target_pairs={{24,16},{25,17},{26,18},{27,19},{28,20},{29,21},{30,22},{31,23}} | collective-permute-start | bytes 1769480 | tf_op jit(solution)/shard_map/ppermute | solution.py:52
  566.6 17.8 %slice-start = ((s8[9437184]{0:T(1024)(128)(4,1)}), s8[1048576]{0:T(1024)(128)(4,1)S(1)}, s32[]{:S(2)}) async-start(s8[9437184]{0:T(1024)(128)(4,1)} %bitcast.330), calls=%async_computation.16 | async-start | bytes 2097152
  566.6 42.6 %all-to-all-start.12 = ((f32[8,2,4,48,256]{4,3,2,1,0:T(8,128)}), f32[8,2,4,48,256]{4,3,2,1,0:T(8,128)}, u32[]{:S(2)}, u32[]{:S(2)}) async-start(f32[8,2,4,48,256]{4,3,2,1,0:T(8,128)} %copy.236), calls=%async_computation.12 | async-start | bytes 6291456 | tf_op jit(solution)/shard_map/all_to_all | solution.py:10
  572.7 9.8 %copy-start.35 = (f32[12,48,256]{2,0,1:T(8,128)S(1)}, f32[12,48,256]{2,0,1:T(8,128)}, u32[]{:S(2)}) copy-start(f32[12,48,256]{2,0,1:T(8,128)} %get-tuple-element.78) | copy-start | bytes 1769476
  572.7 11.6 %slice-start.1 = ((s8[9437184]{0:T(1024)(128)(4,1)}), s8[4194304]{0:T(1024)(128)(4,1)S(1)}, s32[]{:S(2)}) async-start(s8[9437184]{0:T(1024)(128)(4,1)} %bitcast.330), calls=%async_computation.17 | async-start | bytes 8388608
  572.7 11.6 %slice-start.2 = ((s8[9437184]{0:T(1024)(128)(4,1)}), s8[4194304]{0:T(1024)(128)(4,1)S(1)}, s32[]{:S(2)}) async-start(s8[9437184]{0:T(1024)(128)(4,1)} %bitcast.330), calls=%async_computation.18 | async-start | bytes 8388608
  580.1 14.6 %collective-permute-start.14 = (f32[12,48,256]{2,1,0:T(8,128)S(1)}, f32[12,48,256]{2,1,0:T(8,128)}, u32[]{:S(2)}, u32[]{:S(2)}) collective-permute-start(f32[12,48,256]{2,1,0:T(8,128)S(1)} %copy.234), channel_id=1, source_target_pairs={{0,8},{8,16},{1,9},{9,17},{2,10},{10,18},{3,11},{11,19},{4,12},{12... | collective-permute-start | bytes 1769480 | tf_op jit(solution)/shard_map/ppermute | solution.py:51
  582.8 11.8 %collective-permute-start.15 = (f32[12,48,256]{2,1,0:T(8,128)S(1)}, f32[12,48,256]{2,1,0:T(8,128)}, u32[]{:S(2)}, u32[]{:S(2)}) collective-permute-start(f32[12,48,256]{2,1,0:T(8,128)S(1)} %copy.235), channel_id=1, source_target_pairs={{16,8},{24,16},{17,9},{25,17},{18,10},{26,18},{19,11},{27,19},{20,... | collective-permute-start | bytes 1769480 | tf_op jit(solution)/shard_map/ppermute | solution.py:52
  588.4 20.8 %copy-start.2 = (f32[4,48,256,12]{2,3,1,0:T(8,128)S(1)}, f32[4,48,256,12]{2,3,1,0:T(8,128)}, u32[]{:S(2)}) copy-start(f32[4,48,256,12]{2,3,1,0:T(8,128)} %copy-done.1) | copy-start | bytes 7077892
  614.5 41.5 %all-to-all-start.13 = ((f32[8,2,4,48,256]{4,3,2,1,0:T(8,128)}), f32[8,2,4,48,256]{4,3,2,1,0:T(8,128)S(1)}, u32[]{:S(2)}, u32[]{:S(2)}) async-start(f32[8,2,4,48,256]{4,3,2,1,0:T(8,128)} %copy.241), calls=%async_computation.13 | async-start | bytes 6291456 | tf_op jit(solution)/shard_map/all_to_all | solution.py:10
  621.0 15.5 %collective-permute-start.16 = (f32[12,48,256]{2,1,0:T(8,128)S(1)}, f32[12,48,256]{2,1,0:T(8,128)S(1)}, u32[]{:S(2)}, u32[]{:S(2)}) collective-permute-start(f32[12,48,256]{2,1,0:T(8,128)S(1)} %copy.239), channel_id=1, source_target_pairs={{0,8},{8,16},{16,24},{1,9},{9,17},{17,25},{2,10},{10,18},{18,26},{... | collective-permute-start | bytes 1769480 | tf_op jit(solution)/shard_map/ppermute | solution.py:51
  624.0 17.2 %collective-permute-start.17 = (f32[12,48,256]{2,1,0:T(8,128)S(1)}, f32[12,48,256]{2,1,0:T(8,128)}, u32[]{:S(2)}, u32[]{:S(2)}) collective-permute-start(f32[12,48,256]{2,1,0:T(8,128)S(1)} %copy.240), channel_id=1, source_target_pairs={{8,0},{16,8},{24,16},{9,1},{17,9},{25,17},{10,2},{18,10},{26,18},{... | collective-permute-start | bytes 1769480 | tf_op jit(solution)/shard_map/ppermute | solution.py:52
  663.3 2.5 collective-permute-start.21
  664.4 14.4 %collective-permute-start.18 = (f32[12,48,256]{2,1,0:T(8,128)S(1)}, f32[12,48,256]{2,1,0:T(8,128)S(1)}, u32[]{:S(2)}, u32[]{:S(2)}) collective-permute-start(f32[12,48,256]{2,1,0:T(8,128)S(1)} %copy.248), channel_id=1, source_target_pairs={{0,8},{1,9},{2,10},{3,11},{4,12},{5,13},{6,14},{7,15}} | collective-permute-start | bytes 1769480 | tf_op jit(solution)/shard_map/ppermute | solution.py:51
  666.2 35.8 %copy-start.37 = (f32[1,48,256,12]{2,3,1,0:T(8,128)S(1)}, f32[1,48,256,12]{2,3,1,0:T(8,128)}, u32[]{:S(2)}) copy-start(f32[1,48,256,12]{2,3,1,0:T(8,128)} %get-tuple-element.92) | copy-start | bytes 1769476
  666.2 35.8 %copy-start.40 = (f32[12,48,256]{2,1,0:T(8,128)S(1)}, f32[12,48,256]{2,1,0:T(8,128)}, u32[]{:S(2)}) copy-start(f32[12,48,256]{2,1,0:T(8,128)} %copy-done.39) | copy-start | bytes 1769476
  666.2 17.3 %collective-permute-start.22 = (f32[12,48,256]{2,1,0:T(8,128)S(1)}, f32[12,48,256]{2,1,0:T(8,128)S(1)}, u32[]{:S(2)}, u32[]{:S(2)}) collective-permute-start(f32[12,48,256]{2,1,0:T(8,128)S(1)} %fusion.34), channel_id=1, source_target_pairs={{16,8},{24,16},{17,9},{25,17},{18,10},{26,18},{19,11},{27,19},{20,... | collective-permute-start | bytes 1769480 | tf_op jit(solution)/shard_map/ppermute | solution.py:52
  679.1 16.5 %collective-permute-start.19 = (f32[12,48,256]{2,1,0:T(8,128)S(1)}, f32[12,48,256]{2,1,0:T(8,128)S(1)}, u32[]{:S(2)}, u32[]{:S(2)}) collective-permute-start(f32[12,48,256]{2,1,0:T(8,128)S(1)} %fusion.36), channel_id=1, source_target_pairs={{0,8},{8,16},{1,9},{9,17},{2,10},{10,18},{3,11},{11,19},{4,12},{12... | collective-permute-start | bytes 1769480 | tf_op jit(solution)/shard_map/ppermute | solution.py:51
  684.7 27.1 %collective-permute-start.23 = (f32[12,48,256]{2,1,0:T(8,128)}, f32[12,48,256]{2,1,0:T(8,128)}, u32[]{:S(2)}, u32[]{:S(2)}) collective-permute-start(f32[12,48,256]{2,1,0:T(8,128)} %fusion.33), channel_id=1, source_target_pairs={{8,0},{16,8},{24,16},{9,1},{17,9},{25,17},{10,2},{18,10},{26,18},{... | collective-permute-start | bytes 1769480 | tf_op jit(solution)/shard_map/ppermute | solution.py:52
  696.8 16.0 %collective-permute-start.20 = (f32[12,48,256]{2,1,0:T(8,128)}, f32[12,48,256]{2,1,0:T(8,128)}, u32[]{:S(2)}, u32[]{:S(2)}) collective-permute-start(f32[12,48,256]{2,1,0:T(8,128)} %fusion.35), channel_id=1, source_target_pairs={{0,8},{8,16},{16,24},{1,9},{9,17},{17,25},{2,10},{10,18},{18,26},{... | collective-permute-start | bytes 1769480 | tf_op jit(solution)/shard_map/ppermute | solution.py:51
  707.6 13.1 %all-to-all-start.14 = ((f32[576,8,32]{0,2,1:T(8,128)}), f32[576,8,32]{0,2,1:T(8,128)}, u32[]{:S(2)}, u32[]{:S(2)}) async-start(f32[576,8,32]{0,2,1:T(8,128)} %copy.271), calls=%async_computation.14 | async-start | bytes 1310720 | tf_op jit(solution)/shard_map/all_to_all | solution.py:139
  720.7 14.6 %all-to-all-start.15 = ((f32[576,8,32]{0,2,1:T(8,128)}), f32[576,8,32]{0,2,1:T(8,128)S(1)}, u32[]{:S(2)}, u32[]{:S(2)}) async-start(f32[576,8,32]{0,2,1:T(8,128)} %copy.272), calls=%async_computation.15 | async-start | bytes 1310720 | tf_op jit(solution)/shard_map/all_to_all | solution.py:139
  (41 other events, 164.8 us)

commit v11 on v9

--- a/solution.py
+++ b/solution.py
@@ -33,7 +33,7 @@
     return spare[:count], carried
 
 
-def line_reduce(parts, axis, count, riders=()):
+def line_reduce(parts, axis, count, riders=(), exchange=band_exchange):
     index = lax.axis_index(axis)
 
     def part_for(target):
@@ -51,9 +51,9 @@
         rightward = lax.ppermute(send_right, axis, [(i, i + 1) for i in range(0, step)])
         leftward = lax.ppermute(send_left, axis, [(i, i - 1) for i in range(count - step, count)])
         if rider:
-            rightward, leftward, load = lax.optimization_barrier((rightward, leftward, band_exchange(load)))
+            rightward, leftward, load = lax.optimization_barrier((rightward, leftward, exchange(load)))
             carried.append(load)
-    carried += [band_exchange(load) for load in riders[len(carried):]]
+    carried += [exchange(load) for load in riders[len(carried):]]
     return part_for(index) + rightward + leftward, carried
 
 
@@ -126,14 +126,14 @@
         return jnp.einsum("srk,srgpn->gkpn", one_hot, gathered, precision=lax.Precision.HIGHEST)
 
     first_home, second_returned = line_reduce(sum_blocks(returned[0]), "grp", group_count, held)
-    second_home, _ = line_reduce(sum_blocks(second_returned), "grp", group_count)
-    home = [
-        lax.all_to_all(
-            rows.reshape(block_count * piece_rows, half), "band", split_axis=1, concat_axis=0, tiled=True
-        )
-        for rows in (first_home, second_home)
-    ]
-    return jnp.concatenate(home, axis=1)
+    def home_rows(rows):
+        rows = rows.reshape(block_count * piece_rows, half)
+        return lax.all_to_all(rows, "band", split_axis=1, concat_axis=0, tiled=True)
+
+    second_home, first_home = line_reduce(
+        sum_blocks(second_returned), "grp", group_count, [first_home], home_rows
+    )
+    return jnp.concatenate([first_home[0], home_rows(second_home)], axis=1)
 
 
 def solution(mesh):

time: 723 us -> 730 us (level)
  blocking collectives: 13.7 us -> 40.9 us
  starting transfers between devices: 129 us -> 120 us
  waiting for transfers between devices: 229 us -> 220 us
    all_to_all x0 -> x2, blocking collectives: none -> 27.1 us  [home_rows(): return lax.all_to_all(rows, 'band', split_axis=1, concat_axis=0, tiled=True)]
    all_to_all x2 -> x0, waiting for transfers between devices: 8.06 us -> none  [body(): lax.all_to_all(rows.reshape(block_count * piece_rows, half), 'band', spli...]
    all_to_all x2 -> x0, starting transfers between devices: 7.69 us -> none  [body(): lax.all_to_all(rows.reshape(block_count * piece_rows, half), 'band', spli...]
    optimization_barrier x9 -> x12, local copies, waits for them, and re-layouts: 10.3 us -> 15.9 us  [line_reduce(): lax.optimization_barrier((send_right, send_left, riders[step - 1]))]
  transfers between devices with their start and end apart: 39 -> 37, of which waited for: 23 -> 24; matrix products, arithmetic and copies ran while one was open for 38% -> 36% of each run, Pallas kernels for 0% -> 0%
where the time goes in v11:
time: 730 us; the launch traced here: 718 us
  waiting for transfers between devices  220 us (30%)
  local copies, waits for them, and re-layouts  156 us (21%)
  matrix products  129 us (18%)
  starting transfers between devices  120 us (16%)
  other arithmetic  47 us (6%)
  blocking collectives  40.9 us (6%)
    all_to_all x12, waiting for transfers between devices, band_exchange(): lax.all_to_all(outgoing, 'band', split_axis=0, concat_axis=0, tiled=True)  124 us
    all_to_all x12, starting transfers between devices, band_exchange(): lax.all_to_all(outgoing, 'band', split_axis=0, concat_axis=0, tiled=True)  68.1 us
    ppermute x6, waiting for transfers between devices, line_gather(): lax.ppermute(leftward, axis, [(i + 1, i) for i in range(0, count - step)])  53.2 us
    dot_general x6, matrix products, body(): jnp.dot(r[0], r[1].T, precision=PRECISION, preferred_element_type=jnp.flo...  52 us
    dot_general x6, matrix products, body(): jnp.dot(kernel, rows[h][1], precision=PRECISION, preferred_element_type=j...  42.2 us
    ppermute x6, waiting for transfers between devices, line_reduce(): lax.ppermute(send_right, axis, [(i, i + 1) for i in range(0, step)])  33.8 us
    dot_general x3, local copies, waits for them, and re-layouts, body(): jnp.dot(kernel.T, rows[h][0], precision=PRECISION, preferred_element_type...  29.1 us
    dot_general x6, matrix products, body(): jnp.dot(kernel.T, rows[h][0], precision=PRECISION, preferred_element_type...  27.6 us
  transfers between devices with their start and end apart: 37, of which 24 were waited for; matrix products, arithmetic and copies ran while one was open for 36% of the time, Pallas kernels for 0%

profile of v11, /device:TPU:2, one launch (start us, length us, event | category | flops | bytes accessed | tf_op | source)
XLA Modules:
  0.0 718.1 jit_solution(8600504466140210168)
XLA Ops:
  1.7 13.7 %all_to_all.136 = f32[8,576,32]{1,2,0:T(8,128)S(1)} all-to-all(f32[8,576,32]{1,2,0:T(8,128)S(1)} %copy.186), channel_id=1, replica_groups=mesh['grp'=4,'band'=8] {'band'}, dimensions={0} | all-to-all | bytes 1179648 | tf_op jit(solution)/shard_map/all_to_all | solution.py:72
  16.5 4.3 collective-permute-start
  21.9 4.9 all-to-all-start
  35.4 9.0 %collective-permute-done.1 = f32[576,256]{1,0:T(8,128)S(1)} collective-permute-done((f32[576,256]{1,0:T(8,128)}, f32[576,256]{1,0:T(8,128)S(1)}, u32[]{:S(2)}, u32[]{:S(2)}) %collective-permute-start.1) | collective-permute-done | bytes 589856 | tf_op jit(solution)/shard_map/ppermute | solution.py:24
  47.9 12.9 %collective-permute-done.3 = f32[576,256]{1,0:T(8,128)S(1)} collective-permute-done((f32[576,256]{1,0:T(8,128)S(1)}, f32[576,256]{1,0:T(8,128)S(1)}, u32[]{:S(2)}, u32[]{:S(2)}) %collective-permute-start.3) | collective-permute-done | bytes 589856 | tf_op jit(solution)/shard_map/ppermute | solution.py:24
  63.3 13.0 %collective-permute-done.5 = f32[576,256]{1,0:T(8,128)S(1)} collective-permute-done((f32[576,256]{1,0:T(8,128)S(1)}, f32[576,256]{1,0:T(8,128)S(1)}, u32[]{:S(2)}, u32[]{:S(2)}) %collective-permute-start.5) | collective-permute-done | bytes 589856 | tf_op jit(solution)/shard_map/ppermute | solution.py:24
  83.0 5.2 all-to-all-start.2
  91.6 4.6 collective-permute-start.6
  101.3 4.1 fusion.25
  109.1 15.6 %all-to-all-done.2 = f32[8,2,4,48,256]{4,3,2,1,0:T(8,128)} async-done(((f32[8,2,4,48,256]{4,3,2,1,0:T(8,128)}), f32[8,2,4,48,256]{4,3,2,1,0:T(8,128)}, u32[]{:S(2)}, u32[]{:S(2)}) %all-to-all-start.2) | async-done | bytes 3145760 | tf_op jit(solution)/shard_map/all_to_all | solution.py:10
  124.7 5.9 all-to-all-start.3
  145.0 4.4 collective-permute-done.9
  149.4 17.6 %all-to-all-done.3 = f32[8,2,4,48,256]{4,3,2,1,0:T(8,128)} async-done(((f32[8,2,4,48,256]{4,3,2,1,0:T(8,128)}), f32[8,2,4,48,256]{4,3,2,1,0:T(8,128)}, u32[]{:S(2)}, u32[]{:S(2)}) %all-to-all-start.3) | async-done | bytes 3145760 | tf_op jit(solution)/shard_map/all_to_all | solution.py:10
  167.0 5.1 all-to-all-start.4
  182.3 11.5 %collective-permute-done.11 = f32[576,256]{1,0:T(8,128)} collective-permute-done((f32[576,256]{1,0:T(8,128)}, f32[576,256]{1,0:T(8,128)}, u32[]{:S(2)}, u32[]{:S(2)}) %collective-permute-start.11) | collective-permute-done | bytes 589856 | tf_op jit(solution)/shard_map/ppermute | solution.py:24
  193.8 14.7 %all-to-all-done.4 = f32[8,2,4,48,256]{4,3,2,1,0:T(8,128)S(1)} async-done(((f32[8,2,4,48,256]{4,3,2,1,0:T(8,128)}), f32[8,2,4,48,256]{4,3,2,1,0:T(8,128)S(1)}, u32[]{:S(2)}, u32[]{:S(2)}) %all-to-all-start.4) | async-done | bytes 3145760 | tf_op jit(solution)/shard_map/all_to_all | solution.py:10
  221.0 6.0 all-to-all-start.9
  237.8 25.6 %all-to-all-done.9 = f32[8,2,4,48,256]{4,3,2,1,0:T(8,128)} async-done(((f32[8,2,4,48,256]{4,3,2,1,0:T(8,128)}), f32[8,2,4,48,256]{4,3,2,1,0:T(8,128)}, u32[]{:S(2)}, u32[]{:S(2)}) %all-to-all-start.9) | async-done | bytes 3145760 | tf_op jit(solution)/shard_map/all_to_all | solution.py:10
  263.4 6.2 all-to-all-start.7
  272.1 6.4 fusion.56
  282.6 6.4 fusion.57
  297.5 6.4 fusion.58
  306.1 6.4 all-to-all-start.5
  318.3 9.7 %fusion = f32[1536,1536]{1,0:T(8,128)} fusion(f32[1536,1536]{1,0:T(8,128)S(1)} %copy-done.3, f32[1536,256]{1,0:T(8,128)S(1)} %bitcast.365, f32[1536,256]{1,0:T(8,128)S(1)} %bitcast.367, f32[3,1536,1536]{2,1,0:T(8,128)} %param.7), kind=kOutput, calls=%fused_computation.7 | convolution fusion | flops 3628597248 | bytes 31457280 | tf_op jit(solution)/shard_map/dot_general | solution.py:108
  328.0 9.7 %copy.223 = f32[1536,1536]{1,0:T(8,128)} copy(f32[1536,1536]{0,1:T(8,128)} %bitcast.328) | data formatting | bytes 18874368 | tf_op jit(solution)/shard_map/dot_general | solution.py:114
  337.7 6.9 convolution_bitcast_fusion.7
  344.6 4.0 convolution_bitcast_fusion.6
  351.0 4.6 all-to-all-start.10
  358.1 11.9 %fusion.2 = f32[1536,1536]{1,0:T(8,128)} fusion(f32[1536,1536]{1,0:T(8,128)} %fusion.56, f32[1536,256]{1,0:T(8,128)S(1)} %bitcast.375, f32[1536,256]{1,0:T(8,128)S(1)} %bitcast.373, f32[3,1536,1536]{2,1,0:T(8,128)} %param.7), kind=kOutput, calls=%fused_computation.11 | convolution fusion | flops 3628597248 | bytes 31457280 | tf_op jit(solution)/shard_map/dot_general | solution.py:108
  370.0 9.7 %copy.207 = f32[1536,1536]{1,0:T(8,128)} copy(f32[1536,1536]{0,1:T(8,128)} %bitcast.334) | data formatting | bytes 18874368 | tf_op jit(solution)/shard_map/dot_general | solution.py:114
  379.7 7.0 convolution_bitcast_fusion.11
  386.6 4.1 convolution_bitcast_fusion.10
  393.2 5.1 all-to-all-start.6
  400.6 11.3 %fusion.1 = f32[1536,1536]{1,0:T(8,128)} fusion(f32[1536,1536]{1,0:T(8,128)} %fusion.57, f32[1536,256]{1,0:T(8,128)S(1)} %bitcast.369, f32[1536,256]{1,0:T(8,128)S(1)} %bitcast.371, f32[3,1536,1536]{2,1,0:T(8,128)} %param.7), kind=kOutput, calls=%fused_computation.9 | convolution fusion | flops 3628597248 | bytes 31457280 | tf_op jit(solution)/shard_map/dot_general | solution.py:108
  411.9 9.7 %copy.215 = f32[1536,1536]{1,0:T(8,128)} copy(f32[1536,1536]{0,1:T(8,128)} %bitcast.331) | data formatting | bytes 18874368 | tf_op jit(solution)/shard_map/dot_general | solution.py:114
  421.6 6.9 convolution_bitcast_fusion.9
  428.6 4.1 convolution_bitcast_fusion.8
  435.1 5.4 all-to-all-start.8
  440.5 6.9 convolution_bitcast_fusion.5
  447.5 7.3 %convolution_bitcast_fusion.4 = f32[1,4,8,48,256]{4,3,2,1,0:T(8,128)S(1)} fusion(f32[4,8,48,1536]{3,2,1,0:T(8,128)} %bitcast.345, f32[1536,256,1,1]{1,0,3,2:T(8,128)S(1)} %bitcast.376), kind=kOutput, calls=%fused_computation.54 | convolution fusion | flops 3623878656 | bytes 12582912 | tf_op jit(solution)/shard_map/dot_general | solution.py:114
  456.7 5.4 copy.227
  462.1 5.4 copy.225
  467.4 9.6 %all-to-all-done.8 = f32[8,2,4,48,256]{4,3,2,1,0:T(8,128)} async-done(((f32[8,2,4,48,256]{4,3,2,1,0:T(8,128)}), f32[8,2,4,48,256]{4,3,2,1,0:T(8,128)}, u32[]{:S(2)}, u32[]{:S(2)}) %all-to-all-start.8) | async-done | bytes 3145760 | tf_op jit(solution)/shard_map/all_to_all | solution.py:10
  490.0 6.2 all-to-all-start.11
  496.3 7.4 %convolution_bitcast_fusion.3 = f32[1,4,8,48,256]{4,3,2,1,0:T(8,128)S(1)} fusion(f32[4,8,48,1536]{3,2,1,0:T(8,128)} %bitcast.333, f32[1536,256,1,1]{1,0,3,2:T(8,128)} %bitcast.372), kind=kOutput, calls=%fused_computation.53 | convolution fusion | flops 3623878656 | bytes 12582912 | tf_op jit(solution)/shard_map/dot_general | solution.py:113
  508.2 4.0 convolution_bitcast_fusion.2
  514.4 6.0 collective-permute-done.12
  520.4 12.3 %all-to-all-done.11 = f32[8,2,4,48,256]{4,3,2,1,0:T(8,128)} async-done(((f32[8,2,4,48,256]{4,3,2,1,0:T(8,128)}), f32[8,2,4,48,256]{4,3,2,1,0:T(8,128)}, u32[]{:S(2)}, u32[]{:S(2)}) %all-to-all-start.11) | async-done | bytes 3145760 | tf_op jit(solution)/shard_map/all_to_all | solution.py:10
  538.0 6.1 all-to-all-start.12
  544.2 7.0 convolution_bitcast_fusion.1
  555.9 4.1 convolution_bitcast_fusion
  562.0 5.8 collective-permute-done.14
  567.8 12.8 %all-to-all-done.12 = f32[8,2,4,48,256]{4,3,2,1,0:T(8,128)} async-done(((f32[8,2,4,48,256]{4,3,2,1,0:T(8,128)}), f32[8,2,4,48,256]{4,3,2,1,0:T(8,128)}, u32[]{:S(2)}, u32[]{:S(2)}) %all-to-all-start.12) | async-done | bytes 3145760 | tf_op jit(solution)/shard_map/all_to_all | solution.py:10
  585.9 5.8 all-to-all-start.13
  597.7 5.4 collective-permute-start.16
  603.0 5.4 copy.241
  608.4 5.4 copy.242
  615.1 13.1 %all-to-all-done.13 = f32[8,2,4,48,256]{4,3,2,1,0:T(8,128)} async-done(((f32[8,2,4,48,256]{4,3,2,1,0:T(8,128)}), f32[8,2,4,48,256]{4,3,2,1,0:T(8,128)}, u32[]{:S(2)}, u32[]{:S(2)}) %all-to-all-start.13) | async-done | bytes 3145760 | tf_op jit(solution)/shard_map/all_to_all | solution.py:10
  649.0 13.7 %all_to_all.137 = f32[576,8,32]{0,2,1:T(8,128)S(1)} all-to-all(f32[576,8,32]{0,2,1:T(8,128)S(1)} %all_to_all.112), channel_id=1, replica_groups=mesh['grp'=4,'band'=8] {'band'}, dimensions={1} | all-to-all | bytes 1179648 | tf_op jit(solution)/shard_map/all_to_all | solution.py:131
  669.3 10.6 %collective-permute-done.20 = f32[12,48,256]{2,1,0:T(8,128)S(1)} collective-permute-done((f32[12,48,256]{2,1,0:T(8,128)S(1)}, f32[12,48,256]{2,1,0:T(8,128)S(1)}, u32[]{:S(2)}, u32[]{:S(2)}) %collective-permute-start.20) | collective-permute-done | bytes 589856 | tf_op jit(solution)/shard_map/ppermute | solution.py:51
  680.2 4.4 collective-permute-start.21
  686.4 10.2 %collective-permute-done.21 = f32[12,48,256]{2,1,0:T(8,128)S(1)} collective-permute-done((f32[12,48,256]{2,1,0:T(8,128)S(1)}, f32[12,48,256]{2,1,0:T(8,128)S(1)}, u32[]{:S(2)}, u32[]{:S(2)}) %collective-permute-start.21) | collective-permute-done | bytes 589856 | tf_op jit(solution)/shard_map/ppermute | solution.py:51
  696.6 4.5 collective-permute-done.23
  702.9 13.4 %all_to_all.138 = f32[576,8,32]{0,2,1:T(8,128)S(1)} all-to-all(f32[576,8,32]{0,2,1:T(8,128)S(1)} %copy.272), channel_id=1, replica_groups=mesh['grp'=4,'band'=8] {'band'}, dimensions={1} | all-to-all | bytes 1179648 | tf_op jit(solution)/shard_map/all_to_all | solution.py:131
  (304 shorter events, 194.7 us)
Async XLA Ops:
  1.7 25.2 %copy-start.57 = (s32[32,6]{0,1:T(8,128)S(1)}, s32[32,6]{0,1:T(8,128)}, u32[]{:S(2)}) copy-start(s32[32,6]{0,1:T(8,128)} %param.6) | copy-start | bytes 2308
  16.5 16.3 %collective-permute-start = (f32[576,256]{1,0:T(8,128)}, f32[576,256]{1,0:T(8,128)}, u32[]{:S(2)}, u32[]{:S(2)}) collective-permute-start(f32[576,256]{1,0:T(8,128)} %copy.188), channel_id=1, source_target_pairs={{0,8},{8,16},{16,24},{1,9},{9,17},{17,25},{2,10},{10,18},{18,26},{... | collective-permute-start | bytes 1769480 | tf_op jit(solution)/shard_map/ppermute | solution.py:23
  21.9 61.1 %all-to-all-start = ((f32[8,576,32]{1,2,0:T(8,128)}), f32[8,576,32]{1,2,0:T(8,128)S(1)}, u32[]{:S(2)}, u32[]{:S(2)}) async-start(f32[8,576,32]{1,2,0:T(8,128)} %copy.184), calls=%async_computation | async-start | bytes 1310720 | tf_op jit(solution)/shard_map/all_to_all | solution.py:72
  26.9 20.2 %copy-start.52 = (s32[8,6]{0,1:T(8,128)}, s32[8,6]{0,1:T(8,128)S(1)}, u32[]{:S(2)}) copy-start(s32[8,6]{0,1:T(8,128)S(1)} %get-tuple-element.91) | copy-start | bytes 580
  26.9 17.5 %collective-permute-start.1 = (f32[576,256]{1,0:T(8,128)}, f32[576,256]{1,0:T(8,128)S(1)}, u32[]{:S(2)}, u32[]{:S(2)}) collective-permute-start(f32[576,256]{1,0:T(8,128)} %copy.188), channel_id=1, source_target_pairs={{8,0},{16,8},{24,16},{9,1},{17,9},{25,17},{10,2},{18,10},{26,18},{... | collective-permute-start | bytes 1769480 | tf_op jit(solution)/shard_map/ppermute | solution.py:24
  32.7 14.4 %collective-permute-start.2 = (f32[576,256]{1,0:T(8,128)}, f32[576,256]{1,0:T(8,128)}, u32[]{:S(2)}, u32[]{:S(2)}) collective-permute-start(f32[576,256]{1,0:T(8,128)} %collective-permute-done), channel_id=1, source_target_pairs={{8,16},{16,24},{9,17},{17,25},{10,18},{18,26},{11,19},{19,27},{12,... | collective-permute-start | bytes 1769480 | tf_op jit(solution)/shard_map/ppermute | solution.py:23
  34.9 44.1 %copy-start.59 = (pred[8,2]{1,0:T(8,128)(4,1)}, pred[8,2]{1,0:T(8,128)(4,1)S(1)}, u32[]{:S(2)}) copy-start(pred[8,2]{1,0:T(8,128)(4,1)S(1)} %copy.185) | copy-start | bytes 52
  44.4 16.4 %collective-permute-start.3 = (f32[576,256]{1,0:T(8,128)S(1)}, f32[576,256]{1,0:T(8,128)S(1)}, u32[]{:S(2)}, u32[]{:S(2)}) collective-permute-start(f32[576,256]{1,0:T(8,128)S(1)} %collective-permute-done.1), channel_id=1, source_target_pairs={{8,0},{16,8},{9,1},{17,9},{10,2},{18,10},{11,3},{19,11},{12,4},{20... | collective-permute-start | bytes 1769480 | tf_op jit(solution)/shard_map/ppermute | solution.py:24
  47.1 16.2 %collective-permute-start.4 = (f32[576,256]{1,0:T(8,128)}, f32[576,256]{1,0:T(8,128)S(1)}, u32[]{:S(2)}, u32[]{:S(2)}) collective-permute-start(f32[576,256]{1,0:T(8,128)} %collective-permute-done.2), channel_id=1, source_target_pairs={{16,24},{17,25},{18,26},{19,27},{20,28},{21,29},{22,30},{23,31}} | collective-permute-start | bytes 1769480 | tf_op jit(solution)/shard_map/ppermute | solution.py:23
  60.8 15.5 %collective-permute-start.5 = (f32[576,256]{1,0:T(8,128)S(1)}, f32[576,256]{1,0:T(8,128)S(1)}, u32[]{:S(2)}, u32[]{:S(2)}) collective-permute-start(f32[576,256]{1,0:T(8,128)S(1)} %collective-permute-done.3), channel_id=1, source_target_pairs={{8,0},{9,1},{10,2},{11,3},{12,4},{13,5},{14,6},{15,7}} | collective-permute-start | bytes 1769480 | tf_op jit(solution)/shard_map/ppermute | solution.py:24
  83.0 13.2 %copy-start.64 = (pred[8,2]{0,1:T(4,128)(4,1)S(1)}, pred[8,2]{0,1:T(4,128)(4,1)}, u32[]{:S(2)}) copy-start(pred[8,2]{0,1:T(4,128)(4,1)} %get-tuple-element.126) | copy-start | bytes 52
  83.0 41.7 %all-to-all-start.2 = ((f32[8,2,4,48,256]{4,3,2,1,0:T(8,128)}), f32[8,2,4,48,256]{4,3,2,1,0:T(8,128)}, u32[]{:S(2)}, u32[]{:S(2)}) async-start(f32[8,2,4,48,256]{4,3,2,1,0:T(8,128)} %fusion.26), calls=%async_computation.2 | async-start | bytes 6291456 | tf_op jit(solution)/shard_map/all_to_all | solution.py:10
  90.3 17.5 %collective-permute-start.7 = (f32[576,256]{1,0:T(8,128)}, f32[576,256]{1,0:T(8,128)S(1)}, u32[]{:S(2)}, u32[]{:S(2)}) collective-permute-start(f32[576,256]{1,0:T(8,128)} %copy.193), channel_id=1, source_target_pairs={{8,0},{16,8},{24,16},{9,1},{17,9},{25,17},{10,2},{18,10},{26,18},{... | collective-permute-start | bytes 1769480 | tf_op jit(solution)/shard_map/ppermute | solution.py:24
  91.6 17.5 %collective-permute-start.6 = (f32[576,256]{1,0:T(8,128)}, f32[576,256]{1,0:T(8,128)S(1)}, u32[]{:S(2)}, u32[]{:S(2)}) collective-permute-start(f32[576,256]{1,0:T(8,128)} %copy.192), channel_id=1, source_target_pairs={{0,8},{8,16},{16,24},{1,9},{9,17},{17,25},{2,10},{10,18},{18,26},{... | collective-permute-start | bytes 1769480 | tf_op jit(solution)/shard_map/ppermute | solution.py:23
  105.4 27.9 %copy-start.63 = (pred[8,2]{0,1:T(4,128)(4,1)S(1)}, pred[8,2]{0,1:T(4,128)(4,1)}, u32[]{:S(2)}) copy-start(pred[8,2]{0,1:T(4,128)(4,1)} %get-tuple-element.125) | copy-start | bytes 52
  107.8 24.2 %copy-start.47 = (f32[576,256]{1,0:T(8,128)}, f32[576,256]{1,0:T(8,128)S(1)}, u32[]{:S(2)}) copy-start(f32[576,256]{1,0:T(8,128)S(1)} %collective-permute-done.7) | copy-start | bytes 1769476
  109.1 21.5 %copy-start.49 = (f32[576,256]{1,0:T(8,128)}, f32[576,256]{1,0:T(8,128)S(1)}, u32[]{:S(2)}) copy-start(f32[576,256]{1,0:T(8,128)S(1)} %collective-permute-done.6) | copy-start | bytes 1769476
  124.7 42.4 %all-to-all-start.3 = ((f32[8,2,4,48,256]{4,3,2,1,0:T(8,128)}), f32[8,2,4,48,256]{4,3,2,1,0:T(8,128)}, u32[]{:S(2)}, u32[]{:S(2)}) async-start(f32[8,2,4,48,256]{4,3,2,1,0:T(8,128)} %fusion.25), calls=%async_computation.3 | async-start | bytes 6291456 | tf_op jit(solution)/shard_map/all_to_all | solution.py:10
  130.6 14.5 %collective-permute-start.8 = (f32[576,256]{1,0:T(8,128)S(1)}, f32[576,256]{1,0:T(8,128)}, u32[]{:S(2)}, u32[]{:S(2)}) collective-permute-start(f32[576,256]{1,0:T(8,128)S(1)} %collective-permute-done.6), channel_id=1, source_target_pairs={{8,16},{16,24},{9,17},{17,25},{10,18},{18,26},{11,19},{19,27},{12,... | collective-permute-start | bytes 1769480 | tf_op jit(solution)/shard_map/ppermute | solution.py:23
  132.0 17.4 %collective-permute-start.9 = (f32[576,256]{1,0:T(8,128)S(1)}, f32[576,256]{1,0:T(8,128)}, u32[]{:S(2)}, u32[]{:S(2)}) collective-permute-start(f32[576,256]{1,0:T(8,128)S(1)} %collective-permute-done.7), channel_id=1, source_target_pairs={{8,0},{16,8},{9,1},{17,9},{10,2},{18,10},{11,3},{19,11},{12,4},{20... | collective-permute-start | bytes 1769480 | tf_op jit(solution)/shard_map/ppermute | solution.py:24
  167.0 41.5 %all-to-all-start.4 = ((f32[8,2,4,48,256]{4,3,2,1,0:T(8,128)}), f32[8,2,4,48,256]{4,3,2,1,0:T(8,128)S(1)}, u32[]{:S(2)}, u32[]{:S(2)}) async-start(f32[8,2,4,48,256]{4,3,2,1,0:T(8,128)} %fusion.24), calls=%async_computation.4 | async-start | bytes 6291456 | tf_op jit(solution)/shard_map/all_to_all | solution.py:10
  175.5 4.3 collective-permute-start.10
  176.3 17.6 %collective-permute-start.11 = (f32[576,256]{1,0:T(8,128)}, f32[576,256]{1,0:T(8,128)}, u32[]{:S(2)}, u32[]{:S(2)}) collective-permute-start(f32[576,256]{1,0:T(8,128)} %collective-permute-done.9), channel_id=1, source_target_pairs={{8,0},{9,1},{10,2},{11,3},{12,4},{13,5},{14,6},{15,7}} | collective-permute-start | bytes 1769480 | tf_op jit(solution)/shard_map/ppermute | solution.py:24
  221.0 42.5 %all-to-all-start.9 = ((f32[8,2,4,48,256]{4,3,2,1,0:T(8,128)}), f32[8,2,4,48,256]{4,3,2,1,0:T(8,128)}, u32[]{:S(2)}, u32[]{:S(2)}) async-start(f32[8,2,4,48,256]{4,3,2,1,0:T(8,128)} %fusion.21), calls=%async_computation.9 | async-start | bytes 6291456 | tf_op jit(solution)/shard_map/all_to_all | solution.py:10
  263.4 42.7 %all-to-all-start.7 = ((f32[8,2,4,48,256]{4,3,2,1,0:T(8,128)}), f32[8,2,4,48,256]{4,3,2,1,0:T(8,128)}, u32[]{:S(2)}, u32[]{:S(2)}) async-start(f32[8,2,4,48,256]{4,3,2,1,0:T(8,128)} %fusion.22), calls=%async_computation.7 | async-start | bytes 6291456 | tf_op jit(solution)/shard_map/all_to_all | solution.py:10
  306.1 44.9 %all-to-all-start.5 = ((f32[8,2,4,48,256]{4,3,2,1,0:T(8,128)}), f32[8,2,4,48,256]{4,3,2,1,0:T(8,128)}, u32[]{:S(2)}, u32[]{:S(2)}) async-start(f32[8,2,4,48,256]{4,3,2,1,0:T(8,128)} %fusion.23), calls=%async_computation.5 | async-start | bytes 6291456 | tf_op jit(solution)/shard_map/all_to_all | solution.py:10
  315.0 13.0 %copy-start.17 = (f32[1,4,8,48,256]{4,3,2,1,0:T(8,128)}, f32[1,4,8,48,256]{4,3,2,1,0:T(8,128)S(1)}, u32[]{:S(2)}) copy-start(f32[1,4,8,48,256]{4,3,2,1,0:T(8,128)S(1)} %copy.222) | copy-start | bytes 4718596
  315.1 12.9 %copy-start.15 = (f32[1,4,8,48,256]{4,3,2,1,0:T(8,128)}, f32[1,4,8,48,256]{4,3,2,1,0:T(8,128)S(1)}, u32[]{:S(2)}) copy-start(f32[1,4,8,48,256]{4,3,2,1,0:T(8,128)S(1)} %copy.221) | copy-start | bytes 4718596
  351.0 42.2 %all-to-all-start.10 = ((f32[8,2,4,48,256]{4,3,2,1,0:T(8,128)}), f32[8,2,4,48,256]{4,3,2,1,0:T(8,128)}, u32[]{:S(2)}, u32[]{:S(2)}) async-start(f32[8,2,4,48,256]{4,3,2,1,0:T(8,128)} %copy.224), calls=%async_computation.10 | async-start | bytes 6291456 | tf_op jit(solution)/shard_map/all_to_all | solution.py:10
  358.0 12.0 %copy-start.20 = (f32[1,4,8,48,256]{4,3,2,1,0:T(8,128)}, f32[1,4,8,48,256]{4,3,2,1,0:T(8,128)S(1)}, u32[]{:S(2)}) copy-start(f32[1,4,8,48,256]{4,3,2,1,0:T(8,128)S(1)} %copy.206) | copy-start | bytes 4718596
  358.1 11.9 %copy-start.22 = (f32[1,4,8,48,256]{4,3,2,1,0:T(8,128)}, f32[1,4,8,48,256]{4,3,2,1,0:T(8,128)S(1)}, u32[]{:S(2)}) copy-start(f32[1,4,8,48,256]{4,3,2,1,0:T(8,128)S(1)} %copy.205) | copy-start | bytes 4718596
  393.2 41.9 %all-to-all-start.6 = ((f32[8,2,4,48,256]{4,3,2,1,0:T(8,128)}), f32[8,2,4,48,256]{4,3,2,1,0:T(8,128)}, u32[]{:S(2)}, u32[]{:S(2)}) async-start(f32[8,2,4,48,256]{4,3,2,1,0:T(8,128)} %copy.208), calls=%async_computation.6 | async-start | bytes 6291456 | tf_op jit(solution)/shard_map/all_to_all | solution.py:10
  400.5 11.4 %copy-start.19 = (f32[1,4,8,48,256]{4,3,2,1,0:T(8,128)}, f32[1,4,8,48,256]{4,3,2,1,0:T(8,128)S(1)}, u32[]{:S(2)}) copy-start(f32[1,4,8,48,256]{4,3,2,1,0:T(8,128)S(1)} %copy.214) | copy-start | bytes 4718596
  435.1 41.9 %all-to-all-start.8 = ((f32[8,2,4,48,256]{4,3,2,1,0:T(8,128)}), f32[8,2,4,48,256]{4,3,2,1,0:T(8,128)}, u32[]{:S(2)}, u32[]{:S(2)}) async-start(f32[8,2,4,48,256]{4,3,2,1,0:T(8,128)} %copy.216), calls=%async_computation.8 | async-start | bytes 6291456 | tf_op jit(solution)/shard_map/all_to_all | solution.py:10
  462.1 18.8 %copy-start.53 = (s32[8,6]{0,1:T(8,128)S(1)}, s32[8,6]{0,1:T(8,128)}, u32[]{:S(2)}) copy-start(s32[8,6]{0,1:T(8,128)} %copy-done.52) | copy-start | bytes 580
  490.0 18.2 %slice-start.3 = ((s8[9437184]{0:T(1024)(128)(4,1)}), s8[1048576]{0:T(1024)(128)(4,1)S(1)}, s32[]{:S(2)}) async-start(s8[9437184]{0:T(1024)(128)(4,1)} %bitcast.342), calls=%async_computation.19 | async-start | bytes 2097152
  490.0 42.7 %all-to-all-start.11 = ((f32[8,2,4,48,256]{4,3,2,1,0:T(8,128)}), f32[8,2,4,48,256]{4,3,2,1,0:T(8,128)}, u32[]{:S(2)}, u32[]{:S(2)}) async-start(f32[8,2,4,48,256]{4,3,2,1,0:T(8,128)} %copy.230), calls=%async_computation.11 | async-start | bytes 6291456 | tf_op jit(solution)/shard_map/all_to_all | solution.py:10
  496.2 12.0 %slice-start.4 = ((s8[9437184]{0:T(1024)(128)(4,1)}), s8[4194304]{0:T(1024)(128)(4,1)S(1)}, s32[]{:S(2)}) async-start(s8[9437184]{0:T(1024)(128)(4,1)} %bitcast.342), calls=%async_computation.20 | async-start | bytes 8388608
  496.2 12.0 %slice-start.5 = ((s8[9437184]{0:T(1024)(128)(4,1)}), s8[4194304]{0:T(1024)(128)(4,1)S(1)}, s32[]{:S(2)}) async-start(s8[9437184]{0:T(1024)(128)(4,1)} %bitcast.342), calls=%async_computation.21 | async-start | bytes 8388608
  504.4 9.9 %collective-permute-start.13 = (f32[12,48,256]{2,1,0:T(8,128)S(1)}, f32[12,48,256]{2,1,0:T(8,128)}, u32[]{:S(2)}, u32[]{:S(2)}) collective-permute-start(f32[12,48,256]{2,1,0:T(8,128)S(1)} %copy.229), channel_id=1, source_target_pairs={{24,16},{25,17},{26,18},{27,19},{28,20},{29,21},{30,22},{31,23}} | collective-permute-start | bytes 1769480 | tf_op jit(solution)/shard_map/ppermute | solution.py:52
  505.9 14.4 %collective-permute-start.12 = (f32[12,48,256]{2,1,0:T(8,128)S(1)}, f32[12,48,256]{2,1,0:T(8,128)}, u32[]{:S(2)}, u32[]{:S(2)}) collective-permute-start(f32[12,48,256]{2,1,0:T(8,128)S(1)} %copy.228), channel_id=1, source_target_pairs={{0,8},{1,9},{2,10},{3,11},{4,12},{5,13},{6,14},{7,15}} | collective-permute-start | bytes 1769480 | tf_op jit(solution)/shard_map/ppermute | solution.py:51
  512.3 20.4 %copy-start.5 = (f32[4,48,256,12]{2,3,1,0:T(8,128)S(1)}, f32[4,48,256,12]{2,3,1,0:T(8,128)}, u32[]{:S(2)}) copy-start(f32[4,48,256,12]{2,3,1,0:T(8,128)} %copy-done.4) | copy-start | bytes 7077892
  538.0 17.9 %slice-start = ((s8[9437184]{0:T(1024)(128)(4,1)}), s8[1048576]{0:T(1024)(128)(4,1)S(1)}, s32[]{:S(2)}) async-start(s8[9437184]{0:T(1024)(128)(4,1)} %bitcast.338), calls=%async_computation.16 | async-start | bytes 2097152
  538.0 42.6 %all-to-all-start.12 = ((f32[8,2,4,48,256]{4,3,2,1,0:T(8,128)}), f32[8,2,4,48,256]{4,3,2,1,0:T(8,128)}, u32[]{:S(2)}, u32[]{:S(2)}) async-start(f32[8,2,4,48,256]{4,3,2,1,0:T(8,128)} %copy.235), calls=%async_computation.12 | async-start | bytes 6291456 | tf_op jit(solution)/shard_map/all_to_all | solution.py:10
  544.2 11.7 %slice-start.1 = ((s8[9437184]{0:T(1024)(128)(4,1)}), s8[4194304]{0:T(1024)(128)(4,1)S(1)}, s32[]{:S(2)}) async-start(s8[9437184]{0:T(1024)(128)(4,1)} %bitcast.338), calls=%async_computation.17 | async-start | bytes 8388608
  544.2 11.7 %slice-start.2 = ((s8[9437184]{0:T(1024)(128)(4,1)}), s8[4194304]{0:T(1024)(128)(4,1)S(1)}, s32[]{:S(2)}) async-start(s8[9437184]{0:T(1024)(128)(4,1)} %bitcast.338), calls=%async_computation.18 | async-start | bytes 8388608
  551.9 10.2 %collective-permute-start.15 = (f32[12,48,256]{2,1,0:T(8,128)S(1)}, f32[12,48,256]{2,1,0:T(8,128)}, u32[]{:S(2)}, u32[]{:S(2)}) collective-permute-start(f32[12,48,256]{2,1,0:T(8,128)S(1)} %copy.234), channel_id=1, source_target_pairs={{16,8},{24,16},{17,9},{25,17},{18,10},{26,18},{19,11},{27,19},{20,... | collective-permute-start | bytes 1769480 | tf_op jit(solution)/shard_map/ppermute | solution.py:52
  553.4 14.4 %collective-permute-start.14 = (f32[12,48,256]{2,1,0:T(8,128)S(1)}, f32[12,48,256]{2,1,0:T(8,128)}, u32[]{:S(2)}, u32[]{:S(2)}) collective-permute-start(f32[12,48,256]{2,1,0:T(8,128)S(1)} %copy.233), channel_id=1, source_target_pairs={{0,8},{8,16},{1,9},{9,17},{2,10},{10,18},{3,11},{11,19},{4,12},{12... | collective-permute-start | bytes 1769480 | tf_op jit(solution)/shard_map/ppermute | solution.py:51
  560.0 20.6 %copy-start.6 = (f32[4,48,256,12]{2,3,1,0:T(8,128)S(1)}, f32[4,48,256,12]{2,3,1,0:T(8,128)}, u32[]{:S(2)}) copy-start(f32[4,48,256,12]{2,3,1,0:T(8,128)} %copy-done.4) | copy-start | bytes 7077892
  585.9 42.3 %all-to-all-start.13 = ((f32[8,2,4,48,256]{4,3,2,1,0:T(8,128)}), f32[8,2,4,48,256]{4,3,2,1,0:T(8,128)}, u32[]{:S(2)}, u32[]{:S(2)}) async-start(f32[8,2,4,48,256]{4,3,2,1,0:T(8,128)} %copy.240), calls=%async_computation.13 | async-start | bytes 6291456 | tf_op jit(solution)/shard_map/all_to_all | solution.py:10
  596.4 17.6 %collective-permute-start.17 = (f32[12,48,256]{2,1,0:T(8,128)}, f32[12,48,256]{2,1,0:T(8,128)}, u32[]{:S(2)}, u32[]{:S(2)}) collective-permute-start(f32[12,48,256]{2,1,0:T(8,128)} %copy.239), channel_id=1, source_target_pairs={{8,0},{16,8},{24,16},{9,1},{17,9},{25,17},{10,2},{18,10},{26,18},{... | collective-permute-start | bytes 1769480 | tf_op jit(solution)/shard_map/ppermute | solution.py:52
  597.7 17.5 %collective-permute-start.16 = (f32[12,48,256]{2,1,0:T(8,128)}, f32[12,48,256]{2,1,0:T(8,128)}, u32[]{:S(2)}, u32[]{:S(2)}) collective-permute-start(f32[12,48,256]{2,1,0:T(8,128)} %copy.238), channel_id=1, source_target_pairs={{0,8},{8,16},{16,24},{1,9},{9,17},{17,25},{2,10},{10,18},{18,26},{... | collective-permute-start | bytes 1769480 | tf_op jit(solution)/shard_map/ppermute | solution.py:51
  642.9 21.3 %collective-permute-start.19 = (f32[12,48,256]{2,1,0:T(8,128)}, f32[12,48,256]{2,1,0:T(8,128)}, u32[]{:S(2)}, u32[]{:S(2)}) collective-permute-start(f32[12,48,256]{2,1,0:T(8,128)} %copy.247), channel_id=1, source_target_pairs={{24,16},{25,17},{26,18},{27,19},{28,20},{29,21},{30,22},{31,23}} | collective-permute-start | bytes 1769480 | tf_op jit(solution)/shard_map/ppermute | solution.py:52
  644.4 19.8 %collective-permute-start.18 = (f32[12,48,256]{2,1,0:T(8,128)}, f32[12,48,256]{2,1,0:T(8,128)}, u32[]{:S(2)}, u32[]{:S(2)}) collective-permute-start(f32[12,48,256]{2,1,0:T(8,128)} %copy.246), channel_id=1, source_target_pairs={{0,8},{1,9},{2,10},{3,11},{4,12},{5,13},{6,14},{7,15}} | collective-permute-start | bytes 1769480 | tf_op jit(solution)/shard_map/ppermute | solution.py:51
  648.3 15.9 %copy-start.39 = (f32[1,48,256,12]{2,3,1,0:T(8,128)S(1)}, f32[1,48,256,12]{2,3,1,0:T(8,128)}, u32[]{:S(2)}) copy-start(f32[1,48,256,12]{2,3,1,0:T(8,128)} %get-tuple-element.95) | copy-start | bytes 1769476
  649.0 18.1 %copy-start.38 = (f32[1,48,256,12]{2,3,1,0:T(8,128)S(1)}, f32[1,48,256,12]{2,3,1,0:T(8,128)}, u32[]{:S(2)}) copy-start(f32[1,48,256,12]{2,3,1,0:T(8,128)} %get-tuple-element.93) | copy-start | bytes 1769476
  662.7 17.1 %copy-start.37 = (f32[1,48,256,12]{2,3,1,0:T(8,128)S(1)}, f32[1,48,256,12]{2,3,1,0:T(8,128)}, u32[]{:S(2)}) copy-start(f32[1,48,256,12]{2,3,1,0:T(8,128)} %get-tuple-element.94) | copy-start | bytes 1769476
  664.1 20.5 %copy-start.36 = (f32[1,48,256,12]{2,3,1,0:T(8,128)S(1)}, f32[1,48,256,12]{2,3,1,0:T(8,128)}, u32[]{:S(2)}) copy-start(f32[1,48,256,12]{2,3,1,0:T(8,128)} %get-tuple-element.96) | copy-start | bytes 1769476
  665.7 35.4 %copy-start.35 = (f32[1,48,256,12]{2,3,1,0:T(8,128)S(1)}, f32[1,48,256,12]{2,3,1,0:T(8,128)}, u32[]{:S(2)}) copy-start(f32[1,48,256,12]{2,3,1,0:T(8,128)} %get-tuple-element.92) | copy-start | bytes 1769476
  665.7 14.2 %collective-permute-start.20 = (f32[12,48,256]{2,1,0:T(8,128)S(1)}, f32[12,48,256]{2,1,0:T(8,128)S(1)}, u32[]{:S(2)}, u32[]{:S(2)}) collective-permute-start(f32[12,48,256]{2,1,0:T(8,128)S(1)} %fusion.37), channel_id=1, source_target_pairs={{0,8},{8,16},{1,9},{9,17},{2,10},{10,18},{3,11},{11,19},{4,12},{12... | collective-permute-start | bytes 1769480 | tf_op jit(solution)/shard_map/ppermute | solution.py:51
  668.6 16.1 %collective-permute-start.22 = (f32[12,48,256]{2,1,0:T(8,128)S(1)}, f32[12,48,256]{2,1,0:T(8,128)S(1)}, u32[]{:S(2)}, u32[]{:S(2)}) collective-permute-start(f32[12,48,256]{2,1,0:T(8,128)S(1)} %fusion.35), channel_id=1, source_target_pairs={{16,8},{24,16},{17,9},{25,17},{18,10},{26,18},{19,11},{27,19},{20,... | collective-permute-start | bytes 1769480 | tf_op jit(solution)/shard_map/ppermute | solution.py:52
  680.2 16.3 %collective-permute-start.21 = (f32[12,48,256]{2,1,0:T(8,128)S(1)}, f32[12,48,256]{2,1,0:T(8,128)S(1)}, u32[]{:S(2)}, u32[]{:S(2)}) collective-permute-start(f32[12,48,256]{2,1,0:T(8,128)S(1)} %fusion.36), channel_id=1, source_target_pairs={{0,8},{8,16},{16,24},{1,9},{9,17},{17,25},{2,10},{10,18},{18,26},{... | collective-permute-start | bytes 1769480 | tf_op jit(solution)/shard_map/ppermute | solution.py:51
  685.1 16.0 %collective-permute-start.23 = (f32[12,48,256]{2,1,0:T(8,128)S(1)}, f32[12,48,256]{2,1,0:T(8,128)S(1)}, u32[]{:S(2)}, u32[]{:S(2)}) collective-permute-start(f32[12,48,256]{2,1,0:T(8,128)S(1)} %fusion.34), channel_id=1, source_target_pairs={{8,0},{16,8},{24,16},{9,1},{17,9},{25,17},{10,2},{18,10},{26,18},{... | collective-permute-start | bytes 1769480 | tf_op jit(solution)/shard_map/ppermute | solution.py:52
  702.9 14.0 %copy-start.46 = (f32[4608,32]{0,1:T(8,128)S(1)}, f32[4608,32]{0,1:T(8,128)}, u32[]{:S(2)}) copy-start(f32[4608,32]{0,1:T(8,128)} %all_to_all.115) | copy-start | bytes 1769476
  (44 other events, 210.9 us)

commit v12 on v8

--- a/solution.py
+++ b/solution.py
@@ -62,12 +62,15 @@
     band_count = lax.axis_size("band")
     devices = group_count * band_count
     blk = coulomb.shape[1]
-    orbital_width = orbitals.shape[1] * band_count
-    half = orbital_width // 2
     piece_rows = blk // devices
     slot_count = coulomb.shape[0]
     block_count = orbitals.shape[0] // (band_count * piece_rows)
-    own_rows = lax.all_to_all(orbitals, "band", split_axis=0, concat_axis=1, tiled=True)
+    quarter = orbitals.shape[1] // 4
+    bounds = [(0, quarter), (quarter, 3 * quarter), (3 * quarter, 4 * quarter)]
+    own_rows = [
+        lax.all_to_all(orbitals[:, lo:hi], "band", split_axis=0, concat_axis=1, tiled=True)
+        for lo, hi in bounds
+    ]
     group_index = lax.axis_index("grp")
     band_index = lax.axis_index("band")
     group_requests = lax.dynamic_slice_in_dim(requests, group_index * band_count, band_count, 0)
@@ -84,47 +87,52 @@
         return outgoing.transpose(1, 2, 0, 3, 4)
 
     def shape_pieces(gathered):
-        return gathered.reshape(group_count, block_count, piece_rows, half)
+        return gathered.reshape(group_count, block_count, piece_rows, gathered.shape[-1])
 
-    first_pieces = shape_pieces(line_gather(own_rows[:, :half], "grp", group_count)[0])
-    first_loads = [requested(first_pieces, slot) for slot in range(slot_count)]
-    second_pieces, first_arrived = line_gather(own_rows[:, half:], "grp", group_count, first_loads)
-    second_pieces = shape_pieces(second_pieces)
-    second_arrived = [band_exchange(requested(second_pieces, slot)) for slot in range(slot_count)]
-    returned = [[], []]
-    held = []
+    pieces = shape_pieces(line_gather(own_rows[0], "grp", group_count)[0])
+    arrived = []
+    for chunk in range(1, len(bounds)):
+        loads = [requested(pieces, slot) for slot in range(slot_count)]
+        gathered, carried = line_gather(own_rows[chunk], "grp", group_count, loads)
+        arrived.append(carried)
+        pieces = shape_pieces(gathered)
+    arrived.append([band_exchange(requested(pieces, slot)) for slot in range(slot_count)])
+    returned = [[] for _ in bounds]
+    held = [[] for _ in bounds]
     for slot in range(slot_count):
         rows = [
-            arrived.transpose(1, 2, 0, 3, 4).reshape(2, blk, half)
-            for arrived in (first_arrived[slot], second_arrived[slot])
+            part[slot].transpose(1, 2, 0, 3, 4).reshape(2, blk, part[slot].shape[-1]) for part in arrived
         ]
         density = sum(
             jnp.dot(r[0], r[1].T, precision=PRECISION, preferred_element_type=jnp.float32) for r in rows
         )
         kernel = density * coulomb[slot]
         scale = jnp.where(own_pairs[2 * slot] == own_pairs[2 * slot + 1], 0.5, 1.0)
-        for h in range(2):
-            onto_first = jnp.dot(kernel, rows[h][1], precision=PRECISION, preferred_element_type=jnp.float32)
-            onto_second = jnp.dot(kernel.T, rows[h][0], precision=PRECISION, preferred_element_type=jnp.float32)
+        for chunk, r in enumerate(rows):
+            onto_first = jnp.dot(kernel, r[1], precision=PRECISION, preferred_element_type=jnp.float32)
+            onto_second = jnp.dot(kernel.T, r[0], precision=PRECISION, preferred_element_type=jnp.float32)
             outbound = (jnp.stack([onto_first, onto_second], 0) * scale).reshape(
-                2, group_count, band_count, piece_rows, half
+                2, group_count, band_count, piece_rows, r.shape[-1]
             )
             outbound = outbound.transpose(2, 0, 1, 3, 4)
-            if h == 0:
+            if chunk == 0:
                 returned[0].append(band_exchange(outbound))
             else:
-                held.append(outbound)
+                held[chunk].append(outbound)
 
     def sum_blocks(returned):
         gathered = jnp.concatenate(returned, axis=1)
         return jnp.einsum("srk,srgpn->gkpn", one_hot, gathered, precision=lax.Precision.HIGHEST)
 
-    first_home, second_returned = line_reduce(sum_blocks(returned[0]), "grp", group_count, held)
-    second_home, _ = line_reduce(sum_blocks(second_returned), "grp", group_count)
-    home_rows = jnp.concatenate([first_home, second_home], axis=-1).reshape(
-        block_count * piece_rows, orbital_width
-    )
-    return lax.all_to_all(home_rows, "band", split_axis=1, concat_axis=0, tiled=True)
+    home = []
+    for chunk in range(len(bounds)):
+        riders = held[chunk + 1] if chunk + 1 < len(bounds) else []
+        summed, carried = line_reduce(sum_blocks(returned[chunk]), "grp", group_count, riders)
+        if riders:
+            returned[chunk + 1] = carried
+        rows = summed.reshape(block_count * piece_rows, summed.shape[-1])
+        home.append(lax.all_to_all(rows, "band", split_axis=1, concat_axis=0, tiled=True))
+    return jnp.concatenate(home, axis=1)
 
 
 def solution(mesh):

time: 733 us -> 808 us (1.10)
  starting transfers between devices: 116 us -> 210 us
  waiting for transfers between devices: 231 us -> 161 us
  matrix products: 129 us -> 193 us
  blocking collectives: 40.8 us -> 0 us
  local copies, waits for them, and re-layouts: 153 us -> 175 us
    all_to_all x12 -> x18, waiting for transfers between devices: 125 us -> 77.9 us  [band_exchange(): lax.all_to_all(outgoing, 'band', split_axis=0, concat_axis=0, tiled=True)]
    dot_general x12 -> x18, matrix products: 69.7 us -> 115 us  [the longest x9 63.3 us: body(): jnp.dot(kernel, r[1], precision=PRECISION, preferred_element_type=jnp.flo...]
    all_to_all x2 -> x0, blocking collectives: 40.8 us -> none  [the longest x1 20.8 us: body(): lax.all_to_all(orbitals, 'band', split_axis=0, concat_axis=1, tiled=True)]
    all_to_all x0 -> x6, starting transfers between devices: none -> 26.9 us  [the longest x3 14.6 us: body(): lax.all_to_all(orbitals[:, lo:hi], 'band', split_axis=0, concat_axis=1, t...]
    ppermute x6 -> x9, waiting for transfers between devices: 41.8 us -> 16.1 us  [line_reduce(): lax.ppermute(send_right, axis, [(i, i + 1) for i in range(0, step)])]
    ppermute x6 -> x9, starting transfers between devices: 21 us -> 45.5 us  [line_reduce(): lax.ppermute(send_right, axis, [(i, i + 1) for i in range(0, step)])]
    all_to_all x12 -> x18, starting transfers between devices: 67.3 us -> 91.5 us  [band_exchange(): lax.all_to_all(outgoing, 'band', split_axis=0, concat_axis=0, tiled=True)]
    dot_general x6 -> x9, matrix products: 52 us -> 70.1 us  [body(): jnp.dot(r[0], r[1].T, precision=PRECISION, preferred_element_type=jnp.flo...]
  transfers between devices with their start and end apart: 36 -> 60, of which waited for: 24 -> 26; matrix products, arithmetic and copies ran while one was open for 35% -> 44% of each run, Pallas kernels for 0% -> 0%
where the time goes in v12:
time: 808 us; the launch traced here: 793 us
  starting transfers between devices  210 us (26%)
  matrix products  193 us (24%)
  local copies, waits for them, and re-layouts  175 us (22%)
  waiting for transfers between devices  161 us (20%)
  other arithmetic  49.1 us (6%)
    all_to_all x18, starting transfers between devices, band_exchange(): lax.all_to_all(outgoing, 'band', split_axis=0, concat_axis=0, tiled=True)  91.5 us
    all_to_all x18, waiting for transfers between devices, band_exchange(): lax.all_to_all(outgoing, 'band', split_axis=0, concat_axis=0, tiled=True)  77.9 us
    dot_general x9, matrix products, body(): jnp.dot(r[0], r[1].T, precision=PRECISION, preferred_element_type=jnp.flo...  70.1 us
    dot_general x9, matrix products, body(): jnp.dot(kernel, r[1], precision=PRECISION, preferred_element_type=jnp.flo...  63.3 us
    dot_general x9, matrix products, body(): jnp.dot(kernel.T, r[0], precision=PRECISION, preferred_element_type=jnp.f...  52 us
    ppermute x9, starting transfers between devices, line_reduce(): lax.ppermute(send_right, axis, [(i, i + 1) for i in range(0, step)])  45.5 us
    ppermute x9, waiting for transfers between devices, line_gather(): lax.ppermute(leftward, axis, [(i + 1, i) for i in range(0, count - step)])  43.2 us
    dot_general x3, local copies, waits for them, and re-layouts, body(): jnp.dot(kernel.T, r[0], precision=PRECISION, preferred_element_type=jnp.f...  28.8 us
  transfers between devices with their start and end apart: 60, of which 26 were waited for; matrix products, arithmetic and copies ran while one was open for 44% of the time, Pallas kernels for 0%

profile of v12, /device:TPU:2, one launch (start us, length us, event | category | flops | bytes accessed | tf_op | source)
XLA Modules:
  0.0 793.2 jit_solution(14812584663551919716)
XLA Ops:
  8.2 4.9 all-to-all-done.1
  13.2 4.9 all-to-all-start
  19.4 4.6 collective-permute-start
  24.1 5.7 collective-permute-done.1
  34.3 6.6 collective-permute-done.3
  45.3 5.9 collective-permute-done.5
  62.5 5.4 collective-permute-start.6
  72.8 6.0 collective-permute-done.7
  81.1 4.6 all-to-all-start.4
  91.0 16.8 %collective-permute-done.9 = f32[576,256]{1,0:T(8,128)} collective-permute-done((f32[576,256]{1,0:T(8,128)}, f32[576,256]{1,0:T(8,128)}, u32[]{:S(2)}, u32[]{:S(2)}) %collective-permute-start.9) | collective-permute-done | bytes 589856 | tf_op jit(solution)/shard_map/ppermute | solution.py:24
  125.6 5.9 all-to-all-done.5
  131.5 5.5 all-to-all-start.3
  157.7 5.3 collective-permute-start.12
  168.5 19.6 %all-to-all-done.6 = f32[8,2,4,48,256]{4,3,2,1,0:T(8,128)} async-done(((f32[8,2,4,48,256]{4,3,2,1,0:T(8,128)}), f32[8,2,4,48,256]{4,3,2,1,0:T(8,128)}, u32[]{:S(2)}, u32[]{:S(2)}) %all-to-all-start.6) | async-done | bytes 3145760 | tf_op jit(solution)/shard_map/all_to_all | solution.py:10
  188.1 5.9 all-to-all-start.7
  219.8 6.5 fusion.74
  230.6 5.8 all-to-all-start.8
  236.3 8.6 %convolution_add_fusion.5 = f32[1536,1536]{1,0:T(8,128)} fusion(f32[1536,1536]{1,0:T(8,128)} %fusion.74, f32[1536,128]{1,0:T(8,128)S(1)} %bitcast.517, f32[1536,128]{1,0:T(8,128)S(1)} %bitcast.515), kind=kOutput, calls=%fused_computation.14 | convolution fusion | flops 1814298624 | bytes 20447232 | tf_op jit(solution)/shard_map/dot_general | solution.py:107
  253.6 6.7 convolution_add_fusion.3
  263.7 9.1 %all-to-all-done.8 = f32[8,2,4,48,256]{4,3,2,1,0:T(8,128)} async-done(((f32[8,2,4,48,256]{4,3,2,1,0:T(8,128)}), f32[8,2,4,48,256]{4,3,2,1,0:T(8,128)}, u32[]{:S(2)}, u32[]{:S(2)}) %all-to-all-start.8) | async-done | bytes 3145760 | tf_op jit(solution)/shard_map/all_to_all | solution.py:10
  284.1 6.1 all-to-all-start.13
  302.3 6.7 convolution_add_fusion.1
  309.8 6.2 all-to-all-start.9
  317.6 11.3 %fusion.2 = f32[1536,1536]{1,0:T(8,128)} fusion(f32[1536,1536]{1,0:T(8,128)} %convolution_add_fusion.1, f32[1536,128]{1,0:T(8,128)S(1)} %bitcast.523, f32[1536,128]{1,0:T(8,128)S(1)} %bitcast.525, f32[3,1536,1536]{2,1,0:T(8,128)} %param.9), kind=kOutput, calls=%fused_computation.17 | convolution fusion | flops 1816657920 | bytes 29884416 | tf_op jit(solution)/shard_map/dot_general | solution.py:107
  328.9 9.5 %copy.312 = f32[1536,1536]{1,0:T(8,128)} copy(f32[1536,1536]{0,1:T(8,128)} %bitcast.463) | data formatting | bytes 18874368 | tf_op jit(solution)/shard_map/dot_general | solution.py:113
  338.5 7.4 convolution_bitcast_fusion.13
  358.5 10.8 %fusion = f32[1536,1536]{1,0:T(8,128)} fusion(f32[1536,1536]{1,0:T(8,128)} %convolution_add_fusion.5, f32[1536,128]{1,0:T(8,128)S(1)} %bitcast.531, f32[1536,128]{1,0:T(8,128)S(1)} %bitcast.533, f32[3,1536,1536]{2,1,0:T(8,128)} %param.9), kind=kOutput, calls=%fused_computation.15 | convolution fusion | flops 1816657920 | bytes 29884416 | tf_op jit(solution)/shard_map/dot_general | solution.py:107
  373.6 5.9 all-to-all-start.14
  383.0 9.6 %copy.292 = f32[1536,1536]{1,0:T(8,128)} copy(f32[1536,1536]{0,1:T(8,128)} %bitcast.471) | data formatting | bytes 18874368 | tf_op jit(solution)/shard_map/dot_general | solution.py:113
  392.6 6.7 convolution_bitcast_fusion.17
  404.8 4.6 all-to-all-start.10
  409.5 11.2 %fusion.1 = f32[1536,1536]{1,0:T(8,128)} fusion(f32[1536,1536]{1,0:T(8,128)} %convolution_add_fusion.3, f32[1536,128]{1,0:T(8,128)S(1)} %bitcast.527, f32[1536,128]{1,0:T(8,128)} %bitcast.529, f32[3,1536,1536]{2,1,0:T(8,128)} %param.9), kind=kOutput, calls=%fused_computation.16 | convolution fusion | flops 1816657920 | bytes 29884416 | tf_op jit(solution)/shard_map/dot_general | solution.py:107
  420.7 9.6 %copy.302 = f32[1536,1536]{1,0:T(8,128)} copy(f32[1536,1536]{0,1:T(8,128)} %bitcast.467) | data formatting | bytes 18874368 | tf_op jit(solution)/shard_map/dot_general | solution.py:113
  430.3 6.7 convolution_bitcast_fusion.15
  442.4 4.7 all-to-all-start.12
  447.1 7.4 convolution_bitcast_fusion.5
  454.6 6.9 convolution_bitcast_fusion.4
  483.1 7.3 convolution_bitcast_fusion.3
  496.4 6.8 convolution_bitcast_fusion.2
  503.5 16.0 %all-to-all-done.15 = f32[8,2,4,48,256]{4,3,2,1,0:T(8,128)} async-done(((f32[8,2,4,48,256]{4,3,2,1,0:T(8,128)}), f32[8,2,4,48,256]{4,3,2,1,0:T(8,128)}, u32[]{:S(2)}, u32[]{:S(2)}) %all-to-all-start.15) | async-done | bytes 3145760 | tf_op jit(solution)/shard_map/all_to_all | solution.py:10
  523.7 6.0 all-to-all-start.16
  529.7 6.9 convolution_bitcast_fusion.1
  541.8 6.9 convolution_bitcast_fusion
  549.7 16.4 %all-to-all-done.16 = f32[8,2,4,48,256]{4,3,2,1,0:T(8,128)} async-done(((f32[8,2,4,48,256]{4,3,2,1,0:T(8,128)}), f32[8,2,4,48,256]{4,3,2,1,0:T(8,128)}, u32[]{:S(2)}, u32[]{:S(2)}) %all-to-all-start.16) | async-done | bytes 3145760 | tf_op jit(solution)/shard_map/all_to_all | solution.py:10
  570.5 5.1 all-to-all-start.17
  575.6 6.9 convolution_bitcast_fusion.11
  587.8 6.6 convolution_bitcast_fusion.10
  595.7 5.3 copy.322
  601.0 5.3 copy.323
  606.4 5.6 all-to-all-done.17
  621.9 6.2 all-to-all-start.19
  628.1 6.9 convolution_bitcast_fusion.9
  641.8 6.6 convolution_bitcast_fusion.8
  663.0 6.9 convolution_bitcast_fusion.7
  672.2 5.3 collective-permute-start.26
  677.4 6.6 convolution_bitcast_fusion.6
  700.3 5.9 collective-permute-start.28
  712.1 5.1 collective-permute-done.29
  726.9 7.5 collective-permute-done.30
  735.4 5.1 collective-permute-start.31
  751.0 8.4 %collective-permute-start.32 = (f32[12,48,128]{2,0,1:T(8,128)}, f32[12,48,128]{2,0,1:T(8,128)}, u32[]{:S(2)}, u32[]{:S(2)}) collective-permute-start(f32[12,48,128]{2,0,1:T(8,128)} %get-tuple-element.166), channel_id=1, source_target_pairs={{0,8},{8,16},{16,24},{1,9},{9,17},{17,25},{2,10},{10,18},{18,26},{... | collective-permute-start | bytes 884744 | tf_op jit(solution)/shard_map/ppermute | solution.py:51
  773.8 6.8 all-to-all-done.22
  780.7 4.8 all-to-all-start.23
  786.3 5.4 all-to-all-done.23
  (406 shorter events, 323.6 us)
Async XLA Ops:
  2.7 10.4 %all-to-all-start.1 = ((f32[8,576,16]{1,2,0:T(8,128)}), f32[8,576,16]{1,2,0:T(8,128)S(1)}, u32[]{:S(2)}, u32[]{:S(2)}) async-start(f32[8,576,16]{1,2,0:T(8,128)} %copy.252), calls=%async_computation.1 | async-start | bytes 655360 | tf_op jit(solution)/shard_map/all_to_all | solution.py:71
  13.2 41.6 %all-to-all-start = ((f32[8,576,32]{1,2,0:T(8,128)}), f32[8,576,32]{1,2,0:T(8,128)S(1)}, u32[]{:S(2)}, u32[]{:S(2)}) async-start(f32[8,576,32]{1,2,0:T(8,128)} %copy.250), calls=%async_computation | async-start | bytes 1310720 | tf_op jit(solution)/shard_map/all_to_all | solution.py:71
  18.1 11.8 %collective-permute-start.1 = (f32[576,128]{0,1:T(8,128)S(1)}, f32[576,128]{0,1:T(8,128)}, u32[]{:S(2)}, u32[]{:S(2)}) collective-permute-start(f32[576,128]{0,1:T(8,128)S(1)} %bitcast.544), channel_id=1, source_target_pairs={{8,0},{16,8},{24,16},{9,1},{17,9},{25,17},{10,2},{18,10},{26,18},{... | collective-permute-start | bytes 884744 | tf_op jit(solution)/shard_map/ppermute | solution.py:24
  19.4 11.8 %collective-permute-start = (f32[576,128]{0,1:T(8,128)S(1)}, f32[576,128]{0,1:T(8,128)S(1)}, u32[]{:S(2)}, u32[]{:S(2)}) collective-permute-start(f32[576,128]{0,1:T(8,128)S(1)} %bitcast.545), channel_id=1, source_target_pairs={{0,8},{8,16},{16,24},{1,9},{9,17},{17,25},{2,10},{10,18},{18,26},{... | collective-permute-start | bytes 884744 | tf_op jit(solution)/shard_map/ppermute | solution.py:23
  29.8 11.1 %collective-permute-start.3 = (f32[576,128]{0,1:T(8,128)}, f32[576,128]{0,1:T(8,128)}, u32[]{:S(2)}, u32[]{:S(2)}) collective-permute-start(f32[576,128]{0,1:T(8,128)} %collective-permute-done.1), channel_id=1, source_target_pairs={{8,0},{16,8},{9,1},{17,9},{10,2},{18,10},{11,3},{19,11},{12,4},{20... | collective-permute-start | bytes 884744 | tf_op jit(solution)/shard_map/ppermute | solution.py:24
  31.1 11.1 %collective-permute-start.2 = (f32[576,128]{0,1:T(8,128)S(1)}, f32[576,128]{0,1:T(8,128)}, u32[]{:S(2)}, u32[]{:S(2)}) collective-permute-start(f32[576,128]{0,1:T(8,128)S(1)} %collective-permute-done), channel_id=1, source_target_pairs={{8,16},{16,24},{9,17},{17,25},{10,18},{18,26},{11,19},{19,27},{12,... | collective-permute-start | bytes 884744 | tf_op jit(solution)/shard_map/ppermute | solution.py:23
  32.6 110.4 %copy-start.66 = (pred[8,2]{1,0:T(8,128)(4,1)}, pred[8,2]{1,0:T(8,128)(4,1)S(1)}, u32[]{:S(2)}) copy-start(pred[8,2]{1,0:T(8,128)(4,1)S(1)} %copy.251) | copy-start | bytes 52
  41.0 10.2 %collective-permute-start.5 = (f32[576,128]{0,1:T(8,128)}, f32[576,128]{0,1:T(8,128)}, u32[]{:S(2)}, u32[]{:S(2)}) collective-permute-start(f32[576,128]{0,1:T(8,128)} %collective-permute-done.3), channel_id=1, source_target_pairs={{8,0},{9,1},{10,2},{11,3},{12,4},{13,5},{14,6},{15,7}} | collective-permute-start | bytes 884744 | tf_op jit(solution)/shard_map/ppermute | solution.py:24
  42.3 10.0 %collective-permute-start.4 = (f32[576,128]{0,1:T(8,128)}, f32[576,128]{0,1:T(8,128)S(1)}, u32[]{:S(2)}, u32[]{:S(2)}) collective-permute-start(f32[576,128]{0,1:T(8,128)} %collective-permute-done.2), channel_id=1, source_target_pairs={{16,24},{17,25},{18,26},{19,27},{20,28},{21,29},{22,30},{23,31}} | collective-permute-start | bytes 884744 | tf_op jit(solution)/shard_map/ppermute | solution.py:23
  54.7 25.2 %all-to-all-start.2 = ((f32[8,2,4,48,128]{4,3,2,1,0:T(8,128)}), f32[8,2,4,48,128]{4,3,2,1,0:T(8,128)S(1)}, u32[]{:S(2)}, u32[]{:S(2)}) async-start(f32[8,2,4,48,128]{4,3,2,1,0:T(8,128)} %fusion.41), calls=%async_computation.2 | async-start | bytes 3145728 | tf_op jit(solution)/shard_map/all_to_all | solution.py:10
  61.2 17.6 %collective-permute-start.7 = (f32[576,256]{1,0:T(8,128)}, f32[576,256]{1,0:T(8,128)}, u32[]{:S(2)}, u32[]{:S(2)}) collective-permute-start(f32[576,256]{1,0:T(8,128)} %copy.263), channel_id=1, source_target_pairs={{8,0},{16,8},{24,16},{9,1},{17,9},{25,17},{10,2},{18,10},{26,18},{... | collective-permute-start | bytes 1769480 | tf_op jit(solution)/shard_map/ppermute | solution.py:24
  62.5 17.5 %collective-permute-start.6 = (f32[576,256]{1,0:T(8,128)}, f32[576,256]{1,0:T(8,128)}, u32[]{:S(2)}, u32[]{:S(2)}) collective-permute-start(f32[576,256]{1,0:T(8,128)} %copy.262), channel_id=1, source_target_pairs={{0,8},{8,16},{16,24},{1,9},{9,17},{17,25},{2,10},{10,18},{18,26},{... | collective-permute-start | bytes 1769480 | tf_op jit(solution)/shard_map/ppermute | solution.py:23
  67.9 95.0 %copy-start.68 = (pred[8,2]{1,0:T(8,128)(4,1)}, pred[8,2]{1,0:T(8,128)(4,1)S(1)}, u32[]{:S(2)}) copy-start(pred[8,2]{1,0:T(8,128)(4,1)S(1)} %copy.269) | copy-start | bytes 52
  68.2 83.5 %copy-start.62 = (s32[1024]{0:T(1024)}, s32[1024]{0:T(1024)S(1)}, u32[]{:S(2)}) copy-start(s32[1024]{0:T(1024)S(1)} %pad_clamp_fusion.1) | copy-start | bytes 12292
  81.1 26.7 %all-to-all-start.4 = ((f32[8,2,4,48,128]{4,3,2,1,0:T(8,128)}), f32[8,2,4,48,128]{4,3,2,1,0:T(8,128)}, u32[]{:S(2)}, u32[]{:S(2)}) async-start(f32[8,2,4,48,128]{4,3,2,1,0:T(8,128)} %fusion.40), calls=%async_computation.4 | async-start | bytes 3145728 | tf_op jit(solution)/shard_map/all_to_all | solution.py:10
  85.7 5.3 collective-permute-start.8
  87.2 20.5 %collective-permute-start.9 = (f32[576,256]{1,0:T(8,128)}, f32[576,256]{1,0:T(8,128)}, u32[]{:S(2)}, u32[]{:S(2)}) collective-permute-start(f32[576,256]{1,0:T(8,128)} %collective-permute-done.7), channel_id=1, source_target_pairs={{8,0},{16,8},{9,1},{17,9},{10,2},{18,10},{11,3},{19,11},{12,4},{20... | collective-permute-start | bytes 1769480 | tf_op jit(solution)/shard_map/ppermute | solution.py:24
  91.0 21.0 %copy-start.51 = (f32[4608,16]{0,1:T(8,128)S(1)}, f32[4608,16]{0,1:T(8,128)}, u32[]{:S(2)}) copy-start(f32[4608,16]{0,1:T(8,128)} %get-tuple-element.191) | copy-start | bytes 884740
  107.8 23.7 %all-to-all-start.5 = ((f32[8,2,4,48,128]{4,3,2,1,0:T(8,128)}), f32[8,2,4,48,128]{4,3,2,1,0:T(8,128)S(1)}, u32[]{:S(2)}, u32[]{:S(2)}) async-start(f32[8,2,4,48,128]{4,3,2,1,0:T(8,128)} %fusion.39), calls=%async_computation.5 | async-start | bytes 3145728 | tf_op jit(solution)/shard_map/all_to_all | solution.py:10
  117.8 19.2 %collective-permute-start.10 = (f32[576,256]{1,0:T(8,128)}, f32[576,256]{1,0:T(8,128)S(1)}, u32[]{:S(2)}, u32[]{:S(2)}) collective-permute-start(f32[576,256]{1,0:T(8,128)} %collective-permute-done.8), channel_id=1, source_target_pairs={{16,24},{17,25},{18,26},{19,27},{20,28},{21,29},{22,30},{23,31}} | collective-permute-start | bytes 1769480 | tf_op jit(solution)/shard_map/ppermute | solution.py:23
  118.5 18.5 %collective-permute-start.11 = (f32[576,256]{1,0:T(8,128)}, f32[576,256]{1,0:T(8,128)S(1)}, u32[]{:S(2)}, u32[]{:S(2)}) collective-permute-start(f32[576,256]{1,0:T(8,128)} %collective-permute-done.9), channel_id=1, source_target_pairs={{8,0},{9,1},{10,2},{11,3},{12,4},{13,5},{14,6},{15,7}} | collective-permute-start | bytes 1769480 | tf_op jit(solution)/shard_map/ppermute | solution.py:24
  131.5 15.6 %all-to-all-start.3 = ((f32[8,576,16]{1,2,0:T(8,128)}), f32[8,576,16]{1,2,0:T(8,128)}, u32[]{:S(2)}, u32[]{:S(2)}) async-start(f32[8,576,16]{1,2,0:T(8,128)} %copy.266), calls=%async_computation.3 | async-start | bytes 655360 | tf_op jit(solution)/shard_map/all_to_all | solution.py:71
  147.1 41.0 %all-to-all-start.6 = ((f32[8,2,4,48,256]{4,3,2,1,0:T(8,128)}), f32[8,2,4,48,256]{4,3,2,1,0:T(8,128)}, u32[]{:S(2)}, u32[]{:S(2)}) async-start(f32[8,2,4,48,256]{4,3,2,1,0:T(8,128)} %fusion.26), calls=%async_computation.6 | async-start | bytes 6291456 | tf_op jit(solution)/shard_map/all_to_all | solution.py:10
  156.4 11.0 %collective-permute-start.13 = (f32[576,128]{1,0:T(8,128)S(1)}, f32[576,128]{1,0:T(8,128)S(1)}, u32[]{:S(2)}, u32[]{:S(2)}) collective-permute-start(f32[576,128]{1,0:T(8,128)S(1)} %copy.278), channel_id=1, source_target_pairs={{8,0},{16,8},{24,16},{9,1},{17,9},{25,17},{10,2},{18,10},{26,18},{... | collective-permute-start | bytes 884744 | tf_op jit(solution)/shard_map/ppermute | solution.py:24
  157.7 10.9 %collective-permute-start.12 = (f32[576,128]{1,0:T(8,128)S(1)}, f32[576,128]{1,0:T(8,128)}, u32[]{:S(2)}, u32[]{:S(2)}) collective-permute-start(f32[576,128]{1,0:T(8,128)S(1)} %copy.277), channel_id=1, source_target_pairs={{0,8},{8,16},{16,24},{1,9},{9,17},{17,25},{2,10},{10,18},{18,26},{... | collective-permute-start | bytes 884744 | tf_op jit(solution)/shard_map/ppermute | solution.py:23
  188.1 42.5 %all-to-all-start.7 = ((f32[8,2,4,48,256]{4,3,2,1,0:T(8,128)}), f32[8,2,4,48,256]{4,3,2,1,0:T(8,128)}, u32[]{:S(2)}, u32[]{:S(2)}) async-start(f32[8,2,4,48,256]{4,3,2,1,0:T(8,128)} %fusion.25), calls=%async_computation.7 | async-start | bytes 6291456 | tf_op jit(solution)/shard_map/all_to_all | solution.py:10
  216.8 11.9 %collective-permute-start.14 = (f32[576,128]{1,0:T(8,128)}, f32[576,128]{1,0:T(8,128)}, u32[]{:S(2)}, u32[]{:S(2)}) collective-permute-start(f32[576,128]{1,0:T(8,128)} %collective-permute-done.12), channel_id=1, source_target_pairs={{8,16},{16,24},{9,17},{17,25},{10,18},{18,26},{11,19},{19,27},{12,... | collective-permute-start | bytes 884744 | tf_op jit(solution)/shard_map/ppermute | solution.py:23
  218.2 12.4 %collective-permute-start.15 = (f32[576,128]{1,0:T(8,128)S(1)}, f32[576,128]{1,0:T(8,128)}, u32[]{:S(2)}, u32[]{:S(2)}) collective-permute-start(f32[576,128]{1,0:T(8,128)S(1)} %copy-done.59), channel_id=1, source_target_pairs={{8,0},{16,8},{9,1},{17,9},{10,2},{18,10},{11,3},{19,11},{12,4},{20... | collective-permute-start | bytes 884744 | tf_op jit(solution)/shard_map/ppermute | solution.py:24
  230.6 42.3 %all-to-all-start.8 = ((f32[8,2,4,48,256]{4,3,2,1,0:T(8,128)}), f32[8,2,4,48,256]{4,3,2,1,0:T(8,128)}, u32[]{:S(2)}, u32[]{:S(2)}) async-start(f32[8,2,4,48,256]{4,3,2,1,0:T(8,128)} %fusion.24), calls=%async_computation.8 | async-start | bytes 6291456 | tf_op jit(solution)/shard_map/all_to_all | solution.py:10
  247.3 16.4 %collective-permute-start.16 = (f32[576,128]{1,0:T(8,128)}, f32[576,128]{1,0:T(8,128)S(1)}, u32[]{:S(2)}, u32[]{:S(2)}) collective-permute-start(f32[576,128]{1,0:T(8,128)} %collective-permute-done.14), channel_id=1, source_target_pairs={{16,24},{17,25},{18,26},{19,27},{20,28},{21,29},{22,30},{23,31}} | collective-permute-start | bytes 884744 | tf_op jit(solution)/shard_map/ppermute | solution.py:23
  248.0 15.7 %collective-permute-start.17 = (f32[576,128]{1,0:T(8,128)}, f32[576,128]{1,0:T(8,128)S(1)}, u32[]{:S(2)}, u32[]{:S(2)}) collective-permute-start(f32[576,128]{1,0:T(8,128)} %collective-permute-done.15), channel_id=1, source_target_pairs={{8,0},{9,1},{10,2},{11,3},{12,4},{13,5},{14,6},{15,7}} | collective-permute-start | bytes 884744 | tf_op jit(solution)/shard_map/ppermute | solution.py:24
  284.1 25.7 %all-to-all-start.13 = ((f32[8,2,4,48,128]{4,3,2,1,0:T(8,128)}), f32[8,2,4,48,128]{4,3,2,1,0:T(8,128)}, u32[]{:S(2)}, u32[]{:S(2)}) async-start(f32[8,2,4,48,128]{4,3,2,1,0:T(8,128)} %fusion.36), calls=%async_computation.13 | async-start | bytes 3145728 | tf_op jit(solution)/shard_map/all_to_all | solution.py:10
  309.8 39.9 %all-to-all-start.9 = ((f32[8,2,4,48,128]{4,3,2,1,0:T(8,128)}), f32[8,2,4,48,128]{4,3,2,1,0:T(8,128)}, u32[]{:S(2)}, u32[]{:S(2)}) async-start(f32[8,2,4,48,128]{4,3,2,1,0:T(8,128)} %fusion.38), calls=%async_computation.9 | async-start | bytes 3145728 | tf_op jit(solution)/shard_map/all_to_all | solution.py:10
  349.7 23.9 %all-to-all-start.11 = ((f32[8,2,4,48,128]{4,3,2,1,0:T(8,128)}), f32[8,2,4,48,128]{4,3,2,1,0:T(8,128)}, u32[]{:S(2)}, u32[]{:S(2)}) async-start(f32[8,2,4,48,128]{4,3,2,1,0:T(8,128)} %fusion.37), calls=%async_computation.11 | async-start | bytes 3145728 | tf_op jit(solution)/shard_map/all_to_all | solution.py:10
  373.6 31.2 %all-to-all-start.14 = ((f32[8,2,4,48,128]{4,3,2,1,0:T(8,128)}), f32[8,2,4,48,128]{4,3,2,1,0:T(8,128)}, u32[]{:S(2)}, u32[]{:S(2)}) async-start(f32[8,2,4,48,128]{4,3,2,1,0:T(8,128)} %copy.313), calls=%async_computation.14 | async-start | bytes 3145728 | tf_op jit(solution)/shard_map/all_to_all | solution.py:10
  404.8 37.6 %all-to-all-start.10 = ((f32[8,2,4,48,128]{4,3,2,1,0:T(8,128)}), f32[8,2,4,48,128]{4,3,2,1,0:T(8,128)}, u32[]{:S(2)}, u32[]{:S(2)}) async-start(f32[8,2,4,48,128]{4,3,2,1,0:T(8,128)} %copy.293), calls=%async_computation.10 | async-start | bytes 3145728 | tf_op jit(solution)/shard_map/all_to_all | solution.py:10
  442.4 28.0 %all-to-all-start.12 = ((f32[8,2,4,48,128]{4,3,2,1,0:T(8,128)}), f32[8,2,4,48,128]{4,3,2,1,0:T(8,128)}, u32[]{:S(2)}, u32[]{:S(2)}) async-start(f32[8,2,4,48,128]{4,3,2,1,0:T(8,128)} %copy.303), calls=%async_computation.12 | async-start | bytes 3145728 | tf_op jit(solution)/shard_map/all_to_all | solution.py:10
  478.6 40.9 %all-to-all-start.15 = ((f32[8,2,4,48,256]{4,3,2,1,0:T(8,128)}), f32[8,2,4,48,256]{4,3,2,1,0:T(8,128)}, u32[]{:S(2)}, u32[]{:S(2)}) async-start(f32[8,2,4,48,256]{4,3,2,1,0:T(8,128)} %copy.317), calls=%async_computation.15 | async-start | bytes 6291456 | tf_op jit(solution)/shard_map/all_to_all | solution.py:10
  490.4 13.1 %collective-permute-start.18 = (f32[12,48,128]{2,0,1:T(8,128)}, f32[12,48,128]{2,0,1:T(8,128)}, u32[]{:S(2)}, u32[]{:S(2)}) collective-permute-start(f32[12,48,128]{2,0,1:T(8,128)} %get-tuple-element.115), channel_id=1, source_target_pairs={{0,8},{1,9},{2,10},{3,11},{4,12},{5,13},{6,14},{7,15}} | collective-permute-start | bytes 884744 | tf_op jit(solution)/shard_map/ppermute | solution.py:51
  494.8 8.7 %collective-permute-start.19 = (f32[12,48,128]{2,0,1:T(8,128)S(1)}, f32[12,48,128]{2,0,1:T(8,128)}, u32[]{:S(2)}, u32[]{:S(2)}) collective-permute-start(f32[12,48,128]{2,0,1:T(8,128)S(1)} %get-tuple-element.116), channel_id=1, source_target_pairs={{24,16},{25,17},{26,18},{27,19},{28,20},{29,21},{30,22},{31,23}} | collective-permute-start | bytes 884744 | tf_op jit(solution)/shard_map/ppermute | solution.py:52
  523.7 42.5 %all-to-all-start.16 = ((f32[8,2,4,48,256]{4,3,2,1,0:T(8,128)}), f32[8,2,4,48,256]{4,3,2,1,0:T(8,128)}, u32[]{:S(2)}, u32[]{:S(2)}) async-start(f32[8,2,4,48,256]{4,3,2,1,0:T(8,128)} %copy.318), calls=%async_computation.16 | async-start | bytes 6291456 | tf_op jit(solution)/shard_map/all_to_all | solution.py:10
  536.7 12.3 %collective-permute-start.20 = (f32[12,48,128]{2,0,1:T(8,128)S(1)}, f32[12,48,128]{2,0,1:T(8,128)S(1)}, u32[]{:S(2)}, u32[]{:S(2)}) collective-permute-start(f32[12,48,128]{2,0,1:T(8,128)S(1)} %copy-done.56), channel_id=1, source_target_pairs={{0,8},{8,16},{1,9},{9,17},{2,10},{10,18},{3,11},{11,19},{4,12},{12... | collective-permute-start | bytes 884744 | tf_op jit(solution)/shard_map/ppermute | solution.py:51
  540.4 9.4 %collective-permute-start.21 = (f32[12,48,128]{2,0,1:T(8,128)S(1)}, f32[12,48,128]{2,0,1:T(8,128)}, u32[]{:S(2)}, u32[]{:S(2)}) collective-permute-start(f32[12,48,128]{2,0,1:T(8,128)S(1)} %get-tuple-element.121), channel_id=1, source_target_pairs={{16,8},{24,16},{17,9},{25,17},{18,10},{26,18},{19,11},{27,19},{20,... | collective-permute-start | bytes 884744 | tf_op jit(solution)/shard_map/ppermute | solution.py:52
  570.5 41.5 %all-to-all-start.17 = ((f32[8,2,4,48,256]{4,3,2,1,0:T(8,128)}), f32[8,2,4,48,256]{4,3,2,1,0:T(8,128)S(1)}, u32[]{:S(2)}, u32[]{:S(2)}) async-start(f32[8,2,4,48,256]{4,3,2,1,0:T(8,128)} %copy.319), calls=%async_computation.17 | async-start | bytes 6291456 | tf_op jit(solution)/shard_map/all_to_all | solution.py:10
  582.6 23.8 %collective-permute-start.22 = (f32[12,48,128]{2,0,1:T(8,128)S(1)}, f32[12,48,128]{2,0,1:T(8,128)S(1)}, u32[]{:S(2)}, u32[]{:S(2)}) collective-permute-start(f32[12,48,128]{2,0,1:T(8,128)S(1)} %copy-done.55), channel_id=1, source_target_pairs={{0,8},{8,16},{16,24},{1,9},{9,17},{17,25},{2,10},{10,18},{18,26},{... | collective-permute-start | bytes 884744 | tf_op jit(solution)/shard_map/ppermute | solution.py:51
  586.3 20.1 %collective-permute-start.23 = (f32[12,48,128]{2,0,1:T(8,128)S(1)}, f32[12,48,128]{2,0,1:T(8,128)}, u32[]{:S(2)}, u32[]{:S(2)}) collective-permute-start(f32[12,48,128]{2,0,1:T(8,128)S(1)} %copy-done.54), channel_id=1, source_target_pairs={{8,0},{16,8},{24,16},{9,1},{17,9},{25,17},{10,2},{18,10},{26,18},{... | collective-permute-start | bytes 884744 | tf_op jit(solution)/shard_map/ppermute | solution.py:52
  621.9 31.9 %all-to-all-start.19 = ((f32[8,2,4,48,128]{4,3,2,1,0:T(8,128)}), f32[8,2,4,48,128]{4,3,2,1,0:T(8,128)}, u32[]{:S(2)}, u32[]{:S(2)}) async-start(f32[8,2,4,48,128]{4,3,2,1,0:T(8,128)} %copy.328), calls=%async_computation.19 | async-start | bytes 3145728 | tf_op jit(solution)/shard_map/all_to_all | solution.py:10
  635.8 13.9 %collective-permute-start.25 = (f32[12,48,256]{2,1,0:T(8,128)S(1)}, f32[12,48,256]{2,1,0:T(8,128)}, u32[]{:S(2)}, u32[]{:S(2)}) collective-permute-start(f32[12,48,256]{2,1,0:T(8,128)S(1)} %copy.327), channel_id=1, source_target_pairs={{24,16},{25,17},{26,18},{27,19},{28,20},{29,21},{30,22},{31,23}} | collective-permute-start | bytes 1769480 | tf_op jit(solution)/shard_map/ppermute | solution.py:52
  637.3 16.5 %collective-permute-start.24 = (f32[12,48,256]{2,1,0:T(8,128)S(1)}, f32[12,48,256]{2,1,0:T(8,128)}, u32[]{:S(2)}, u32[]{:S(2)}) collective-permute-start(f32[12,48,256]{2,1,0:T(8,128)S(1)} %copy.326), channel_id=1, source_target_pairs={{0,8},{1,9},{2,10},{3,11},{4,12},{5,13},{6,14},{7,15}} | collective-permute-start | bytes 1769480 | tf_op jit(solution)/shard_map/ppermute | solution.py:51
  658.4 30.9 %all-to-all-start.20 = ((f32[8,2,4,48,128]{4,3,2,1,0:T(8,128)}), f32[8,2,4,48,128]{4,3,2,1,0:T(8,128)}, u32[]{:S(2)}, u32[]{:S(2)}) async-start(f32[8,2,4,48,128]{4,3,2,1,0:T(8,128)} %copy.333), calls=%async_computation.20 | async-start | bytes 3145728 | tf_op jit(solution)/shard_map/all_to_all | solution.py:10
  670.7 14.7 %collective-permute-start.27 = (f32[12,48,256]{2,1,0:T(8,128)S(1)}, f32[12,48,256]{2,1,0:T(8,128)}, u32[]{:S(2)}, u32[]{:S(2)}) collective-permute-start(f32[12,48,256]{2,1,0:T(8,128)S(1)} %copy.332), channel_id=1, source_target_pairs={{16,8},{24,16},{17,9},{25,17},{18,10},{26,18},{19,11},{27,19},{20,... | collective-permute-start | bytes 1769480 | tf_op jit(solution)/shard_map/ppermute | solution.py:52
  672.2 17.2 %collective-permute-start.26 = (f32[12,48,256]{2,1,0:T(8,128)S(1)}, f32[12,48,256]{2,1,0:T(8,128)}, u32[]{:S(2)}, u32[]{:S(2)}) collective-permute-start(f32[12,48,256]{2,1,0:T(8,128)S(1)} %copy.331), channel_id=1, source_target_pairs={{0,8},{8,16},{1,9},{9,17},{2,10},{10,18},{3,11},{11,19},{4,12},{12... | collective-permute-start | bytes 1769480 | tf_op jit(solution)/shard_map/ppermute | solution.py:51
  694.0 24.4 %all-to-all-start.21 = ((f32[8,2,4,48,128]{4,3,2,1,0:T(8,128)}), f32[8,2,4,48,128]{4,3,2,1,0:T(8,128)S(1)}, u32[]{:S(2)}, u32[]{:S(2)}) async-start(f32[8,2,4,48,128]{4,3,2,1,0:T(8,128)} %copy.338), calls=%async_computation.21 | async-start | bytes 3145728 | tf_op jit(solution)/shard_map/all_to_all | solution.py:10
  699.0 18.1 %collective-permute-start.29 = (f32[12,48,256]{2,1,0:T(8,128)S(1)}, f32[12,48,256]{2,1,0:T(8,128)S(1)}, u32[]{:S(2)}, u32[]{:S(2)}) collective-permute-start(f32[12,48,256]{2,1,0:T(8,128)S(1)} %copy.337), channel_id=1, source_target_pairs={{8,0},{16,8},{24,16},{9,1},{17,9},{25,17},{10,2},{18,10},{26,18},{... | collective-permute-start | bytes 1769480 | tf_op jit(solution)/shard_map/ppermute | solution.py:52
  700.3 18.0 %collective-permute-start.28 = (f32[12,48,256]{2,1,0:T(8,128)S(1)}, f32[12,48,256]{2,1,0:T(8,128)}, u32[]{:S(2)}, u32[]{:S(2)}) collective-permute-start(f32[12,48,256]{2,1,0:T(8,128)S(1)} %copy.336), channel_id=1, source_target_pairs={{0,8},{8,16},{16,24},{1,9},{9,17},{17,25},{2,10},{10,18},{18,26},{... | collective-permute-start | bytes 1769480 | tf_op jit(solution)/shard_map/ppermute | solution.py:51
  721.7 12.7 %collective-permute-start.30 = (f32[12,48,128]{2,0,1:T(8,128)S(1)}, f32[12,48,128]{2,0,1:T(8,128)S(1)}, u32[]{:S(2)}, u32[]{:S(2)}) collective-permute-start(f32[12,48,128]{2,0,1:T(8,128)S(1)} %get-tuple-element.170), channel_id=1, source_target_pairs={{0,8},{1,9},{2,10},{3,11},{4,12},{5,13},{6,14},{7,15}} | collective-permute-start | bytes 884744 | tf_op jit(solution)/shard_map/ppermute | solution.py:51
  726.2 8.2 %collective-permute-start.33 = (f32[12,48,128]{2,0,1:T(8,128)S(1)}, f32[12,48,128]{2,0,1:T(8,128)S(1)}, u32[]{:S(2)}, u32[]{:S(2)}) collective-permute-start(f32[12,48,128]{2,0,1:T(8,128)S(1)} %get-tuple-element.171), channel_id=1, source_target_pairs={{24,16},{25,17},{26,18},{27,19},{28,20},{29,21},{30,22},{31,23}} | collective-permute-start | bytes 884744 | tf_op jit(solution)/shard_map/ppermute | solution.py:52
  735.4 13.4 %collective-permute-start.31 = (f32[12,48,128]{2,0,1:T(8,128)}, f32[12,48,128]{2,0,1:T(8,128)}, u32[]{:S(2)}, u32[]{:S(2)}) collective-permute-start(f32[12,48,128]{2,0,1:T(8,128)} %get-tuple-element.168), channel_id=1, source_target_pairs={{0,8},{8,16},{1,9},{9,17},{2,10},{10,18},{3,11},{11,19},{4,12},{12... | collective-permute-start | bytes 884744 | tf_op jit(solution)/shard_map/ppermute | solution.py:51
  740.5 8.2 %collective-permute-start.34 = (f32[12,48,128]{2,0,1:T(8,128)}, f32[12,48,128]{2,0,1:T(8,128)}, u32[]{:S(2)}, u32[]{:S(2)}) collective-permute-start(f32[12,48,128]{2,0,1:T(8,128)} %get-tuple-element.169), channel_id=1, source_target_pairs={{16,8},{24,16},{17,9},{25,17},{18,10},{26,18},{19,11},{27,19},{20,... | collective-permute-start | bytes 884744 | tf_op jit(solution)/shard_map/ppermute | solution.py:52
  744.8 22.7 %all-to-all-start.18 = ((f32[576,8,16]{0,2,1:T(8,128)}), f32[576,8,16]{0,2,1:T(8,128)S(1)}, u32[]{:S(2)}, u32[]{:S(2)}) async-start(f32[576,8,16]{0,2,1:T(8,128)} %all_to_all.165), calls=%async_computation.18 | async-start | bytes 655360 | tf_op jit(solution)/shard_map/all_to_all | solution.py:134
  751.0 20.0 %collective-permute-start.32 = (f32[12,48,128]{2,0,1:T(8,128)}, f32[12,48,128]{2,0,1:T(8,128)}, u32[]{:S(2)}, u32[]{:S(2)}) collective-permute-start(f32[12,48,128]{2,0,1:T(8,128)} %get-tuple-element.166), channel_id=1, source_target_pairs={{0,8},{8,16},{16,24},{1,9},{9,17},{17,25},{2,10},{10,18},{18,26},{... | collective-permute-start | bytes 884744 | tf_op jit(solution)/shard_map/ppermute | solution.py:51
  759.3 11.7 %collective-permute-start.35 = (f32[12,48,128]{2,0,1:T(8,128)}, f32[12,48,128]{2,0,1:T(8,128)}, u32[]{:S(2)}, u32[]{:S(2)}) collective-permute-start(f32[12,48,128]{2,0,1:T(8,128)} %get-tuple-element.167), channel_id=1, source_target_pairs={{8,0},{16,8},{24,16},{9,1},{17,9},{25,17},{10,2},{18,10},{26,18},{... | collective-permute-start | bytes 884744 | tf_op jit(solution)/shard_map/ppermute | solution.py:52
  767.5 13.2 %all-to-all-start.22 = ((f32[576,8,32]{0,2,1:T(8,128)}), f32[576,8,32]{0,2,1:T(8,128)S(1)}, u32[]{:S(2)}, u32[]{:S(2)}) async-start(f32[576,8,32]{0,2,1:T(8,128)} %copy.368), calls=%async_computation.22 | async-start | bytes 1310720 | tf_op jit(solution)/shard_map/all_to_all | solution.py:134
  780.7 11.0 %all-to-all-start.23 = ((f32[576,8,16]{0,2,1:T(8,128)}), f32[576,8,16]{0,2,1:T(8,128)S(1)}, u32[]{:S(2)}, u32[]{:S(2)}) async-start(f32[576,8,16]{0,2,1:T(8,128)} %all_to_all.176), calls=%async_computation.23 | async-start | bytes 655360 | tf_op jit(solution)/shard_map/all_to_all | solution.py:134
  (69 other events, 365.7 us)

commit v13 on v12

--- a/solution.py
+++ b/solution.py
@@ -66,7 +66,7 @@
     slot_count = coulomb.shape[0]
     block_count = orbitals.shape[0] // (band_count * piece_rows)
     quarter = orbitals.shape[1] // 4
-    bounds = [(0, quarter), (quarter, 3 * quarter), (3 * quarter, 4 * quarter)]
+    bounds = [(0, quarter), (quarter, 4 * quarter)]
     own_rows = [
         lax.all_to_all(orbitals[:, lo:hi], "band", split_axis=0, concat_axis=1, tiled=True)
         for lo, hi in bounds

time: 808 us -> 802 us (level)
  waiting for transfers between devices: 161 us -> 291 us
  starting transfers between devices: 210 us -> 123 us
  matrix products: 193 us -> 163 us
  other arithmetic: 49.1 us -> 38.8 us
    all_to_all x18 -> x12, waiting for transfers between devices: 77.9 us -> 158 us  [band_exchange(): lax.all_to_all(outgoing, 'band', split_axis=0, concat_axis=0, tiled=True)]
    all_to_all x18 -> x12, starting transfers between devices: 91.5 us -> 61.3 us  [band_exchange(): lax.all_to_all(outgoing, 'band', split_axis=0, concat_axis=0, tiled=True)]
    ppermute x9 -> x6, starting transfers between devices: 45.5 us -> 16.9 us  [line_reduce(): lax.ppermute(send_right, axis, [(i, i + 1) for i in range(0, step)])]
    ppermute x9 -> x6, waiting for transfers between devices: 16.1 us -> 43.7 us  [line_reduce(): lax.ppermute(send_right, axis, [(i, i + 1) for i in range(0, step)])]
    ppermute x9 -> x6, waiting for transfers between devices: 43.2 us -> 65.1 us  [line_gather(): lax.ppermute(leftward, axis, [(i + 1, i) for i in range(0, count - step)])]
    dot_general x9 -> x6, matrix products: 70.1 us -> 53.8 us  [body(): jnp.dot(r[0], r[1].T, precision=PRECISION, preferred_element_type=jnp.flo...]
    dot_general x9 -> x6, matrix products: 63.3 us -> 51.7 us  [body(): jnp.dot(kernel, r[1], precision=PRECISION, preferred_element_type=jnp.flo...]
    ppermute x9 -> x6, starting transfers between devices: 21.6 us -> 12.8 us  [line_gather(): lax.ppermute(rightward, axis, [(i, i + 1) for i in range(step - 1, count...]
  transfers between devices with their start and end apart: 60 -> 40, of which waited for: 26 -> 18; matrix products, arithmetic and copies ran while one was open for 44% -> 38% of each run, Pallas kernels for 0% -> 0%
where the time goes in v13:
time: 802 us; the launch traced here: 788 us
  waiting for transfers between devices  291 us (36%)
  local copies, waits for them, and re-layouts  169 us (21%)
  matrix products  163 us (20%)
  starting transfers between devices  123 us (15%)
  other arithmetic  38.8 us (5%)
    all_to_all x12, waiting for transfers between devices, band_exchange(): lax.all_to_all(outgoing, 'band', split_axis=0, concat_axis=0, tiled=True)  158 us
    ppermute x6, waiting for transfers between devices, line_gather(): lax.ppermute(leftward, axis, [(i + 1, i) for i in range(0, count - step)])  65.1 us
    all_to_all x12, starting transfers between devices, band_exchange(): lax.all_to_all(outgoing, 'band', split_axis=0, concat_axis=0, tiled=True)  61.3 us
    dot_general x6, matrix products, body(): jnp.dot(r[0], r[1].T, precision=PRECISION, preferred_element_type=jnp.flo...  53.8 us
    dot_general x6, matrix products, body(): jnp.dot(kernel, r[1], precision=PRECISION, preferred_element_type=jnp.flo...  51.7 us
    dot_general x6, matrix products, body(): jnp.dot(kernel.T, r[0], precision=PRECISION, preferred_element_type=jnp.f...  46.1 us
    ppermute x6, waiting for transfers between devices, line_reduce(): lax.ppermute(send_right, axis, [(i, i + 1) for i in range(0, step)])  43.7 us
    dot_general x3, local copies, waits for them, and re-layouts, body(): jnp.dot(kernel.T, r[0], precision=PRECISION, preferred_element_type=jnp.f...  28.9 us
  transfers between devices with their start and end apart: 40, of which 18 were waited for; matrix products, arithmetic and copies ran while one was open for 38% of the time, Pallas kernels for 0%

profile of v13, /device:TPU:2, one launch (start us, length us, event | category | flops | bytes accessed | tf_op | source)
XLA Modules:
  0.0 788.4 jit_solution(2936184241124098748)
XLA Ops:
  2.0 4.3 all-to-all-start.1
  7.8 4.7 all-to-all-done.1
  12.4 4.9 all-to-all-start
  18.6 4.6 collective-permute-start
  23.4 5.6 collective-permute-done.1
  34.4 5.4 collective-permute-done.3
  44.3 5.4 collective-permute-done.5
  57.5 5.0 all-to-all-start.2
  65.4 5.5 collective-permute-start.6
  75.8 12.2 %collective-permute-done.7 = f32[576,384]{1,0:T(8,128)} collective-permute-done((f32[576,384]{1,0:T(8,128)}, f32[576,384]{1,0:T(8,128)}, u32[]{:S(2)}, u32[]{:S(2)}) %collective-permute-start.7) | collective-permute-done | bytes 884768 | tf_op jit(solution)/shard_map/ppermute | solution.py:24
  88.8 4.5 all-to-all-start.3
  100.3 21.5 %collective-permute-done.9 = f32[576,384]{1,0:T(8,128)} collective-permute-done((f32[576,384]{1,0:T(8,128)}, f32[576,384]{1,0:T(8,128)}, u32[]{:S(2)}, u32[]{:S(2)}) %collective-permute-start.9) | collective-permute-done | bytes 884768 | tf_op jit(solution)/shard_map/ppermute | solution.py:24
  121.9 4.5 all-to-all-start.4
  139.6 15.0 %collective-permute-done.11 = f32[576,384]{1,0:T(8,128)S(1)} collective-permute-done((f32[576,384]{1,0:T(8,128)}, f32[576,384]{1,0:T(8,128)S(1)}, u32[]{:S(2)}, u32[]{:S(2)}) %collective-permute-start.11) | collective-permute-done | bytes 884768 | tf_op jit(solution)/shard_map/ppermute | solution.py:24
  162.0 5.1 fusion.19
  167.1 4.8 all-to-all-start.7
  174.9 5.1 fusion.20
  180.0 45.3 %all-to-all-done.7 = f32[8,2,4,48,384]{4,3,2,1,0:T(8,128)} async-done(((f32[8,2,4,48,384]{4,3,2,1,0:T(8,128)}), f32[8,2,4,48,384]{4,3,2,1,0:T(8,128)}, u32[]{:S(2)}, u32[]{:S(2)}) %all-to-all-start.7) | async-done | bytes 4718624 | tf_op jit(solution)/shard_map/all_to_all | solution.py:10
  225.3 6.0 all-to-all-start.5
  251.3 4.2 fusion.48
  257.2 27.5 %all-to-all-done.5 = f32[8,2,4,48,384]{4,3,2,1,0:T(8,128)} async-done(((f32[8,2,4,48,384]{4,3,2,1,0:T(8,128)}), f32[8,2,4,48,384]{4,3,2,1,0:T(8,128)}, u32[]{:S(2)}, u32[]{:S(2)}) %all-to-all-start.5) | async-done | bytes 4718624 | tf_op jit(solution)/shard_map/all_to_all | solution.py:10
  284.6 6.3 all-to-all-start.9
  300.5 7.5 fusion.56
  308.0 9.0 %fusion.7 = f32[1536,1536]{1,0:T(8,128)} fusion(f32[1536,1536]{1,0:T(8,128)S(1)} %fusion.56, f32[1536,128]{1,0:T(8,128)S(1)} %bitcast.373, f32[1536,128]{1,0:T(8,128)S(1)} %bitcast.372, f32[3,1536,1536]{2,1,0:T(8,128)} %param.9), kind=kOutput, calls=%fused_computation.16 | convolution fusion | flops 1816657920 | bytes 29884416 | tf_op jit(solution)/shard_map/dot_general | solution.py:107
  317.0 9.7 %copy.223 = f32[1536,1536]{1,0:T(8,128)} copy(f32[1536,1536]{0,1:T(8,128)} %bitcast.322) | data formatting | bytes 18874368 | tf_op jit(solution)/shard_map/dot_general | solution.py:113
  326.7 7.2 convolution_bitcast_fusion.9
  340.2 7.5 fusion.55
  347.7 8.6 %fusion.6 = f32[1536,1536]{1,0:T(8,128)S(1)} fusion(f32[1536,1536]{1,0:T(8,128)S(1)} %fusion.55, f32[1536,128]{1,0:T(8,128)S(1)} %bitcast.368, f32[1536,128]{1,0:T(8,128)} %bitcast.369, f32[3,1536,1536]{2,1,0:T(8,128)} %param.9), kind=kOutput, calls=%fused_computation.15 | convolution fusion | flops 1816657920 | bytes 29884416 | tf_op jit(solution)/shard_map/dot_general | solution.py:107
  360.0 4.7 convolution_bitcast_fusion.11
  364.7 4.5 all-to-all-start.8
  373.8 9.6 %copy.214 = f32[1536,1536]{1,0:T(8,128)} copy(f32[1536,1536]{0,1:T(8,128)} %bitcast.329) | data formatting | bytes 18874368 | tf_op jit(solution)/shard_map/dot_general | solution.py:113
  383.5 6.9 convolution_bitcast_fusion.10
  392.7 10.1 %fusion.57 = f32[1536,1536]{1,0:T(8,128)} fusion(f32[1536,384]{1,0:T(8,128)S(1)} %bitcast.343, f32[1536,384]{1,0:T(8,128)S(1)} %bitcast.352), kind=kOutput, calls=%fused_computation.131 | convolution fusion | flops 5435817984 | bytes 14155776 | tf_op jit(solution)/shard_map/dot_general | solution.py:107
  402.8 4.5 all-to-all-start.6
  407.3 11.1 %fusion.8 = f32[1536,1536]{1,0:T(8,128)} fusion(f32[1536,1536]{1,0:T(8,128)} %fusion.57, f32[1536,128]{1,0:T(8,128)} %bitcast.365, f32[1536,128]{1,0:T(8,128)S(1)} %bitcast.363, f32[3,1536,1536]{2,1,0:T(8,128)} %param.9), kind=kOutput, calls=%fused_computation.17 | convolution fusion | flops 1816657920 | bytes 29884416 | tf_op jit(solution)/shard_map/dot_general | solution.py:107
  418.4 9.7 %copy.232 = f32[1536,1536]{1,0:T(8,128)} copy(f32[1536,1536]{0,1:T(8,128)} %bitcast.325) | data formatting | bytes 18874368 | tf_op jit(solution)/shard_map/dot_general | solution.py:113
  428.0 6.7 convolution_bitcast_fusion.7
  440.2 4.5 all-to-all-start.10
  444.7 11.1 %convolution_bitcast_fusion.5 = f32[1,4,8,48,384]{4,3,2,1,0:T(8,128)S(1)} fusion(f32[4,8,48,1536]{3,2,1,0:T(8,128)} %bitcast.330, f32[1536,384,1,1]{1,0,3,2:T(8,128)} %bitcast.353), kind=kOutput, calls=%fused_computation.42 | convolution fusion | flops 5435817984 | bytes 14155776 | tf_op jit(solution)/shard_map/dot_general | solution.py:112
  455.8 10.8 %convolution_bitcast_fusion.4 = f32[1,4,8,48,384]{4,3,2,1,0:T(8,128)S(1)} fusion(f32[4,8,48,1536]{3,2,1,0:T(8,128)} %bitcast.339, f32[1536,384,1,1]{1,0,3,2:T(8,128)S(1)} %bitcast.348), kind=kOutput, calls=%fused_computation.41 | convolution fusion | flops 5435817984 | bytes 14155776 | tf_op jit(solution)/shard_map/dot_general | solution.py:113
  486.2 4.6 all-to-all-start.11
  490.8 11.1 %convolution_bitcast_fusion.3 = f32[1,4,8,48,384]{4,3,2,1,0:T(8,128)S(1)} fusion(f32[4,8,48,1536]{3,2,1,0:T(8,128)} %bitcast.324, f32[1536,384,1,1]{1,0,3,2:T(8,128)} %bitcast.349), kind=kOutput, calls=%fused_computation.40 | convolution fusion | flops 5435817984 | bytes 14155776 | tf_op jit(solution)/shard_map/dot_general | solution.py:112
  505.0 10.4 %convolution_bitcast_fusion.2 = f32[1,4,8,48,384]{4,3,2,1,0:T(8,128)S(1)} fusion(f32[4,8,48,1536]{3,2,1,0:T(8,128)} %bitcast.334, f32[1536,384,1,1]{1,0,3,2:T(8,128)S(1)} %bitcast.346), kind=kOutput, calls=%fused_computation.39 | convolution fusion | flops 5435817984 | bytes 14155776 | tf_op jit(solution)/shard_map/dot_general | solution.py:113
  518.8 25.3 %all-to-all-done.11 = f32[8,2,4,48,384]{4,3,2,1,0:T(8,128)} async-done(((f32[8,2,4,48,384]{4,3,2,1,0:T(8,128)}), f32[8,2,4,48,384]{4,3,2,1,0:T(8,128)}, u32[]{:S(2)}, u32[]{:S(2)}) %all-to-all-start.11) | async-done | bytes 4718624 | tf_op jit(solution)/shard_map/all_to_all | solution.py:10
  546.3 5.0 copy.238
  551.3 6.0 all-to-all-start.12
  557.3 10.9 %convolution_bitcast_fusion.1 = f32[1,4,8,48,384]{4,3,2,1,0:T(8,128)S(1)} fusion(f32[4,8,48,1536]{3,2,1,0:T(8,128)} %bitcast.327, f32[1536,384,1,1]{1,0,3,2:T(8,128)} %bitcast.351), kind=kOutput, calls=%fused_computation.38 | convolution fusion | flops 5435817984 | bytes 14155776 | tf_op jit(solution)/shard_map/dot_general | solution.py:112
  572.0 10.2 %convolution_bitcast_fusion = f32[1,4,8,48,384]{4,3,2,1,0:T(8,128)S(1)} fusion(f32[4,8,48,1536]{3,2,1,0:T(8,128)} %bitcast.336, f32[1536,384,1,1]{1,0,3,2:T(8,128)S(1)} %bitcast.344), kind=kOutput, calls=%fused_computation.37 | convolution fusion | flops 5435817984 | bytes 14155776 | tf_op jit(solution)/shard_map/dot_general | solution.py:113
  584.8 25.8 %all-to-all-done.12 = f32[8,2,4,48,384]{4,3,2,1,0:T(8,128)} async-done(((f32[8,2,4,48,384]{4,3,2,1,0:T(8,128)}), f32[8,2,4,48,384]{4,3,2,1,0:T(8,128)}, u32[]{:S(2)}, u32[]{:S(2)}) %all-to-all-start.12) | async-done | bytes 4718624 | tf_op jit(solution)/shard_map/all_to_all | solution.py:10
  611.9 5.1 copy.239
  617.0 6.0 all-to-all-start.13
  626.1 7.3 copy.242
  633.4 7.2 copy.243
  642.0 34.3 %all-to-all-done.13 = f32[8,2,4,48,384]{4,3,2,1,0:T(8,128)} async-done(((f32[8,2,4,48,384]{4,3,2,1,0:T(8,128)}), f32[8,2,4,48,384]{4,3,2,1,0:T(8,128)}, u32[]{:S(2)}, u32[]{:S(2)}) %all-to-all-start.13) | async-done | bytes 4718624 | tf_op jit(solution)/shard_map/all_to_all | solution.py:10
  676.3 7.4 copy.244
  683.8 7.2 fusion.21
  694.8 18.0 %collective-permute-done.18 = f32[12,48,384]{2,1,0:T(8,128)S(1)} collective-permute-done((f32[12,48,384]{2,1,0:T(8,128)S(1)}, f32[12,48,384]{2,1,0:T(8,128)S(1)}, u32[]{:S(2)}, u32[]{:S(2)}) %collective-permute-start.18) | collective-permute-done | bytes 884768 | tf_op jit(solution)/shard_map/ppermute | solution.py:51
  713.2 4.4 collective-permute-start.19
  718.6 17.2 %collective-permute-done.19 = f32[12,48,384]{2,1,0:T(8,128)S(1)} collective-permute-done((f32[12,48,384]{2,1,0:T(8,128)S(1)}, f32[12,48,384]{2,1,0:T(8,128)S(1)}, u32[]{:S(2)}, u32[]{:S(2)}) %collective-permute-start.19) | collective-permute-done | bytes 884768 | tf_op jit(solution)/shard_map/ppermute | solution.py:51
  737.0 5.3 collective-permute-start.20
  746.6 4.0 all-to-all-start.14
  750.7 8.4 %collective-permute-done.20 = f32[12,48,384]{2,1,0:T(8,128)} collective-permute-done((f32[12,48,384]{2,1,0:T(8,128)}, f32[12,48,384]{2,1,0:T(8,128)}, u32[]{:S(2)}, u32[]{:S(2)}) %collective-permute-start.20) | collective-permute-done | bytes 884768 | tf_op jit(solution)/shard_map/ppermute | solution.py:51
  759.1 6.2 collective-permute-done.23
  774.6 11.8 %all-to-all-done.15 = f32[576,8,48]{0,2,1:T(8,128)S(1)} async-done(((f32[576,8,48]{0,2,1:T(8,128)}), f32[576,8,48]{0,2,1:T(8,128)S(1)}, u32[]{:S(2)}, u32[]{:S(2)}) %all-to-all-start.15) | async-done | bytes 884768 | tf_op jit(solution)/shard_map/all_to_all | solution.py:134
  (249 shorter events, 172.9 us)
Async XLA Ops:
  0.0 6.3 slice-start.2
  0.0 6.2 copy-start.33
  2.0 10.4 %all-to-all-start.1 = ((f32[8,576,16]{1,2,0:T(8,128)}), f32[8,576,16]{1,2,0:T(8,128)S(1)}, u32[]{:S(2)}, u32[]{:S(2)}) async-start(f32[8,576,16]{1,2,0:T(8,128)} %copy.188), calls=%async_computation.1 | async-start | bytes 655360 | tf_op jit(solution)/shard_map/all_to_all | solution.py:71
  6.3 16.9 %copy-start.28 = (s32[8,6]{0,1:T(8,128)}, s32[8,6]{0,1:T(8,128)S(1)}, u32[]{:S(2)}) copy-start(s32[8,6]{0,1:T(8,128)S(1)} %get-tuple-element.80) | copy-start | bytes 580
  12.4 45.1 %all-to-all-start = ((f32[8,576,48]{1,2,0:T(8,128)}), f32[8,576,48]{1,2,0:T(8,128)S(1)}, u32[]{:S(2)}, u32[]{:S(2)}) async-start(f32[8,576,48]{1,2,0:T(8,128)} %copy.186), calls=%async_computation | async-start | bytes 1966080 | tf_op jit(solution)/shard_map/all_to_all | solution.py:71
  17.4 11.6 %collective-permute-start.1 = (f32[576,128]{0,1:T(8,128)S(1)}, f32[576,128]{0,1:T(8,128)S(1)}, u32[]{:S(2)}, u32[]{:S(2)}) collective-permute-start(f32[576,128]{0,1:T(8,128)S(1)} %bitcast.379), channel_id=1, source_target_pairs={{8,0},{16,8},{24,16},{9,1},{17,9},{25,17},{10,2},{18,10},{26,18},{... | collective-permute-start | bytes 884744 | tf_op jit(solution)/shard_map/ppermute | solution.py:24
  18.6 11.7 %collective-permute-start = (f32[576,128]{0,1:T(8,128)S(1)}, f32[576,128]{0,1:T(8,128)S(1)}, u32[]{:S(2)}, u32[]{:S(2)}) collective-permute-start(f32[576,128]{0,1:T(8,128)S(1)} %bitcast.380), channel_id=1, source_target_pairs={{0,8},{8,16},{16,24},{1,9},{9,17},{17,25},{2,10},{10,18},{18,26},{... | collective-permute-start | bytes 884744 | tf_op jit(solution)/shard_map/ppermute | solution.py:23
  29.0 10.8 %collective-permute-start.3 = (f32[576,128]{0,1:T(8,128)S(1)}, f32[576,128]{0,1:T(8,128)S(1)}, u32[]{:S(2)}, u32[]{:S(2)}) collective-permute-start(f32[576,128]{0,1:T(8,128)S(1)} %collective-permute-done.1), channel_id=1, source_target_pairs={{8,0},{16,8},{9,1},{17,9},{10,2},{18,10},{11,3},{19,11},{12,4},{20... | collective-permute-start | bytes 884744 | tf_op jit(solution)/shard_map/ppermute | solution.py:24
  30.3 10.8 %collective-permute-start.2 = (f32[576,128]{0,1:T(8,128)S(1)}, f32[576,128]{0,1:T(8,128)S(1)}, u32[]{:S(2)}, u32[]{:S(2)}) collective-permute-start(f32[576,128]{0,1:T(8,128)S(1)} %collective-permute-done), channel_id=1, source_target_pairs={{8,16},{16,24},{9,17},{17,25},{10,18},{18,26},{11,19},{19,27},{12,... | collective-permute-start | bytes 884744 | tf_op jit(solution)/shard_map/ppermute | solution.py:23
  31.1 23.6 %copy-start.35 = (pred[8,2]{1,0:T(8,128)(4,1)}, pred[8,2]{1,0:T(8,128)(4,1)S(1)}, u32[]{:S(2)}) copy-start(pred[8,2]{1,0:T(8,128)(4,1)S(1)} %copy.187) | copy-start | bytes 52
  39.8 9.9 %collective-permute-start.5 = (f32[576,128]{0,1:T(8,128)S(1)}, f32[576,128]{0,1:T(8,128)S(1)}, u32[]{:S(2)}, u32[]{:S(2)}) collective-permute-start(f32[576,128]{0,1:T(8,128)S(1)} %collective-permute-done.3), channel_id=1, source_target_pairs={{8,0},{9,1},{10,2},{11,3},{12,4},{13,5},{14,6},{15,7}} | collective-permute-start | bytes 884744 | tf_op jit(solution)/shard_map/ppermute | solution.py:24
  41.1 8.7 %collective-permute-start.4 = (f32[576,128]{0,1:T(8,128)S(1)}, f32[576,128]{0,1:T(8,128)S(1)}, u32[]{:S(2)}, u32[]{:S(2)}) collective-permute-start(f32[576,128]{0,1:T(8,128)S(1)} %collective-permute-done.2), channel_id=1, source_target_pairs={{16,24},{17,25},{18,26},{19,27},{20,28},{21,29},{22,30},{23,31}} | collective-permute-start | bytes 884744 | tf_op jit(solution)/shard_map/ppermute | solution.py:23
  57.5 31.4 %all-to-all-start.2 = ((f32[8,2,4,48,128]{4,3,2,1,0:T(8,128)}), f32[8,2,4,48,128]{4,3,2,1,0:T(8,128)}, u32[]{:S(2)}, u32[]{:S(2)}) async-start(f32[8,2,4,48,128]{4,3,2,1,0:T(8,128)} %fusion.29), calls=%async_computation.2 | async-start | bytes 3145728 | tf_op jit(solution)/shard_map/all_to_all | solution.py:10
  64.1 23.9 %collective-permute-start.7 = (f32[576,384]{1,0:T(8,128)}, f32[576,384]{1,0:T(8,128)}, u32[]{:S(2)}, u32[]{:S(2)}) collective-permute-start(f32[576,384]{1,0:T(8,128)} %copy.199), channel_id=1, source_target_pairs={{8,0},{16,8},{24,16},{9,1},{17,9},{25,17},{10,2},{18,10},{26,18},{... | collective-permute-start | bytes 2654216 | tf_op jit(solution)/shard_map/ppermute | solution.py:24
  65.4 23.5 %collective-permute-start.6 = (f32[576,384]{1,0:T(8,128)S(1)}, f32[576,384]{1,0:T(8,128)}, u32[]{:S(2)}, u32[]{:S(2)}) collective-permute-start(f32[576,384]{1,0:T(8,128)S(1)} %copy.198), channel_id=1, source_target_pairs={{0,8},{8,16},{16,24},{1,9},{9,17},{17,25},{2,10},{10,18},{18,26},{... | collective-permute-start | bytes 2654216 | tf_op jit(solution)/shard_map/ppermute | solution.py:23
  88.8 33.0 %all-to-all-start.3 = ((f32[8,2,4,48,128]{4,3,2,1,0:T(8,128)}), f32[8,2,4,48,128]{4,3,2,1,0:T(8,128)}, u32[]{:S(2)}, u32[]{:S(2)}) async-start(f32[8,2,4,48,128]{4,3,2,1,0:T(8,128)} %fusion.28), calls=%async_computation.3 | async-start | bytes 3145728 | tf_op jit(solution)/shard_map/all_to_all | solution.py:10
  93.4 7.0 collective-permute-start.8
  94.1 27.8 %collective-permute-start.9 = (f32[576,384]{1,0:T(8,128)}, f32[576,384]{1,0:T(8,128)}, u32[]{:S(2)}, u32[]{:S(2)}) collective-permute-start(f32[576,384]{1,0:T(8,128)} %collective-permute-done.7), channel_id=1, source_target_pairs={{8,0},{16,8},{9,1},{17,9},{10,2},{18,10},{11,3},{19,11},{12,4},{20... | collective-permute-start | bytes 2654216 | tf_op jit(solution)/shard_map/ppermute | solution.py:24
  121.9 32.7 %all-to-all-start.4 = ((f32[8,2,4,48,128]{4,3,2,1,0:T(8,128)}), f32[8,2,4,48,128]{4,3,2,1,0:T(8,128)}, u32[]{:S(2)}, u32[]{:S(2)}) async-start(f32[8,2,4,48,128]{4,3,2,1,0:T(8,128)} %fusion.27), calls=%async_computation.4 | async-start | bytes 3145728 | tf_op jit(solution)/shard_map/all_to_all | solution.py:10
  130.1 9.5 %collective-permute-start.10 = (f32[576,384]{1,0:T(8,128)S(1)}, f32[576,384]{1,0:T(8,128)S(1)}, u32[]{:S(2)}, u32[]{:S(2)}) collective-permute-start(f32[576,384]{1,0:T(8,128)S(1)} %collective-permute-done.8), channel_id=1, source_target_pairs={{16,24},{17,25},{18,26},{19,27},{20,28},{21,29},{22,30},{23,31}} | collective-permute-start | bytes 2654216 | tf_op jit(solution)/shard_map/ppermute | solution.py:23
  130.8 23.8 %collective-permute-start.11 = (f32[576,384]{1,0:T(8,128)}, f32[576,384]{1,0:T(8,128)S(1)}, u32[]{:S(2)}, u32[]{:S(2)}) collective-permute-start(f32[576,384]{1,0:T(8,128)} %collective-permute-done.9), channel_id=1, source_target_pairs={{8,0},{9,1},{10,2},{11,3},{12,4},{13,5},{14,6},{15,7}} | collective-permute-start | bytes 2654216 | tf_op jit(solution)/shard_map/ppermute | solution.py:24
  167.1 58.2 %all-to-all-start.7 = ((f32[8,2,4,48,384]{4,3,2,1,0:T(8,128)}), f32[8,2,4,48,384]{4,3,2,1,0:T(8,128)}, u32[]{:S(2)}, u32[]{:S(2)}) async-start(f32[8,2,4,48,384]{4,3,2,1,0:T(8,128)} %fusion.19), calls=%async_computation.7 | async-start | bytes 9437184 | tf_op jit(solution)/shard_map/all_to_all | solution.py:10
  180.0 51.3 %copy-start.34 = (s32[32,6]{0,1:T(8,128)S(1)}, s32[32,6]{0,1:T(8,128)}, u32[]{:S(2)}) copy-start(s32[32,6]{0,1:T(8,128)} %param.8) | copy-start | bytes 2308
  225.3 59.3 %all-to-all-start.5 = ((f32[8,2,4,48,384]{4,3,2,1,0:T(8,128)}), f32[8,2,4,48,384]{4,3,2,1,0:T(8,128)}, u32[]{:S(2)}, u32[]{:S(2)}) async-start(f32[8,2,4,48,384]{4,3,2,1,0:T(8,128)} %fusion.20), calls=%async_computation.5 | async-start | bytes 9437184 | tf_op jit(solution)/shard_map/all_to_all | solution.py:10
  284.6 80.1 %all-to-all-start.9 = ((f32[8,2,4,48,384]{4,3,2,1,0:T(8,128)}), f32[8,2,4,48,384]{4,3,2,1,0:T(8,128)}, u32[]{:S(2)}, u32[]{:S(2)}) async-start(f32[8,2,4,48,384]{4,3,2,1,0:T(8,128)} %fusion.18), calls=%async_computation.9 | async-start | bytes 9437184 | tf_op jit(solution)/shard_map/all_to_all | solution.py:10
  295.6 43.7 %copy-start.5 = (f32[1,4,8,48,384]{4,3,2,1,0:T(8,128)}, f32[1,4,8,48,384]{4,3,2,1,0:T(8,128)S(1)}, u32[]{:S(2)}) copy-start(f32[1,4,8,48,384]{4,3,2,1,0:T(8,128)S(1)} %copy.212) | copy-start | bytes 7077892
  298.1 9.9 %copy-start.3 = (f32[1,4,8,48,384]{4,3,2,1,0:T(8,128)}, f32[1,4,8,48,384]{4,3,2,1,0:T(8,128)S(1)}, u32[]{:S(2)}) copy-start(f32[1,4,8,48,384]{4,3,2,1,0:T(8,128)S(1)} %copy.221) | copy-start | bytes 7077892
  300.5 7.6 copy-start.19
  300.5 7.6 copy-start.20
  326.7 7.2 copy-start.1
  326.7 7.2 copy-start.21
  340.2 7.5 copy-start.17
  347.7 12.2 %copy-start.18 = (f32[1,4,8,48,128]{4,3,2,1,0:T(8,128)S(1)}, f32[1,4,8,48,128]{4,3,2,1,0:T(8,128)}, u32[]{:S(2)}) copy-start(f32[1,4,8,48,128]{4,3,2,1,0:T(8,128)} %copy.201) | copy-start | bytes 2359300
  364.7 38.1 %all-to-all-start.8 = ((f32[8,2,4,48,128]{4,3,2,1,0:T(8,128)}), f32[8,2,4,48,128]{4,3,2,1,0:T(8,128)}, u32[]{:S(2)}, u32[]{:S(2)}) async-start(f32[8,2,4,48,128]{4,3,2,1,0:T(8,128)} %copy.224), calls=%async_computation.8 | async-start | bytes 3145728 | tf_op jit(solution)/shard_map/all_to_all | solution.py:10
  383.4 6.9 copy-start.22
  402.8 37.4 %all-to-all-start.6 = ((f32[8,2,4,48,128]{4,3,2,1,0:T(8,128)}), f32[8,2,4,48,128]{4,3,2,1,0:T(8,128)}, u32[]{:S(2)}, u32[]{:S(2)}) async-start(f32[8,2,4,48,128]{4,3,2,1,0:T(8,128)} %copy.215), calls=%async_computation.6 | async-start | bytes 3145728 | tf_op jit(solution)/shard_map/all_to_all | solution.py:10
  428.0 6.7 copy-start.2
  428.0 6.8 copy-start.16
  440.2 35.9 %all-to-all-start.10 = ((f32[8,2,4,48,128]{4,3,2,1,0:T(8,128)}), f32[8,2,4,48,128]{4,3,2,1,0:T(8,128)}, u32[]{:S(2)}, u32[]{:S(2)}) async-start(f32[8,2,4,48,128]{4,3,2,1,0:T(8,128)} %copy.233), calls=%async_computation.10 | async-start | bytes 3145728 | tf_op jit(solution)/shard_map/all_to_all | solution.py:10
  444.7 11.1 %copy-start.6 = (f32[1,4,8,48,384]{4,3,2,1,0:T(8,128)S(1)}, f32[1,4,8,48,384]{4,3,2,1,0:T(8,128)}, u32[]{:S(2)}) copy-start(f32[1,4,8,48,384]{4,3,2,1,0:T(8,128)} %copy-done.5) | copy-start | bytes 7077892
  476.1 7.4 slice-start
  486.2 57.9 %all-to-all-start.11 = ((f32[8,2,4,48,384]{4,3,2,1,0:T(8,128)}), f32[8,2,4,48,384]{4,3,2,1,0:T(8,128)}, u32[]{:S(2)}, u32[]{:S(2)}) async-start(f32[8,2,4,48,384]{4,3,2,1,0:T(8,128)} %copy.237), calls=%async_computation.11 | async-start | bytes 9437184 | tf_op jit(solution)/shard_map/all_to_all | solution.py:10
  490.8 14.1 %copy-start.4 = (f32[1,4,8,48,384]{4,3,2,1,0:T(8,128)S(1)}, f32[1,4,8,48,384]{4,3,2,1,0:T(8,128)}, u32[]{:S(2)}) copy-start(f32[1,4,8,48,384]{4,3,2,1,0:T(8,128)} %copy-done.3) | copy-start | bytes 7077892
  501.9 16.2 %collective-permute-start.12 = (f32[12,48,128]{2,0,1:T(8,128)S(1)}, f32[12,48,128]{2,0,1:T(8,128)S(1)}, u32[]{:S(2)}, u32[]{:S(2)}) collective-permute-start(f32[12,48,128]{2,0,1:T(8,128)S(1)} %get-tuple-element.61), channel_id=1, source_target_pairs={{0,8},{1,9},{2,10},{3,11},{4,12},{5,13},{6,14},{7,15}} | collective-permute-start | bytes 884744 | tf_op jit(solution)/shard_map/ppermute | solution.py:51
  503.5 15.3 %collective-permute-start.13 = (f32[12,48,128]{2,0,1:T(8,128)S(1)}, f32[12,48,128]{2,0,1:T(8,128)}, u32[]{:S(2)}, u32[]{:S(2)}) collective-permute-start(f32[12,48,128]{2,0,1:T(8,128)S(1)} %get-tuple-element.62), channel_id=1, source_target_pairs={{24,16},{25,17},{26,18},{27,19},{28,20},{29,21},{30,22},{31,23}} | collective-permute-start | bytes 884744 | tf_op jit(solution)/shard_map/ppermute | solution.py:52
  551.3 59.3 %all-to-all-start.12 = ((f32[8,2,4,48,384]{4,3,2,1,0:T(8,128)}), f32[8,2,4,48,384]{4,3,2,1,0:T(8,128)}, u32[]{:S(2)}, u32[]{:S(2)}) async-start(f32[8,2,4,48,384]{4,3,2,1,0:T(8,128)} %copy.238), calls=%async_computation.12 | async-start | bytes 9437184 | tf_op jit(solution)/shard_map/all_to_all | solution.py:10
  568.3 16.6 %collective-permute-start.14 = (f32[12,48,128]{2,0,1:T(8,128)}, f32[12,48,128]{2,0,1:T(8,128)}, u32[]{:S(2)}, u32[]{:S(2)}) collective-permute-start(f32[12,48,128]{2,0,1:T(8,128)} %get-tuple-element.66), channel_id=1, source_target_pairs={{0,8},{8,16},{1,9},{9,17},{2,10},{10,18},{3,11},{11,19},{4,12},{12... | collective-permute-start | bytes 884744 | tf_op jit(solution)/shard_map/ppermute | solution.py:51
  570.6 14.2 %collective-permute-start.15 = (f32[12,48,128]{2,0,1:T(8,128)S(1)}, f32[12,48,128]{2,0,1:T(8,128)}, u32[]{:S(2)}, u32[]{:S(2)}) collective-permute-start(f32[12,48,128]{2,0,1:T(8,128)S(1)} %get-tuple-element.67), channel_id=1, source_target_pairs={{16,8},{24,16},{17,9},{25,17},{18,10},{26,18},{19,11},{27,19},{20,... | collective-permute-start | bytes 884744 | tf_op jit(solution)/shard_map/ppermute | solution.py:52
  582.2 28.4 %copy-start.14 = (f32[4,48,128,12]{2,3,1,0:T(8,128)S(1)}, f32[4,48,128,12]{2,3,1,0:T(8,128)}, u32[]{:S(2)}) copy-start(f32[4,48,128,12]{2,3,1,0:T(8,128)} %copy-done.13) | copy-start | bytes 3538948
  617.0 59.4 %all-to-all-start.13 = ((f32[8,2,4,48,384]{4,3,2,1,0:T(8,128)}), f32[8,2,4,48,384]{4,3,2,1,0:T(8,128)}, u32[]{:S(2)}, u32[]{:S(2)}) async-start(f32[8,2,4,48,384]{4,3,2,1,0:T(8,128)} %copy.239), calls=%async_computation.13 | async-start | bytes 9437184 | tf_op jit(solution)/shard_map/all_to_all | solution.py:10
  623.0 17.5 %collective-permute-start.16 = (f32[12,48,128]{2,0,1:T(8,128)S(1)}, f32[12,48,128]{2,0,1:T(8,128)S(1)}, u32[]{:S(2)}, u32[]{:S(2)}) collective-permute-start(f32[12,48,128]{2,0,1:T(8,128)S(1)} %get-tuple-element.71), channel_id=1, source_target_pairs={{0,8},{8,16},{16,24},{1,9},{9,17},{17,25},{2,10},{10,18},{18,26},{... | collective-permute-start | bytes 884744 | tf_op jit(solution)/shard_map/ppermute | solution.py:51
  624.6 15.9 %collective-permute-start.17 = (f32[12,48,128]{2,0,1:T(8,128)S(1)}, f32[12,48,128]{2,0,1:T(8,128)S(1)}, u32[]{:S(2)}, u32[]{:S(2)}) collective-permute-start(f32[12,48,128]{2,0,1:T(8,128)S(1)} %get-tuple-element.72), channel_id=1, source_target_pairs={{8,0},{16,8},{24,16},{9,1},{17,9},{25,17},{10,2},{18,10},{26,18},{... | collective-permute-start | bytes 884744 | tf_op jit(solution)/shard_map/ppermute | solution.py:52
  676.3 7.4 copy-start.10
  676.3 7.5 copy-start.11
  692.2 20.7 %collective-permute-start.18 = (f32[12,48,384]{2,1,0:T(8,128)S(1)}, f32[12,48,384]{2,1,0:T(8,128)S(1)}, u32[]{:S(2)}, u32[]{:S(2)}) collective-permute-start(f32[12,48,384]{2,1,0:T(8,128)S(1)} %copy.246), channel_id=1, source_target_pairs={{0,8},{1,9},{2,10},{3,11},{4,12},{5,13},{6,14},{7,15}} | collective-permute-start | bytes 2654216 | tf_op jit(solution)/shard_map/ppermute | solution.py:51
  694.1 23.5 %collective-permute-start.21 = (f32[12,48,384]{2,1,0:T(8,128)S(1)}, f32[12,48,384]{2,1,0:T(8,128)S(1)}, u32[]{:S(2)}, u32[]{:S(2)}) collective-permute-start(f32[12,48,384]{2,1,0:T(8,128)S(1)} %copy.249), channel_id=1, source_target_pairs={{24,16},{25,17},{26,18},{27,19},{28,20},{29,21},{30,22},{31,23}} | collective-permute-start | bytes 2654216 | tf_op jit(solution)/shard_map/ppermute | solution.py:52
  713.2 22.7 %collective-permute-start.19 = (f32[12,48,384]{2,1,0:T(8,128)S(1)}, f32[12,48,384]{2,1,0:T(8,128)S(1)}, u32[]{:S(2)}, u32[]{:S(2)}) collective-permute-start(f32[12,48,384]{2,1,0:T(8,128)S(1)} %fusion.36), channel_id=1, source_target_pairs={{0,8},{8,16},{1,9},{9,17},{2,10},{10,18},{3,11},{11,19},{4,12},{12... | collective-permute-start | bytes 2654216 | tf_op jit(solution)/shard_map/ppermute | solution.py:51
  717.9 24.4 %collective-permute-start.22 = (f32[12,48,384]{2,1,0:T(8,128)S(1)}, f32[12,48,384]{2,1,0:T(8,128)S(1)}, u32[]{:S(2)}, u32[]{:S(2)}) collective-permute-start(f32[12,48,384]{2,1,0:T(8,128)S(1)} %fusion.34), channel_id=1, source_target_pairs={{16,8},{24,16},{17,9},{25,17},{18,10},{26,18},{19,11},{27,19},{20,... | collective-permute-start | bytes 2654216 | tf_op jit(solution)/shard_map/ppermute | solution.py:52
  735.8 9.0 %copy-start.24 = (f32[12,48,128]{2,0,1:T(8,128)S(1)}, f32[12,48,128]{2,0,1:T(8,128)}, u32[]{:S(2)}) copy-start(f32[12,48,128]{2,0,1:T(8,128)} %copy-done.23) | copy-start | bytes 884740
  735.8 9.0 %copy-start.26 = (f32[12,48,128]{2,0,1:T(8,128)S(1)}, f32[12,48,128]{2,0,1:T(8,128)}, u32[]{:S(2)}) copy-start(f32[12,48,128]{2,0,1:T(8,128)} %copy-done.25) | copy-start | bytes 884740
  737.0 22.1 %collective-permute-start.20 = (f32[12,48,384]{2,1,0:T(8,128)}, f32[12,48,384]{2,1,0:T(8,128)}, u32[]{:S(2)}, u32[]{:S(2)}) collective-permute-start(f32[12,48,384]{2,1,0:T(8,128)} %fusion.35), channel_id=1, source_target_pairs={{0,8},{8,16},{16,24},{1,9},{9,17},{17,25},{2,10},{10,18},{18,26},{... | collective-permute-start | bytes 2654216 | tf_op jit(solution)/shard_map/ppermute | solution.py:51
  743.6 21.8 %collective-permute-start.23 = (f32[12,48,384]{2,1,0:T(8,128)}, f32[12,48,384]{2,1,0:T(8,128)}, u32[]{:S(2)}, u32[]{:S(2)}) collective-permute-start(f32[12,48,384]{2,1,0:T(8,128)} %fusion.33), channel_id=1, source_target_pairs={{8,0},{16,8},{24,16},{9,1},{17,9},{25,17},{10,2},{18,10},{26,18},{... | collective-permute-start | bytes 2654216 | tf_op jit(solution)/shard_map/ppermute | solution.py:52
  746.6 23.2 %all-to-all-start.14 = ((f32[576,8,16]{0,2,1:T(8,128)}), f32[576,8,16]{0,2,1:T(8,128)}, u32[]{:S(2)}, u32[]{:S(2)}) async-start(f32[576,8,16]{0,2,1:T(8,128)} %all_to_all.112), calls=%async_computation.14 | async-start | bytes 655360 | tf_op jit(solution)/shard_map/all_to_all | solution.py:134
  769.9 16.5 %all-to-all-start.15 = ((f32[576,8,48]{0,2,1:T(8,128)}), f32[576,8,48]{0,2,1:T(8,128)S(1)}, u32[]{:S(2)}, u32[]{:S(2)}) async-start(f32[576,8,48]{0,2,1:T(8,128)} %copy.252), calls=%async_computation.15 | async-start | bytes 1966080 | tf_op jit(solution)/shard_map/all_to_all | solution.py:134
  (19 other events, 52.2 us)

commit v14 on v9

--- a/solution.py
+++ b/solution.py
@@ -123,7 +123,7 @@
 
     def sum_blocks(returned):
         gathered = jnp.concatenate(returned, axis=1)
-        return jnp.einsum("srk,srgpn->gkpn", one_hot, gathered, precision=lax.Precision.HIGHEST)
+        return jnp.einsum("srk,srgpn->gkpn", one_hot, gathered, precision=PRECISION)
 
     first_home, second_returned = line_reduce(sum_blocks(returned[0]), "grp", group_count, held)
     second_home, _ = line_reduce(sum_blocks(second_returned), "grp", group_count)

time: 723 us -> 720 us (level)
  transfers between devices with their start and end apart: 39 -> 39, of which waited for: 23 -> 23; matrix products, arithmetic and copies ran while one was open for 38% -> 39% of each run, Pallas kernels for 0% -> 0%
where the time goes in v14:
time: 720 us; the launch traced here: 708 us
  waiting for transfers between devices  229 us (32%)
  local copies, waits for them, and re-layouts  155 us (22%)
  starting transfers between devices  129 us (18%)
  matrix products  126 us (18%)
  other arithmetic  48.3 us (7%)
  blocking collectives  13.7 us (2%)
    all_to_all x12, waiting for transfers between devices, band_exchange(): lax.all_to_all(outgoing, 'band', split_axis=0, concat_axis=0, tiled=True)  125 us
    all_to_all x12, starting transfers between devices, band_exchange(): lax.all_to_all(outgoing, 'band', split_axis=0, concat_axis=0, tiled=True)  66.9 us
    ppermute x6, waiting for transfers between devices, line_gather(): lax.ppermute(leftward, axis, [(i + 1, i) for i in range(0, count - step)])  53.1 us
    dot_general x6, matrix products, body(): jnp.dot(r[0], r[1].T, precision=PRECISION, preferred_element_type=jnp.flo...  52.4 us
    dot_general x6, matrix products, body(): jnp.dot(kernel, rows[h][1], precision=PRECISION, preferred_element_type=j...  42.1 us
    ppermute x6, waiting for transfers between devices, line_reduce(): lax.ppermute(send_right, axis, [(i, i + 1) for i in range(0, step)])  34.8 us
    dot_general x3, local copies, waits for them, and re-layouts, body(): jnp.dot(kernel.T, rows[h][0], precision=PRECISION, preferred_element_type...  29.2 us
    dot_general x6, matrix products, body(): jnp.dot(kernel.T, rows[h][0], precision=PRECISION, preferred_element_type...  27.6 us
  transfers between devices with their start and end apart: 39, of which 23 were waited for; matrix products, arithmetic and copies ran while one was open for 39% of the time, Pallas kernels for 0%

profile of v14, /device:TPU:2, one launch (start us, length us, event | category | flops | bytes accessed | tf_op | source)
XLA Modules:
  0.0 707.7 jit_solution(15057769948706408563)
XLA Ops:
  1.7 13.7 %all_to_all.136 = f32[8,576,32]{1,2,0:T(8,128)S(1)} all-to-all(f32[8,576,32]{1,2,0:T(8,128)S(1)} %copy.186), channel_id=1, replica_groups=mesh['grp'=4,'band'=8] {'band'}, dimensions={0} | all-to-all | bytes 1179648 | tf_op jit(solution)/shard_map/all_to_all | solution.py:72
  16.5 4.3 collective-permute-start
  22.0 4.9 all-to-all-start
  35.4 9.0 %collective-permute-done.1 = f32[576,256]{1,0:T(8,128)S(1)} collective-permute-done((f32[576,256]{1,0:T(8,128)}, f32[576,256]{1,0:T(8,128)S(1)}, u32[]{:S(2)}, u32[]{:S(2)}) %collective-permute-start.1) | collective-permute-done | bytes 589856 | tf_op jit(solution)/shard_map/ppermute | solution.py:24
  47.9 12.9 %collective-permute-done.3 = f32[576,256]{1,0:T(8,128)S(1)} collective-permute-done((f32[576,256]{1,0:T(8,128)S(1)}, f32[576,256]{1,0:T(8,128)S(1)}, u32[]{:S(2)}, u32[]{:S(2)}) %collective-permute-start.3) | collective-permute-done | bytes 589856 | tf_op jit(solution)/shard_map/ppermute | solution.py:24
  63.4 13.0 %collective-permute-done.5 = f32[576,256]{1,0:T(8,128)S(1)} collective-permute-done((f32[576,256]{1,0:T(8,128)S(1)}, f32[576,256]{1,0:T(8,128)S(1)}, u32[]{:S(2)}, u32[]{:S(2)}) %collective-permute-start.5) | collective-permute-done | bytes 589856 | tf_op jit(solution)/shard_map/ppermute | solution.py:24
  83.0 5.2 all-to-all-start.2
  91.6 4.6 collective-permute-start.6
  101.3 4.1 fusion.25
  109.1 15.6 %all-to-all-done.2 = f32[8,2,4,48,256]{4,3,2,1,0:T(8,128)} async-done(((f32[8,2,4,48,256]{4,3,2,1,0:T(8,128)}), f32[8,2,4,48,256]{4,3,2,1,0:T(8,128)}, u32[]{:S(2)}, u32[]{:S(2)}) %all-to-all-start.2) | async-done | bytes 3145760 | tf_op jit(solution)/shard_map/all_to_all | solution.py:10
  124.7 5.9 all-to-all-start.3
  141.2 4.1 fusion.24
  145.3 4.1 collective-permute-done.9
  149.4 17.6 %all-to-all-done.3 = f32[8,2,4,48,256]{4,3,2,1,0:T(8,128)} async-done(((f32[8,2,4,48,256]{4,3,2,1,0:T(8,128)}), f32[8,2,4,48,256]{4,3,2,1,0:T(8,128)}, u32[]{:S(2)}, u32[]{:S(2)}) %all-to-all-start.3) | async-done | bytes 3145760 | tf_op jit(solution)/shard_map/all_to_all | solution.py:10
  167.1 5.1 all-to-all-start.4
  182.3 11.6 %collective-permute-done.11 = f32[576,256]{1,0:T(8,128)} collective-permute-done((f32[576,256]{1,0:T(8,128)}, f32[576,256]{1,0:T(8,128)}, u32[]{:S(2)}, u32[]{:S(2)}) %collective-permute-start.11) | collective-permute-done | bytes 589856 | tf_op jit(solution)/shard_map/ppermute | solution.py:24
  193.9 14.6 %all-to-all-done.4 = f32[8,2,4,48,256]{4,3,2,1,0:T(8,128)S(1)} async-done(((f32[8,2,4,48,256]{4,3,2,1,0:T(8,128)}), f32[8,2,4,48,256]{4,3,2,1,0:T(8,128)S(1)}, u32[]{:S(2)}, u32[]{:S(2)}) %all-to-all-start.4) | async-done | bytes 3145760 | tf_op jit(solution)/shard_map/all_to_all | solution.py:10
  217.1 4.1 fusion.21
  221.1 6.0 all-to-all-start.9
  234.1 4.1 fusion.22
  238.2 25.4 %all-to-all-done.9 = f32[8,2,4,48,256]{4,3,2,1,0:T(8,128)} async-done(((f32[8,2,4,48,256]{4,3,2,1,0:T(8,128)}), f32[8,2,4,48,256]{4,3,2,1,0:T(8,128)}, u32[]{:S(2)}, u32[]{:S(2)}) %all-to-all-start.9) | async-done | bytes 3145760 | tf_op jit(solution)/shard_map/all_to_all | solution.py:10
  263.6 6.1 all-to-all-start.7
  272.2 6.5 fusion.57
  282.7 6.5 fusion.58
  297.7 6.6 fusion.59
  306.2 6.3 all-to-all-start.5
  318.3 9.6 %fusion = f32[1536,1536]{1,0:T(8,128)} fusion(f32[1536,1536]{1,0:T(8,128)S(1)} %copy-done.3, f32[1536,256]{1,0:T(8,128)S(1)} %bitcast.365, f32[1536,256]{1,0:T(8,128)S(1)} %bitcast.367, f32[3,1536,1536]{2,1,0:T(8,128)} %param.7), kind=kOutput, calls=%fused_computation.7 | convolution fusion | flops 3628597248 | bytes 31457280 | tf_op jit(solution)/shard_map/dot_general | solution.py:108
  327.9 9.6 %copy.223 = f32[1536,1536]{1,0:T(8,128)} copy(f32[1536,1536]{0,1:T(8,128)} %bitcast.328) | data formatting | bytes 18874368 | tf_op jit(solution)/shard_map/dot_general | solution.py:114
  337.5 6.9 convolution_bitcast_fusion.7
  350.9 4.6 all-to-all-start.10
  358.0 11.9 %fusion.2 = f32[1536,1536]{1,0:T(8,128)} fusion(f32[1536,1536]{1,0:T(8,128)} %fusion.57, f32[1536,256]{1,0:T(8,128)S(1)} %bitcast.375, f32[1536,256]{1,0:T(8,128)S(1)} %bitcast.373, f32[3,1536,1536]{2,1,0:T(8,128)} %param.7), kind=kOutput, calls=%fused_computation.11 | convolution fusion | flops 3628597248 | bytes 31457280 | tf_op jit(solution)/shard_map/dot_general | solution.py:108
  369.9 9.7 %copy.207 = f32[1536,1536]{1,0:T(8,128)} copy(f32[1536,1536]{0,1:T(8,128)} %bitcast.334) | data formatting | bytes 18874368 | tf_op jit(solution)/shard_map/dot_general | solution.py:114
  379.6 7.0 convolution_bitcast_fusion.11
  392.9 5.1 all-to-all-start.6
  400.5 11.4 %fusion.1 = f32[1536,1536]{1,0:T(8,128)} fusion(f32[1536,1536]{1,0:T(8,128)} %fusion.58, f32[1536,256]{1,0:T(8,128)S(1)} %bitcast.369, f32[1536,256]{1,0:T(8,128)S(1)} %bitcast.371, f32[3,1536,1536]{2,1,0:T(8,128)} %param.7), kind=kOutput, calls=%fused_computation.9 | convolution fusion | flops 3628597248 | bytes 31457280 | tf_op jit(solution)/shard_map/dot_general | solution.py:108
  411.8 9.8 %copy.215 = f32[1536,1536]{1,0:T(8,128)} copy(f32[1536,1536]{0,1:T(8,128)} %bitcast.331) | data formatting | bytes 18874368 | tf_op jit(solution)/shard_map/dot_general | solution.py:114
  421.7 6.9 convolution_bitcast_fusion.9
  435.0 5.4 all-to-all-start.8
  440.4 6.9 convolution_bitcast_fusion.5
  447.3 7.3 %convolution_bitcast_fusion.4 = f32[1,4,8,48,256]{4,3,2,1,0:T(8,128)S(1)} fusion(f32[4,8,48,1536]{3,2,1,0:T(8,128)} %bitcast.345, f32[1536,256,1,1]{1,0,3,2:T(8,128)S(1)} %bitcast.376), kind=kOutput, calls=%fused_computation.54 | convolution fusion | flops 3623878656 | bytes 12582912 | tf_op jit(solution)/shard_map/dot_general | solution.py:114
  456.7 5.3 copy.227
  462.0 5.3 copy.225
  467.4 9.5 %all-to-all-done.8 = f32[8,2,4,48,256]{4,3,2,1,0:T(8,128)} async-done(((f32[8,2,4,48,256]{4,3,2,1,0:T(8,128)}), f32[8,2,4,48,256]{4,3,2,1,0:T(8,128)}, u32[]{:S(2)}, u32[]{:S(2)}) %all-to-all-start.8) | async-done | bytes 3145760 | tf_op jit(solution)/shard_map/all_to_all | solution.py:10
  488.6 6.0 all-to-all-start.11
  494.7 7.4 %convolution_bitcast_fusion.3 = f32[1,4,8,48,256]{4,3,2,1,0:T(8,128)S(1)} fusion(f32[4,8,48,1536]{3,2,1,0:T(8,128)} %bitcast.333, f32[1536,256,1,1]{1,0,3,2:T(8,128)} %bitcast.372), kind=kOutput, calls=%fused_computation.53 | convolution fusion | flops 3623878656 | bytes 12582912 | tf_op jit(solution)/shard_map/dot_general | solution.py:113
  512.9 5.9 collective-permute-done.12
  518.8 12.3 %all-to-all-done.11 = f32[8,2,4,48,256]{4,3,2,1,0:T(8,128)} async-done(((f32[8,2,4,48,256]{4,3,2,1,0:T(8,128)}), f32[8,2,4,48,256]{4,3,2,1,0:T(8,128)}, u32[]{:S(2)}, u32[]{:S(2)}) %all-to-all-start.11) | async-done | bytes 3145760 | tf_op jit(solution)/shard_map/all_to_all | solution.py:10
  536.5 6.1 all-to-all-start.12
  542.6 7.0 convolution_bitcast_fusion.1
  554.0 4.1 convolution_bitcast_fusion
  560.2 6.1 collective-permute-done.14
  566.3 12.8 %all-to-all-done.12 = f32[8,2,4,48,256]{4,3,2,1,0:T(8,128)} async-done(((f32[8,2,4,48,256]{4,3,2,1,0:T(8,128)}), f32[8,2,4,48,256]{4,3,2,1,0:T(8,128)}, u32[]{:S(2)}, u32[]{:S(2)}) %all-to-all-start.12) | async-done | bytes 3145760 | tf_op jit(solution)/shard_map/all_to_all | solution.py:10
  584.4 5.1 all-to-all-start.13
  593.7 5.6 collective-permute-start.16
  599.3 5.5 copy.244
  604.8 5.4 copy.245
  611.1 14.8 %all-to-all-done.13 = f32[8,2,4,48,256]{4,3,2,1,0:T(8,128)S(1)} async-done(((f32[8,2,4,48,256]{4,3,2,1,0:T(8,128)}), f32[8,2,4,48,256]{4,3,2,1,0:T(8,128)S(1)}, u32[]{:S(2)}, u32[]{:S(2)}) %all-to-all-start.13) | async-done | bytes 3145760 | tf_op jit(solution)/shard_map/all_to_all | solution.py:10
  634.3 11.8 %collective-permute-done.18 = f32[12,48,256]{2,1,0:T(8,128)S(1)} collective-permute-done((f32[12,48,256]{2,1,0:T(8,128)S(1)}, f32[12,48,256]{2,1,0:T(8,128)S(1)}, u32[]{:S(2)}, u32[]{:S(2)}) %collective-permute-start.18) | collective-permute-done | bytes 589856 | tf_op jit(solution)/shard_map/ppermute | solution.py:51
  646.5 4.6 collective-permute-start.19
  652.2 11.0 %collective-permute-done.19 = f32[12,48,256]{2,1,0:T(8,128)S(1)} collective-permute-done((f32[12,48,256]{2,1,0:T(8,128)S(1)}, f32[12,48,256]{2,1,0:T(8,128)S(1)}, u32[]{:S(2)}, u32[]{:S(2)}) %collective-permute-start.19) | collective-permute-done | bytes 589856 | tf_op jit(solution)/shard_map/ppermute | solution.py:51
  664.3 5.2 collective-permute-start.20
  677.9 4.1 all-to-all-start.14
  682.0 4.3 collective-permute-done.23
  697.5 8.1 %all-to-all-done.15 = f32[576,8,32]{0,2,1:T(8,128)S(1)} async-done(((f32[576,8,32]{0,2,1:T(8,128)}), f32[576,8,32]{0,2,1:T(8,128)S(1)}, u32[]{:S(2)}, u32[]{:S(2)}) %all-to-all-start.15) | async-done | bytes 589856 | tf_op jit(solution)/shard_map/all_to_all | solution.py:131
  (298 shorter events, 194.6 us)
Async XLA Ops:
  1.7 25.2 %copy-start.53 = (s32[32,6]{0,1:T(8,128)S(1)}, s32[32,6]{0,1:T(8,128)}, u32[]{:S(2)}) copy-start(s32[32,6]{0,1:T(8,128)} %param.6) | copy-start | bytes 2308
  16.5 16.3 %collective-permute-start = (f32[576,256]{1,0:T(8,128)}, f32[576,256]{1,0:T(8,128)}, u32[]{:S(2)}, u32[]{:S(2)}) collective-permute-start(f32[576,256]{1,0:T(8,128)} %copy.188), channel_id=1, source_target_pairs={{0,8},{8,16},{16,24},{1,9},{9,17},{17,25},{2,10},{10,18},{18,26},{... | collective-permute-start | bytes 1769480 | tf_op jit(solution)/shard_map/ppermute | solution.py:23
  22.0 61.1 %all-to-all-start = ((f32[8,576,32]{1,2,0:T(8,128)}), f32[8,576,32]{1,2,0:T(8,128)S(1)}, u32[]{:S(2)}, u32[]{:S(2)}) async-start(f32[8,576,32]{1,2,0:T(8,128)} %copy.184), calls=%async_computation | async-start | bytes 1310720 | tf_op jit(solution)/shard_map/all_to_all | solution.py:72
  26.9 20.2 %copy-start.48 = (s32[8,6]{0,1:T(8,128)}, s32[8,6]{0,1:T(8,128)S(1)}, u32[]{:S(2)}) copy-start(s32[8,6]{0,1:T(8,128)S(1)} %get-tuple-element.79) | copy-start | bytes 580
  26.9 17.5 %collective-permute-start.1 = (f32[576,256]{1,0:T(8,128)}, f32[576,256]{1,0:T(8,128)S(1)}, u32[]{:S(2)}, u32[]{:S(2)}) collective-permute-start(f32[576,256]{1,0:T(8,128)} %copy.188), channel_id=1, source_target_pairs={{8,0},{16,8},{24,16},{9,1},{17,9},{25,17},{10,2},{18,10},{26,18},{... | collective-permute-start | bytes 1769480 | tf_op jit(solution)/shard_map/ppermute | solution.py:24
  32.8 14.4 %collective-permute-start.2 = (f32[576,256]{1,0:T(8,128)}, f32[576,256]{1,0:T(8,128)}, u32[]{:S(2)}, u32[]{:S(2)}) collective-permute-start(f32[576,256]{1,0:T(8,128)} %collective-permute-done), channel_id=1, source_target_pairs={{8,16},{16,24},{9,17},{17,25},{10,18},{18,26},{11,19},{19,27},{12,... | collective-permute-start | bytes 1769480 | tf_op jit(solution)/shard_map/ppermute | solution.py:23
  35.0 44.1 %copy-start.55 = (pred[8,2]{1,0:T(8,128)(4,1)}, pred[8,2]{1,0:T(8,128)(4,1)S(1)}, u32[]{:S(2)}) copy-start(pred[8,2]{1,0:T(8,128)(4,1)S(1)} %copy.185) | copy-start | bytes 52
  44.4 16.4 %collective-permute-start.3 = (f32[576,256]{1,0:T(8,128)S(1)}, f32[576,256]{1,0:T(8,128)S(1)}, u32[]{:S(2)}, u32[]{:S(2)}) collective-permute-start(f32[576,256]{1,0:T(8,128)S(1)} %collective-permute-done.1), channel_id=1, source_target_pairs={{8,0},{16,8},{9,1},{17,9},{10,2},{18,10},{11,3},{19,11},{12,4},{20... | collective-permute-start | bytes 1769480 | tf_op jit(solution)/shard_map/ppermute | solution.py:24
  47.2 16.2 %collective-permute-start.4 = (f32[576,256]{1,0:T(8,128)}, f32[576,256]{1,0:T(8,128)S(1)}, u32[]{:S(2)}, u32[]{:S(2)}) collective-permute-start(f32[576,256]{1,0:T(8,128)} %collective-permute-done.2), channel_id=1, source_target_pairs={{16,24},{17,25},{18,26},{19,27},{20,28},{21,29},{22,30},{23,31}} | collective-permute-start | bytes 1769480 | tf_op jit(solution)/shard_map/ppermute | solution.py:23
  60.9 15.5 %collective-permute-start.5 = (f32[576,256]{1,0:T(8,128)S(1)}, f32[576,256]{1,0:T(8,128)S(1)}, u32[]{:S(2)}, u32[]{:S(2)}) collective-permute-start(f32[576,256]{1,0:T(8,128)S(1)} %collective-permute-done.3), channel_id=1, source_target_pairs={{8,0},{9,1},{10,2},{11,3},{12,4},{13,5},{14,6},{15,7}} | collective-permute-start | bytes 1769480 | tf_op jit(solution)/shard_map/ppermute | solution.py:24
  83.0 13.2 %copy-start.60 = (pred[8,2]{0,1:T(4,128)(4,1)S(1)}, pred[8,2]{0,1:T(4,128)(4,1)}, u32[]{:S(2)}) copy-start(pred[8,2]{0,1:T(4,128)(4,1)} %get-tuple-element.115) | copy-start | bytes 52
  83.0 41.7 %all-to-all-start.2 = ((f32[8,2,4,48,256]{4,3,2,1,0:T(8,128)}), f32[8,2,4,48,256]{4,3,2,1,0:T(8,128)}, u32[]{:S(2)}, u32[]{:S(2)}) async-start(f32[8,2,4,48,256]{4,3,2,1,0:T(8,128)} %fusion.26), calls=%async_computation.2 | async-start | bytes 6291456 | tf_op jit(solution)/shard_map/all_to_all | solution.py:10
  90.3 17.5 %collective-permute-start.7 = (f32[576,256]{1,0:T(8,128)}, f32[576,256]{1,0:T(8,128)S(1)}, u32[]{:S(2)}, u32[]{:S(2)}) collective-permute-start(f32[576,256]{1,0:T(8,128)} %copy.193), channel_id=1, source_target_pairs={{8,0},{16,8},{24,16},{9,1},{17,9},{25,17},{10,2},{18,10},{26,18},{... | collective-permute-start | bytes 1769480 | tf_op jit(solution)/shard_map/ppermute | solution.py:24
  91.6 17.5 %collective-permute-start.6 = (f32[576,256]{1,0:T(8,128)}, f32[576,256]{1,0:T(8,128)S(1)}, u32[]{:S(2)}, u32[]{:S(2)}) collective-permute-start(f32[576,256]{1,0:T(8,128)} %copy.192), channel_id=1, source_target_pairs={{0,8},{8,16},{16,24},{1,9},{9,17},{17,25},{2,10},{10,18},{18,26},{... | collective-permute-start | bytes 1769480 | tf_op jit(solution)/shard_map/ppermute | solution.py:23
  105.4 28.0 %copy-start.59 = (pred[8,2]{0,1:T(4,128)(4,1)S(1)}, pred[8,2]{0,1:T(4,128)(4,1)}, u32[]{:S(2)}) copy-start(pred[8,2]{0,1:T(4,128)(4,1)} %get-tuple-element.114) | copy-start | bytes 52
  107.8 24.3 %copy-start.43 = (f32[576,256]{1,0:T(8,128)}, f32[576,256]{1,0:T(8,128)S(1)}, u32[]{:S(2)}) copy-start(f32[576,256]{1,0:T(8,128)S(1)} %collective-permute-done.7) | copy-start | bytes 1769476
  109.1 21.5 %copy-start.45 = (f32[576,256]{1,0:T(8,128)}, f32[576,256]{1,0:T(8,128)S(1)}, u32[]{:S(2)}) copy-start(f32[576,256]{1,0:T(8,128)S(1)} %collective-permute-done.6) | copy-start | bytes 1769476
  124.7 42.4 %all-to-all-start.3 = ((f32[8,2,4,48,256]{4,3,2,1,0:T(8,128)}), f32[8,2,4,48,256]{4,3,2,1,0:T(8,128)}, u32[]{:S(2)}, u32[]{:S(2)}) async-start(f32[8,2,4,48,256]{4,3,2,1,0:T(8,128)} %fusion.25), calls=%async_computation.3 | async-start | bytes 6291456 | tf_op jit(solution)/shard_map/all_to_all | solution.py:10
  130.6 14.7 %collective-permute-start.8 = (f32[576,256]{1,0:T(8,128)S(1)}, f32[576,256]{1,0:T(8,128)}, u32[]{:S(2)}, u32[]{:S(2)}) collective-permute-start(f32[576,256]{1,0:T(8,128)S(1)} %collective-permute-done.6), channel_id=1, source_target_pairs={{8,16},{16,24},{9,17},{17,25},{10,18},{18,26},{11,19},{19,27},{12,... | collective-permute-start | bytes 1769480 | tf_op jit(solution)/shard_map/ppermute | solution.py:23
  132.1 17.4 %collective-permute-start.9 = (f32[576,256]{1,0:T(8,128)S(1)}, f32[576,256]{1,0:T(8,128)}, u32[]{:S(2)}, u32[]{:S(2)}) collective-permute-start(f32[576,256]{1,0:T(8,128)S(1)} %collective-permute-done.7), channel_id=1, source_target_pairs={{8,0},{16,8},{9,1},{17,9},{10,2},{18,10},{11,3},{19,11},{12,4},{20... | collective-permute-start | bytes 1769480 | tf_op jit(solution)/shard_map/ppermute | solution.py:24
  167.1 41.5 %all-to-all-start.4 = ((f32[8,2,4,48,256]{4,3,2,1,0:T(8,128)}), f32[8,2,4,48,256]{4,3,2,1,0:T(8,128)S(1)}, u32[]{:S(2)}, u32[]{:S(2)}) async-start(f32[8,2,4,48,256]{4,3,2,1,0:T(8,128)} %fusion.24), calls=%async_computation.4 | async-start | bytes 6291456 | tf_op jit(solution)/shard_map/all_to_all | solution.py:10
  175.6 4.3 collective-permute-start.10
  176.3 17.6 %collective-permute-start.11 = (f32[576,256]{1,0:T(8,128)}, f32[576,256]{1,0:T(8,128)}, u32[]{:S(2)}, u32[]{:S(2)}) collective-permute-start(f32[576,256]{1,0:T(8,128)} %collective-permute-done.9), channel_id=1, source_target_pairs={{8,0},{9,1},{10,2},{11,3},{12,4},{13,5},{14,6},{15,7}} | collective-permute-start | bytes 1769480 | tf_op jit(solution)/shard_map/ppermute | solution.py:24
  221.1 10.5 %copy-start.51 = (s32[1024]{0:T(1024)S(1)}, s32[1024]{0:T(1024)}, u32[]{:S(2)}) copy-start(s32[1024]{0:T(1024)} %copy-done.50) | copy-start | bytes 12292
  221.1 42.5 %all-to-all-start.9 = ((f32[8,2,4,48,256]{4,3,2,1,0:T(8,128)}), f32[8,2,4,48,256]{4,3,2,1,0:T(8,128)}, u32[]{:S(2)}, u32[]{:S(2)}) async-start(f32[8,2,4,48,256]{4,3,2,1,0:T(8,128)} %fusion.21), calls=%async_computation.9 | async-start | bytes 6291456 | tf_op jit(solution)/shard_map/all_to_all | solution.py:10
  263.6 42.6 %all-to-all-start.7 = ((f32[8,2,4,48,256]{4,3,2,1,0:T(8,128)}), f32[8,2,4,48,256]{4,3,2,1,0:T(8,128)}, u32[]{:S(2)}, u32[]{:S(2)}) async-start(f32[8,2,4,48,256]{4,3,2,1,0:T(8,128)} %fusion.22), calls=%async_computation.7 | async-start | bytes 6291456 | tf_op jit(solution)/shard_map/all_to_all | solution.py:10
  306.2 44.7 %all-to-all-start.5 = ((f32[8,2,4,48,256]{4,3,2,1,0:T(8,128)}), f32[8,2,4,48,256]{4,3,2,1,0:T(8,128)}, u32[]{:S(2)}, u32[]{:S(2)}) async-start(f32[8,2,4,48,256]{4,3,2,1,0:T(8,128)} %fusion.23), calls=%async_computation.5 | async-start | bytes 6291456 | tf_op jit(solution)/shard_map/all_to_all | solution.py:10
  314.9 12.9 %copy-start.17 = (f32[1,4,8,48,256]{4,3,2,1,0:T(8,128)}, f32[1,4,8,48,256]{4,3,2,1,0:T(8,128)S(1)}, u32[]{:S(2)}) copy-start(f32[1,4,8,48,256]{4,3,2,1,0:T(8,128)S(1)} %copy.222) | copy-start | bytes 4718596
  315.1 12.8 %copy-start.15 = (f32[1,4,8,48,256]{4,3,2,1,0:T(8,128)}, f32[1,4,8,48,256]{4,3,2,1,0:T(8,128)S(1)}, u32[]{:S(2)}) copy-start(f32[1,4,8,48,256]{4,3,2,1,0:T(8,128)S(1)} %copy.221) | copy-start | bytes 4718596
  350.9 42.1 %all-to-all-start.10 = ((f32[8,2,4,48,256]{4,3,2,1,0:T(8,128)}), f32[8,2,4,48,256]{4,3,2,1,0:T(8,128)}, u32[]{:S(2)}, u32[]{:S(2)}) async-start(f32[8,2,4,48,256]{4,3,2,1,0:T(8,128)} %copy.224), calls=%async_computation.10 | async-start | bytes 6291456 | tf_op jit(solution)/shard_map/all_to_all | solution.py:10
  357.8 12.0 %copy-start.20 = (f32[1,4,8,48,256]{4,3,2,1,0:T(8,128)}, f32[1,4,8,48,256]{4,3,2,1,0:T(8,128)S(1)}, u32[]{:S(2)}) copy-start(f32[1,4,8,48,256]{4,3,2,1,0:T(8,128)S(1)} %copy.206) | copy-start | bytes 4718596
  358.0 11.9 %copy-start.22 = (f32[1,4,8,48,256]{4,3,2,1,0:T(8,128)}, f32[1,4,8,48,256]{4,3,2,1,0:T(8,128)S(1)}, u32[]{:S(2)}) copy-start(f32[1,4,8,48,256]{4,3,2,1,0:T(8,128)S(1)} %copy.205) | copy-start | bytes 4718596
  392.9 42.0 %all-to-all-start.6 = ((f32[8,2,4,48,256]{4,3,2,1,0:T(8,128)}), f32[8,2,4,48,256]{4,3,2,1,0:T(8,128)}, u32[]{:S(2)}, u32[]{:S(2)}) async-start(f32[8,2,4,48,256]{4,3,2,1,0:T(8,128)} %copy.208), calls=%async_computation.6 | async-start | bytes 6291456 | tf_op jit(solution)/shard_map/all_to_all | solution.py:10
  400.3 11.5 %copy-start.19 = (f32[1,4,8,48,256]{4,3,2,1,0:T(8,128)}, f32[1,4,8,48,256]{4,3,2,1,0:T(8,128)S(1)}, u32[]{:S(2)}) copy-start(f32[1,4,8,48,256]{4,3,2,1,0:T(8,128)S(1)} %copy.214) | copy-start | bytes 4718596
  411.8 9.8 %copy-start.12 = (f32[1,4,8,48,256]{4,3,2,1,0:T(8,128)S(1)}, f32[1,4,8,48,256]{4,3,2,1,0:T(8,128)}, u32[]{:S(2)}) copy-start(f32[1,4,8,48,256]{4,3,2,1,0:T(8,128)} %copy-done.11) | copy-start | bytes 4718596
  435.0 41.9 %all-to-all-start.8 = ((f32[8,2,4,48,256]{4,3,2,1,0:T(8,128)}), f32[8,2,4,48,256]{4,3,2,1,0:T(8,128)}, u32[]{:S(2)}, u32[]{:S(2)}) async-start(f32[8,2,4,48,256]{4,3,2,1,0:T(8,128)} %copy.216), calls=%async_computation.8 | async-start | bytes 6291456 | tf_op jit(solution)/shard_map/all_to_all | solution.py:10
  462.0 18.7 %copy-start.49 = (s32[8,6]{0,1:T(8,128)S(1)}, s32[8,6]{0,1:T(8,128)}, u32[]{:S(2)}) copy-start(s32[8,6]{0,1:T(8,128)} %copy-done.48) | copy-start | bytes 580
  488.6 18.2 %slice-start.3 = ((s8[9437184]{0:T(1024)(128)(4,1)}), s8[1048576]{0:T(1024)(128)(4,1)S(1)}, s32[]{:S(2)}) async-start(s8[9437184]{0:T(1024)(128)(4,1)} %bitcast.342), calls=%async_computation.19 | async-start | bytes 2097152
  488.6 42.5 %all-to-all-start.11 = ((f32[8,2,4,48,256]{4,3,2,1,0:T(8,128)}), f32[8,2,4,48,256]{4,3,2,1,0:T(8,128)}, u32[]{:S(2)}, u32[]{:S(2)}) async-start(f32[8,2,4,48,256]{4,3,2,1,0:T(8,128)} %copy.231), calls=%async_computation.11 | async-start | bytes 6291456 | tf_op jit(solution)/shard_map/all_to_all | solution.py:10
  494.7 12.2 %slice-start.4 = ((s8[9437184]{0:T(1024)(128)(4,1)}), s8[4194304]{0:T(1024)(128)(4,1)S(1)}, s32[]{:S(2)}) async-start(s8[9437184]{0:T(1024)(128)(4,1)} %bitcast.342), calls=%async_computation.20 | async-start | bytes 8388608
  494.7 12.2 %slice-start.5 = ((s8[9437184]{0:T(1024)(128)(4,1)}), s8[4194304]{0:T(1024)(128)(4,1)S(1)}, s32[]{:S(2)}) async-start(s8[9437184]{0:T(1024)(128)(4,1)} %bitcast.342), calls=%async_computation.21 | async-start | bytes 8388608
  502.9 10.1 %collective-permute-start.13 = (f32[12,48,256]{2,1,0:T(8,128)S(1)}, f32[12,48,256]{2,1,0:T(8,128)}, u32[]{:S(2)}, u32[]{:S(2)}) collective-permute-start(f32[12,48,256]{2,1,0:T(8,128)S(1)} %copy.230), channel_id=1, source_target_pairs={{24,16},{25,17},{26,18},{27,19},{28,20},{29,21},{30,22},{31,23}} | collective-permute-start | bytes 1769480 | tf_op jit(solution)/shard_map/ppermute | solution.py:52
  504.4 14.4 %collective-permute-start.12 = (f32[12,48,256]{2,1,0:T(8,128)S(1)}, f32[12,48,256]{2,1,0:T(8,128)}, u32[]{:S(2)}, u32[]{:S(2)}) collective-permute-start(f32[12,48,256]{2,1,0:T(8,128)S(1)} %copy.229), channel_id=1, source_target_pairs={{0,8},{1,9},{2,10},{3,11},{4,12},{5,13},{6,14},{7,15}} | collective-permute-start | bytes 1769480 | tf_op jit(solution)/shard_map/ppermute | solution.py:51
  510.9 20.3 %copy-start.5 = (f32[4,48,256,12]{2,3,1,0:T(8,128)S(1)}, f32[4,48,256,12]{2,3,1,0:T(8,128)}, u32[]{:S(2)}) copy-start(f32[4,48,256,12]{2,3,1,0:T(8,128)} %copy-done.4) | copy-start | bytes 7077892
  536.5 17.5 %slice-start = ((s8[9437184]{0:T(1024)(128)(4,1)}), s8[1048576]{0:T(1024)(128)(4,1)S(1)}, s32[]{:S(2)}) async-start(s8[9437184]{0:T(1024)(128)(4,1)} %bitcast.338), calls=%async_computation.16 | async-start | bytes 2097152
  536.5 42.6 %all-to-all-start.12 = ((f32[8,2,4,48,256]{4,3,2,1,0:T(8,128)}), f32[8,2,4,48,256]{4,3,2,1,0:T(8,128)}, u32[]{:S(2)}, u32[]{:S(2)}) async-start(f32[8,2,4,48,256]{4,3,2,1,0:T(8,128)} %copy.236), calls=%async_computation.12 | async-start | bytes 6291456 | tf_op jit(solution)/shard_map/all_to_all | solution.py:10
  542.6 11.4 %slice-start.1 = ((s8[9437184]{0:T(1024)(128)(4,1)}), s8[4194304]{0:T(1024)(128)(4,1)S(1)}, s32[]{:S(2)}) async-start(s8[9437184]{0:T(1024)(128)(4,1)} %bitcast.338), calls=%async_computation.17 | async-start | bytes 8388608
  542.6 11.3 %slice-start.2 = ((s8[9437184]{0:T(1024)(128)(4,1)}), s8[4194304]{0:T(1024)(128)(4,1)S(1)}, s32[]{:S(2)}) async-start(s8[9437184]{0:T(1024)(128)(4,1)} %bitcast.338), calls=%async_computation.18 | async-start | bytes 8388608
  550.3 9.9 %collective-permute-start.15 = (f32[12,48,256]{2,1,0:T(8,128)S(1)}, f32[12,48,256]{2,1,0:T(8,128)}, u32[]{:S(2)}, u32[]{:S(2)}) collective-permute-start(f32[12,48,256]{2,1,0:T(8,128)S(1)} %copy.235), channel_id=1, source_target_pairs={{16,8},{24,16},{17,9},{25,17},{18,10},{26,18},{19,11},{27,19},{20,... | collective-permute-start | bytes 1769480 | tf_op jit(solution)/shard_map/ppermute | solution.py:52
  551.8 14.4 %collective-permute-start.14 = (f32[12,48,256]{2,1,0:T(8,128)S(1)}, f32[12,48,256]{2,1,0:T(8,128)}, u32[]{:S(2)}, u32[]{:S(2)}) collective-permute-start(f32[12,48,256]{2,1,0:T(8,128)S(1)} %copy.234), channel_id=1, source_target_pairs={{0,8},{8,16},{1,9},{9,17},{2,10},{10,18},{3,11},{11,19},{4,12},{12... | collective-permute-start | bytes 1769480 | tf_op jit(solution)/shard_map/ppermute | solution.py:51
  558.0 21.0 %copy-start.6 = (f32[4,48,256,12]{2,3,1,0:T(8,128)S(1)}, f32[4,48,256,12]{2,3,1,0:T(8,128)}, u32[]{:S(2)}) copy-start(f32[4,48,256,12]{2,3,1,0:T(8,128)} %copy-done.4) | copy-start | bytes 7077892
  584.4 41.5 %all-to-all-start.13 = ((f32[8,2,4,48,256]{4,3,2,1,0:T(8,128)}), f32[8,2,4,48,256]{4,3,2,1,0:T(8,128)S(1)}, u32[]{:S(2)}, u32[]{:S(2)}) async-start(f32[8,2,4,48,256]{4,3,2,1,0:T(8,128)} %copy.241), calls=%async_computation.13 | async-start | bytes 6291456 | tf_op jit(solution)/shard_map/all_to_all | solution.py:10
  592.4 17.8 %collective-permute-start.17 = (f32[12,48,256]{2,1,0:T(8,128)S(1)}, f32[12,48,256]{2,1,0:T(8,128)S(1)}, u32[]{:S(2)}, u32[]{:S(2)}) collective-permute-start(f32[12,48,256]{2,1,0:T(8,128)S(1)} %copy.240), channel_id=1, source_target_pairs={{8,0},{16,8},{24,16},{9,1},{17,9},{25,17},{10,2},{18,10},{26,18},{... | collective-permute-start | bytes 1769480 | tf_op jit(solution)/shard_map/ppermute | solution.py:52
  593.7 17.3 %collective-permute-start.16 = (f32[12,48,256]{2,1,0:T(8,128)S(1)}, f32[12,48,256]{2,1,0:T(8,128)}, u32[]{:S(2)}, u32[]{:S(2)}) collective-permute-start(f32[12,48,256]{2,1,0:T(8,128)S(1)} %copy.239), channel_id=1, source_target_pairs={{0,8},{8,16},{16,24},{1,9},{9,17},{17,25},{2,10},{10,18},{18,26},{... | collective-permute-start | bytes 1769480 | tf_op jit(solution)/shard_map/ppermute | solution.py:51
  631.8 14.4 %collective-permute-start.18 = (f32[12,48,256]{2,1,0:T(8,128)S(1)}, f32[12,48,256]{2,1,0:T(8,128)S(1)}, u32[]{:S(2)}, u32[]{:S(2)}) collective-permute-start(f32[12,48,256]{2,1,0:T(8,128)S(1)} %copy.248), channel_id=1, source_target_pairs={{0,8},{1,9},{2,10},{3,11},{4,12},{5,13},{6,14},{7,15}} | collective-permute-start | bytes 1769480 | tf_op jit(solution)/shard_map/ppermute | solution.py:51
  633.6 17.5 %collective-permute-start.21 = (f32[12,48,256]{2,1,0:T(8,128)S(1)}, f32[12,48,256]{2,1,0:T(8,128)S(1)}, u32[]{:S(2)}, u32[]{:S(2)}) collective-permute-start(f32[12,48,256]{2,1,0:T(8,128)S(1)} %copy.251), channel_id=1, source_target_pairs={{24,16},{25,17},{26,18},{27,19},{28,20},{29,21},{30,22},{31,23}} | collective-permute-start | bytes 1769480 | tf_op jit(solution)/shard_map/ppermute | solution.py:52
  646.5 25.8 %copy-start.37 = (f32[1,48,256,12]{2,3,1,0:T(8,128)S(1)}, f32[1,48,256,12]{2,3,1,0:T(8,128)}, u32[]{:S(2)}) copy-start(f32[1,48,256,12]{2,3,1,0:T(8,128)} %get-tuple-element.80) | copy-start | bytes 1769476
  646.5 25.8 %copy-start.42 = (f32[12,48,256]{2,1,0:T(8,128)S(1)}, f32[12,48,256]{2,1,0:T(8,128)}, u32[]{:S(2)}) copy-start(f32[12,48,256]{2,1,0:T(8,128)} %copy-done.41) | copy-start | bytes 1769476
  646.5 16.6 %collective-permute-start.19 = (f32[12,48,256]{2,1,0:T(8,128)S(1)}, f32[12,48,256]{2,1,0:T(8,128)S(1)}, u32[]{:S(2)}, u32[]{:S(2)}) collective-permute-start(f32[12,48,256]{2,1,0:T(8,128)S(1)} %fusion.36), channel_id=1, source_target_pairs={{0,8},{8,16},{1,9},{9,17},{2,10},{10,18},{3,11},{11,19},{4,12},{12... | collective-permute-start | bytes 1769480 | tf_op jit(solution)/shard_map/ppermute | solution.py:51
  651.5 18.1 %collective-permute-start.22 = (f32[12,48,256]{2,1,0:T(8,128)S(1)}, f32[12,48,256]{2,1,0:T(8,128)S(1)}, u32[]{:S(2)}, u32[]{:S(2)}) collective-permute-start(f32[12,48,256]{2,1,0:T(8,128)S(1)} %fusion.34), channel_id=1, source_target_pairs={{16,8},{24,16},{17,9},{25,17},{18,10},{26,18},{19,11},{27,19},{20,... | collective-permute-start | bytes 1769480 | tf_op jit(solution)/shard_map/ppermute | solution.py:52
  664.3 17.7 %collective-permute-start.20 = (f32[12,48,256]{2,1,0:T(8,128)}, f32[12,48,256]{2,1,0:T(8,128)}, u32[]{:S(2)}, u32[]{:S(2)}) collective-permute-start(f32[12,48,256]{2,1,0:T(8,128)} %fusion.35), channel_id=1, source_target_pairs={{0,8},{8,16},{16,24},{1,9},{9,17},{17,25},{2,10},{10,18},{18,26},{... | collective-permute-start | bytes 1769480 | tf_op jit(solution)/shard_map/ppermute | solution.py:51
  670.7 15.6 %collective-permute-start.23 = (f32[12,48,256]{2,1,0:T(8,128)}, f32[12,48,256]{2,1,0:T(8,128)}, u32[]{:S(2)}, u32[]{:S(2)}) collective-permute-start(f32[12,48,256]{2,1,0:T(8,128)} %fusion.33), channel_id=1, source_target_pairs={{8,0},{16,8},{24,16},{9,1},{17,9},{25,17},{10,2},{18,10},{26,18},{... | collective-permute-start | bytes 1769480 | tf_op jit(solution)/shard_map/ppermute | solution.py:52
  677.9 14.2 %all-to-all-start.14 = ((f32[576,8,32]{0,2,1:T(8,128)}), f32[576,8,32]{0,2,1:T(8,128)}, u32[]{:S(2)}, u32[]{:S(2)}) async-start(f32[576,8,32]{0,2,1:T(8,128)} %copy.271), calls=%async_computation.14 | async-start | bytes 1310720 | tf_op jit(solution)/shard_map/all_to_all | solution.py:131
  692.1 13.5 %all-to-all-start.15 = ((f32[576,8,32]{0,2,1:T(8,128)}), f32[576,8,32]{0,2,1:T(8,128)S(1)}, u32[]{:S(2)}, u32[]{:S(2)}) async-start(f32[576,8,32]{0,2,1:T(8,128)} %copy.272), calls=%async_computation.15 | async-start | bytes 1310720 | tf_op jit(solution)/shard_map/all_to_all | solution.py:131
  (42 other events, 182.5 us)

commit v15 on v14

--- a/solution.py
+++ b/solution.py
@@ -107,12 +107,12 @@
         density = sum(
             jnp.dot(r[0], r[1].T, precision=PRECISION, preferred_element_type=jnp.float32) for r in rows
         )
-        kernel = density * coulomb[slot]
         scale = jnp.where(own_pairs[2 * slot] == own_pairs[2 * slot + 1], 0.5, 1.0)
+        kernel = density * (coulomb[slot] * scale)
         for h in range(2):
             onto_first = jnp.dot(kernel, rows[h][1], precision=PRECISION, preferred_element_type=jnp.float32)
             onto_second = jnp.dot(kernel.T, rows[h][0], precision=PRECISION, preferred_element_type=jnp.float32)
-            outbound = (jnp.stack([onto_first, onto_second], 0) * scale).reshape(
+            outbound = jnp.stack([onto_first, onto_second], 0).reshape(
                 2, group_count, band_count, piece_rows, half
             )
             outbound = outbound.transpose(2, 0, 1, 3, 4)

time: 720 us -> 720 us (level)
  no operation moved by 1% of the time
where the time goes in v15:
time: 720 us; the launch traced here: 708 us
  waiting for transfers between devices  230 us (32%)
  local copies, waits for them, and re-layouts  155 us (22%)
  starting transfers between devices  128 us (18%)
  matrix products  128 us (18%)
  other arithmetic  47.6 us (7%)
  blocking collectives  13.7 us (2%)
    all_to_all x12, waiting for transfers between devices, band_exchange(): lax.all_to_all(outgoing, 'band', split_axis=0, concat_axis=0, tiled=True)  125 us
    all_to_all x12, starting transfers between devices, band_exchange(): lax.all_to_all(outgoing, 'band', split_axis=0, concat_axis=0, tiled=True)  66.1 us
    ppermute x6, waiting for transfers between devices, line_gather(): lax.ppermute(leftward, axis, [(i + 1, i) for i in range(0, count - step)])  53.3 us
    dot_general x6, matrix products, body(): jnp.dot(r[0], r[1].T, precision=PRECISION, preferred_element_type=jnp.flo...  53.1 us
    dot_general x6, matrix products, body(): jnp.dot(kernel, rows[h][1], precision=PRECISION, preferred_element_type=j...  43.1 us
    ppermute x6, waiting for transfers between devices, line_reduce(): lax.ppermute(send_right, axis, [(i, i + 1) for i in range(0, step)])  34.8 us
    dot_general x3, local copies, waits for them, and re-layouts, body(): jnp.dot(kernel.T, rows[h][0], precision=PRECISION, preferred_element_type...  28.9 us
    dot_general x6, matrix products, body(): jnp.dot(kernel.T, rows[h][0], precision=PRECISION, preferred_element_type...  27.6 us
  transfers between devices with their start and end apart: 39, of which 23 were waited for; matrix products, arithmetic and copies ran while one was open for 39% of the time, Pallas kernels for 0%

profile of v15, /device:TPU:2, one launch (start us, length us, event | category | flops | bytes accessed | tf_op | source)
XLA Modules:
  0.0 707.7 jit_solution(3334405043756366164)
XLA Ops:
  1.7 13.7 %all_to_all.136 = f32[8,576,32]{1,2,0:T(8,128)S(1)} all-to-all(f32[8,576,32]{1,2,0:T(8,128)S(1)} %copy.186), channel_id=1, replica_groups=mesh['grp'=4,'band'=8] {'band'}, dimensions={0} | all-to-all | bytes 1179648 | tf_op jit(solution)/shard_map/all_to_all | solution.py:72
  16.5 4.3 collective-permute-start
  21.9 4.9 all-to-all-start
  35.4 9.0 %collective-permute-done.1 = f32[576,256]{1,0:T(8,128)S(1)} collective-permute-done((f32[576,256]{1,0:T(8,128)}, f32[576,256]{1,0:T(8,128)S(1)}, u32[]{:S(2)}, u32[]{:S(2)}) %collective-permute-start.1) | collective-permute-done | bytes 589856 | tf_op jit(solution)/shard_map/ppermute | solution.py:24
  47.9 12.9 %collective-permute-done.3 = f32[576,256]{1,0:T(8,128)S(1)} collective-permute-done((f32[576,256]{1,0:T(8,128)S(1)}, f32[576,256]{1,0:T(8,128)S(1)}, u32[]{:S(2)}, u32[]{:S(2)}) %collective-permute-start.3) | collective-permute-done | bytes 589856 | tf_op jit(solution)/shard_map/ppermute | solution.py:24
  63.4 13.0 %collective-permute-done.5 = f32[576,256]{1,0:T(8,128)S(1)} collective-permute-done((f32[576,256]{1,0:T(8,128)S(1)}, f32[576,256]{1,0:T(8,128)S(1)}, u32[]{:S(2)}, u32[]{:S(2)}) %collective-permute-start.5) | collective-permute-done | bytes 589856 | tf_op jit(solution)/shard_map/ppermute | solution.py:24
  83.0 5.2 all-to-all-start.2
  91.6 4.6 collective-permute-start.6
  101.3 4.1 fusion.19
  109.1 15.6 %all-to-all-done.2 = f32[8,2,4,48,256]{4,3,2,1,0:T(8,128)} async-done(((f32[8,2,4,48,256]{4,3,2,1,0:T(8,128)}), f32[8,2,4,48,256]{4,3,2,1,0:T(8,128)}, u32[]{:S(2)}, u32[]{:S(2)}) %all-to-all-start.2) | async-done | bytes 3145760 | tf_op jit(solution)/shard_map/all_to_all | solution.py:10
  124.7 5.9 all-to-all-start.3
  145.0 4.4 collective-permute-done.9
  149.4 17.6 %all-to-all-done.3 = f32[8,2,4,48,256]{4,3,2,1,0:T(8,128)} async-done(((f32[8,2,4,48,256]{4,3,2,1,0:T(8,128)}), f32[8,2,4,48,256]{4,3,2,1,0:T(8,128)}, u32[]{:S(2)}, u32[]{:S(2)}) %all-to-all-start.3) | async-done | bytes 3145760 | tf_op jit(solution)/shard_map/all_to_all | solution.py:10
  167.0 5.1 all-to-all-start.4
  182.4 11.5 %collective-permute-done.11 = f32[576,256]{1,0:T(8,128)} collective-permute-done((f32[576,256]{1,0:T(8,128)}, f32[576,256]{1,0:T(8,128)}, u32[]{:S(2)}, u32[]{:S(2)}) %collective-permute-start.11) | collective-permute-done | bytes 589856 | tf_op jit(solution)/shard_map/ppermute | solution.py:24
  193.9 14.7 %all-to-all-done.4 = f32[8,2,4,48,256]{4,3,2,1,0:T(8,128)S(1)} async-done(((f32[8,2,4,48,256]{4,3,2,1,0:T(8,128)}), f32[8,2,4,48,256]{4,3,2,1,0:T(8,128)S(1)}, u32[]{:S(2)}, u32[]{:S(2)}) %all-to-all-start.4) | async-done | bytes 3145760 | tf_op jit(solution)/shard_map/all_to_all | solution.py:10
  221.0 6.0 all-to-all-start.9
  237.8 25.6 %all-to-all-done.9 = f32[8,2,4,48,256]{4,3,2,1,0:T(8,128)} async-done(((f32[8,2,4,48,256]{4,3,2,1,0:T(8,128)}), f32[8,2,4,48,256]{4,3,2,1,0:T(8,128)}, u32[]{:S(2)}, u32[]{:S(2)}) %all-to-all-start.9) | async-done | bytes 3145760 | tf_op jit(solution)/shard_map/all_to_all | solution.py:10
  263.4 6.1 all-to-all-start.7
  272.0 6.6 fusion.51
  282.6 6.4 fusion.52
  297.6 6.3 fusion.53
  306.0 6.3 all-to-all-start.5
  318.1 10.0 %fusion = f32[1536,1536]{1,0:T(8,128)} fusion(f32[1536,1536]{1,0:T(8,128)S(1)} %copy-done.3, f32[1536,256]{1,0:T(8,128)S(1)} %bitcast.359, f32[1536,256]{1,0:T(8,128)S(1)} %bitcast.361, f32[3,1536,1536]{2,1,0:T(8,128)} %param.7, f32[]{:T(128)} %bitcast.81), kind=kOutput, calls=%fused_computation.7 | convolution fusion | flops 3630956544 | bytes 31457284 | tf_op jit(solution)/shard_map/dot_general | solution.py:108
  328.1 9.6 %copy.223 = f32[1536,1536]{1,0:T(8,128)} copy(f32[1536,1536]{0,1:T(8,128)} %bitcast.328) | data formatting | bytes 18874368 | tf_op jit(solution)/shard_map/dot_general | solution.py:114
  337.8 6.9 convolution_bitcast_fusion.7
  344.7 4.0 convolution_bitcast_fusion.6
  351.0 4.6 all-to-all-start.10
  358.1 12.2 %fusion.2 = f32[1536,1536]{1,0:T(8,128)} fusion(f32[1536,1536]{1,0:T(8,128)} %fusion.51, f32[1536,256]{1,0:T(8,128)S(1)} %bitcast.369, f32[1536,256]{1,0:T(8,128)S(1)} %bitcast.367, f32[3,1536,1536]{2,1,0:T(8,128)} %param.7, f32[]{:T(128)} %bitcast.39), kind=kOutput, calls=%fused_computation.11 | convolution fusion | flops 3630956544 | bytes 31457284 | tf_op jit(solution)/shard_map/dot_general | solution.py:108
  370.3 9.7 %copy.207 = f32[1536,1536]{1,0:T(8,128)} copy(f32[1536,1536]{0,1:T(8,128)} %bitcast.334) | data formatting | bytes 18874368 | tf_op jit(solution)/shard_map/dot_general | solution.py:114
  380.0 7.0 convolution_bitcast_fusion.11
  387.0 4.1 convolution_bitcast_fusion.10
  393.5 4.7 all-to-all-start.6
  400.6 11.5 %fusion.1 = f32[1536,1536]{1,0:T(8,128)} fusion(f32[1536,1536]{1,0:T(8,128)} %fusion.52, f32[1536,256]{1,0:T(8,128)S(1)} %bitcast.363, f32[1536,256]{1,0:T(8,128)S(1)} %bitcast.365, f32[3,1536,1536]{2,1,0:T(8,128)} %param.7, f32[]{:T(128)} %bitcast.60), kind=kOutput, calls=%fused_computation.9 | convolution fusion | flops 3630956544 | bytes 31457284 | tf_op jit(solution)/shard_map/dot_general | solution.py:108
  412.1 9.6 %copy.215 = f32[1536,1536]{1,0:T(8,128)} copy(f32[1536,1536]{0,1:T(8,128)} %bitcast.331) | data formatting | bytes 18874368 | tf_op jit(solution)/shard_map/dot_general | solution.py:114
  421.7 7.4 %convolution_bitcast_fusion.9 = f32[1,4,8,48,256]{4,3,2,1,0:T(8,128)S(1)} fusion(f32[4,8,48,1536]{3,2,1,0:T(8,128)} %bitcast.332, f32[1536,256,1,1]{1,0,3,2:T(8,128)} %bitcast.372), kind=kOutput, calls=%fused_computation.53 | convolution fusion | flops 3623878656 | bytes 12582912 | tf_op jit(solution)/shard_map/dot_general | solution.py:113
  429.1 4.1 convolution_bitcast_fusion.8
  435.5 5.0 all-to-all-start.8
  440.5 7.4 %convolution_bitcast_fusion.5 = f32[1,4,8,48,256]{4,3,2,1,0:T(8,128)S(1)} fusion(f32[4,8,48,1536]{3,2,1,0:T(8,128)} %bitcast.336, f32[1536,256,1,1]{1,0,3,2:T(8,128)} %bitcast.368), kind=kOutput, calls=%fused_computation.49 | convolution fusion | flops 3623878656 | bytes 12582912 | tf_op jit(solution)/shard_map/dot_general | solution.py:113
  447.9 7.3 %convolution_bitcast_fusion.4 = f32[1,4,8,48,256]{4,3,2,1,0:T(8,128)S(1)} fusion(f32[4,8,48,1536]{3,2,1,0:T(8,128)} %bitcast.345, f32[1536,256,1,1]{1,0,3,2:T(8,128)S(1)} %bitcast.370), kind=kOutput, calls=%fused_computation.48 | convolution fusion | flops 3623878656 | bytes 12582912 | tf_op jit(solution)/shard_map/dot_general | solution.py:114
  457.3 5.3 copy.227
  462.6 5.4 copy.225
  468.0 9.0 %all-to-all-done.8 = f32[8,2,4,48,256]{4,3,2,1,0:T(8,128)} async-done(((f32[8,2,4,48,256]{4,3,2,1,0:T(8,128)}), f32[8,2,4,48,256]{4,3,2,1,0:T(8,128)}, u32[]{:S(2)}, u32[]{:S(2)}) %all-to-all-start.8) | async-done | bytes 3145760 | tf_op jit(solution)/shard_map/all_to_all | solution.py:10
  488.5 6.0 all-to-all-start.11
  494.6 7.4 %convolution_bitcast_fusion.3 = f32[1,4,8,48,256]{4,3,2,1,0:T(8,128)S(1)} fusion(f32[4,8,48,1536]{3,2,1,0:T(8,128)} %bitcast.333, f32[1536,256,1,1]{1,0,3,2:T(8,128)} %bitcast.366), kind=kOutput, calls=%fused_computation.47 | convolution fusion | flops 3623878656 | bytes 12582912 | tf_op jit(solution)/shard_map/dot_general | solution.py:113
  512.8 5.8 collective-permute-done.12
  518.7 12.4 %all-to-all-done.11 = f32[8,2,4,48,256]{4,3,2,1,0:T(8,128)} async-done(((f32[8,2,4,48,256]{4,3,2,1,0:T(8,128)}), f32[8,2,4,48,256]{4,3,2,1,0:T(8,128)}, u32[]{:S(2)}, u32[]{:S(2)}) %all-to-all-start.11) | async-done | bytes 3145760 | tf_op jit(solution)/shard_map/all_to_all | solution.py:10
  536.4 6.1 all-to-all-start.12
  542.5 7.0 convolution_bitcast_fusion.1
  553.9 4.1 convolution_bitcast_fusion
  560.0 6.2 collective-permute-done.14
  566.2 12.8 %all-to-all-done.12 = f32[8,2,4,48,256]{4,3,2,1,0:T(8,128)} async-done(((f32[8,2,4,48,256]{4,3,2,1,0:T(8,128)}), f32[8,2,4,48,256]{4,3,2,1,0:T(8,128)}, u32[]{:S(2)}, u32[]{:S(2)}) %all-to-all-start.12) | async-done | bytes 3145760 | tf_op jit(solution)/shard_map/all_to_all | solution.py:10
  584.3 5.1 all-to-all-start.13
  593.7 5.6 collective-permute-start.16
  599.3 5.4 copy.244
  604.6 5.5 copy.245
  610.9 14.9 %all-to-all-done.13 = f32[8,2,4,48,256]{4,3,2,1,0:T(8,128)S(1)} async-done(((f32[8,2,4,48,256]{4,3,2,1,0:T(8,128)}), f32[8,2,4,48,256]{4,3,2,1,0:T(8,128)S(1)}, u32[]{:S(2)}, u32[]{:S(2)}) %all-to-all-start.13) | async-done | bytes 3145760 | tf_op jit(solution)/shard_map/all_to_all | solution.py:10
  634.3 11.8 %collective-permute-done.18 = f32[12,48,256]{2,1,0:T(8,128)S(1)} collective-permute-done((f32[12,48,256]{2,1,0:T(8,128)S(1)}, f32[12,48,256]{2,1,0:T(8,128)S(1)}, u32[]{:S(2)}, u32[]{:S(2)}) %collective-permute-start.18) | collective-permute-done | bytes 589856 | tf_op jit(solution)/shard_map/ppermute | solution.py:51
  646.5 4.6 collective-permute-start.19
  652.1 11.0 %collective-permute-done.19 = f32[12,48,256]{2,1,0:T(8,128)S(1)} collective-permute-done((f32[12,48,256]{2,1,0:T(8,128)S(1)}, f32[12,48,256]{2,1,0:T(8,128)S(1)}, u32[]{:S(2)}, u32[]{:S(2)}) %collective-permute-start.19) | collective-permute-done | bytes 589856 | tf_op jit(solution)/shard_map/ppermute | solution.py:51
  664.3 5.2 collective-permute-start.20
  677.9 4.2 all-to-all-start.14
  682.0 4.3 collective-permute-done.23
  697.5 8.1 %all-to-all-done.15 = f32[576,8,32]{0,2,1:T(8,128)S(1)} async-done(((f32[576,8,32]{0,2,1:T(8,128)}), f32[576,8,32]{0,2,1:T(8,128)S(1)}, u32[]{:S(2)}, u32[]{:S(2)}) %all-to-all-start.15) | async-done | bytes 589856 | tf_op jit(solution)/shard_map/all_to_all | solution.py:131
  (292 shorter events, 194.2 us)
Async XLA Ops:
  1.7 25.2 %copy-start.50 = (s32[32,6]{0,1:T(8,128)S(1)}, s32[32,6]{0,1:T(8,128)}, u32[]{:S(2)}) copy-start(s32[32,6]{0,1:T(8,128)} %param.6) | copy-start | bytes 2308
  16.5 16.3 %collective-permute-start = (f32[576,256]{1,0:T(8,128)}, f32[576,256]{1,0:T(8,128)}, u32[]{:S(2)}, u32[]{:S(2)}) collective-permute-start(f32[576,256]{1,0:T(8,128)} %copy.188), channel_id=1, source_target_pairs={{0,8},{8,16},{16,24},{1,9},{9,17},{17,25},{2,10},{10,18},{18,26},{... | collective-permute-start | bytes 1769480 | tf_op jit(solution)/shard_map/ppermute | solution.py:23
  21.9 61.1 %all-to-all-start = ((f32[8,576,32]{1,2,0:T(8,128)}), f32[8,576,32]{1,2,0:T(8,128)S(1)}, u32[]{:S(2)}, u32[]{:S(2)}) async-start(f32[8,576,32]{1,2,0:T(8,128)} %copy.184), calls=%async_computation | async-start | bytes 1310720 | tf_op jit(solution)/shard_map/all_to_all | solution.py:72
  26.9 20.2 %copy-start.45 = (s32[8,6]{0,1:T(8,128)}, s32[8,6]{0,1:T(8,128)S(1)}, u32[]{:S(2)}) copy-start(s32[8,6]{0,1:T(8,128)S(1)} %get-tuple-element.79) | copy-start | bytes 580
  26.9 17.5 %collective-permute-start.1 = (f32[576,256]{1,0:T(8,128)}, f32[576,256]{1,0:T(8,128)S(1)}, u32[]{:S(2)}, u32[]{:S(2)}) collective-permute-start(f32[576,256]{1,0:T(8,128)} %copy.188), channel_id=1, source_target_pairs={{8,0},{16,8},{24,16},{9,1},{17,9},{25,17},{10,2},{18,10},{26,18},{... | collective-permute-start | bytes 1769480 | tf_op jit(solution)/shard_map/ppermute | solution.py:24
  32.8 14.4 %collective-permute-start.2 = (f32[576,256]{1,0:T(8,128)}, f32[576,256]{1,0:T(8,128)}, u32[]{:S(2)}, u32[]{:S(2)}) collective-permute-start(f32[576,256]{1,0:T(8,128)} %collective-permute-done), channel_id=1, source_target_pairs={{8,16},{16,24},{9,17},{17,25},{10,18},{18,26},{11,19},{19,27},{12,... | collective-permute-start | bytes 1769480 | tf_op jit(solution)/shard_map/ppermute | solution.py:23
  34.9 44.1 %copy-start.52 = (pred[8,2]{1,0:T(8,128)(4,1)}, pred[8,2]{1,0:T(8,128)(4,1)S(1)}, u32[]{:S(2)}) copy-start(pred[8,2]{1,0:T(8,128)(4,1)S(1)} %copy.185) | copy-start | bytes 52
  44.4 16.4 %collective-permute-start.3 = (f32[576,256]{1,0:T(8,128)S(1)}, f32[576,256]{1,0:T(8,128)S(1)}, u32[]{:S(2)}, u32[]{:S(2)}) collective-permute-start(f32[576,256]{1,0:T(8,128)S(1)} %collective-permute-done.1), channel_id=1, source_target_pairs={{8,0},{16,8},{9,1},{17,9},{10,2},{18,10},{11,3},{19,11},{12,4},{20... | collective-permute-start | bytes 1769480 | tf_op jit(solution)/shard_map/ppermute | solution.py:24
  47.1 16.2 %collective-permute-start.4 = (f32[576,256]{1,0:T(8,128)}, f32[576,256]{1,0:T(8,128)S(1)}, u32[]{:S(2)}, u32[]{:S(2)}) collective-permute-start(f32[576,256]{1,0:T(8,128)} %collective-permute-done.2), channel_id=1, source_target_pairs={{16,24},{17,25},{18,26},{19,27},{20,28},{21,29},{22,30},{23,31}} | collective-permute-start | bytes 1769480 | tf_op jit(solution)/shard_map/ppermute | solution.py:23
  60.8 15.5 %collective-permute-start.5 = (f32[576,256]{1,0:T(8,128)S(1)}, f32[576,256]{1,0:T(8,128)S(1)}, u32[]{:S(2)}, u32[]{:S(2)}) collective-permute-start(f32[576,256]{1,0:T(8,128)S(1)} %collective-permute-done.3), channel_id=1, source_target_pairs={{8,0},{9,1},{10,2},{11,3},{12,4},{13,5},{14,6},{15,7}} | collective-permute-start | bytes 1769480 | tf_op jit(solution)/shard_map/ppermute | solution.py:24
  83.0 13.2 %copy-start.57 = (pred[8,2]{0,1:T(4,128)(4,1)S(1)}, pred[8,2]{0,1:T(4,128)(4,1)}, u32[]{:S(2)}) copy-start(pred[8,2]{0,1:T(4,128)(4,1)} %get-tuple-element.115) | copy-start | bytes 52
  83.0 41.7 %all-to-all-start.2 = ((f32[8,2,4,48,256]{4,3,2,1,0:T(8,128)}), f32[8,2,4,48,256]{4,3,2,1,0:T(8,128)}, u32[]{:S(2)}, u32[]{:S(2)}) async-start(f32[8,2,4,48,256]{4,3,2,1,0:T(8,128)} %fusion.20), calls=%async_computation.2 | async-start | bytes 6291456 | tf_op jit(solution)/shard_map/all_to_all | solution.py:10
  90.3 17.5 %collective-permute-start.7 = (f32[576,256]{1,0:T(8,128)}, f32[576,256]{1,0:T(8,128)S(1)}, u32[]{:S(2)}, u32[]{:S(2)}) collective-permute-start(f32[576,256]{1,0:T(8,128)} %copy.193), channel_id=1, source_target_pairs={{8,0},{16,8},{24,16},{9,1},{17,9},{25,17},{10,2},{18,10},{26,18},{... | collective-permute-start | bytes 1769480 | tf_op jit(solution)/shard_map/ppermute | solution.py:24
  91.6 17.5 %collective-permute-start.6 = (f32[576,256]{1,0:T(8,128)}, f32[576,256]{1,0:T(8,128)S(1)}, u32[]{:S(2)}, u32[]{:S(2)}) collective-permute-start(f32[576,256]{1,0:T(8,128)} %copy.192), channel_id=1, source_target_pairs={{0,8},{8,16},{16,24},{1,9},{9,17},{17,25},{2,10},{10,18},{18,26},{... | collective-permute-start | bytes 1769480 | tf_op jit(solution)/shard_map/ppermute | solution.py:23
  105.4 28.0 %copy-start.56 = (pred[8,2]{0,1:T(4,128)(4,1)S(1)}, pred[8,2]{0,1:T(4,128)(4,1)}, u32[]{:S(2)}) copy-start(pred[8,2]{0,1:T(4,128)(4,1)} %get-tuple-element.114) | copy-start | bytes 52
  107.8 24.2 %copy-start.40 = (f32[576,256]{1,0:T(8,128)}, f32[576,256]{1,0:T(8,128)S(1)}, u32[]{:S(2)}) copy-start(f32[576,256]{1,0:T(8,128)S(1)} %collective-permute-done.7) | copy-start | bytes 1769476
  109.1 21.5 %copy-start.42 = (f32[576,256]{1,0:T(8,128)}, f32[576,256]{1,0:T(8,128)S(1)}, u32[]{:S(2)}) copy-start(f32[576,256]{1,0:T(8,128)S(1)} %collective-permute-done.6) | copy-start | bytes 1769476
  124.7 42.4 %all-to-all-start.3 = ((f32[8,2,4,48,256]{4,3,2,1,0:T(8,128)}), f32[8,2,4,48,256]{4,3,2,1,0:T(8,128)}, u32[]{:S(2)}, u32[]{:S(2)}) async-start(f32[8,2,4,48,256]{4,3,2,1,0:T(8,128)} %fusion.19), calls=%async_computation.3 | async-start | bytes 6291456 | tf_op jit(solution)/shard_map/all_to_all | solution.py:10
  130.6 14.4 %collective-permute-start.8 = (f32[576,256]{1,0:T(8,128)S(1)}, f32[576,256]{1,0:T(8,128)}, u32[]{:S(2)}, u32[]{:S(2)}) collective-permute-start(f32[576,256]{1,0:T(8,128)S(1)} %collective-permute-done.6), channel_id=1, source_target_pairs={{8,16},{16,24},{9,17},{17,25},{10,18},{18,26},{11,19},{19,27},{12,... | collective-permute-start | bytes 1769480 | tf_op jit(solution)/shard_map/ppermute | solution.py:23
  132.0 17.4 %collective-permute-start.9 = (f32[576,256]{1,0:T(8,128)S(1)}, f32[576,256]{1,0:T(8,128)}, u32[]{:S(2)}, u32[]{:S(2)}) collective-permute-start(f32[576,256]{1,0:T(8,128)S(1)} %collective-permute-done.7), channel_id=1, source_target_pairs={{8,0},{16,8},{9,1},{17,9},{10,2},{18,10},{11,3},{19,11},{12,4},{20... | collective-permute-start | bytes 1769480 | tf_op jit(solution)/shard_map/ppermute | solution.py:24
  167.0 41.5 %all-to-all-start.4 = ((f32[8,2,4,48,256]{4,3,2,1,0:T(8,128)}), f32[8,2,4,48,256]{4,3,2,1,0:T(8,128)S(1)}, u32[]{:S(2)}, u32[]{:S(2)}) async-start(f32[8,2,4,48,256]{4,3,2,1,0:T(8,128)} %fusion.18), calls=%async_computation.4 | async-start | bytes 6291456 | tf_op jit(solution)/shard_map/all_to_all | solution.py:10
  175.6 4.3 collective-permute-start.10
  176.3 17.6 %collective-permute-start.11 = (f32[576,256]{1,0:T(8,128)}, f32[576,256]{1,0:T(8,128)}, u32[]{:S(2)}, u32[]{:S(2)}) collective-permute-start(f32[576,256]{1,0:T(8,128)} %collective-permute-done.9), channel_id=1, source_target_pairs={{8,0},{9,1},{10,2},{11,3},{12,4},{13,5},{14,6},{15,7}} | collective-permute-start | bytes 1769480 | tf_op jit(solution)/shard_map/ppermute | solution.py:24
  221.0 10.4 %copy-start.48 = (s32[1024]{0:T(1024)S(1)}, s32[1024]{0:T(1024)}, u32[]{:S(2)}) copy-start(s32[1024]{0:T(1024)} %copy-done.47) | copy-start | bytes 12292
  221.0 42.5 %all-to-all-start.9 = ((f32[8,2,4,48,256]{4,3,2,1,0:T(8,128)}), f32[8,2,4,48,256]{4,3,2,1,0:T(8,128)}, u32[]{:S(2)}, u32[]{:S(2)}) async-start(f32[8,2,4,48,256]{4,3,2,1,0:T(8,128)} %fusion.15), calls=%async_computation.9 | async-start | bytes 6291456 | tf_op jit(solution)/shard_map/all_to_all | solution.py:10
  263.4 42.6 %all-to-all-start.7 = ((f32[8,2,4,48,256]{4,3,2,1,0:T(8,128)}), f32[8,2,4,48,256]{4,3,2,1,0:T(8,128)}, u32[]{:S(2)}, u32[]{:S(2)}) async-start(f32[8,2,4,48,256]{4,3,2,1,0:T(8,128)} %fusion.16), calls=%async_computation.7 | async-start | bytes 6291456 | tf_op jit(solution)/shard_map/all_to_all | solution.py:10
  306.0 45.0 %all-to-all-start.5 = ((f32[8,2,4,48,256]{4,3,2,1,0:T(8,128)}), f32[8,2,4,48,256]{4,3,2,1,0:T(8,128)}, u32[]{:S(2)}, u32[]{:S(2)}) async-start(f32[8,2,4,48,256]{4,3,2,1,0:T(8,128)} %fusion.17), calls=%async_computation.5 | async-start | bytes 6291456 | tf_op jit(solution)/shard_map/all_to_all | solution.py:10
  314.8 13.4 %copy-start.13 = (f32[1,4,8,48,256]{4,3,2,1,0:T(8,128)}, f32[1,4,8,48,256]{4,3,2,1,0:T(8,128)S(1)}, u32[]{:S(2)}) copy-start(f32[1,4,8,48,256]{4,3,2,1,0:T(8,128)S(1)} %copy.222) | copy-start | bytes 4718596
  314.9 13.2 %copy-start.11 = (f32[1,4,8,48,256]{4,3,2,1,0:T(8,128)}, f32[1,4,8,48,256]{4,3,2,1,0:T(8,128)S(1)}, u32[]{:S(2)}) copy-start(f32[1,4,8,48,256]{4,3,2,1,0:T(8,128)S(1)} %copy.221) | copy-start | bytes 4718596
  351.0 42.5 %all-to-all-start.10 = ((f32[8,2,4,48,256]{4,3,2,1,0:T(8,128)}), f32[8,2,4,48,256]{4,3,2,1,0:T(8,128)}, u32[]{:S(2)}, u32[]{:S(2)}) async-start(f32[8,2,4,48,256]{4,3,2,1,0:T(8,128)} %copy.224), calls=%async_computation.10 | async-start | bytes 6291456 | tf_op jit(solution)/shard_map/all_to_all | solution.py:10
  358.0 12.4 %copy-start.16 = (f32[1,4,8,48,256]{4,3,2,1,0:T(8,128)}, f32[1,4,8,48,256]{4,3,2,1,0:T(8,128)S(1)}, u32[]{:S(2)}) copy-start(f32[1,4,8,48,256]{4,3,2,1,0:T(8,128)S(1)} %copy.206) | copy-start | bytes 4718596
  358.1 12.3 %copy-start.17 = (f32[1,4,8,48,256]{4,3,2,1,0:T(8,128)}, f32[1,4,8,48,256]{4,3,2,1,0:T(8,128)S(1)}, u32[]{:S(2)}) copy-start(f32[1,4,8,48,256]{4,3,2,1,0:T(8,128)S(1)} %copy.205) | copy-start | bytes 4718596
  370.3 9.7 %copy-start.21 = (f32[1,4,8,48,256]{4,3,2,1,0:T(8,128)S(1)}, f32[1,4,8,48,256]{4,3,2,1,0:T(8,128)}, u32[]{:S(2)}) copy-start(f32[1,4,8,48,256]{4,3,2,1,0:T(8,128)} %copy-done.20) | copy-start | bytes 4718596
  393.5 42.0 %all-to-all-start.6 = ((f32[8,2,4,48,256]{4,3,2,1,0:T(8,128)}), f32[8,2,4,48,256]{4,3,2,1,0:T(8,128)}, u32[]{:S(2)}, u32[]{:S(2)}) async-start(f32[8,2,4,48,256]{4,3,2,1,0:T(8,128)} %copy.208), calls=%async_computation.6 | async-start | bytes 6291456 | tf_op jit(solution)/shard_map/all_to_all | solution.py:10
  400.5 11.6 %copy-start.15 = (f32[1,4,8,48,256]{4,3,2,1,0:T(8,128)}, f32[1,4,8,48,256]{4,3,2,1,0:T(8,128)S(1)}, u32[]{:S(2)}) copy-start(f32[1,4,8,48,256]{4,3,2,1,0:T(8,128)S(1)} %copy.214) | copy-start | bytes 4718596
  435.5 41.5 %all-to-all-start.8 = ((f32[8,2,4,48,256]{4,3,2,1,0:T(8,128)}), f32[8,2,4,48,256]{4,3,2,1,0:T(8,128)}, u32[]{:S(2)}, u32[]{:S(2)}) async-start(f32[8,2,4,48,256]{4,3,2,1,0:T(8,128)} %copy.216), calls=%async_computation.8 | async-start | bytes 6291456 | tf_op jit(solution)/shard_map/all_to_all | solution.py:10
  462.6 18.3 %copy-start.46 = (s32[8,6]{0,1:T(8,128)S(1)}, s32[8,6]{0,1:T(8,128)}, u32[]{:S(2)}) copy-start(s32[8,6]{0,1:T(8,128)} %copy-done.45) | copy-start | bytes 580
  488.5 18.1 %slice-start.3 = ((s8[9437184]{0:T(1024)(128)(4,1)}), s8[1048576]{0:T(1024)(128)(4,1)S(1)}, s32[]{:S(2)}) async-start(s8[9437184]{0:T(1024)(128)(4,1)} %bitcast.342), calls=%async_computation.19 | async-start | bytes 2097152
  488.5 42.5 %all-to-all-start.11 = ((f32[8,2,4,48,256]{4,3,2,1,0:T(8,128)}), f32[8,2,4,48,256]{4,3,2,1,0:T(8,128)}, u32[]{:S(2)}, u32[]{:S(2)}) async-start(f32[8,2,4,48,256]{4,3,2,1,0:T(8,128)} %copy.231), calls=%async_computation.11 | async-start | bytes 6291456 | tf_op jit(solution)/shard_map/all_to_all | solution.py:10
  494.5 12.1 %slice-start.4 = ((s8[9437184]{0:T(1024)(128)(4,1)}), s8[4194304]{0:T(1024)(128)(4,1)S(1)}, s32[]{:S(2)}) async-start(s8[9437184]{0:T(1024)(128)(4,1)} %bitcast.342), calls=%async_computation.20 | async-start | bytes 8388608
  494.5 12.1 %slice-start.5 = ((s8[9437184]{0:T(1024)(128)(4,1)}), s8[4194304]{0:T(1024)(128)(4,1)S(1)}, s32[]{:S(2)}) async-start(s8[9437184]{0:T(1024)(128)(4,1)} %bitcast.342), calls=%async_computation.21 | async-start | bytes 8388608
  502.7 10.1 %collective-permute-start.13 = (f32[12,48,256]{2,1,0:T(8,128)S(1)}, f32[12,48,256]{2,1,0:T(8,128)}, u32[]{:S(2)}, u32[]{:S(2)}) collective-permute-start(f32[12,48,256]{2,1,0:T(8,128)S(1)} %copy.230), channel_id=1, source_target_pairs={{24,16},{25,17},{26,18},{27,19},{28,20},{29,21},{30,22},{31,23}} | collective-permute-start | bytes 1769480 | tf_op jit(solution)/shard_map/ppermute | solution.py:52
  504.2 14.4 %collective-permute-start.12 = (f32[12,48,256]{2,1,0:T(8,128)S(1)}, f32[12,48,256]{2,1,0:T(8,128)}, u32[]{:S(2)}, u32[]{:S(2)}) collective-permute-start(f32[12,48,256]{2,1,0:T(8,128)S(1)} %copy.229), channel_id=1, source_target_pairs={{0,8},{1,9},{2,10},{3,11},{4,12},{5,13},{6,14},{7,15}} | collective-permute-start | bytes 1769480 | tf_op jit(solution)/shard_map/ppermute | solution.py:51
  510.8 20.3 %copy-start.5 = (f32[4,48,256,12]{2,3,1,0:T(8,128)S(1)}, f32[4,48,256,12]{2,3,1,0:T(8,128)}, u32[]{:S(2)}) copy-start(f32[4,48,256,12]{2,3,1,0:T(8,128)} %copy-done.4) | copy-start | bytes 7077892
  536.4 17.4 %slice-start = ((s8[9437184]{0:T(1024)(128)(4,1)}), s8[1048576]{0:T(1024)(128)(4,1)S(1)}, s32[]{:S(2)}) async-start(s8[9437184]{0:T(1024)(128)(4,1)} %bitcast.338), calls=%async_computation.16 | async-start | bytes 2097152
  536.4 42.6 %all-to-all-start.12 = ((f32[8,2,4,48,256]{4,3,2,1,0:T(8,128)}), f32[8,2,4,48,256]{4,3,2,1,0:T(8,128)}, u32[]{:S(2)}, u32[]{:S(2)}) async-start(f32[8,2,4,48,256]{4,3,2,1,0:T(8,128)} %copy.236), calls=%async_computation.12 | async-start | bytes 6291456 | tf_op jit(solution)/shard_map/all_to_all | solution.py:10
  542.5 11.3 %slice-start.1 = ((s8[9437184]{0:T(1024)(128)(4,1)}), s8[4194304]{0:T(1024)(128)(4,1)S(1)}, s32[]{:S(2)}) async-start(s8[9437184]{0:T(1024)(128)(4,1)} %bitcast.338), calls=%async_computation.17 | async-start | bytes 8388608
  542.5 11.3 %slice-start.2 = ((s8[9437184]{0:T(1024)(128)(4,1)}), s8[4194304]{0:T(1024)(128)(4,1)S(1)}, s32[]{:S(2)}) async-start(s8[9437184]{0:T(1024)(128)(4,1)} %bitcast.338), calls=%async_computation.18 | async-start | bytes 8388608
  550.2 9.7 %collective-permute-start.15 = (f32[12,48,256]{2,1,0:T(8,128)S(1)}, f32[12,48,256]{2,1,0:T(8,128)}, u32[]{:S(2)}, u32[]{:S(2)}) collective-permute-start(f32[12,48,256]{2,1,0:T(8,128)S(1)} %copy.235), channel_id=1, source_target_pairs={{16,8},{24,16},{17,9},{25,17},{18,10},{26,18},{19,11},{27,19},{20,... | collective-permute-start | bytes 1769480 | tf_op jit(solution)/shard_map/ppermute | solution.py:52
  551.7 14.4 %collective-permute-start.14 = (f32[12,48,256]{2,1,0:T(8,128)S(1)}, f32[12,48,256]{2,1,0:T(8,128)}, u32[]{:S(2)}, u32[]{:S(2)}) collective-permute-start(f32[12,48,256]{2,1,0:T(8,128)S(1)} %copy.234), channel_id=1, source_target_pairs={{0,8},{8,16},{1,9},{9,17},{2,10},{10,18},{3,11},{11,19},{4,12},{12... | collective-permute-start | bytes 1769480 | tf_op jit(solution)/shard_map/ppermute | solution.py:51
  557.9 21.1 %copy-start.6 = (f32[4,48,256,12]{2,3,1,0:T(8,128)S(1)}, f32[4,48,256,12]{2,3,1,0:T(8,128)}, u32[]{:S(2)}) copy-start(f32[4,48,256,12]{2,3,1,0:T(8,128)} %copy-done.4) | copy-start | bytes 7077892
  584.3 41.5 %all-to-all-start.13 = ((f32[8,2,4,48,256]{4,3,2,1,0:T(8,128)}), f32[8,2,4,48,256]{4,3,2,1,0:T(8,128)S(1)}, u32[]{:S(2)}, u32[]{:S(2)}) async-start(f32[8,2,4,48,256]{4,3,2,1,0:T(8,128)} %copy.241), calls=%async_computation.13 | async-start | bytes 6291456 | tf_op jit(solution)/shard_map/all_to_all | solution.py:10
  592.4 17.7 %collective-permute-start.17 = (f32[12,48,256]{2,1,0:T(8,128)S(1)}, f32[12,48,256]{2,1,0:T(8,128)S(1)}, u32[]{:S(2)}, u32[]{:S(2)}) collective-permute-start(f32[12,48,256]{2,1,0:T(8,128)S(1)} %copy.240), channel_id=1, source_target_pairs={{8,0},{16,8},{24,16},{9,1},{17,9},{25,17},{10,2},{18,10},{26,18},{... | collective-permute-start | bytes 1769480 | tf_op jit(solution)/shard_map/ppermute | solution.py:52
  593.7 17.2 %collective-permute-start.16 = (f32[12,48,256]{2,1,0:T(8,128)S(1)}, f32[12,48,256]{2,1,0:T(8,128)}, u32[]{:S(2)}, u32[]{:S(2)}) collective-permute-start(f32[12,48,256]{2,1,0:T(8,128)S(1)} %copy.239), channel_id=1, source_target_pairs={{0,8},{8,16},{16,24},{1,9},{9,17},{17,25},{2,10},{10,18},{18,26},{... | collective-permute-start | bytes 1769480 | tf_op jit(solution)/shard_map/ppermute | solution.py:51
  631.7 14.4 %collective-permute-start.18 = (f32[12,48,256]{2,1,0:T(8,128)S(1)}, f32[12,48,256]{2,1,0:T(8,128)S(1)}, u32[]{:S(2)}, u32[]{:S(2)}) collective-permute-start(f32[12,48,256]{2,1,0:T(8,128)S(1)} %copy.248), channel_id=1, source_target_pairs={{0,8},{1,9},{2,10},{3,11},{4,12},{5,13},{6,14},{7,15}} | collective-permute-start | bytes 1769480 | tf_op jit(solution)/shard_map/ppermute | solution.py:51
  633.6 17.5 %collective-permute-start.21 = (f32[12,48,256]{2,1,0:T(8,128)S(1)}, f32[12,48,256]{2,1,0:T(8,128)S(1)}, u32[]{:S(2)}, u32[]{:S(2)}) collective-permute-start(f32[12,48,256]{2,1,0:T(8,128)S(1)} %copy.251), channel_id=1, source_target_pairs={{24,16},{25,17},{26,18},{27,19},{28,20},{29,21},{30,22},{31,23}} | collective-permute-start | bytes 1769480 | tf_op jit(solution)/shard_map/ppermute | solution.py:52
  646.5 25.8 %copy-start.35 = (f32[1,48,256,12]{2,3,1,0:T(8,128)S(1)}, f32[1,48,256,12]{2,3,1,0:T(8,128)}, u32[]{:S(2)}) copy-start(f32[1,48,256,12]{2,3,1,0:T(8,128)} %get-tuple-element.80) | copy-start | bytes 1769476
  646.5 25.8 %copy-start.39 = (f32[12,48,256]{2,1,0:T(8,128)S(1)}, f32[12,48,256]{2,1,0:T(8,128)}, u32[]{:S(2)}) copy-start(f32[12,48,256]{2,1,0:T(8,128)} %copy-done.38) | copy-start | bytes 1769476
  646.5 16.6 %collective-permute-start.19 = (f32[12,48,256]{2,1,0:T(8,128)S(1)}, f32[12,48,256]{2,1,0:T(8,128)S(1)}, u32[]{:S(2)}, u32[]{:S(2)}) collective-permute-start(f32[12,48,256]{2,1,0:T(8,128)S(1)} %fusion.30), channel_id=1, source_target_pairs={{0,8},{8,16},{1,9},{9,17},{2,10},{10,18},{3,11},{11,19},{4,12},{12... | collective-permute-start | bytes 1769480 | tf_op jit(solution)/shard_map/ppermute | solution.py:51
  651.4 18.1 %collective-permute-start.22 = (f32[12,48,256]{2,1,0:T(8,128)S(1)}, f32[12,48,256]{2,1,0:T(8,128)S(1)}, u32[]{:S(2)}, u32[]{:S(2)}) collective-permute-start(f32[12,48,256]{2,1,0:T(8,128)S(1)} %fusion.28), channel_id=1, source_target_pairs={{16,8},{24,16},{17,9},{25,17},{18,10},{26,18},{19,11},{27,19},{20,... | collective-permute-start | bytes 1769480 | tf_op jit(solution)/shard_map/ppermute | solution.py:52
  664.3 17.7 %collective-permute-start.20 = (f32[12,48,256]{2,1,0:T(8,128)}, f32[12,48,256]{2,1,0:T(8,128)}, u32[]{:S(2)}, u32[]{:S(2)}) collective-permute-start(f32[12,48,256]{2,1,0:T(8,128)} %fusion.29), channel_id=1, source_target_pairs={{0,8},{8,16},{16,24},{1,9},{9,17},{17,25},{2,10},{10,18},{18,26},{... | collective-permute-start | bytes 1769480 | tf_op jit(solution)/shard_map/ppermute | solution.py:51
  670.7 15.6 %collective-permute-start.23 = (f32[12,48,256]{2,1,0:T(8,128)}, f32[12,48,256]{2,1,0:T(8,128)}, u32[]{:S(2)}, u32[]{:S(2)}) collective-permute-start(f32[12,48,256]{2,1,0:T(8,128)} %fusion.27), channel_id=1, source_target_pairs={{8,0},{16,8},{24,16},{9,1},{17,9},{25,17},{10,2},{18,10},{26,18},{... | collective-permute-start | bytes 1769480 | tf_op jit(solution)/shard_map/ppermute | solution.py:52
  677.9 14.2 %all-to-all-start.14 = ((f32[576,8,32]{0,2,1:T(8,128)}), f32[576,8,32]{0,2,1:T(8,128)}, u32[]{:S(2)}, u32[]{:S(2)}) async-start(f32[576,8,32]{0,2,1:T(8,128)} %copy.271), calls=%async_computation.14 | async-start | bytes 1310720 | tf_op jit(solution)/shard_map/all_to_all | solution.py:131
  692.1 13.5 %all-to-all-start.15 = ((f32[576,8,32]{0,2,1:T(8,128)}), f32[576,8,32]{0,2,1:T(8,128)S(1)}, u32[]{:S(2)}, u32[]{:S(2)}) async-start(f32[576,8,32]{0,2,1:T(8,128)} %copy.272), calls=%async_computation.15 | async-start | bytes 1310720 | tf_op jit(solution)/shard_map/all_to_all | solution.py:131
  (39 other events, 160.6 us)

commit v16 on v15

--- a/solution.py
+++ b/solution.py
@@ -77,7 +77,6 @@
     group_index = lax.axis_index("grp")
     band_index = lax.axis_index("band")
     group_requests = lax.dynamic_slice_in_dim(requests, group_index * band_count, band_count, 0)
-    live = (group_requests >= 0).astype(jnp.float32)
     own_pairs = lax.dynamic_index_in_dim(group_requests, band_index, 0, keepdims=False)
     one_hot = (
         group_requests[:, :, None] == jnp.arange(block_count, dtype=jnp.int32)[None, None, :]
@@ -85,8 +84,8 @@
 
     def requested(pieces, slot):
         wanted = group_requests[:, 2 * slot : 2 * slot + 2]
-        mask = live[None, :, 2 * slot : 2 * slot + 2, None, None]
-        outgoing = jnp.take(pieces, jnp.maximum(wanted, 0), axis=1) * mask
+        wanted = jnp.where(wanted >= 0, wanted, block_count)
+        outgoing = jnp.take(pieces, wanted, axis=1, mode="fill", fill_value=0.0)
         return outgoing.transpose(1, 2, 0, 3, 4)
 
     def shape_pieces(gathered):

time: 720 us -> 712 us (0.989)
    transpose x6 -> x0, other arithmetic: 22.3 us -> none  [requested(): return outgoing.transpose(1, 2, 0, 3, 4)]
    select_n x0 -> x6, other arithmetic: none -> 22 us  [requested(): outgoing = jnp.take(pieces, wanted, axis=1, mode='fill', fill_value=0.0)]
  transfers between devices with their start and end apart: 39 -> 39, of which waited for: 23 -> 23; matrix products, arithmetic and copies ran while one was open for 39% -> 38% of each run, Pallas kernels for 0% -> 0%
where the time goes in v16:
time: 712 us; the launch traced here: 701 us
  waiting for transfers between devices  229 us (32%)
  local copies, waits for them, and re-layouts  151 us (21%)
  starting transfers between devices  128 us (18%)
  matrix products  128 us (18%)
  other arithmetic  45.7 us (6%)
  blocking collectives  13.7 us (2%)
    all_to_all x12, waiting for transfers between devices, band_exchange(): lax.all_to_all(outgoing, 'band', split_axis=0, concat_axis=0, tiled=True)  125 us
    all_to_all x12, starting transfers between devices, band_exchange(): lax.all_to_all(outgoing, 'band', split_axis=0, concat_axis=0, tiled=True)  66.3 us
    dot_general x6, matrix products, body(): jnp.dot(r[0], r[1].T, precision=PRECISION, preferred_element_type=jnp.flo...  52.3 us
    ppermute x6, waiting for transfers between devices, line_gather(): lax.ppermute(leftward, axis, [(i + 1, i) for i in range(0, count - step)])  51.4 us
    dot_general x6, matrix products, body(): jnp.dot(kernel, rows[h][1], precision=PRECISION, preferred_element_type=j...  43.4 us
    ppermute x6, waiting for transfers between devices, line_reduce(): lax.ppermute(send_right, axis, [(i, i + 1) for i in range(0, step)])  34.8 us
    dot_general x3, local copies, waits for them, and re-layouts, body(): jnp.dot(kernel.T, rows[h][0], precision=PRECISION, preferred_element_type...  28.9 us
    dot_general x6, matrix products, body(): jnp.dot(kernel.T, rows[h][0], precision=PRECISION, preferred_element_type...  27.7 us
  transfers between devices with their start and end apart: 39, of which 23 were waited for; matrix products, arithmetic and copies ran while one was open for 38% of the time, Pallas kernels for 0%

profile of v16, /device:TPU:2, one launch (start us, length us, event | category | flops | bytes accessed | tf_op | source)
XLA Modules:
  0.0 700.5 jit_solution(11223756371621740991)
XLA Ops:
  1.7 13.7 %all_to_all.136 = f32[8,576,32]{1,2,0:T(8,128)S(1)} all-to-all(f32[8,576,32]{1,2,0:T(8,128)S(1)} %copy.177), channel_id=1, replica_groups=mesh['grp'=4,'band'=8] {'band'}, dimensions={0} | all-to-all | bytes 1179648 | tf_op jit(solution)/shard_map/all_to_all | solution.py:72
  16.5 4.3 collective-permute-start
  23.2 4.9 all-to-all-start
  28.2 4.5 collective-permute-done
  42.3 11.8 %collective-permute-done.3 = f32[576,256]{1,0:T(8,128)S(1)} collective-permute-done((f32[576,256]{1,0:T(8,128)}, f32[576,256]{1,0:T(8,128)S(1)}, u32[]{:S(2)}, u32[]{:S(2)}) %collective-permute-start.3) | collective-permute-done | bytes 589856 | tf_op jit(solution)/shard_map/ppermute | solution.py:24
  55.5 13.6 %collective-permute-done.5 = f32[576,256]{1,0:T(8,128)S(1)} collective-permute-done((f32[576,256]{1,0:T(8,128)S(1)}, f32[576,256]{1,0:T(8,128)S(1)}, u32[]{:S(2)}, u32[]{:S(2)}) %collective-permute-start.5) | collective-permute-done | bytes 589856 | tf_op jit(solution)/shard_map/ppermute | solution.py:24
  75.8 5.4 all-to-all-start.2
  84.6 4.6 collective-permute-start.6
  96.5 4.3 collective-permute-done.7
  102.1 15.6 %all-to-all-done.2 = f32[8,2,4,48,256]{4,3,2,1,0:T(8,128)} async-done(((f32[8,2,4,48,256]{4,3,2,1,0:T(8,128)}), f32[8,2,4,48,256]{4,3,2,1,0:T(8,128)}, u32[]{:S(2)}, u32[]{:S(2)}) %all-to-all-start.2) | async-done | bytes 3145760 | tf_op jit(solution)/shard_map/all_to_all | solution.py:10
  117.7 5.9 all-to-all-start.3
  135.4 7.0 %collective-permute-done.9 = f32[576,256]{1,0:T(8,128)} collective-permute-done((f32[576,256]{1,0:T(8,128)S(1)}, f32[576,256]{1,0:T(8,128)}, u32[]{:S(2)}, u32[]{:S(2)}) %collective-permute-start.9) | collective-permute-done | bytes 589856 | tf_op jit(solution)/shard_map/ppermute | solution.py:24
  142.4 17.6 %all-to-all-done.3 = f32[8,2,4,48,256]{4,3,2,1,0:T(8,128)} async-done(((f32[8,2,4,48,256]{4,3,2,1,0:T(8,128)}), f32[8,2,4,48,256]{4,3,2,1,0:T(8,128)}, u32[]{:S(2)}, u32[]{:S(2)}) %all-to-all-start.3) | async-done | bytes 3145760 | tf_op jit(solution)/shard_map/all_to_all | solution.py:10
  160.0 5.1 all-to-all-start.4
  175.3 11.5 %collective-permute-done.11 = f32[576,256]{1,0:T(8,128)} collective-permute-done((f32[576,256]{1,0:T(8,128)}, f32[576,256]{1,0:T(8,128)}, u32[]{:S(2)}, u32[]{:S(2)}) %collective-permute-start.11) | collective-permute-done | bytes 589856 | tf_op jit(solution)/shard_map/ppermute | solution.py:24
  186.8 14.7 %all-to-all-done.4 = f32[8,2,4,48,256]{4,3,2,1,0:T(8,128)S(1)} async-done(((f32[8,2,4,48,256]{4,3,2,1,0:T(8,128)}), f32[8,2,4,48,256]{4,3,2,1,0:T(8,128)S(1)}, u32[]{:S(2)}, u32[]{:S(2)}) %all-to-all-start.4) | async-done | bytes 3145760 | tf_op jit(solution)/shard_map/all_to_all | solution.py:10
  213.9 5.8 all-to-all-start.9
  230.7 25.5 %all-to-all-done.9 = f32[8,2,4,48,256]{4,3,2,1,0:T(8,128)} async-done(((f32[8,2,4,48,256]{4,3,2,1,0:T(8,128)}), f32[8,2,4,48,256]{4,3,2,1,0:T(8,128)}, u32[]{:S(2)}, u32[]{:S(2)}) %all-to-all-start.9) | async-done | bytes 3145760 | tf_op jit(solution)/shard_map/all_to_all | solution.py:10
  256.2 6.1 all-to-all-start.7
  264.8 6.5 fusion.44
  275.3 6.4 fusion.45
  290.1 6.4 fusion.46
  298.8 6.3 all-to-all-start.5
  310.9 9.6 %fusion = f32[1536,1536]{1,0:T(8,128)} fusion(f32[1536,1536]{1,0:T(8,128)S(1)} %copy-done.5, f32[1536,256]{1,0:T(8,128)S(1)} %bitcast.341, f32[1536,256]{1,0:T(8,128)S(1)} %bitcast.343, f32[3,1536,1536]{2,1,0:T(8,128)} %param.7, f32[]{:T(128)} %bitcast.81), kind=kOutput, calls=%fused_computation.7 | convolution fusion | flops 3630956544 | bytes 31457284 | tf_op jit(solution)/shard_map/dot_general | solution.py:107
  320.5 9.6 %copy.211 = f32[1536,1536]{1,0:T(8,128)} copy(f32[1536,1536]{0,1:T(8,128)} %bitcast.310) | data formatting | bytes 18874368 | tf_op jit(solution)/shard_map/dot_general | solution.py:113
  330.1 7.0 %convolution_bitcast_fusion.7 = f32[1,4,8,48,256]{4,3,2,1,0:T(8,128)S(1)} fusion(f32[4,8,48,1536]{3,2,1,0:T(8,128)} %bitcast.311, f32[1536,256,1,1]{1,0,3,2:T(8,128)S(1)} %bitcast.358), kind=kOutput, calls=%fused_computation.45 | convolution fusion | flops 3623878656 | bytes 12582912 | tf_op jit(solution)/shard_map/dot_general | solution.py:112
  337.1 4.1 convolution_bitcast_fusion.6
  343.4 4.6 all-to-all-start.10
  350.5 12.1 %fusion.2 = f32[1536,1536]{1,0:T(8,128)} fusion(f32[1536,1536]{1,0:T(8,128)} %fusion.44, f32[1536,256]{1,0:T(8,128)S(1)} %bitcast.351, f32[1536,256]{1,0:T(8,128)S(1)} %bitcast.349, f32[3,1536,1536]{2,1,0:T(8,128)} %param.7, f32[]{:T(128)} %bitcast.39), kind=kOutput, calls=%fused_computation.11 | convolution fusion | flops 3630956544 | bytes 31457284 | tf_op jit(solution)/shard_map/dot_general | solution.py:107
  362.6 9.7 %copy.195 = f32[1536,1536]{1,0:T(8,128)} copy(f32[1536,1536]{0,1:T(8,128)} %bitcast.316) | data formatting | bytes 18874368 | tf_op jit(solution)/shard_map/dot_general | solution.py:113
  372.3 7.0 %convolution_bitcast_fusion.11 = f32[1,4,8,48,256]{4,3,2,1,0:T(8,128)S(1)} fusion(f32[4,8,48,1536]{3,2,1,0:T(8,128)} %bitcast.317, f32[1536,256,1,1]{1,0,3,2:T(8,128)S(1)} %bitcast.356), kind=kOutput, calls=%fused_computation.49 | convolution fusion | flops 3623878656 | bytes 12582912 | tf_op jit(solution)/shard_map/dot_general | solution.py:112
  379.4 4.1 convolution_bitcast_fusion.10
  385.8 4.8 all-to-all-start.6
  393.0 11.5 %fusion.1 = f32[1536,1536]{1,0:T(8,128)} fusion(f32[1536,1536]{1,0:T(8,128)} %fusion.45, f32[1536,256]{1,0:T(8,128)S(1)} %bitcast.345, f32[1536,256]{1,0:T(8,128)S(1)} %bitcast.347, f32[3,1536,1536]{2,1,0:T(8,128)} %param.7, f32[]{:T(128)} %bitcast.60), kind=kOutput, calls=%fused_computation.9 | convolution fusion | flops 3630956544 | bytes 31457284 | tf_op jit(solution)/shard_map/dot_general | solution.py:107
  404.4 9.6 %copy.203 = f32[1536,1536]{1,0:T(8,128)} copy(f32[1536,1536]{0,1:T(8,128)} %bitcast.313) | data formatting | bytes 18874368 | tf_op jit(solution)/shard_map/dot_general | solution.py:113
  414.0 7.4 %convolution_bitcast_fusion.9 = f32[1,4,8,48,256]{4,3,2,1,0:T(8,128)S(1)} fusion(f32[4,8,48,1536]{3,2,1,0:T(8,128)} %bitcast.314, f32[1536,256,1,1]{1,0,3,2:T(8,128)} %bitcast.354), kind=kOutput, calls=%fused_computation.47 | convolution fusion | flops 3623878656 | bytes 12582912 | tf_op jit(solution)/shard_map/dot_general | solution.py:112
  427.9 5.1 all-to-all-start.8
  432.9 7.4 %convolution_bitcast_fusion.5 = f32[1,4,8,48,256]{4,3,2,1,0:T(8,128)S(1)} fusion(f32[4,8,48,1536]{3,2,1,0:T(8,128)} %bitcast.318, f32[1536,256,1,1]{1,0,3,2:T(8,128)} %bitcast.350), kind=kOutput, calls=%fused_computation.43 | convolution fusion | flops 3623878656 | bytes 12582912 | tf_op jit(solution)/shard_map/dot_general | solution.py:112
  440.4 7.3 %convolution_bitcast_fusion.4 = f32[1,4,8,48,256]{4,3,2,1,0:T(8,128)S(1)} fusion(f32[4,8,48,1536]{3,2,1,0:T(8,128)} %bitcast.327, f32[1536,256,1,1]{1,0,3,2:T(8,128)S(1)} %bitcast.352), kind=kOutput, calls=%fused_computation.42 | convolution fusion | flops 3623878656 | bytes 12582912 | tf_op jit(solution)/shard_map/dot_general | solution.py:113
  449.7 5.3 copy.215
  455.0 5.4 copy.213
  460.4 9.0 %all-to-all-done.8 = f32[8,2,4,48,256]{4,3,2,1,0:T(8,128)} async-done(((f32[8,2,4,48,256]{4,3,2,1,0:T(8,128)}), f32[8,2,4,48,256]{4,3,2,1,0:T(8,128)}, u32[]{:S(2)}, u32[]{:S(2)}) %all-to-all-start.8) | async-done | bytes 3145760 | tf_op jit(solution)/shard_map/all_to_all | solution.py:10
  481.1 6.0 all-to-all-start.11
  487.1 7.5 %convolution_bitcast_fusion.3 = f32[1,4,8,48,256]{4,3,2,1,0:T(8,128)S(1)} fusion(f32[4,8,48,1536]{3,2,1,0:T(8,128)} %bitcast.315, f32[1536,256,1,1]{1,0,3,2:T(8,128)} %bitcast.348), kind=kOutput, calls=%fused_computation.41 | convolution fusion | flops 3623878656 | bytes 12582912 | tf_op jit(solution)/shard_map/dot_general | solution.py:112
  499.3 4.1 convolution_bitcast_fusion.2
  505.4 5.8 collective-permute-done.12
  511.2 12.4 %all-to-all-done.11 = f32[8,2,4,48,256]{4,3,2,1,0:T(8,128)} async-done(((f32[8,2,4,48,256]{4,3,2,1,0:T(8,128)}), f32[8,2,4,48,256]{4,3,2,1,0:T(8,128)}, u32[]{:S(2)}, u32[]{:S(2)}) %all-to-all-start.11) | async-done | bytes 3145760 | tf_op jit(solution)/shard_map/all_to_all | solution.py:10
  529.0 6.1 all-to-all-start.12
  535.1 7.0 %convolution_bitcast_fusion.1 = f32[1,4,8,48,256]{4,3,2,1,0:T(8,128)S(1)} fusion(f32[4,8,48,1536]{3,2,1,0:T(8,128)} %bitcast.312, f32[1536,256,1,1]{1,0,3,2:T(8,128)S(1)} %bitcast.344), kind=kOutput, calls=%fused_computation.39 | convolution fusion | flops 3623878656 | bytes 12582912 | tf_op jit(solution)/shard_map/dot_general | solution.py:112
  546.5 4.1 convolution_bitcast_fusion
  552.7 6.2 collective-permute-done.14
  558.9 12.8 %all-to-all-done.12 = f32[8,2,4,48,256]{4,3,2,1,0:T(8,128)} async-done(((f32[8,2,4,48,256]{4,3,2,1,0:T(8,128)}), f32[8,2,4,48,256]{4,3,2,1,0:T(8,128)}, u32[]{:S(2)}, u32[]{:S(2)}) %all-to-all-start.12) | async-done | bytes 3145760 | tf_op jit(solution)/shard_map/all_to_all | solution.py:10
  577.0 5.1 all-to-all-start.13
  586.3 5.6 collective-permute-start.16
  591.9 5.4 copy.232
  597.3 5.4 copy.233
  603.6 14.9 %all-to-all-done.13 = f32[8,2,4,48,256]{4,3,2,1,0:T(8,128)S(1)} async-done(((f32[8,2,4,48,256]{4,3,2,1,0:T(8,128)}), f32[8,2,4,48,256]{4,3,2,1,0:T(8,128)S(1)}, u32[]{:S(2)}, u32[]{:S(2)}) %all-to-all-start.13) | async-done | bytes 3145760 | tf_op jit(solution)/shard_map/all_to_all | solution.py:10
  627.1 11.8 %collective-permute-done.18 = f32[12,48,256]{2,1,0:T(8,128)S(1)} collective-permute-done((f32[12,48,256]{2,1,0:T(8,128)S(1)}, f32[12,48,256]{2,1,0:T(8,128)S(1)}, u32[]{:S(2)}, u32[]{:S(2)}) %collective-permute-start.18) | collective-permute-done | bytes 589856 | tf_op jit(solution)/shard_map/ppermute | solution.py:51
  639.3 4.6 collective-permute-start.19
  644.9 11.0 %collective-permute-done.19 = f32[12,48,256]{2,1,0:T(8,128)S(1)} collective-permute-done((f32[12,48,256]{2,1,0:T(8,128)S(1)}, f32[12,48,256]{2,1,0:T(8,128)S(1)}, u32[]{:S(2)}, u32[]{:S(2)}) %collective-permute-start.19) | collective-permute-done | bytes 589856 | tf_op jit(solution)/shard_map/ppermute | solution.py:51
  657.1 5.2 collective-permute-start.20
  670.7 4.2 all-to-all-start.14
  674.9 4.2 collective-permute-done.23
  690.4 8.0 %all-to-all-done.15 = f32[576,8,32]{0,2,1:T(8,128)S(1)} async-done(((f32[576,8,32]{0,2,1:T(8,128)}), f32[576,8,32]{0,2,1:T(8,128)S(1)}, u32[]{:S(2)}, u32[]{:S(2)}) %all-to-all-start.15) | async-done | bytes 589856 | tf_op jit(solution)/shard_map/all_to_all | solution.py:130
  (283 shorter events, 189.6 us)
Async XLA Ops:
  0.0 28.2 %copy-start = (s32[32,6]{0,1:T(8,128)S(1)}, s32[32,6]{0,1:T(8,128)}, u32[]{:S(2)}) copy-start(s32[32,6]{0,1:T(8,128)} %param.6) | copy-start | bytes 2308
  16.5 16.3 %collective-permute-start = (f32[576,256]{1,0:T(8,128)}, f32[576,256]{1,0:T(8,128)}, u32[]{:S(2)}, u32[]{:S(2)}) collective-permute-start(f32[576,256]{1,0:T(8,128)} %copy.179), channel_id=1, source_target_pairs={{0,8},{8,16},{16,24},{1,9},{9,17},{17,25},{2,10},{10,18},{18,26},{... | collective-permute-start | bytes 1769480 | tf_op jit(solution)/shard_map/ppermute | solution.py:23
  20.8 16.9 %collective-permute-start.1 = (f32[576,256]{1,0:T(8,128)}, f32[576,256]{1,0:T(8,128)}, u32[]{:S(2)}, u32[]{:S(2)}) collective-permute-start(f32[576,256]{1,0:T(8,128)} %copy.179), channel_id=1, source_target_pairs={{8,0},{16,8},{24,16},{9,1},{17,9},{25,17},{10,2},{18,10},{26,18},{... | collective-permute-start | bytes 1769480 | tf_op jit(solution)/shard_map/ppermute | solution.py:24
  23.2 52.5 %all-to-all-start = ((f32[8,576,32]{1,2,0:T(8,128)}), f32[8,576,32]{1,2,0:T(8,128)S(1)}, u32[]{:S(2)}, u32[]{:S(2)}) async-start(f32[8,576,32]{1,2,0:T(8,128)} %copy.175), calls=%async_computation | async-start | bytes 1310720 | tf_op jit(solution)/shard_map/all_to_all | solution.py:72
  28.2 12.2 %copy-start.47 = (s32[8,6]{0,1:T(8,128)}, s32[8,6]{0,1:T(8,128)S(1)}, u32[]{:S(2)}) copy-start(s32[8,6]{0,1:T(8,128)S(1)} %constant_dynamic-slice_fusion.7) | copy-start | bytes 580
  32.8 7.7 %collective-permute-start.2 = (f32[576,256]{1,0:T(8,128)}, f32[576,256]{1,0:T(8,128)S(1)}, u32[]{:S(2)}, u32[]{:S(2)}) collective-permute-start(f32[576,256]{1,0:T(8,128)} %collective-permute-done), channel_id=1, source_target_pairs={{8,16},{16,24},{9,17},{17,25},{10,18},{18,26},{11,19},{19,27},{12,... | collective-permute-start | bytes 1769480 | tf_op jit(solution)/shard_map/ppermute | solution.py:23
  34.1 37.6 %copy-start.49 = (pred[8,2]{1,0:T(8,128)(4,1)}, pred[8,2]{1,0:T(8,128)(4,1)S(1)}, u32[]{:S(2)}) copy-start(pred[8,2]{1,0:T(8,128)(4,1)S(1)} %copy.176) | copy-start | bytes 52
  37.7 16.4 %collective-permute-start.3 = (f32[576,256]{1,0:T(8,128)}, f32[576,256]{1,0:T(8,128)S(1)}, u32[]{:S(2)}, u32[]{:S(2)}) collective-permute-start(f32[576,256]{1,0:T(8,128)} %collective-permute-done.1), channel_id=1, source_target_pairs={{8,0},{16,8},{9,1},{17,9},{10,2},{18,10},{11,3},{19,11},{12,4},{20... | collective-permute-start | bytes 1769480 | tf_op jit(solution)/shard_map/ppermute | solution.py:24
  40.4 15.0 %collective-permute-start.4 = (f32[576,256]{1,0:T(8,128)S(1)}, f32[576,256]{1,0:T(8,128)S(1)}, u32[]{:S(2)}, u32[]{:S(2)}) collective-permute-start(f32[576,256]{1,0:T(8,128)S(1)} %collective-permute-done.2), channel_id=1, source_target_pairs={{16,24},{17,25},{18,26},{19,27},{20,28},{21,29},{22,30},{23,31}} | collective-permute-start | bytes 1769480 | tf_op jit(solution)/shard_map/ppermute | solution.py:23
  54.1 15.1 %collective-permute-start.5 = (f32[576,256]{1,0:T(8,128)S(1)}, f32[576,256]{1,0:T(8,128)S(1)}, u32[]{:S(2)}, u32[]{:S(2)}) collective-permute-start(f32[576,256]{1,0:T(8,128)S(1)} %collective-permute-done.3), channel_id=1, source_target_pairs={{8,0},{9,1},{10,2},{11,3},{12,4},{13,5},{14,6},{15,7}} | collective-permute-start | bytes 1769480 | tf_op jit(solution)/shard_map/ppermute | solution.py:24
  75.8 13.4 %copy-start.55 = (pred[8,2]{0,1:T(4,128)(4,1)S(1)}, pred[8,2]{0,1:T(4,128)(4,1)}, u32[]{:S(2)}) copy-start(pred[8,2]{0,1:T(4,128)(4,1)} %get-tuple-element.118) | copy-start | bytes 52
  75.8 41.9 %all-to-all-start.2 = ((f32[8,2,4,48,256]{4,3,2,1,0:T(8,128)}), f32[8,2,4,48,256]{4,3,2,1,0:T(8,128)}, u32[]{:S(2)}, u32[]{:S(2)}) async-start(f32[8,2,4,48,256]{4,3,2,1,0:T(8,128)} %broadcast_select_fusion.5), calls=%async_computation.2 | async-start | bytes 6291456 | tf_op jit(solution)/shard_map/all_to_all | solution.py:10
  83.3 17.5 %collective-permute-start.7 = (f32[576,256]{1,0:T(8,128)}, f32[576,256]{1,0:T(8,128)S(1)}, u32[]{:S(2)}, u32[]{:S(2)}) collective-permute-start(f32[576,256]{1,0:T(8,128)} %copy.183), channel_id=1, source_target_pairs={{8,0},{16,8},{24,16},{9,1},{17,9},{25,17},{10,2},{18,10},{26,18},{... | collective-permute-start | bytes 1769480 | tf_op jit(solution)/shard_map/ppermute | solution.py:24
  84.6 17.5 %collective-permute-start.6 = (f32[576,256]{1,0:T(8,128)}, f32[576,256]{1,0:T(8,128)S(1)}, u32[]{:S(2)}, u32[]{:S(2)}) collective-permute-start(f32[576,256]{1,0:T(8,128)} %copy.182), channel_id=1, source_target_pairs={{0,8},{8,16},{16,24},{1,9},{9,17},{17,25},{2,10},{10,18},{18,26},{... | collective-permute-start | bytes 1769480 | tf_op jit(solution)/shard_map/ppermute | solution.py:23
  96.5 29.8 %copy-start.54 = (pred[8,2]{0,1:T(4,128)(4,1)S(1)}, pred[8,2]{0,1:T(4,128)(4,1)}, u32[]{:S(2)}) copy-start(pred[8,2]{0,1:T(4,128)(4,1)} %get-tuple-element.78) | copy-start | bytes 52
  100.8 24.2 %copy-start.42 = (f32[576,256]{1,0:T(8,128)}, f32[576,256]{1,0:T(8,128)S(1)}, u32[]{:S(2)}) copy-start(f32[576,256]{1,0:T(8,128)S(1)} %collective-permute-done.7) | copy-start | bytes 1769476
  102.1 21.5 %copy-start.44 = (f32[576,256]{1,0:T(8,128)}, f32[576,256]{1,0:T(8,128)S(1)}, u32[]{:S(2)}) copy-start(f32[576,256]{1,0:T(8,128)S(1)} %collective-permute-done.6) | copy-start | bytes 1769476
  117.7 42.4 %all-to-all-start.3 = ((f32[8,2,4,48,256]{4,3,2,1,0:T(8,128)}), f32[8,2,4,48,256]{4,3,2,1,0:T(8,128)}, u32[]{:S(2)}, u32[]{:S(2)}) async-start(f32[8,2,4,48,256]{4,3,2,1,0:T(8,128)} %broadcast_select_fusion.4), calls=%async_computation.3 | async-start | bytes 6291456 | tf_op jit(solution)/shard_map/all_to_all | solution.py:10
  123.5 11.8 %collective-permute-start.8 = (f32[576,256]{1,0:T(8,128)S(1)}, f32[576,256]{1,0:T(8,128)}, u32[]{:S(2)}, u32[]{:S(2)}) collective-permute-start(f32[576,256]{1,0:T(8,128)S(1)} %collective-permute-done.6), channel_id=1, source_target_pairs={{8,16},{16,24},{9,17},{17,25},{10,18},{18,26},{11,19},{19,27},{12,... | collective-permute-start | bytes 1769480 | tf_op jit(solution)/shard_map/ppermute | solution.py:23
  125.0 17.4 %collective-permute-start.9 = (f32[576,256]{1,0:T(8,128)S(1)}, f32[576,256]{1,0:T(8,128)}, u32[]{:S(2)}, u32[]{:S(2)}) collective-permute-start(f32[576,256]{1,0:T(8,128)S(1)} %collective-permute-done.7), channel_id=1, source_target_pairs={{8,0},{16,8},{9,1},{17,9},{10,2},{18,10},{11,3},{19,11},{12,4},{20... | collective-permute-start | bytes 1769480 | tf_op jit(solution)/shard_map/ppermute | solution.py:24
  160.0 41.5 %all-to-all-start.4 = ((f32[8,2,4,48,256]{4,3,2,1,0:T(8,128)}), f32[8,2,4,48,256]{4,3,2,1,0:T(8,128)S(1)}, u32[]{:S(2)}, u32[]{:S(2)}) async-start(f32[8,2,4,48,256]{4,3,2,1,0:T(8,128)} %broadcast_select_fusion.3), calls=%async_computation.4 | async-start | bytes 6291456 | tf_op jit(solution)/shard_map/all_to_all | solution.py:10
  168.5 4.3 collective-permute-start.10
  169.2 17.6 %collective-permute-start.11 = (f32[576,256]{1,0:T(8,128)}, f32[576,256]{1,0:T(8,128)}, u32[]{:S(2)}, u32[]{:S(2)}) collective-permute-start(f32[576,256]{1,0:T(8,128)} %collective-permute-done.9), channel_id=1, source_target_pairs={{8,0},{9,1},{10,2},{11,3},{12,4},{13,5},{14,6},{15,7}} | collective-permute-start | bytes 1769480 | tf_op jit(solution)/shard_map/ppermute | solution.py:24
  213.9 42.3 %all-to-all-start.9 = ((f32[8,2,4,48,256]{4,3,2,1,0:T(8,128)}), f32[8,2,4,48,256]{4,3,2,1,0:T(8,128)}, u32[]{:S(2)}, u32[]{:S(2)}) async-start(f32[8,2,4,48,256]{4,3,2,1,0:T(8,128)} %broadcast_select_fusion), calls=%async_computation.9 | async-start | bytes 6291456 | tf_op jit(solution)/shard_map/all_to_all | solution.py:10
  256.2 42.6 %all-to-all-start.7 = ((f32[8,2,4,48,256]{4,3,2,1,0:T(8,128)}), f32[8,2,4,48,256]{4,3,2,1,0:T(8,128)}, u32[]{:S(2)}, u32[]{:S(2)}) async-start(f32[8,2,4,48,256]{4,3,2,1,0:T(8,128)} %broadcast_select_fusion.1), calls=%async_computation.7 | async-start | bytes 6291456 | tf_op jit(solution)/shard_map/all_to_all | solution.py:10
  298.8 44.6 %all-to-all-start.5 = ((f32[8,2,4,48,256]{4,3,2,1,0:T(8,128)}), f32[8,2,4,48,256]{4,3,2,1,0:T(8,128)}, u32[]{:S(2)}, u32[]{:S(2)}) async-start(f32[8,2,4,48,256]{4,3,2,1,0:T(8,128)} %broadcast_select_fusion.2), calls=%async_computation.5 | async-start | bytes 6291456 | tf_op jit(solution)/shard_map/all_to_all | solution.py:10
  307.5 12.9 %copy-start.15 = (f32[1,4,8,48,256]{4,3,2,1,0:T(8,128)}, f32[1,4,8,48,256]{4,3,2,1,0:T(8,128)S(1)}, u32[]{:S(2)}) copy-start(f32[1,4,8,48,256]{4,3,2,1,0:T(8,128)S(1)} %copy.210) | copy-start | bytes 4718596
  307.7 12.8 %copy-start.13 = (f32[1,4,8,48,256]{4,3,2,1,0:T(8,128)}, f32[1,4,8,48,256]{4,3,2,1,0:T(8,128)S(1)}, u32[]{:S(2)}) copy-start(f32[1,4,8,48,256]{4,3,2,1,0:T(8,128)S(1)} %copy.209) | copy-start | bytes 4718596
  343.4 42.4 %all-to-all-start.10 = ((f32[8,2,4,48,256]{4,3,2,1,0:T(8,128)}), f32[8,2,4,48,256]{4,3,2,1,0:T(8,128)}, u32[]{:S(2)}, u32[]{:S(2)}) async-start(f32[8,2,4,48,256]{4,3,2,1,0:T(8,128)} %copy.212), calls=%async_computation.10 | async-start | bytes 6291456 | tf_op jit(solution)/shard_map/all_to_all | solution.py:10
  350.4 12.2 %copy-start.18 = (f32[1,4,8,48,256]{4,3,2,1,0:T(8,128)}, f32[1,4,8,48,256]{4,3,2,1,0:T(8,128)S(1)}, u32[]{:S(2)}) copy-start(f32[1,4,8,48,256]{4,3,2,1,0:T(8,128)S(1)} %copy.194) | copy-start | bytes 4718596
  350.5 12.1 %copy-start.19 = (f32[1,4,8,48,256]{4,3,2,1,0:T(8,128)}, f32[1,4,8,48,256]{4,3,2,1,0:T(8,128)S(1)}, u32[]{:S(2)}) copy-start(f32[1,4,8,48,256]{4,3,2,1,0:T(8,128)S(1)} %copy.193) | copy-start | bytes 4718596
  362.6 9.7 %copy-start.23 = (f32[1,4,8,48,256]{4,3,2,1,0:T(8,128)S(1)}, f32[1,4,8,48,256]{4,3,2,1,0:T(8,128)}, u32[]{:S(2)}) copy-start(f32[1,4,8,48,256]{4,3,2,1,0:T(8,128)} %copy-done.22) | copy-start | bytes 4718596
  385.8 42.1 %all-to-all-start.6 = ((f32[8,2,4,48,256]{4,3,2,1,0:T(8,128)}), f32[8,2,4,48,256]{4,3,2,1,0:T(8,128)}, u32[]{:S(2)}, u32[]{:S(2)}) async-start(f32[8,2,4,48,256]{4,3,2,1,0:T(8,128)} %copy.196), calls=%async_computation.6 | async-start | bytes 6291456 | tf_op jit(solution)/shard_map/all_to_all | solution.py:10
  392.9 11.6 %copy-start.17 = (f32[1,4,8,48,256]{4,3,2,1,0:T(8,128)}, f32[1,4,8,48,256]{4,3,2,1,0:T(8,128)S(1)}, u32[]{:S(2)}) copy-start(f32[1,4,8,48,256]{4,3,2,1,0:T(8,128)S(1)} %copy.202) | copy-start | bytes 4718596
  427.9 41.6 %all-to-all-start.8 = ((f32[8,2,4,48,256]{4,3,2,1,0:T(8,128)}), f32[8,2,4,48,256]{4,3,2,1,0:T(8,128)}, u32[]{:S(2)}, u32[]{:S(2)}) async-start(f32[8,2,4,48,256]{4,3,2,1,0:T(8,128)} %copy.204), calls=%async_computation.8 | async-start | bytes 6291456 | tf_op jit(solution)/shard_map/all_to_all | solution.py:10
  455.0 18.3 %copy-start.48 = (s32[8,6]{0,1:T(8,128)S(1)}, s32[8,6]{0,1:T(8,128)}, u32[]{:S(2)}) copy-start(s32[8,6]{0,1:T(8,128)} %copy-done.47) | copy-start | bytes 580
  481.1 18.1 %slice-start.3 = ((s8[9437184]{0:T(1024)(128)(4,1)}), s8[1048576]{0:T(1024)(128)(4,1)S(1)}, s32[]{:S(2)}) async-start(s8[9437184]{0:T(1024)(128)(4,1)} %bitcast.324), calls=%async_computation.19 | async-start | bytes 2097152
  481.1 42.5 %all-to-all-start.11 = ((f32[8,2,4,48,256]{4,3,2,1,0:T(8,128)}), f32[8,2,4,48,256]{4,3,2,1,0:T(8,128)}, u32[]{:S(2)}, u32[]{:S(2)}) async-start(f32[8,2,4,48,256]{4,3,2,1,0:T(8,128)} %copy.219), calls=%async_computation.11 | async-start | bytes 6291456 | tf_op jit(solution)/shard_map/all_to_all | solution.py:10
  487.1 12.1 %slice-start.4 = ((s8[9437184]{0:T(1024)(128)(4,1)}), s8[4194304]{0:T(1024)(128)(4,1)S(1)}, s32[]{:S(2)}) async-start(s8[9437184]{0:T(1024)(128)(4,1)} %bitcast.324), calls=%async_computation.20 | async-start | bytes 8388608
  487.1 12.1 %slice-start.5 = ((s8[9437184]{0:T(1024)(128)(4,1)}), s8[4194304]{0:T(1024)(128)(4,1)S(1)}, s32[]{:S(2)}) async-start(s8[9437184]{0:T(1024)(128)(4,1)} %bitcast.324), calls=%async_computation.21 | async-start | bytes 8388608
  495.3 10.1 %collective-permute-start.13 = (f32[12,48,256]{2,1,0:T(8,128)S(1)}, f32[12,48,256]{2,1,0:T(8,128)}, u32[]{:S(2)}, u32[]{:S(2)}) collective-permute-start(f32[12,48,256]{2,1,0:T(8,128)S(1)} %copy.218), channel_id=1, source_target_pairs={{24,16},{25,17},{26,18},{27,19},{28,20},{29,21},{30,22},{31,23}} | collective-permute-start | bytes 1769480 | tf_op jit(solution)/shard_map/ppermute | solution.py:52
  496.8 14.4 %collective-permute-start.12 = (f32[12,48,256]{2,1,0:T(8,128)S(1)}, f32[12,48,256]{2,1,0:T(8,128)}, u32[]{:S(2)}, u32[]{:S(2)}) collective-permute-start(f32[12,48,256]{2,1,0:T(8,128)S(1)} %copy.217), channel_id=1, source_target_pairs={{0,8},{1,9},{2,10},{3,11},{4,12},{5,13},{6,14},{7,15}} | collective-permute-start | bytes 1769480 | tf_op jit(solution)/shard_map/ppermute | solution.py:51
  503.4 20.2 %copy-start.7 = (f32[4,48,256,12]{2,3,1,0:T(8,128)S(1)}, f32[4,48,256,12]{2,3,1,0:T(8,128)}, u32[]{:S(2)}) copy-start(f32[4,48,256,12]{2,3,1,0:T(8,128)} %copy-done.6) | copy-start | bytes 7077892
  529.0 17.5 %slice-start = ((s8[9437184]{0:T(1024)(128)(4,1)}), s8[1048576]{0:T(1024)(128)(4,1)S(1)}, s32[]{:S(2)}) async-start(s8[9437184]{0:T(1024)(128)(4,1)} %bitcast.320), calls=%async_computation.16 | async-start | bytes 2097152
  529.0 42.6 %all-to-all-start.12 = ((f32[8,2,4,48,256]{4,3,2,1,0:T(8,128)}), f32[8,2,4,48,256]{4,3,2,1,0:T(8,128)}, u32[]{:S(2)}, u32[]{:S(2)}) async-start(f32[8,2,4,48,256]{4,3,2,1,0:T(8,128)} %copy.224), calls=%async_computation.12 | async-start | bytes 6291456 | tf_op jit(solution)/shard_map/all_to_all | solution.py:10
  535.1 11.4 %slice-start.1 = ((s8[9437184]{0:T(1024)(128)(4,1)}), s8[4194304]{0:T(1024)(128)(4,1)S(1)}, s32[]{:S(2)}) async-start(s8[9437184]{0:T(1024)(128)(4,1)} %bitcast.320), calls=%async_computation.17 | async-start | bytes 8388608
  535.1 11.4 %slice-start.2 = ((s8[9437184]{0:T(1024)(128)(4,1)}), s8[4194304]{0:T(1024)(128)(4,1)S(1)}, s32[]{:S(2)}) async-start(s8[9437184]{0:T(1024)(128)(4,1)} %bitcast.320), calls=%async_computation.18 | async-start | bytes 8388608
  542.9 9.7 %collective-permute-start.15 = (f32[12,48,256]{2,1,0:T(8,128)S(1)}, f32[12,48,256]{2,1,0:T(8,128)}, u32[]{:S(2)}, u32[]{:S(2)}) collective-permute-start(f32[12,48,256]{2,1,0:T(8,128)S(1)} %copy.223), channel_id=1, source_target_pairs={{16,8},{24,16},{17,9},{25,17},{18,10},{26,18},{19,11},{27,19},{20,... | collective-permute-start | bytes 1769480 | tf_op jit(solution)/shard_map/ppermute | solution.py:52
  544.4 14.4 %collective-permute-start.14 = (f32[12,48,256]{2,1,0:T(8,128)S(1)}, f32[12,48,256]{2,1,0:T(8,128)}, u32[]{:S(2)}, u32[]{:S(2)}) collective-permute-start(f32[12,48,256]{2,1,0:T(8,128)S(1)} %copy.222), channel_id=1, source_target_pairs={{0,8},{8,16},{1,9},{9,17},{2,10},{10,18},{3,11},{11,19},{4,12},{12... | collective-permute-start | bytes 1769480 | tf_op jit(solution)/shard_map/ppermute | solution.py:51
  550.6 21.0 %copy-start.8 = (f32[4,48,256,12]{2,3,1,0:T(8,128)S(1)}, f32[4,48,256,12]{2,3,1,0:T(8,128)}, u32[]{:S(2)}) copy-start(f32[4,48,256,12]{2,3,1,0:T(8,128)} %copy-done.6) | copy-start | bytes 7077892
  577.0 41.5 %all-to-all-start.13 = ((f32[8,2,4,48,256]{4,3,2,1,0:T(8,128)}), f32[8,2,4,48,256]{4,3,2,1,0:T(8,128)S(1)}, u32[]{:S(2)}, u32[]{:S(2)}) async-start(f32[8,2,4,48,256]{4,3,2,1,0:T(8,128)} %copy.229), calls=%async_computation.13 | async-start | bytes 6291456 | tf_op jit(solution)/shard_map/all_to_all | solution.py:10
  585.0 17.7 %collective-permute-start.17 = (f32[12,48,256]{2,1,0:T(8,128)S(1)}, f32[12,48,256]{2,1,0:T(8,128)S(1)}, u32[]{:S(2)}, u32[]{:S(2)}) collective-permute-start(f32[12,48,256]{2,1,0:T(8,128)S(1)} %copy.228), channel_id=1, source_target_pairs={{8,0},{16,8},{24,16},{9,1},{17,9},{25,17},{10,2},{18,10},{26,18},{... | collective-permute-start | bytes 1769480 | tf_op jit(solution)/shard_map/ppermute | solution.py:52
  586.3 17.3 %collective-permute-start.16 = (f32[12,48,256]{2,1,0:T(8,128)S(1)}, f32[12,48,256]{2,1,0:T(8,128)}, u32[]{:S(2)}, u32[]{:S(2)}) collective-permute-start(f32[12,48,256]{2,1,0:T(8,128)S(1)} %copy.227), channel_id=1, source_target_pairs={{0,8},{8,16},{16,24},{1,9},{9,17},{17,25},{2,10},{10,18},{18,26},{... | collective-permute-start | bytes 1769480 | tf_op jit(solution)/shard_map/ppermute | solution.py:51
  624.5 14.4 %collective-permute-start.18 = (f32[12,48,256]{2,1,0:T(8,128)S(1)}, f32[12,48,256]{2,1,0:T(8,128)S(1)}, u32[]{:S(2)}, u32[]{:S(2)}) collective-permute-start(f32[12,48,256]{2,1,0:T(8,128)S(1)} %copy.236), channel_id=1, source_target_pairs={{0,8},{1,9},{2,10},{3,11},{4,12},{5,13},{6,14},{7,15}} | collective-permute-start | bytes 1769480 | tf_op jit(solution)/shard_map/ppermute | solution.py:51
  626.4 17.5 %collective-permute-start.21 = (f32[12,48,256]{2,1,0:T(8,128)S(1)}, f32[12,48,256]{2,1,0:T(8,128)S(1)}, u32[]{:S(2)}, u32[]{:S(2)}) collective-permute-start(f32[12,48,256]{2,1,0:T(8,128)S(1)} %copy.239), channel_id=1, source_target_pairs={{24,16},{25,17},{26,18},{27,19},{28,20},{29,21},{30,22},{31,23}} | collective-permute-start | bytes 1769480 | tf_op jit(solution)/shard_map/ppermute | solution.py:52
  639.3 25.8 %copy-start.37 = (f32[1,48,256,12]{2,3,1,0:T(8,128)S(1)}, f32[1,48,256,12]{2,3,1,0:T(8,128)}, u32[]{:S(2)}) copy-start(f32[1,48,256,12]{2,3,1,0:T(8,128)} %get-tuple-element.84) | copy-start | bytes 1769476
  639.3 25.8 %copy-start.41 = (f32[12,48,256]{2,1,0:T(8,128)S(1)}, f32[12,48,256]{2,1,0:T(8,128)}, u32[]{:S(2)}) copy-start(f32[12,48,256]{2,1,0:T(8,128)} %copy-done.40) | copy-start | bytes 1769476
  639.3 16.6 %collective-permute-start.19 = (f32[12,48,256]{2,1,0:T(8,128)S(1)}, f32[12,48,256]{2,1,0:T(8,128)S(1)}, u32[]{:S(2)}, u32[]{:S(2)}) collective-permute-start(f32[12,48,256]{2,1,0:T(8,128)S(1)} %fusion.24), channel_id=1, source_target_pairs={{0,8},{8,16},{1,9},{9,17},{2,10},{10,18},{3,11},{11,19},{4,12},{12... | collective-permute-start | bytes 1769480 | tf_op jit(solution)/shard_map/ppermute | solution.py:51
  644.2 18.1 %collective-permute-start.22 = (f32[12,48,256]{2,1,0:T(8,128)S(1)}, f32[12,48,256]{2,1,0:T(8,128)S(1)}, u32[]{:S(2)}, u32[]{:S(2)}) collective-permute-start(f32[12,48,256]{2,1,0:T(8,128)S(1)} %fusion.22), channel_id=1, source_target_pairs={{16,8},{24,16},{17,9},{25,17},{18,10},{26,18},{19,11},{27,19},{20,... | collective-permute-start | bytes 1769480 | tf_op jit(solution)/shard_map/ppermute | solution.py:52
  657.1 17.8 %collective-permute-start.20 = (f32[12,48,256]{2,1,0:T(8,128)}, f32[12,48,256]{2,1,0:T(8,128)}, u32[]{:S(2)}, u32[]{:S(2)}) collective-permute-start(f32[12,48,256]{2,1,0:T(8,128)} %fusion.23), channel_id=1, source_target_pairs={{0,8},{8,16},{16,24},{1,9},{9,17},{17,25},{2,10},{10,18},{18,26},{... | collective-permute-start | bytes 1769480 | tf_op jit(solution)/shard_map/ppermute | solution.py:51
  663.5 15.6 %collective-permute-start.23 = (f32[12,48,256]{2,1,0:T(8,128)}, f32[12,48,256]{2,1,0:T(8,128)}, u32[]{:S(2)}, u32[]{:S(2)}) collective-permute-start(f32[12,48,256]{2,1,0:T(8,128)} %fusion.21), channel_id=1, source_target_pairs={{8,0},{16,8},{24,16},{9,1},{17,9},{25,17},{10,2},{18,10},{26,18},{... | collective-permute-start | bytes 1769480 | tf_op jit(solution)/shard_map/ppermute | solution.py:52
  670.7 14.2 %all-to-all-start.14 = ((f32[576,8,32]{0,2,1:T(8,128)}), f32[576,8,32]{0,2,1:T(8,128)}, u32[]{:S(2)}, u32[]{:S(2)}) async-start(f32[576,8,32]{0,2,1:T(8,128)} %copy.259), calls=%async_computation.14 | async-start | bytes 1310720 | tf_op jit(solution)/shard_map/all_to_all | solution.py:130
  684.9 13.5 %all-to-all-start.15 = ((f32[576,8,32]{0,2,1:T(8,128)}), f32[576,8,32]{0,2,1:T(8,128)S(1)}, u32[]{:S(2)}, u32[]{:S(2)}) async-start(f32[576,8,32]{0,2,1:T(8,128)} %copy.260), calls=%async_computation.15 | async-start | bytes 1310720 | tf_op jit(solution)/shard_map/all_to_all | solution.py:130
  688.7 11.4 %copy-start.1 = (s32[32,6]{0,1:T(8,128)S(1)}, s32[32,6]{0,1:T(8,128)}, u32[]{:S(2)}) copy-start(s32[32,6]{0,1:T(8,128)} %param.6) | copy-start | bytes 2308
  (37 other events, 151.3 us)

commit v17 on v16

--- a/solution.py
+++ b/solution.py
@@ -85,11 +85,10 @@
     def requested(pieces, slot):
         wanted = group_requests[:, 2 * slot : 2 * slot + 2]
         wanted = jnp.where(wanted >= 0, wanted, block_count)
-        outgoing = jnp.take(pieces, wanted, axis=1, mode="fill", fill_value=0.0)
-        return outgoing.transpose(1, 2, 0, 3, 4)
+        return jnp.take(pieces, wanted, axis=0, mode="fill", fill_value=0.0)
 
     def shape_pieces(gathered):
-        return gathered.reshape(group_count, block_count, piece_rows, half)
+        return gathered.reshape(group_count, block_count, piece_rows, half).transpose(1, 0, 2, 3)
 
     first_pieces = shape_pieces(line_gather(own_rows[0], "grp", group_count)[0])
     first_loads = [requested(first_pieces, slot) for slot in range(slot_count)]

time: 712 us -> 713 us (level)
  no operation moved by 1% of the time
where the time goes in v17:
time: 713 us; the launch traced here: 701 us
  waiting for transfers between devices  229 us (32%)
  local copies, waits for them, and re-layouts  151 us (21%)
  starting transfers between devices  128 us (18%)
  matrix products  128 us (18%)
  other arithmetic  45.7 us (6%)
  blocking collectives  13.7 us (2%)
    all_to_all x12, waiting for transfers between devices, band_exchange(): lax.all_to_all(outgoing, 'band', split_axis=0, concat_axis=0, tiled=True)  125 us
    all_to_all x12, starting transfers between devices, band_exchange(): lax.all_to_all(outgoing, 'band', split_axis=0, concat_axis=0, tiled=True)  66.3 us
    dot_general x6, matrix products, body(): jnp.dot(r[0], r[1].T, precision=PRECISION, preferred_element_type=jnp.flo...  52.3 us
    ppermute x6, waiting for transfers between devices, line_gather(): lax.ppermute(leftward, axis, [(i + 1, i) for i in range(0, count - step)])  51.4 us
    dot_general x6, matrix products, body(): jnp.dot(kernel, rows[h][1], precision=PRECISION, preferred_element_type=j...  43.4 us
    ppermute x6, waiting for transfers between devices, line_reduce(): lax.ppermute(send_right, axis, [(i, i + 1) for i in range(0, step)])  34.8 us
    dot_general x3, local copies, waits for them, and re-layouts, body(): jnp.dot(kernel.T, rows[h][0], precision=PRECISION, preferred_element_type...  28.9 us
    dot_general x6, matrix products, body(): jnp.dot(kernel.T, rows[h][0], precision=PRECISION, preferred_element_type...  27.7 us
  transfers between devices with their start and end apart: 39, of which 23 were waited for; matrix products, arithmetic and copies ran while one was open for 38% of the time, Pallas kernels for 0%

profile of v17, /device:TPU:2, one launch (start us, length us, event | category | flops | bytes accessed | tf_op | source)
XLA Modules:
  0.0 700.8 jit_solution(3945026038161730424)
XLA Ops:
  1.7 13.7 %all_to_all.136 = f32[8,576,32]{1,2,0:T(8,128)S(1)} all-to-all(f32[8,576,32]{1,2,0:T(8,128)S(1)} %copy.181), channel_id=1, replica_groups=mesh['grp'=4,'band'=8] {'band'}, dimensions={0} | all-to-all | bytes 1179648 | tf_op jit(solution)/shard_map/all_to_all | solution.py:72
  16.5 4.3 collective-permute-start
  23.2 4.9 all-to-all-start
  28.2 4.5 collective-permute-done
  42.3 11.8 %collective-permute-done.3 = f32[576,256]{1,0:T(8,128)S(1)} collective-permute-done((f32[576,256]{1,0:T(8,128)}, f32[576,256]{1,0:T(8,128)S(1)}, u32[]{:S(2)}, u32[]{:S(2)}) %collective-permute-start.3) | collective-permute-done | bytes 589856 | tf_op jit(solution)/shard_map/ppermute | solution.py:24
  55.5 13.6 %collective-permute-done.5 = f32[576,256]{1,0:T(8,128)S(1)} collective-permute-done((f32[576,256]{1,0:T(8,128)S(1)}, f32[576,256]{1,0:T(8,128)S(1)}, u32[]{:S(2)}, u32[]{:S(2)}) %collective-permute-start.5) | collective-permute-done | bytes 589856 | tf_op jit(solution)/shard_map/ppermute | solution.py:24
  75.9 5.4 all-to-all-start.2
  84.7 4.6 collective-permute-start.6
  96.6 4.3 collective-permute-done.7
  102.2 15.6 %all-to-all-done.2 = f32[8,2,4,48,256]{4,3,2,1,0:T(8,128)} async-done(((f32[8,2,4,48,256]{4,3,2,1,0:T(8,128)}), f32[8,2,4,48,256]{4,3,2,1,0:T(8,128)}, u32[]{:S(2)}, u32[]{:S(2)}) %all-to-all-start.2) | async-done | bytes 3145760 | tf_op jit(solution)/shard_map/all_to_all | solution.py:10
  117.8 5.9 all-to-all-start.3
  135.5 7.0 %collective-permute-done.9 = f32[576,256]{1,0:T(8,128)} collective-permute-done((f32[576,256]{1,0:T(8,128)S(1)}, f32[576,256]{1,0:T(8,128)}, u32[]{:S(2)}, u32[]{:S(2)}) %collective-permute-start.9) | collective-permute-done | bytes 589856 | tf_op jit(solution)/shard_map/ppermute | solution.py:24
  142.6 17.6 %all-to-all-done.3 = f32[8,2,4,48,256]{4,3,2,1,0:T(8,128)} async-done(((f32[8,2,4,48,256]{4,3,2,1,0:T(8,128)}), f32[8,2,4,48,256]{4,3,2,1,0:T(8,128)}, u32[]{:S(2)}, u32[]{:S(2)}) %all-to-all-start.3) | async-done | bytes 3145760 | tf_op jit(solution)/shard_map/all_to_all | solution.py:10
  160.2 5.1 all-to-all-start.4
  175.5 11.5 %collective-permute-done.11 = f32[576,256]{1,0:T(8,128)} collective-permute-done((f32[576,256]{1,0:T(8,128)}, f32[576,256]{1,0:T(8,128)}, u32[]{:S(2)}, u32[]{:S(2)}) %collective-permute-start.11) | collective-permute-done | bytes 589856 | tf_op jit(solution)/shard_map/ppermute | solution.py:24
  187.0 14.7 %all-to-all-done.4 = f32[8,2,4,48,256]{4,3,2,1,0:T(8,128)S(1)} async-done(((f32[8,2,4,48,256]{4,3,2,1,0:T(8,128)}), f32[8,2,4,48,256]{4,3,2,1,0:T(8,128)S(1)}, u32[]{:S(2)}, u32[]{:S(2)}) %all-to-all-start.4) | async-done | bytes 3145760 | tf_op jit(solution)/shard_map/all_to_all | solution.py:10
  214.2 5.8 all-to-all-start.9
  231.0 25.5 %all-to-all-done.9 = f32[8,2,4,48,256]{4,3,2,1,0:T(8,128)} async-done(((f32[8,2,4,48,256]{4,3,2,1,0:T(8,128)}), f32[8,2,4,48,256]{4,3,2,1,0:T(8,128)}, u32[]{:S(2)}, u32[]{:S(2)}) %all-to-all-start.9) | async-done | bytes 3145760 | tf_op jit(solution)/shard_map/all_to_all | solution.py:10
  256.6 6.1 all-to-all-start.7
  265.2 6.5 fusion.44
  275.6 6.4 fusion.45
  290.5 6.4 fusion.46
  299.1 6.3 all-to-all-start.5
  311.2 9.6 %fusion = f32[1536,1536]{1,0:T(8,128)} fusion(f32[1536,1536]{1,0:T(8,128)S(1)} %copy-done.5, f32[1536,256]{1,0:T(8,128)S(1)} %bitcast.329, f32[1536,256]{1,0:T(8,128)S(1)} %bitcast.331, f32[3,1536,1536]{2,1,0:T(8,128)} %param.7, f32[]{:T(128)} %bitcast.71), kind=kOutput, calls=%fused_computation.7 | convolution fusion | flops 3630956544 | bytes 31457284 | tf_op jit(solution)/shard_map/dot_general | solution.py:106
  320.8 9.6 %copy.217 = f32[1536,1536]{1,0:T(8,128)} copy(f32[1536,1536]{0,1:T(8,128)} %bitcast.298) | data formatting | bytes 18874368 | tf_op jit(solution)/shard_map/dot_general | solution.py:112
  330.4 7.0 %convolution_bitcast_fusion.7 = f32[1,4,8,48,256]{4,3,2,1,0:T(8,128)S(1)} fusion(f32[4,8,48,1536]{3,2,1,0:T(8,128)} %bitcast.299, f32[1536,256,1,1]{1,0,3,2:T(8,128)S(1)} %bitcast.346), kind=kOutput, calls=%fused_computation.47 | convolution fusion | flops 3623878656 | bytes 12582912 | tf_op jit(solution)/shard_map/dot_general | solution.py:111
  337.5 4.1 convolution_bitcast_fusion.6
  343.8 4.6 all-to-all-start.10
  350.8 12.1 %fusion.2 = f32[1536,1536]{1,0:T(8,128)} fusion(f32[1536,1536]{1,0:T(8,128)} %fusion.44, f32[1536,256]{1,0:T(8,128)S(1)} %bitcast.339, f32[1536,256]{1,0:T(8,128)S(1)} %bitcast.337, f32[3,1536,1536]{2,1,0:T(8,128)} %param.7, f32[]{:T(128)} %bitcast.33), kind=kOutput, calls=%fused_computation.11 | convolution fusion | flops 3630956544 | bytes 31457284 | tf_op jit(solution)/shard_map/dot_general | solution.py:106
  362.9 9.7 %copy.201 = f32[1536,1536]{1,0:T(8,128)} copy(f32[1536,1536]{0,1:T(8,128)} %bitcast.304) | data formatting | bytes 18874368 | tf_op jit(solution)/shard_map/dot_general | solution.py:112
  372.6 7.0 %convolution_bitcast_fusion.11 = f32[1,4,8,48,256]{4,3,2,1,0:T(8,128)S(1)} fusion(f32[4,8,48,1536]{3,2,1,0:T(8,128)} %bitcast.305, f32[1536,256,1,1]{1,0,3,2:T(8,128)S(1)} %bitcast.344), kind=kOutput, calls=%fused_computation.51 | convolution fusion | flops 3623878656 | bytes 12582912 | tf_op jit(solution)/shard_map/dot_general | solution.py:111
  386.2 4.8 all-to-all-start.6
  393.3 11.5 %fusion.1 = f32[1536,1536]{1,0:T(8,128)} fusion(f32[1536,1536]{1,0:T(8,128)} %fusion.45, f32[1536,256]{1,0:T(8,128)S(1)} %bitcast.333, f32[1536,256]{1,0:T(8,128)S(1)} %bitcast.335, f32[3,1536,1536]{2,1,0:T(8,128)} %param.7, f32[]{:T(128)} %bitcast.52), kind=kOutput, calls=%fused_computation.9 | convolution fusion | flops 3630956544 | bytes 31457284 | tf_op jit(solution)/shard_map/dot_general | solution.py:106
  404.8 9.6 %copy.209 = f32[1536,1536]{1,0:T(8,128)} copy(f32[1536,1536]{0,1:T(8,128)} %bitcast.301) | data formatting | bytes 18874368 | tf_op jit(solution)/shard_map/dot_general | solution.py:112
  414.4 7.4 %convolution_bitcast_fusion.9 = f32[1,4,8,48,256]{4,3,2,1,0:T(8,128)S(1)} fusion(f32[4,8,48,1536]{3,2,1,0:T(8,128)} %bitcast.302, f32[1536,256,1,1]{1,0,3,2:T(8,128)} %bitcast.342), kind=kOutput, calls=%fused_computation.49 | convolution fusion | flops 3623878656 | bytes 12582912 | tf_op jit(solution)/shard_map/dot_general | solution.py:111
  421.8 4.1 convolution_bitcast_fusion.8
  428.2 5.1 all-to-all-start.8
  433.3 7.4 %convolution_bitcast_fusion.5 = f32[1,4,8,48,256]{4,3,2,1,0:T(8,128)S(1)} fusion(f32[4,8,48,1536]{3,2,1,0:T(8,128)} %bitcast.306, f32[1536,256,1,1]{1,0,3,2:T(8,128)} %bitcast.338), kind=kOutput, calls=%fused_computation.45 | convolution fusion | flops 3623878656 | bytes 12582912 | tf_op jit(solution)/shard_map/dot_general | solution.py:111
  440.7 7.3 %convolution_bitcast_fusion.4 = f32[1,4,8,48,256]{4,3,2,1,0:T(8,128)S(1)} fusion(f32[4,8,48,1536]{3,2,1,0:T(8,128)} %bitcast.315, f32[1536,256,1,1]{1,0,3,2:T(8,128)S(1)} %bitcast.340), kind=kOutput, calls=%fused_computation.44 | convolution fusion | flops 3623878656 | bytes 12582912 | tf_op jit(solution)/shard_map/dot_general | solution.py:112
  450.0 5.3 copy.221
  455.4 5.4 copy.219
  460.7 9.0 %all-to-all-done.8 = f32[8,2,4,48,256]{4,3,2,1,0:T(8,128)} async-done(((f32[8,2,4,48,256]{4,3,2,1,0:T(8,128)}), f32[8,2,4,48,256]{4,3,2,1,0:T(8,128)}, u32[]{:S(2)}, u32[]{:S(2)}) %all-to-all-start.8) | async-done | bytes 3145760 | tf_op jit(solution)/shard_map/all_to_all | solution.py:10
  481.4 6.0 all-to-all-start.11
  487.4 7.5 %convolution_bitcast_fusion.3 = f32[1,4,8,48,256]{4,3,2,1,0:T(8,128)S(1)} fusion(f32[4,8,48,1536]{3,2,1,0:T(8,128)} %bitcast.303, f32[1536,256,1,1]{1,0,3,2:T(8,128)} %bitcast.336), kind=kOutput, calls=%fused_computation.43 | convolution fusion | flops 3623878656 | bytes 12582912 | tf_op jit(solution)/shard_map/dot_general | solution.py:111
  499.6 4.1 convolution_bitcast_fusion.2
  505.8 5.8 collective-permute-done.12
  511.6 12.4 %all-to-all-done.11 = f32[8,2,4,48,256]{4,3,2,1,0:T(8,128)} async-done(((f32[8,2,4,48,256]{4,3,2,1,0:T(8,128)}), f32[8,2,4,48,256]{4,3,2,1,0:T(8,128)}, u32[]{:S(2)}, u32[]{:S(2)}) %all-to-all-start.11) | async-done | bytes 3145760 | tf_op jit(solution)/shard_map/all_to_all | solution.py:10
  529.3 6.1 all-to-all-start.12
  535.5 7.0 %convolution_bitcast_fusion.1 = f32[1,4,8,48,256]{4,3,2,1,0:T(8,128)S(1)} fusion(f32[4,8,48,1536]{3,2,1,0:T(8,128)} %bitcast.300, f32[1536,256,1,1]{1,0,3,2:T(8,128)S(1)} %bitcast.332), kind=kOutput, calls=%fused_computation.41 | convolution fusion | flops 3623878656 | bytes 12582912 | tf_op jit(solution)/shard_map/dot_general | solution.py:111
  546.9 4.1 convolution_bitcast_fusion
  553.0 6.2 collective-permute-done.14
  559.2 12.7 %all-to-all-done.12 = f32[8,2,4,48,256]{4,3,2,1,0:T(8,128)} async-done(((f32[8,2,4,48,256]{4,3,2,1,0:T(8,128)}), f32[8,2,4,48,256]{4,3,2,1,0:T(8,128)}, u32[]{:S(2)}, u32[]{:S(2)}) %all-to-all-start.12) | async-done | bytes 3145760 | tf_op jit(solution)/shard_map/all_to_all | solution.py:10
  577.3 5.1 all-to-all-start.13
  586.7 5.6 collective-permute-start.16
  592.2 5.4 copy.238
  597.6 5.4 copy.239
  603.9 14.9 %all-to-all-done.13 = f32[8,2,4,48,256]{4,3,2,1,0:T(8,128)S(1)} async-done(((f32[8,2,4,48,256]{4,3,2,1,0:T(8,128)}), f32[8,2,4,48,256]{4,3,2,1,0:T(8,128)S(1)}, u32[]{:S(2)}, u32[]{:S(2)}) %all-to-all-start.13) | async-done | bytes 3145760 | tf_op jit(solution)/shard_map/all_to_all | solution.py:10
  627.4 11.8 %collective-permute-done.18 = f32[12,48,256]{2,1,0:T(8,128)S(1)} collective-permute-done((f32[12,48,256]{2,1,0:T(8,128)S(1)}, f32[12,48,256]{2,1,0:T(8,128)S(1)}, u32[]{:S(2)}, u32[]{:S(2)}) %collective-permute-start.18) | collective-permute-done | bytes 589856 | tf_op jit(solution)/shard_map/ppermute | solution.py:51
  639.6 4.6 collective-permute-start.19
  645.3 11.0 %collective-permute-done.19 = f32[12,48,256]{2,1,0:T(8,128)S(1)} collective-permute-done((f32[12,48,256]{2,1,0:T(8,128)S(1)}, f32[12,48,256]{2,1,0:T(8,128)S(1)}, u32[]{:S(2)}, u32[]{:S(2)}) %collective-permute-start.19) | collective-permute-done | bytes 589856 | tf_op jit(solution)/shard_map/ppermute | solution.py:51
  657.4 5.2 collective-permute-start.20
  671.0 4.2 all-to-all-start.14
  675.2 4.2 collective-permute-done.23
  690.7 8.0 %all-to-all-done.15 = f32[576,8,32]{0,2,1:T(8,128)S(1)} async-done(((f32[576,8,32]{0,2,1:T(8,128)}), f32[576,8,32]{0,2,1:T(8,128)S(1)}, u32[]{:S(2)}, u32[]{:S(2)}) %all-to-all-start.15) | async-done | bytes 589856 | tf_op jit(solution)/shard_map/all_to_all | solution.py:129
  (285 shorter events, 189.9 us)
Async XLA Ops:
  0.0 28.2 %copy-start = (s32[32,6]{0,1:T(8,128)S(1)}, s32[32,6]{0,1:T(8,128)}, u32[]{:S(2)}) copy-start(s32[32,6]{0,1:T(8,128)} %param.6) | copy-start | bytes 2308
  16.5 16.3 %collective-permute-start = (f32[576,256]{1,0:T(8,128)}, f32[576,256]{1,0:T(8,128)}, u32[]{:S(2)}, u32[]{:S(2)}) collective-permute-start(f32[576,256]{1,0:T(8,128)} %copy.183), channel_id=1, source_target_pairs={{0,8},{8,16},{16,24},{1,9},{9,17},{17,25},{2,10},{10,18},{18,26},{... | collective-permute-start | bytes 1769480 | tf_op jit(solution)/shard_map/ppermute | solution.py:23
  20.8 16.9 %collective-permute-start.1 = (f32[576,256]{1,0:T(8,128)}, f32[576,256]{1,0:T(8,128)}, u32[]{:S(2)}, u32[]{:S(2)}) collective-permute-start(f32[576,256]{1,0:T(8,128)} %copy.183), channel_id=1, source_target_pairs={{8,0},{16,8},{24,16},{9,1},{17,9},{25,17},{10,2},{18,10},{26,18},{... | collective-permute-start | bytes 1769480 | tf_op jit(solution)/shard_map/ppermute | solution.py:24
  23.2 52.7 %all-to-all-start = ((f32[8,576,32]{1,2,0:T(8,128)}), f32[8,576,32]{1,2,0:T(8,128)S(1)}, u32[]{:S(2)}, u32[]{:S(2)}) async-start(f32[8,576,32]{1,2,0:T(8,128)} %copy.179), calls=%async_computation | async-start | bytes 1310720 | tf_op jit(solution)/shard_map/all_to_all | solution.py:72
  28.2 12.2 %copy-start.47 = (s32[8,6]{0,1:T(8,128)}, s32[8,6]{0,1:T(8,128)S(1)}, u32[]{:S(2)}) copy-start(s32[8,6]{0,1:T(8,128)S(1)} %constant_dynamic-slice_fusion.7) | copy-start | bytes 580
  32.8 7.7 %collective-permute-start.2 = (f32[576,256]{1,0:T(8,128)}, f32[576,256]{1,0:T(8,128)S(1)}, u32[]{:S(2)}, u32[]{:S(2)}) collective-permute-start(f32[576,256]{1,0:T(8,128)} %collective-permute-done), channel_id=1, source_target_pairs={{8,16},{16,24},{9,17},{17,25},{10,18},{18,26},{11,19},{19,27},{12,... | collective-permute-start | bytes 1769480 | tf_op jit(solution)/shard_map/ppermute | solution.py:23
  34.1 37.8 %copy-start.49 = (pred[8,2]{1,0:T(8,128)(4,1)}, pred[8,2]{1,0:T(8,128)(4,1)S(1)}, u32[]{:S(2)}) copy-start(pred[8,2]{1,0:T(8,128)(4,1)S(1)} %copy.180) | copy-start | bytes 52
  37.7 16.4 %collective-permute-start.3 = (f32[576,256]{1,0:T(8,128)}, f32[576,256]{1,0:T(8,128)S(1)}, u32[]{:S(2)}, u32[]{:S(2)}) collective-permute-start(f32[576,256]{1,0:T(8,128)} %collective-permute-done.1), channel_id=1, source_target_pairs={{8,0},{16,8},{9,1},{17,9},{10,2},{18,10},{11,3},{19,11},{12,4},{20... | collective-permute-start | bytes 1769480 | tf_op jit(solution)/shard_map/ppermute | solution.py:24
  40.4 15.0 %collective-permute-start.4 = (f32[576,256]{1,0:T(8,128)S(1)}, f32[576,256]{1,0:T(8,128)S(1)}, u32[]{:S(2)}, u32[]{:S(2)}) collective-permute-start(f32[576,256]{1,0:T(8,128)S(1)} %collective-permute-done.2), channel_id=1, source_target_pairs={{16,24},{17,25},{18,26},{19,27},{20,28},{21,29},{22,30},{23,31}} | collective-permute-start | bytes 1769480 | tf_op jit(solution)/shard_map/ppermute | solution.py:23
  54.1 15.1 %collective-permute-start.5 = (f32[576,256]{1,0:T(8,128)S(1)}, f32[576,256]{1,0:T(8,128)S(1)}, u32[]{:S(2)}, u32[]{:S(2)}) collective-permute-start(f32[576,256]{1,0:T(8,128)S(1)} %collective-permute-done.3), channel_id=1, source_target_pairs={{8,0},{9,1},{10,2},{11,3},{12,4},{13,5},{14,6},{15,7}} | collective-permute-start | bytes 1769480 | tf_op jit(solution)/shard_map/ppermute | solution.py:24
  75.9 13.4 %copy-start.55 = (pred[8,2]{0,1:T(4,128)(4,1)S(1)}, pred[8,2]{0,1:T(4,128)(4,1)}, u32[]{:S(2)}) copy-start(pred[8,2]{0,1:T(4,128)(4,1)} %get-tuple-element.118) | copy-start | bytes 52
  75.9 41.9 %all-to-all-start.2 = ((f32[8,2,4,48,256]{4,3,2,1,0:T(8,128)}), f32[8,2,4,48,256]{4,3,2,1,0:T(8,128)}, u32[]{:S(2)}, u32[]{:S(2)}) async-start(f32[8,2,4,48,256]{4,3,2,1,0:T(8,128)} %broadcast_select_fusion.5), calls=%async_computation.2 | async-start | bytes 6291456 | tf_op jit(solution)/shard_map/all_to_all | solution.py:10
  83.5 17.5 %collective-permute-start.7 = (f32[576,256]{1,0:T(8,128)}, f32[576,256]{1,0:T(8,128)S(1)}, u32[]{:S(2)}, u32[]{:S(2)}) collective-permute-start(f32[576,256]{1,0:T(8,128)} %copy.188), channel_id=1, source_target_pairs={{8,0},{16,8},{24,16},{9,1},{17,9},{25,17},{10,2},{18,10},{26,18},{... | collective-permute-start | bytes 1769480 | tf_op jit(solution)/shard_map/ppermute | solution.py:24
  84.7 17.5 %collective-permute-start.6 = (f32[576,256]{1,0:T(8,128)}, f32[576,256]{1,0:T(8,128)S(1)}, u32[]{:S(2)}, u32[]{:S(2)}) collective-permute-start(f32[576,256]{1,0:T(8,128)} %copy.187), channel_id=1, source_target_pairs={{0,8},{8,16},{16,24},{1,9},{9,17},{17,25},{2,10},{10,18},{18,26},{... | collective-permute-start | bytes 1769480 | tf_op jit(solution)/shard_map/ppermute | solution.py:23
  96.6 29.8 %copy-start.54 = (pred[8,2]{0,1:T(4,128)(4,1)S(1)}, pred[8,2]{0,1:T(4,128)(4,1)}, u32[]{:S(2)}) copy-start(pred[8,2]{0,1:T(4,128)(4,1)} %get-tuple-element.78) | copy-start | bytes 52
  100.9 24.2 %copy-start.42 = (f32[576,256]{1,0:T(8,128)}, f32[576,256]{1,0:T(8,128)S(1)}, u32[]{:S(2)}) copy-start(f32[576,256]{1,0:T(8,128)S(1)} %collective-permute-done.7) | copy-start | bytes 1769476
  102.2 21.5 %copy-start.44 = (f32[576,256]{1,0:T(8,128)}, f32[576,256]{1,0:T(8,128)S(1)}, u32[]{:S(2)}) copy-start(f32[576,256]{1,0:T(8,128)S(1)} %collective-permute-done.6) | copy-start | bytes 1769476
  117.8 42.4 %all-to-all-start.3 = ((f32[8,2,4,48,256]{4,3,2,1,0:T(8,128)}), f32[8,2,4,48,256]{4,3,2,1,0:T(8,128)}, u32[]{:S(2)}, u32[]{:S(2)}) async-start(f32[8,2,4,48,256]{4,3,2,1,0:T(8,128)} %broadcast_select_fusion.4), calls=%async_computation.3 | async-start | bytes 6291456 | tf_op jit(solution)/shard_map/all_to_all | solution.py:10
  123.7 11.8 %collective-permute-start.8 = (f32[576,256]{1,0:T(8,128)S(1)}, f32[576,256]{1,0:T(8,128)}, u32[]{:S(2)}, u32[]{:S(2)}) collective-permute-start(f32[576,256]{1,0:T(8,128)S(1)} %collective-permute-done.6), channel_id=1, source_target_pairs={{8,16},{16,24},{9,17},{17,25},{10,18},{18,26},{11,19},{19,27},{12,... | collective-permute-start | bytes 1769480 | tf_op jit(solution)/shard_map/ppermute | solution.py:23
  125.2 17.4 %collective-permute-start.9 = (f32[576,256]{1,0:T(8,128)S(1)}, f32[576,256]{1,0:T(8,128)}, u32[]{:S(2)}, u32[]{:S(2)}) collective-permute-start(f32[576,256]{1,0:T(8,128)S(1)} %collective-permute-done.7), channel_id=1, source_target_pairs={{8,0},{16,8},{9,1},{17,9},{10,2},{18,10},{11,3},{19,11},{12,4},{20... | collective-permute-start | bytes 1769480 | tf_op jit(solution)/shard_map/ppermute | solution.py:24
  160.2 41.5 %all-to-all-start.4 = ((f32[8,2,4,48,256]{4,3,2,1,0:T(8,128)}), f32[8,2,4,48,256]{4,3,2,1,0:T(8,128)S(1)}, u32[]{:S(2)}, u32[]{:S(2)}) async-start(f32[8,2,4,48,256]{4,3,2,1,0:T(8,128)} %broadcast_select_fusion.3), calls=%async_computation.4 | async-start | bytes 6291456 | tf_op jit(solution)/shard_map/all_to_all | solution.py:10
  168.7 4.3 collective-permute-start.10
  169.4 17.6 %collective-permute-start.11 = (f32[576,256]{1,0:T(8,128)}, f32[576,256]{1,0:T(8,128)}, u32[]{:S(2)}, u32[]{:S(2)}) collective-permute-start(f32[576,256]{1,0:T(8,128)} %collective-permute-done.9), channel_id=1, source_target_pairs={{8,0},{9,1},{10,2},{11,3},{12,4},{13,5},{14,6},{15,7}} | collective-permute-start | bytes 1769480 | tf_op jit(solution)/shard_map/ppermute | solution.py:24
  214.2 42.3 %all-to-all-start.9 = ((f32[8,2,4,48,256]{4,3,2,1,0:T(8,128)}), f32[8,2,4,48,256]{4,3,2,1,0:T(8,128)}, u32[]{:S(2)}, u32[]{:S(2)}) async-start(f32[8,2,4,48,256]{4,3,2,1,0:T(8,128)} %broadcast_select_fusion), calls=%async_computation.9 | async-start | bytes 6291456 | tf_op jit(solution)/shard_map/all_to_all | solution.py:10
  256.6 42.6 %all-to-all-start.7 = ((f32[8,2,4,48,256]{4,3,2,1,0:T(8,128)}), f32[8,2,4,48,256]{4,3,2,1,0:T(8,128)}, u32[]{:S(2)}, u32[]{:S(2)}) async-start(f32[8,2,4,48,256]{4,3,2,1,0:T(8,128)} %broadcast_select_fusion.1), calls=%async_computation.7 | async-start | bytes 6291456 | tf_op jit(solution)/shard_map/all_to_all | solution.py:10
  299.1 44.6 %all-to-all-start.5 = ((f32[8,2,4,48,256]{4,3,2,1,0:T(8,128)}), f32[8,2,4,48,256]{4,3,2,1,0:T(8,128)}, u32[]{:S(2)}, u32[]{:S(2)}) async-start(f32[8,2,4,48,256]{4,3,2,1,0:T(8,128)} %broadcast_select_fusion.2), calls=%async_computation.5 | async-start | bytes 6291456 | tf_op jit(solution)/shard_map/all_to_all | solution.py:10
  307.9 12.9 %copy-start.15 = (f32[1,4,8,48,256]{4,3,2,1,0:T(8,128)}, f32[1,4,8,48,256]{4,3,2,1,0:T(8,128)S(1)}, u32[]{:S(2)}) copy-start(f32[1,4,8,48,256]{4,3,2,1,0:T(8,128)S(1)} %copy.216) | copy-start | bytes 4718596
  308.0 12.8 %copy-start.13 = (f32[1,4,8,48,256]{4,3,2,1,0:T(8,128)}, f32[1,4,8,48,256]{4,3,2,1,0:T(8,128)S(1)}, u32[]{:S(2)}) copy-start(f32[1,4,8,48,256]{4,3,2,1,0:T(8,128)S(1)} %copy.215) | copy-start | bytes 4718596
  343.8 42.4 %all-to-all-start.10 = ((f32[8,2,4,48,256]{4,3,2,1,0:T(8,128)}), f32[8,2,4,48,256]{4,3,2,1,0:T(8,128)}, u32[]{:S(2)}, u32[]{:S(2)}) async-start(f32[8,2,4,48,256]{4,3,2,1,0:T(8,128)} %copy.218), calls=%async_computation.10 | async-start | bytes 6291456 | tf_op jit(solution)/shard_map/all_to_all | solution.py:10
  350.7 12.2 %copy-start.18 = (f32[1,4,8,48,256]{4,3,2,1,0:T(8,128)}, f32[1,4,8,48,256]{4,3,2,1,0:T(8,128)S(1)}, u32[]{:S(2)}) copy-start(f32[1,4,8,48,256]{4,3,2,1,0:T(8,128)S(1)} %copy.200) | copy-start | bytes 4718596
  350.8 12.1 %copy-start.19 = (f32[1,4,8,48,256]{4,3,2,1,0:T(8,128)}, f32[1,4,8,48,256]{4,3,2,1,0:T(8,128)S(1)}, u32[]{:S(2)}) copy-start(f32[1,4,8,48,256]{4,3,2,1,0:T(8,128)S(1)} %copy.199) | copy-start | bytes 4718596
  362.9 9.7 %copy-start.23 = (f32[1,4,8,48,256]{4,3,2,1,0:T(8,128)S(1)}, f32[1,4,8,48,256]{4,3,2,1,0:T(8,128)}, u32[]{:S(2)}) copy-start(f32[1,4,8,48,256]{4,3,2,1,0:T(8,128)} %copy-done.22) | copy-start | bytes 4718596
  386.2 42.0 %all-to-all-start.6 = ((f32[8,2,4,48,256]{4,3,2,1,0:T(8,128)}), f32[8,2,4,48,256]{4,3,2,1,0:T(8,128)}, u32[]{:S(2)}, u32[]{:S(2)}) async-start(f32[8,2,4,48,256]{4,3,2,1,0:T(8,128)} %copy.202), calls=%async_computation.6 | async-start | bytes 6291456 | tf_op jit(solution)/shard_map/all_to_all | solution.py:10
  393.2 11.6 %copy-start.17 = (f32[1,4,8,48,256]{4,3,2,1,0:T(8,128)}, f32[1,4,8,48,256]{4,3,2,1,0:T(8,128)S(1)}, u32[]{:S(2)}) copy-start(f32[1,4,8,48,256]{4,3,2,1,0:T(8,128)S(1)} %copy.208) | copy-start | bytes 4718596
  428.2 41.6 %all-to-all-start.8 = ((f32[8,2,4,48,256]{4,3,2,1,0:T(8,128)}), f32[8,2,4,48,256]{4,3,2,1,0:T(8,128)}, u32[]{:S(2)}, u32[]{:S(2)}) async-start(f32[8,2,4,48,256]{4,3,2,1,0:T(8,128)} %copy.210), calls=%async_computation.8 | async-start | bytes 6291456 | tf_op jit(solution)/shard_map/all_to_all | solution.py:10
  455.4 18.3 %copy-start.48 = (s32[8,6]{0,1:T(8,128)S(1)}, s32[8,6]{0,1:T(8,128)}, u32[]{:S(2)}) copy-start(s32[8,6]{0,1:T(8,128)} %copy-done.47) | copy-start | bytes 580
  481.4 18.1 %slice-start.3 = ((s8[9437184]{0:T(1024)(128)(4,1)}), s8[1048576]{0:T(1024)(128)(4,1)S(1)}, s32[]{:S(2)}) async-start(s8[9437184]{0:T(1024)(128)(4,1)} %bitcast.312), calls=%async_computation.19 | async-start | bytes 2097152
  481.4 42.5 %all-to-all-start.11 = ((f32[8,2,4,48,256]{4,3,2,1,0:T(8,128)}), f32[8,2,4,48,256]{4,3,2,1,0:T(8,128)}, u32[]{:S(2)}, u32[]{:S(2)}) async-start(f32[8,2,4,48,256]{4,3,2,1,0:T(8,128)} %copy.225), calls=%async_computation.11 | async-start | bytes 6291456 | tf_op jit(solution)/shard_map/all_to_all | solution.py:10
  487.4 12.1 %slice-start.4 = ((s8[9437184]{0:T(1024)(128)(4,1)}), s8[4194304]{0:T(1024)(128)(4,1)S(1)}, s32[]{:S(2)}) async-start(s8[9437184]{0:T(1024)(128)(4,1)} %bitcast.312), calls=%async_computation.20 | async-start | bytes 8388608
  487.4 12.1 %slice-start.5 = ((s8[9437184]{0:T(1024)(128)(4,1)}), s8[4194304]{0:T(1024)(128)(4,1)S(1)}, s32[]{:S(2)}) async-start(s8[9437184]{0:T(1024)(128)(4,1)} %bitcast.312), calls=%async_computation.21 | async-start | bytes 8388608
  495.6 10.1 %collective-permute-start.13 = (f32[12,48,256]{2,1,0:T(8,128)S(1)}, f32[12,48,256]{2,1,0:T(8,128)}, u32[]{:S(2)}, u32[]{:S(2)}) collective-permute-start(f32[12,48,256]{2,1,0:T(8,128)S(1)} %copy.224), channel_id=1, source_target_pairs={{24,16},{25,17},{26,18},{27,19},{28,20},{29,21},{30,22},{31,23}} | collective-permute-start | bytes 1769480 | tf_op jit(solution)/shard_map/ppermute | solution.py:52
  497.1 14.4 %collective-permute-start.12 = (f32[12,48,256]{2,1,0:T(8,128)S(1)}, f32[12,48,256]{2,1,0:T(8,128)}, u32[]{:S(2)}, u32[]{:S(2)}) collective-permute-start(f32[12,48,256]{2,1,0:T(8,128)S(1)} %copy.223), channel_id=1, source_target_pairs={{0,8},{1,9},{2,10},{3,11},{4,12},{5,13},{6,14},{7,15}} | collective-permute-start | bytes 1769480 | tf_op jit(solution)/shard_map/ppermute | solution.py:51
  503.7 20.2 %copy-start.7 = (f32[4,48,256,12]{2,3,1,0:T(8,128)S(1)}, f32[4,48,256,12]{2,3,1,0:T(8,128)}, u32[]{:S(2)}) copy-start(f32[4,48,256,12]{2,3,1,0:T(8,128)} %copy-done.6) | copy-start | bytes 7077892
  529.3 17.5 %slice-start = ((s8[9437184]{0:T(1024)(128)(4,1)}), s8[1048576]{0:T(1024)(128)(4,1)S(1)}, s32[]{:S(2)}) async-start(s8[9437184]{0:T(1024)(128)(4,1)} %bitcast.308), calls=%async_computation.16 | async-start | bytes 2097152
  529.3 42.6 %all-to-all-start.12 = ((f32[8,2,4,48,256]{4,3,2,1,0:T(8,128)}), f32[8,2,4,48,256]{4,3,2,1,0:T(8,128)}, u32[]{:S(2)}, u32[]{:S(2)}) async-start(f32[8,2,4,48,256]{4,3,2,1,0:T(8,128)} %copy.230), calls=%async_computation.12 | async-start | bytes 6291456 | tf_op jit(solution)/shard_map/all_to_all | solution.py:10
  535.5 11.4 %slice-start.1 = ((s8[9437184]{0:T(1024)(128)(4,1)}), s8[4194304]{0:T(1024)(128)(4,1)S(1)}, s32[]{:S(2)}) async-start(s8[9437184]{0:T(1024)(128)(4,1)} %bitcast.308), calls=%async_computation.17 | async-start | bytes 8388608
  535.5 11.4 %slice-start.2 = ((s8[9437184]{0:T(1024)(128)(4,1)}), s8[4194304]{0:T(1024)(128)(4,1)S(1)}, s32[]{:S(2)}) async-start(s8[9437184]{0:T(1024)(128)(4,1)} %bitcast.308), calls=%async_computation.18 | async-start | bytes 8388608
  543.2 9.7 %collective-permute-start.15 = (f32[12,48,256]{2,1,0:T(8,128)S(1)}, f32[12,48,256]{2,1,0:T(8,128)}, u32[]{:S(2)}, u32[]{:S(2)}) collective-permute-start(f32[12,48,256]{2,1,0:T(8,128)S(1)} %copy.229), channel_id=1, source_target_pairs={{16,8},{24,16},{17,9},{25,17},{18,10},{26,18},{19,11},{27,19},{20,... | collective-permute-start | bytes 1769480 | tf_op jit(solution)/shard_map/ppermute | solution.py:52
  544.7 14.4 %collective-permute-start.14 = (f32[12,48,256]{2,1,0:T(8,128)S(1)}, f32[12,48,256]{2,1,0:T(8,128)}, u32[]{:S(2)}, u32[]{:S(2)}) collective-permute-start(f32[12,48,256]{2,1,0:T(8,128)S(1)} %copy.228), channel_id=1, source_target_pairs={{0,8},{8,16},{1,9},{9,17},{2,10},{10,18},{3,11},{11,19},{4,12},{12... | collective-permute-start | bytes 1769480 | tf_op jit(solution)/shard_map/ppermute | solution.py:51
  551.0 21.0 %copy-start.8 = (f32[4,48,256,12]{2,3,1,0:T(8,128)S(1)}, f32[4,48,256,12]{2,3,1,0:T(8,128)}, u32[]{:S(2)}) copy-start(f32[4,48,256,12]{2,3,1,0:T(8,128)} %copy-done.6) | copy-start | bytes 7077892
  577.3 41.5 %all-to-all-start.13 = ((f32[8,2,4,48,256]{4,3,2,1,0:T(8,128)}), f32[8,2,4,48,256]{4,3,2,1,0:T(8,128)S(1)}, u32[]{:S(2)}, u32[]{:S(2)}) async-start(f32[8,2,4,48,256]{4,3,2,1,0:T(8,128)} %copy.235), calls=%async_computation.13 | async-start | bytes 6291456 | tf_op jit(solution)/shard_map/all_to_all | solution.py:10
  585.4 17.7 %collective-permute-start.17 = (f32[12,48,256]{2,1,0:T(8,128)S(1)}, f32[12,48,256]{2,1,0:T(8,128)S(1)}, u32[]{:S(2)}, u32[]{:S(2)}) collective-permute-start(f32[12,48,256]{2,1,0:T(8,128)S(1)} %copy.234), channel_id=1, source_target_pairs={{8,0},{16,8},{24,16},{9,1},{17,9},{25,17},{10,2},{18,10},{26,18},{... | collective-permute-start | bytes 1769480 | tf_op jit(solution)/shard_map/ppermute | solution.py:52
  586.7 17.3 %collective-permute-start.16 = (f32[12,48,256]{2,1,0:T(8,128)S(1)}, f32[12,48,256]{2,1,0:T(8,128)}, u32[]{:S(2)}, u32[]{:S(2)}) collective-permute-start(f32[12,48,256]{2,1,0:T(8,128)S(1)} %copy.233), channel_id=1, source_target_pairs={{0,8},{8,16},{16,24},{1,9},{9,17},{17,25},{2,10},{10,18},{18,26},{... | collective-permute-start | bytes 1769480 | tf_op jit(solution)/shard_map/ppermute | solution.py:51
  624.9 14.4 %collective-permute-start.18 = (f32[12,48,256]{2,1,0:T(8,128)S(1)}, f32[12,48,256]{2,1,0:T(8,128)S(1)}, u32[]{:S(2)}, u32[]{:S(2)}) collective-permute-start(f32[12,48,256]{2,1,0:T(8,128)S(1)} %copy.242), channel_id=1, source_target_pairs={{0,8},{1,9},{2,10},{3,11},{4,12},{5,13},{6,14},{7,15}} | collective-permute-start | bytes 1769480 | tf_op jit(solution)/shard_map/ppermute | solution.py:51
  626.7 17.5 %collective-permute-start.21 = (f32[12,48,256]{2,1,0:T(8,128)S(1)}, f32[12,48,256]{2,1,0:T(8,128)S(1)}, u32[]{:S(2)}, u32[]{:S(2)}) collective-permute-start(f32[12,48,256]{2,1,0:T(8,128)S(1)} %copy.245), channel_id=1, source_target_pairs={{24,16},{25,17},{26,18},{27,19},{28,20},{29,21},{30,22},{31,23}} | collective-permute-start | bytes 1769480 | tf_op jit(solution)/shard_map/ppermute | solution.py:52
  639.6 25.8 %copy-start.37 = (f32[1,48,256,12]{2,3,1,0:T(8,128)S(1)}, f32[1,48,256,12]{2,3,1,0:T(8,128)}, u32[]{:S(2)}) copy-start(f32[1,48,256,12]{2,3,1,0:T(8,128)} %get-tuple-element.84) | copy-start | bytes 1769476
  639.6 25.8 %copy-start.41 = (f32[12,48,256]{2,1,0:T(8,128)S(1)}, f32[12,48,256]{2,1,0:T(8,128)}, u32[]{:S(2)}) copy-start(f32[12,48,256]{2,1,0:T(8,128)} %copy-done.40) | copy-start | bytes 1769476
  639.6 16.6 %collective-permute-start.19 = (f32[12,48,256]{2,1,0:T(8,128)S(1)}, f32[12,48,256]{2,1,0:T(8,128)S(1)}, u32[]{:S(2)}, u32[]{:S(2)}) collective-permute-start(f32[12,48,256]{2,1,0:T(8,128)S(1)} %fusion.24), channel_id=1, source_target_pairs={{0,8},{8,16},{1,9},{9,17},{2,10},{10,18},{3,11},{11,19},{4,12},{12... | collective-permute-start | bytes 1769480 | tf_op jit(solution)/shard_map/ppermute | solution.py:51
  644.6 18.1 %collective-permute-start.22 = (f32[12,48,256]{2,1,0:T(8,128)S(1)}, f32[12,48,256]{2,1,0:T(8,128)S(1)}, u32[]{:S(2)}, u32[]{:S(2)}) collective-permute-start(f32[12,48,256]{2,1,0:T(8,128)S(1)} %fusion.22), channel_id=1, source_target_pairs={{16,8},{24,16},{17,9},{25,17},{18,10},{26,18},{19,11},{27,19},{20,... | collective-permute-start | bytes 1769480 | tf_op jit(solution)/shard_map/ppermute | solution.py:52
  657.4 17.8 %collective-permute-start.20 = (f32[12,48,256]{2,1,0:T(8,128)}, f32[12,48,256]{2,1,0:T(8,128)}, u32[]{:S(2)}, u32[]{:S(2)}) collective-permute-start(f32[12,48,256]{2,1,0:T(8,128)} %fusion.23), channel_id=1, source_target_pairs={{0,8},{8,16},{16,24},{1,9},{9,17},{17,25},{2,10},{10,18},{18,26},{... | collective-permute-start | bytes 1769480 | tf_op jit(solution)/shard_map/ppermute | solution.py:51
  663.8 15.6 %collective-permute-start.23 = (f32[12,48,256]{2,1,0:T(8,128)}, f32[12,48,256]{2,1,0:T(8,128)}, u32[]{:S(2)}, u32[]{:S(2)}) collective-permute-start(f32[12,48,256]{2,1,0:T(8,128)} %fusion.21), channel_id=1, source_target_pairs={{8,0},{16,8},{24,16},{9,1},{17,9},{25,17},{10,2},{18,10},{26,18},{... | collective-permute-start | bytes 1769480 | tf_op jit(solution)/shard_map/ppermute | solution.py:52
  671.0 14.2 %all-to-all-start.14 = ((f32[576,8,32]{0,2,1:T(8,128)}), f32[576,8,32]{0,2,1:T(8,128)}, u32[]{:S(2)}, u32[]{:S(2)}) async-start(f32[576,8,32]{0,2,1:T(8,128)} %copy.265), calls=%async_computation.14 | async-start | bytes 1310720 | tf_op jit(solution)/shard_map/all_to_all | solution.py:129
  685.3 13.5 %all-to-all-start.15 = ((f32[576,8,32]{0,2,1:T(8,128)}), f32[576,8,32]{0,2,1:T(8,128)S(1)}, u32[]{:S(2)}, u32[]{:S(2)}) async-start(f32[576,8,32]{0,2,1:T(8,128)} %copy.266), calls=%async_computation.15 | async-start | bytes 1310720 | tf_op jit(solution)/shard_map/all_to_all | solution.py:129
  689.0 11.4 %copy-start.1 = (s32[32,6]{0,1:T(8,128)S(1)}, s32[32,6]{0,1:T(8,128)}, u32[]{:S(2)}) copy-start(s32[32,6]{0,1:T(8,128)} %param.6) | copy-start | bytes 2308
  (37 other events, 155.1 us)
